TPU v7x, 256 devices: a whole 4x4x8 slice. The times are simulated.
256 devices in a mesh: lat: 16 (over y_hi, x, core), lon: 16 (over z, y_lo).
Axes of the slice: x: 4, y: 4 (y_hi: 2, y_lo: 2; y = y_hi * 2 + y_lo), z: 8, core: 2. Of those that a mesh axis runs over, the one named last changes fastest.
Arguments:
- queries: bfloat16 [256, 256, 1024], P('lat', 'lon'), may hold values from -80 to 80
- keys: bfloat16 [256, 256, 1024], P('lat', 'lon'), may hold values from -6 to 6
- values: bfloat16 [256, 256, 1024], P('lat', 'lon'), may hold values from -6 to 6
- grad_out: bfloat16 [256, 256, 1024], P('lat', 'lon'), may hold values from -6 to 6
- fold_cols: int32 [2, 256], replicated, may hold values from 0 to 255, as said below
Outputs:
- grad_queries: bfloat16 [256, 256, 1024], P('lat', 'lon')
- grad_keys: bfloat16 [256, 256, 1024], P('lat', 'lon')
- grad_values: bfloat16 [256, 256, 1024], P('lat', 'lon')
Inputs may be any that keep to these rules, and one draw needn't show every extreme that they name: Each row of fold_cols maps, for every block b of 16 columns, the runs [b * 16, b * 16 + 4), [b * 16 + 4, (b + 1) * 16 - 4) and [(b + 1) * 16 - 4, (b + 1) * 16) one to one onto the same runs of the block 8 blocks further on the loop.
All inputs are finite; a program needn't handle non-finite values.
Results may differ from a plain program's by a relative error of at most 0.0075.
Values may be sent and summed in bfloat16 or wider, within the bound.
No kernel may reach another device: no remote copies, remote signals or barrier semaphores. Data moves between devices by JAX's collectives and lax.ppermute only.
A program may use at most 128 MiB of HBM per device.

v0:
```python
import jax
import jax.numpy as jnp
from jax import lax
from jax.experimental import pallas as pl
from jax.experimental.pallas import tpu as pltpu
from jax.sharding import PartitionSpec as P

HEADS = 16
HEAD_DIM = 64
RADIUS = 4

SPAN = 2 * RADIUS + 1
TILE_ROWS = 8
LANES = 128


def attention_kernel(width, q_ref, g_ref, k_ref, v_ref, dq_ref, dk_ref, dv_ref, bias_ref):
    scale = HEAD_DIM ** (-0.5)
    ext_w = width + 2 * RADIUS
    tq = TILE_ROWS * width
    tk = (TILE_ROWS + 2 * RADIUS) * ext_w
    step_k = TILE_ROWS * ext_w
    tiles = q_ref.shape[0] // tq
    pairs = q_ref.shape[1] // LANES

    qi = lax.broadcasted_iota(jnp.int32, (tq, tk), 0).astype(jnp.float32)
    ki = lax.broadcasted_iota(jnp.int32, (tq, tk), 1).astype(jnp.float32)
    qr = jnp.floor((qi + 0.5) * (1.0 / width))
    qc = qi - width * qr
    kr = jnp.floor((ki + 0.5) * (1.0 / ext_w))
    kc = ki - ext_w * kr
    dr = kr - qr
    dc = kc - qc
    ok = (dr >= 0) & (dr <= 2 * RADIUS) & (dc >= 0) & (dc <= 2 * RADIUS)
    bias_ref[...] = jnp.where(ok, 0.0, -jnp.inf).astype(jnp.float32)

    nt = (((1,), (1,)), ((), ()))
    tn = (((0,), (0,)), ((), ()))

    def head(qh, gh, kp, vp):
        s = lax.dot_general(qh, kp, nt, preferred_element_type=jnp.float32) * scale + bias_ref[...]
        m = jnp.max(s, axis=1, keepdims=True)
        e = jnp.exp(s - m)
        total = jnp.sum(e, axis=1, keepdims=True)
        w = e * (1.0 / total)
        dw = lax.dot_general(gh, vp, nt, preferred_element_type=jnp.float32)
        corr = jnp.sum(w * dw, axis=1, keepdims=True)
        ds = (w * (dw - corr)).astype(jnp.bfloat16)
        return ds, w.astype(jnp.bfloat16)

    def body(p, carry):
        lanes = pl.ds(pl.multiple_of(p * LANES, LANES), LANES)
        for t in range(tiles):
            qp = q_ref[pl.ds(t * tq, tq), lanes]
            gp = g_ref[pl.ds(t * tq, tq), lanes]
            kp = k_ref[pl.ds(t * step_k, tk), lanes]
            vp = v_ref[pl.ds(t * step_k, tk), lanes]
            lo = lax.broadcasted_iota(jnp.int32, qp.shape, 1) < HEAD_DIM
            zero = jnp.zeros_like(qp)
            qa = jnp.where(lo, qp, zero)
            qb = jnp.where(lo, zero, qp)
            ga = jnp.where(lo, gp, zero)
            gb = jnp.where(lo, zero, gp)
            dsa, wa = head(qa, ga, kp, vp)
            dsb, wb = head(qb, gb, kp, vp)
            dqa = jnp.dot(dsa, kp, preferred_element_type=jnp.float32)
            dqb = jnp.dot(dsb, kp, preferred_element_type=jnp.float32)
            dq = jnp.where(lo, dqa, dqb) * scale
            dq_ref[pl.ds(t * tq, tq), lanes] = dq.astype(dq_ref.dtype)
            dk = (
                lax.dot_general(dsa, qa, tn, preferred_element_type=jnp.float32)
                + lax.dot_general(dsb, qb, tn, preferred_element_type=jnp.float32)
            ) * scale
            dv = lax.dot_general(wa, ga, tn, preferred_element_type=jnp.float32) + lax.dot_general(
                wb, gb, tn, preferred_element_type=jnp.float32
            )
            if t == 0:
                dk_ref[pl.ds(0, tk), lanes] = dk
                dv_ref[pl.ds(0, tk), lanes] = dv
            else:
                shared = tk - step_k
                base = t * step_k
                dk_ref[pl.ds(base, shared), lanes] += dk[:shared]
                dv_ref[pl.ds(base, shared), lanes] += dv[:shared]
                dk_ref[pl.ds(base + shared, step_k), lanes] = dk[shared:]
                dv_ref[pl.ds(base + shared, step_k), lanes] = dv[shared:]
        return carry

    lax.fori_loop(0, pairs, body, 0)


def attention_core(q2, g2, k2, v2, width):
    cells, features = q2.shape
    ext_cells = k2.shape[0]
    ext_w = width + 2 * RADIUS
    tq = TILE_ROWS * width
    tk = (TILE_ROWS + 2 * RADIUS) * ext_w
    tiles = cells // tq
    flops = 10 * 2 * tq * tk * LANES * (features // LANES) * tiles
    vmem = pl.BlockSpec(memory_space=pltpu.VMEM)
    return pl.pallas_call(
        lambda *refs: attention_kernel(width, *refs),
        out_shape=(
            jax.ShapeDtypeStruct((cells, features), jnp.bfloat16),
            jax.ShapeDtypeStruct((ext_cells, features), jnp.float32),
            jax.ShapeDtypeStruct((ext_cells, features), jnp.float32),
        ),
        in_specs=[vmem] * 4,
        out_specs=(vmem, vmem, vmem),
        scratch_shapes=[pltpu.VMEM((tq, tk), jnp.float32)],
        cost_estimate=pl.CostEstimate(
            flops=flops,
            transcendentals=2 * tq * tk * HEADS * tiles,
            bytes_accessed=2 * (2 * cells * features) + 2 * (2 * ext_cells * features)
            + 2 * cells * features + 2 * 4 * ext_cells * features,
        ),
        name="neighbourhood_attention_bwd",
    )(q2, g2, k2, v2)


def on_device(queries, keys, values, grad_out, fold_cols):
    height, width, features = queries.shape
    n_lat = lax.axis_size("lat")
    n_lon = lax.axis_size("lon")
    half = n_lon // 2
    i = lax.axis_index("lat")
    j = lax.axis_index("lon")
    at_north = i == 0
    at_south = i == n_lat - 1
    partner_j = (j + half) % n_lon
    r = RADIUS

    def flat(a, b):
        return a * n_lon + b

    down_pairs = [(flat(a, b), flat(a + 1, b)) for a in range(n_lat - 1) for b in range(n_lon)]
    up_pairs = [(flat(a + 1, b), flat(a, b)) for a in range(n_lat - 1) for b in range(n_lon)]
    pole_pairs = [(flat(a, b), flat(a, (b + half) % n_lon)) for a in (0, n_lat - 1) for b in range(n_lon)]
    right_pairs = [(b, (b + 1) % n_lon) for b in range(n_lon)]
    left_pairs = [(b, (b - 1) % n_lon) for b in range(n_lon)]
    both = ("lat", "lon")

    own_cols = j * width + jnp.arange(width)
    fold_row = jnp.where(at_north, fold_cols[0], fold_cols[1])
    fold_idx = jnp.take(fold_row, own_cols) - partner_j * width
    partner_cols = partner_j * width + jnp.arange(width)
    unfold_idx = (
        jnp.zeros((width,), jnp.int32)
        .at[jnp.take(fold_row, partner_cols) - j * width]
        .set(jnp.arange(width, dtype=jnp.int32))
    )

    kv = jnp.stack([keys, values])
    top_send = kv[:, :r]
    bottom_send = kv[:, height - r :]
    from_above = lax.ppermute(bottom_send, both, down_pairs)
    from_below = lax.ppermute(top_send, both, up_pairs)
    pole_send = jnp.where(at_north, top_send, bottom_send)
    pole_recv = lax.ppermute(pole_send, both, pole_pairs)
    pole_rows = jnp.take(pole_recv, fold_idx, axis=2)[:, ::-1]
    top = jnp.where(at_north, pole_rows, from_above)
    bottom = jnp.where(at_south, pole_rows, from_below)
    colfield = jnp.concatenate([top, kv, bottom], axis=1)
    from_left = lax.ppermute(colfield[:, :, width - r :], "lon", right_pairs)
    from_right = lax.ppermute(colfield[:, :, :r], "lon", left_pairs)
    ext = jnp.concatenate([from_left, colfield, from_right], axis=2)
    ext_rows = height + 2 * r
    ext_w = width + 2 * r
    ext = ext.reshape(2, ext_rows * ext_w, features)

    dq, dk, dv = attention_core(
        queries.reshape(height * width, features),
        grad_out.reshape(height * width, features),
        ext[0],
        ext[1],
        width,
    )

    dkv = jnp.stack([dk, dv]).reshape(2, ext_rows, ext_w, features)
    back_right = lax.ppermute(dkv[:, :, :r].astype(jnp.bfloat16), "lon", left_pairs)
    back_left = lax.ppermute(dkv[:, :, ext_w - r :].astype(jnp.bfloat16), "lon", right_pairs)
    col = jnp.concatenate(
        [
            dkv[:, :, r : 2 * r] + back_left.astype(jnp.float32),
            dkv[:, :, 2 * r : width],
            dkv[:, :, width : width + r] + back_right.astype(jnp.float32),
        ],
        axis=2,
    )
    top_g = col[:, :r].astype(jnp.bfloat16)
    bottom_g = col[:, ext_rows - r :].astype(jnp.bfloat16)
    up_recv = lax.ppermute(top_g, both, up_pairs)
    down_recv = lax.ppermute(bottom_g, both, down_pairs)
    pole_g = lax.ppermute(jnp.where(at_north, top_g, bottom_g), both, pole_pairs)
    unfolded = jnp.take(pole_g[:, ::-1], unfold_idx, axis=2)
    add_top = jnp.where(at_north, unfolded, down_recv).astype(jnp.float32)
    add_bottom = jnp.where(at_south, unfolded, up_recv).astype(jnp.float32)
    grads = jnp.concatenate(
        [
            col[:, r : 2 * r] + add_top,
            col[:, 2 * r : height],
            col[:, height : height + r] + add_bottom,
        ],
        axis=1,
    ).astype(jnp.bfloat16)
    return (dq.reshape(height, width, features), grads[0], grads[1])


def solution(mesh):
    placed = (
        P("lat", "lon", None),
        P("lat", "lon", None),
        P("lat", "lon", None),
        P("lat", "lon", None),
        P(),
    )
    return jax.shard_map(
        on_device,
        mesh=mesh,
        in_specs=placed,
        out_specs=(P("lat", "lon", None), P("lat", "lon", None), P("lat", "lon", None)),
        check_vma=False,
    )
```

profile of v0, /device:TPU:32, one launch (start us, length us, event | category | flops | bytes accessed | tf_op | source)
XLA Modules:
  0.0 115.9 jit_solution(16547653167514272484)
XLA Ops:
  0.6 1.8 %copy_bitcast_fusion = (bf16[1,16,16,1024]{3,1,0,2:T(8,128)(2,1)S(1)}, bf16[1,16,16,1024]{3,1,0,2:T(8,128)(2,1)S(1)}) fusion(bf16[16,16,1024]{2,1,0:T(8,128)(2,1)} %param.11, bf16[16,16,1024]{2,1,0:T(8,128)(2,1)} %param.10), kind=kLoop, calls=%fused_computation.18 | loop fusion | bytes 2097152 | tf_op jit(solution)/shard_map/stack | solution.py:153
  2.8 8.2 %collective-permute-start = (bf16[2,4,16,1024]{3,1,0,2:T(4,128)(2,1)S(1)}, bf16[2,4,16,1024]{3,1,0,2:T(4,128)(2,1)S(1)}, u32[]{:S(2)}, u32[]{:S(2)}) collective-permute-start(bf16[2,4,16,1024]{3,1,0,2:T(4,128)(2,1)S(1)} %get-tuple-element.16), channel_id=1, source_target_pairs={{0,8},{1,9},{2,10},{3,11},{4,12},{5,13},{6,14},{7,15},{8,0},{9,1},... | collective-permute-start | bytes 786440 | tf_op jit(solution)/shard_map/ppermute | solution.py:159
  11.1 1.3 %collective-permute-start.1 = (bf16[2,4,16,1024]{3,1,0,2:T(4,128)(2,1)S(1)}, bf16[2,4,16,1024]{3,1,0,2:T(4,128)(2,1)S(1)}, u32[]{:S(2)}, u32[]{:S(2)}) collective-permute-start(bf16[2,4,16,1024]{3,1,0,2:T(4,128)(2,1)S(1)} %get-tuple-element.17), channel_id=1, source_target_pairs={{0,16},{1,17},{2,18},{3,19},{4,20},{5,21},{6,22},{7,23},{8,24},{9,... | collective-permute-start | bytes 786440 | tf_op jit(solution)/shard_map/ppermute | solution.py:156
  12.4 1.3 %collective-permute-start.2 = (bf16[2,4,16,1024]{3,1,0,2:T(4,128)(2,1)S(1)}, bf16[2,4,16,1024]{3,1,0,2:T(4,128)(2,1)S(1)}, u32[]{:S(2)}, u32[]{:S(2)}) collective-permute-start(bf16[2,4,16,1024]{3,1,0,2:T(4,128)(2,1)S(1)} %get-tuple-element.18), channel_id=1, source_target_pairs={{16,0},{17,1},{18,2},{19,3},{20,4},{21,5},{22,6},{23,7},{24,8},{25... | collective-permute-start | bytes 786440 | tf_op jit(solution)/shard_map/ppermute | solution.py:157
  13.7 0.7 gather_fusion.2
  15.1 3.1 %collective-permute-done = bf16[2,4,16,1024]{3,1,0,2:T(4,128)(2,1)S(1)} collective-permute-done((bf16[2,4,16,1024]{3,1,0,2:T(4,128)(2,1)S(1)}, bf16[2,4,16,1024]{3,1,0,2:T(4,128)(2,1)S(1)}, u32[]{:S(2)}, u32[]{:S(2)}) %collective-permute-start) | collective-permute-done | bytes 262176 | tf_op jit(solution)/shard_map/ppermute | solution.py:159
  18.3 0.8 gather_fusion.1
  19.3 0.7 rev.6
  20.5 1.2 collective-permute-start.4
  21.6 0.9 collective-permute-start.3
  23.2 14.8 %collective-permute-done.4 = bf16[2,24,4,1024]{3,1,0,2:T(8,128)(2,1)S(1)} collective-permute-done((bf16[2,24,4,1024]{3,1,0,2:T(8,128)(2,1)S(1)}, bf16[2,24,4,1024]{3,1,0,2:T(8,128)(2,1)S(1)}, u32[]{:S(2)}, u32[]{:S(2)}) %collective-permute-start.4) | collective-permute-done | bytes 393248 | tf_op jit(solution)/shard_map/ppermute | solution.py:165
  38.0 1.1 pad_maximum_fusion.1
  39.4 1.7 %copy.11 = bf16[1,24,24,1024]{3,2,1,0:T(8,128)(2,1)} copy(bf16[1,24,24,1024]{3,1,0,2:T(8,128)(2,1)S(1)} %get-tuple-element.26) | data formatting | bytes 2359296 | tf_op jit(solution)/shard_map/slice | solution.py:174
  41.1 1.7 %copy.12 = bf16[1,24,24,1024]{3,2,1,0:T(8,128)(2,1)} copy(bf16[1,24,24,1024]{3,1,0,2:T(8,128)(2,1)S(1)} %get-tuple-element.25) | data formatting | bytes 2359296 | tf_op jit(solution)/shard_map/slice | solution.py:175
  42.8 17.4 %neighbourhood_attention_bwd.1 = (bf16[256,1024]{1,0:T(8,128)(2,1)}, f32[576,1024]{1,0:T(8,128)}, f32[576,1024]{1,0:T(8,128)}) custom-call(bf16[256,1024]{1,0:T(8,128)(2,1)} %bitcast.43, bf16[256,1024]{1,0:T(8,128)(2,1)} %bitcast.44, bf16[576,1024]{1,0:T(8,128)(2,1)} %bitcast.38, bf16[576,1024]{1,0:T(8,128)(2,1)} %bitcast.39), custom_call_target="tpu_custom_call" | custom-call | flops 2013265920 | bytes 8650752 | tf_op jit(solution)/shard_map/neighbourhood_attention_bwd/pallas_call | solution.py:101
  60.2 3.2 %copy_dynamic-update-slice_fusion.1 = f32[2,24,24,1024]{3,1,0,2:T(8,128)S(1)} fusion(f32[1,24,24,1024]{3,2,1,0:T(8,128)} %bitcast.37), kind=kLoop, calls=%fused_computation.8 | loop fusion | bytes 4718592
  63.4 1.4 %copy_dynamic-update-slice_fusion = f32[2,24,24,1024]{3,1,0,2:T(8,128)S(1)} fusion(f32[2,24,24,1024]{3,1,0,2:T(8,128)S(1)} %copy_dynamic-update-slice_fusion.1, f32[1,24,24,1024]{3,2,1,0:T(8,128)S(1)} %bitcast.36), kind=kLoop, calls=%fused_computation.7 | loop fusion | bytes 4718592 | tf_op jit(solution)/shard_map/stack | solution.py:179
  65.2 2.1 %collective-permute-start.5 = (bf16[2,24,4,1024]{3,1,0,2:T(8,128)(2,1)S(1)}, bf16[2,24,4,1024]{3,1,0,2:T(8,128)(2,1)S(1)}, u32[]{:S(2)}, u32[]{:S(2)}) collective-permute-start(bf16[2,24,4,1024]{3,1,0,2:T(8,128)(2,1)S(1)} %get-tuple-element.23), channel_id=1, source_target_pairs={{0,1},{1,2},{2,3},{3,4},{4,5},{5,6},{6,7},{7,8},{8,9},{9,10},{10,1... | collective-permute-start | bytes 1179656 | tf_op jit(solution)/shard_map/ppermute | solution.py:181
  67.3 1.2 %collective-permute-start.6 = (bf16[2,24,4,1024]{3,1,0,2:T(8,128)(2,1)S(1)}, bf16[2,24,4,1024]{3,1,0,2:T(8,128)(2,1)S(1)}, u32[]{:S(2)}, u32[]{:S(2)}) collective-permute-start(bf16[2,24,4,1024]{3,1,0,2:T(8,128)(2,1)S(1)} %get-tuple-element.24), channel_id=1, source_target_pairs={{0,15},{1,0},{2,1},{3,2},{4,3},{5,4},{6,5},{7,6},{8,7},{9,8},{10,9... | collective-permute-start | bytes 1179656 | tf_op jit(solution)/shard_map/ppermute | solution.py:180
  68.7 15.2 %collective-permute-done.5 = bf16[2,24,4,1024]{3,1,0,2:T(8,128)(2,1)S(1)} collective-permute-done((bf16[2,24,4,1024]{3,1,0,2:T(8,128)(2,1)S(1)}, bf16[2,24,4,1024]{3,1,0,2:T(8,128)(2,1)S(1)}, u32[]{:S(2)}, u32[]{:S(2)}) %collective-permute-start.5) | collective-permute-done | bytes 393248 | tf_op jit(solution)/shard_map/ppermute | solution.py:181
  83.8 2.1 %collective-permute-done.6 = bf16[2,24,4,1024]{3,1,0,2:T(8,128)(2,1)S(1)} collective-permute-done((bf16[2,24,4,1024]{3,1,0,2:T(8,128)(2,1)S(1)}, bf16[2,24,4,1024]{3,1,0,2:T(8,128)(2,1)S(1)}, u32[]{:S(2)}, u32[]{:S(2)}) %collective-permute-start.6) | collective-permute-done | bytes 393248 | tf_op jit(solution)/shard_map/ppermute | solution.py:180
  86.5 1.3 %fusion.7 = (bf16[2,4,16,1024]{3,1,0,2:T(4,128)(2,1)}, bf16[2,4,16,1024]{3,1,0,2:T(4,128)(2,1)S(1)}, bf16[2,4,16,1024]{3,1,0,2:T(4,128)(2,1)}) fusion(bf16[2,24,16,1024]{3,1,0,2:T(8,128)(2,1)S(1)} %fusion.4, pred[]{:T(512)S(6)} %eq.8), kind=kLoop, calls=%fused_computation.53 | loop fusion | flops 131072 | bytes 1310721 | tf_op jit(solution)/shard_map/slice | solution.py:191
  87.8 2.6 %collective-permute-start.8 = (bf16[2,4,16,1024]{3,1,0,2:T(4,128)(2,1)}, bf16[2,4,16,1024]{3,1,0,2:T(4,128)(2,1)}, u32[]{:S(2)}, u32[]{:S(2)}) collective-permute-start(bf16[2,4,16,1024]{3,1,0,2:T(4,128)(2,1)} %get-tuple-element.27), channel_id=1, source_target_pairs={{0,16},{1,17},{2,18},{3,19},{4,20},{5,21},{6,22},{7,23},{8,24},{9,... | collective-permute-start | bytes 786440 | tf_op jit(solution)/shard_map/ppermute | solution.py:193
  90.4 4.1 %collective-permute-start.7 = (bf16[2,4,16,1024]{3,1,0,2:T(4,128)(2,1)S(1)}, bf16[2,4,16,1024]{3,1,0,2:T(4,128)(2,1)}, u32[]{:S(2)}, u32[]{:S(2)}) collective-permute-start(bf16[2,4,16,1024]{3,1,0,2:T(4,128)(2,1)S(1)} %get-tuple-element.28), channel_id=1, source_target_pairs={{0,8},{1,9},{2,10},{3,11},{4,12},{5,13},{6,14},{7,15},{8,0},{9,1},... | collective-permute-start | bytes 786440 | tf_op jit(solution)/shard_map/ppermute | solution.py:194
  94.5 1.3 %collective-permute-start.9 = (bf16[2,4,16,1024]{3,1,0,2:T(4,128)(2,1)}, bf16[2,4,16,1024]{3,1,0,2:T(4,128)(2,1)}, u32[]{:S(2)}, u32[]{:S(2)}) collective-permute-start(bf16[2,4,16,1024]{3,1,0,2:T(4,128)(2,1)} %get-tuple-element.29), channel_id=1, source_target_pairs={{16,0},{17,1},{18,2},{19,3},{20,4},{21,5},{22,6},{23,7},{24,8},{25... | collective-permute-start | bytes 786440 | tf_op jit(solution)/shard_map/ppermute | solution.py:192
  96.1 9.4 %collective-permute-done.7 = bf16[2,4,16,1024]{3,1,0,2:T(4,128)(2,1)} collective-permute-done((bf16[2,4,16,1024]{3,1,0,2:T(4,128)(2,1)S(1)}, bf16[2,4,16,1024]{3,1,0,2:T(4,128)(2,1)}, u32[]{:S(2)}, u32[]{:S(2)}) %collective-permute-start.7) | collective-permute-done | bytes 262176 | tf_op jit(solution)/shard_map/ppermute | solution.py:194
  105.5 3.4 %rev.7 = bf16[2,4,16,1024]{3,1,0,2:T(4,128)(2,1)S(1)} reverse(bf16[2,4,16,1024]{3,1,0,2:T(4,128)(2,1)} %collective-permute-done.7), dimensions={1} | reverse | bytes 524288 | tf_op jit(solution)/shard_map/rev | solution.py:195
  108.9 0.8 copy.15
  109.7 1.7 %gather_fusion.3 = bf16[16,2,4,1024]{3,2,1,0:T(4,128)(2,1)S(1)} fusion(bf16[2,4,16,1024]{3,1,2,0:T(4,128)(2,1)} %copy.15, s32[1024]{0:T(1024)S(1)} %pad_clamp_fusion), kind=kCustom, calls=%fused_computation.3.clone | custom fusion | bytes 524352 | tf_op jit(solution)/shard_map/jit(_take)/gather | solution.py:195
  111.5 1.5 %fusion.1 = (bf16[2,4,16,1024]{3,1,0,2:T(4,128)(2,1)S(1)}, bf16[2,4,16,1024]{3,1,0,2:T(4,128)(2,1)S(1)}) fusion(f32[2,24,16,1024]{3,1,0,2:T(8,128)S(1)} %pad_maximum_fusion, bf16[2,4,16,1024]{3,1,0,2:T(4,128)(2,1)} %collective-permute-done.8, pred[]{:T(512)S(6)} %eq.8, bf16[16,2,4,1024]{3,2,1,0:T(4,128)(2,1)S(1)} %gather_fusion.3, ...), kind=kLoop, calls=%fused_computation.17 | loop fusion | flops 1179648 | bytes 2359314 | tf_op jit(solution)/shard_map/convert
  113.7 1.1 copy.16
  114.8 1.1 copy.17
  (40 shorter events, 4.8 us)
Async XLA Ops:
  0.6 13.1 %copy-start.2 = (s32[2,256]{1,0:T(2,128)S(1)}, s32[2,256]{1,0:T(2,128)}, u32[]{:S(2)}) copy-start(s32[2,256]{1,0:T(2,128)} %param.13) | copy-start | bytes 6148
  2.8 15.4 %collective-permute-start = (bf16[2,4,16,1024]{3,1,0,2:T(4,128)(2,1)S(1)}, bf16[2,4,16,1024]{3,1,0,2:T(4,128)(2,1)S(1)}, u32[]{:S(2)}, u32[]{:S(2)}) collective-permute-start(bf16[2,4,16,1024]{3,1,0,2:T(4,128)(2,1)S(1)} %get-tuple-element.16), channel_id=1, source_target_pairs={{0,8},{1,9},{2,10},{3,11},{4,12},{5,13},{6,14},{7,15},{8,0},{9,1},... | collective-permute-start | bytes 786440 | tf_op jit(solution)/shard_map/ppermute | solution.py:159
  11.1 9.0 %collective-permute-start.1 = (bf16[2,4,16,1024]{3,1,0,2:T(4,128)(2,1)S(1)}, bf16[2,4,16,1024]{3,1,0,2:T(4,128)(2,1)S(1)}, u32[]{:S(2)}, u32[]{:S(2)}) collective-permute-start(bf16[2,4,16,1024]{3,1,0,2:T(4,128)(2,1)S(1)} %get-tuple-element.17), channel_id=1, source_target_pairs={{0,16},{1,17},{2,18},{3,19},{4,20},{5,21},{6,22},{7,23},{8,24},{9,... | collective-permute-start | bytes 786440 | tf_op jit(solution)/shard_map/ppermute | solution.py:156
  12.4 7.7 %collective-permute-start.2 = (bf16[2,4,16,1024]{3,1,0,2:T(4,128)(2,1)S(1)}, bf16[2,4,16,1024]{3,1,0,2:T(4,128)(2,1)S(1)}, u32[]{:S(2)}, u32[]{:S(2)}) collective-permute-start(bf16[2,4,16,1024]{3,1,0,2:T(4,128)(2,1)S(1)} %get-tuple-element.18), channel_id=1, source_target_pairs={{16,0},{17,1},{18,2},{19,3},{20,4},{21,5},{22,6},{23,7},{24,8},{25... | collective-permute-start | bytes 786440 | tf_op jit(solution)/shard_map/ppermute | solution.py:157
  20.5 17.5 %collective-permute-start.4 = (bf16[2,24,4,1024]{3,1,0,2:T(8,128)(2,1)S(1)}, bf16[2,24,4,1024]{3,1,0,2:T(8,128)(2,1)S(1)}, u32[]{:S(2)}, u32[]{:S(2)}) collective-permute-start(bf16[2,24,4,1024]{3,1,0,2:T(8,128)(2,1)S(1)} %get-tuple-element.31), channel_id=1, source_target_pairs={{0,15},{1,0},{2,1},{3,2},{4,3},{5,4},{6,5},{7,6},{8,7},{9,8},{10,9... | collective-permute-start | bytes 1179656 | tf_op jit(solution)/shard_map/ppermute | solution.py:165
  21.6 16.4 %collective-permute-start.3 = (bf16[2,24,4,1024]{3,1,0,2:T(8,128)(2,1)S(1)}, bf16[2,24,4,1024]{3,1,0,2:T(8,128)(2,1)S(1)}, u32[]{:S(2)}, u32[]{:S(2)}) collective-permute-start(bf16[2,24,4,1024]{3,1,0,2:T(8,128)(2,1)S(1)} %get-tuple-element.30), channel_id=1, source_target_pairs={{0,1},{1,2},{2,3},{3,4},{4,5},{5,6},{6,7},{7,8},{8,9},{9,10},{10,1... | collective-permute-start | bytes 1179656 | tf_op jit(solution)/shard_map/ppermute | solution.py:164
  60.2 3.2 %copy-start.1 = (f32[576,1024]{1,0:T(8,128)S(1)}, f32[576,1024]{1,0:T(8,128)}, u32[]{:S(2)}) copy-start(f32[576,1024]{1,0:T(8,128)} %get-tuple-element.10) | copy-start | bytes 7077892
  65.2 18.6 %collective-permute-start.5 = (bf16[2,24,4,1024]{3,1,0,2:T(8,128)(2,1)S(1)}, bf16[2,24,4,1024]{3,1,0,2:T(8,128)(2,1)S(1)}, u32[]{:S(2)}, u32[]{:S(2)}) collective-permute-start(bf16[2,24,4,1024]{3,1,0,2:T(8,128)(2,1)S(1)} %get-tuple-element.23), channel_id=1, source_target_pairs={{0,1},{1,2},{2,3},{3,4},{4,5},{5,6},{6,7},{7,8},{8,9},{9,10},{10,1... | collective-permute-start | bytes 1179656 | tf_op jit(solution)/shard_map/ppermute | solution.py:181
  67.3 18.6 %collective-permute-start.6 = (bf16[2,24,4,1024]{3,1,0,2:T(8,128)(2,1)S(1)}, bf16[2,24,4,1024]{3,1,0,2:T(8,128)(2,1)S(1)}, u32[]{:S(2)}, u32[]{:S(2)}) collective-permute-start(bf16[2,24,4,1024]{3,1,0,2:T(8,128)(2,1)S(1)} %get-tuple-element.24), channel_id=1, source_target_pairs={{0,15},{1,0},{2,1},{3,2},{4,3},{5,4},{6,5},{7,6},{8,7},{9,8},{10,9... | collective-permute-start | bytes 1179656 | tf_op jit(solution)/shard_map/ppermute | solution.py:180
  86.5 9.6 %copy-start = (bf16[2,24,16,1024]{3,1,0,2:T(8,128)(2,1)}, bf16[2,24,16,1024]{3,1,0,2:T(8,128)(2,1)S(1)}, u32[]{:S(2)}) copy-start(bf16[2,24,16,1024]{3,1,0,2:T(8,128)(2,1)S(1)} %fusion.4) | copy-start | bytes 4718596
  87.8 23.7 %collective-permute-start.8 = (bf16[2,4,16,1024]{3,1,0,2:T(4,128)(2,1)}, bf16[2,4,16,1024]{3,1,0,2:T(4,128)(2,1)}, u32[]{:S(2)}, u32[]{:S(2)}) collective-permute-start(bf16[2,4,16,1024]{3,1,0,2:T(4,128)(2,1)} %get-tuple-element.27), channel_id=1, source_target_pairs={{0,16},{1,17},{2,18},{3,19},{4,20},{5,21},{6,22},{7,23},{8,24},{9,... | collective-permute-start | bytes 786440 | tf_op jit(solution)/shard_map/ppermute | solution.py:193
  90.4 15.1 %collective-permute-start.7 = (bf16[2,4,16,1024]{3,1,0,2:T(4,128)(2,1)S(1)}, bf16[2,4,16,1024]{3,1,0,2:T(4,128)(2,1)}, u32[]{:S(2)}, u32[]{:S(2)}) collective-permute-start(bf16[2,4,16,1024]{3,1,0,2:T(4,128)(2,1)S(1)} %get-tuple-element.28), channel_id=1, source_target_pairs={{0,8},{1,9},{2,10},{3,11},{4,12},{5,13},{6,14},{7,15},{8,0},{9,1},... | collective-permute-start | bytes 786440 | tf_op jit(solution)/shard_map/ppermute | solution.py:194
  94.5 17.0 %collective-permute-start.9 = (bf16[2,4,16,1024]{3,1,0,2:T(4,128)(2,1)}, bf16[2,4,16,1024]{3,1,0,2:T(4,128)(2,1)}, u32[]{:S(2)}, u32[]{:S(2)}) collective-permute-start(bf16[2,4,16,1024]{3,1,0,2:T(4,128)(2,1)} %get-tuple-element.29), channel_id=1, source_target_pairs={{16,0},{17,1},{18,2},{19,3},{20,4},{21,5},{22,6},{23,7},{24,8},{25... | collective-permute-start | bytes 786440 | tf_op jit(solution)/shard_map/ppermute | solution.py:192
  111.4 1.6 %slice-start = ((bf16[2,24,16,1024]{3,1,0,2:T(8,128)(2,1)}), bf16[2,8,16,1024]{3,1,0,2:T(8,128)(2,1)S(1)}, s32[]{:S(2)}) async-start(bf16[2,24,16,1024]{3,1,0,2:T(8,128)(2,1)} %copy-done), calls=%async_computation | async-start | bytes 1048576 | tf_op jit(solution)/shard_map/slice | solution.py:201
where the time goes:
time: 116 us
  waiting for transfers between devices  44.6 us (38%)
  starting transfers between devices  24.2 us (21%)
  local copies, waits for them, and re-layouts  21.9 us (19%)
  Pallas kernels  17.4 us (15%)
  other arithmetic  6.79 us (6%)
    pallas_call x1, Pallas kernels, attention_core(): pl.pallas_call(lambda *refs: attention_kernel(width, *refs), out_shape=(j...  17.4 us
    ppermute x1, waiting for transfers between devices, on_device(): lax.ppermute(dkv[:, :, ext_w - r:].astype(jnp.bfloat16), 'lon', right_pairs)  15.2 us
    ppermute x1, waiting for transfers between devices, on_device(): from_right = lax.ppermute(colfield[:, :, :r], 'lon', left_pairs)  14.8 us
    ppermute x1, waiting for transfers between devices, on_device(): lax.ppermute(jnp.where(at_north, top_g, bottom_g), both, pole_pairs)  9.44 us
    ppermute x1, starting transfers between devices, on_device(): pole_recv = lax.ppermute(pole_send, both, pole_pairs)  8.2 us
    unnamed x9, local copies, waits for them, and re-layouts  5.37 us
    rev x2, local copies, waits for them, and re-layouts, on_device(): unfolded = jnp.take(pole_g[:, ::-1], unfold_idx, axis=2)  4.21 us
    ppermute x1, starting transfers between devices, on_device(): lax.ppermute(jnp.where(at_north, top_g, bottom_g), both, pole_pairs)  4.08 us
  transfers between devices with their start and end apart: 10, of which 5 were waited for; matrix products, arithmetic and copies ran while one was open for 9% of the time, Pallas kernels for 0%

commit v1 on v0

--- a/solution.py
+++ b/solution.py
@@ -140,32 +140,28 @@
     left_pairs = [(b, (b - 1) % n_lon) for b in range(n_lon)]
     both = ("lat", "lon")
 
-    own_cols = j * width + jnp.arange(width)
+    ext_rows = height + 2 * r
+    ext_w = width + 2 * r
+    my_ext_cols = (j * width - r + jnp.arange(ext_w)) % (n_lon * width)
+    partner_ext_cols = (partner_j * width - r + jnp.arange(ext_w)) % (n_lon * width)
     fold_row = jnp.where(at_north, fold_cols[0], fold_cols[1])
-    fold_idx = jnp.take(fold_row, own_cols) - partner_j * width
-    partner_cols = partner_j * width + jnp.arange(width)
-    unfold_idx = (
-        jnp.zeros((width,), jnp.int32)
-        .at[jnp.take(fold_row, partner_cols) - j * width]
-        .set(jnp.arange(width, dtype=jnp.int32))
-    )
+    fold_idx = (jnp.take(fold_row, my_ext_cols) - (partner_j * width - r)) % (n_lon * width)
+    landing = (jnp.take(fold_row, partner_ext_cols) - (j * width - r)) % (n_lon * width)
+    unfold_idx = jnp.zeros((ext_w,), jnp.int32).at[landing].set(jnp.arange(ext_w, dtype=jnp.int32))
 
     kv = jnp.stack([keys, values])
-    top_send = kv[:, :r]
-    bottom_send = kv[:, height - r :]
+    from_left = lax.ppermute(kv[:, :, width - r :], "lon", right_pairs)
+    from_right = lax.ppermute(kv[:, :, :r], "lon", left_pairs)
+    rowfield = jnp.concatenate([from_left, kv, from_right], axis=2)
+    top_send = rowfield[:, :r]
+    bottom_send = rowfield[:, height - r :]
     from_above = lax.ppermute(bottom_send, both, down_pairs)
     from_below = lax.ppermute(top_send, both, up_pairs)
-    pole_send = jnp.where(at_north, top_send, bottom_send)
-    pole_recv = lax.ppermute(pole_send, both, pole_pairs)
+    pole_recv = lax.ppermute(jnp.where(at_north, top_send, bottom_send), both, pole_pairs)
     pole_rows = jnp.take(pole_recv, fold_idx, axis=2)[:, ::-1]
     top = jnp.where(at_north, pole_rows, from_above)
     bottom = jnp.where(at_south, pole_rows, from_below)
-    colfield = jnp.concatenate([top, kv, bottom], axis=1)
-    from_left = lax.ppermute(colfield[:, :, width - r :], "lon", right_pairs)
-    from_right = lax.ppermute(colfield[:, :, :r], "lon", left_pairs)
-    ext = jnp.concatenate([from_left, colfield, from_right], axis=2)
-    ext_rows = height + 2 * r
-    ext_w = width + 2 * r
+    ext = jnp.concatenate([top, rowfield, bottom], axis=1)
     ext = ext.reshape(2, ext_rows * ext_w, features)
 
     dq, dk, dv = attention_core(
@@ -177,31 +173,31 @@
     )
 
     dkv = jnp.stack([dk, dv]).reshape(2, ext_rows, ext_w, features)
-    back_right = lax.ppermute(dkv[:, :, :r].astype(jnp.bfloat16), "lon", left_pairs)
-    back_left = lax.ppermute(dkv[:, :, ext_w - r :].astype(jnp.bfloat16), "lon", right_pairs)
-    col = jnp.concatenate(
-        [
-            dkv[:, :, r : 2 * r] + back_left.astype(jnp.float32),
-            dkv[:, :, 2 * r : width],
-            dkv[:, :, width : width + r] + back_right.astype(jnp.float32),
-        ],
-        axis=2,
-    )
-    top_g = col[:, :r].astype(jnp.bfloat16)
-    bottom_g = col[:, ext_rows - r :].astype(jnp.bfloat16)
+    top_g = dkv[:, :r].astype(jnp.bfloat16)
+    bottom_g = dkv[:, ext_rows - r :].astype(jnp.bfloat16)
     up_recv = lax.ppermute(top_g, both, up_pairs)
     down_recv = lax.ppermute(bottom_g, both, down_pairs)
     pole_g = lax.ppermute(jnp.where(at_north, top_g, bottom_g), both, pole_pairs)
     unfolded = jnp.take(pole_g[:, ::-1], unfold_idx, axis=2)
     add_top = jnp.where(at_north, unfolded, down_recv).astype(jnp.float32)
     add_bottom = jnp.where(at_south, unfolded, up_recv).astype(jnp.float32)
+    rowgrad = jnp.concatenate(
+        [
+            dkv[:, r : 2 * r] + add_top,
+            dkv[:, 2 * r : height],
+            dkv[:, height : height + r] + add_bottom,
+        ],
+        axis=1,
+    )
+    back_right = lax.ppermute(rowgrad[:, :, :r].astype(jnp.bfloat16), "lon", left_pairs)
+    back_left = lax.ppermute(rowgrad[:, :, ext_w - r :].astype(jnp.bfloat16), "lon", right_pairs)
     grads = jnp.concatenate(
         [
-            col[:, r : 2 * r] + add_top,
-            col[:, 2 * r : height],
-            col[:, height : height + r] + add_bottom,
+            rowgrad[:, :, r : 2 * r] + back_left.astype(jnp.float32),
+            rowgrad[:, :, 2 * r : width],
+            rowgrad[:, :, width : width + r] + back_right.astype(jnp.float32),
         ],
-        axis=1,
+        axis=2,
     ).astype(jnp.bfloat16)
     return (dq.reshape(height, width, features), grads[0], grads[1])
 

time: 116 us -> 106 us (0.914)
  waiting for transfers between devices: 44.6 us -> 31.2 us
  local copies, waits for them, and re-layouts: 21.9 us -> 18.6 us
  other arithmetic: 6.79 us -> 9.92 us
  starting transfers between devices: 24.2 us -> 26.7 us
    ppermute x5, waiting for transfers between devices: 35.2 us -> 22.7 us  [the longest x1 10.8 us: on_device(): from_right = lax.ppermute(kv[:, :, :r], 'lon', left_pairs)]
    ppermute x1, starting transfers between devices: 4.08 us -> 8.24 us  [on_device(): lax.ppermute(jnp.where(at_north, top_g, bottom_g), both, pole_pairs)]
    rev x2, local copies, waits for them, and re-layouts: 4.21 us -> 1.09 us  [on_device(): unfolded = jnp.take(pole_g[:, ::-1], unfold_idx, axis=2)]
    add x1, other arithmetic: 0.31 us -> 2.65 us  [on_device(): dkv[:, r:2 * r] + add_top]
    ppermute x1, starting transfers between devices: 2.64 us -> 1.3 us  [on_device(): down_recv = lax.ppermute(bottom_g, both, down_pairs)]
    unnamed x9 -> x11, local copies, waits for them, and re-layouts: 5.37 us -> 5.38 us
  transfers between devices with their start and end apart: 10 -> 10, of which waited for: 5 -> 5; matrix products, arithmetic and copies ran while one was open for 9% -> 7% of each run, Pallas kernels for 0% -> 0%
where the time goes in v1:
time: 106 us; the launch traced here: 105 us
  waiting for transfers between devices  31.2 us (29%)
  starting transfers between devices  26.7 us (25%)
  local copies, waits for them, and re-layouts  18.6 us (18%)
  Pallas kernels  17.4 us (16%)
  other arithmetic  9.92 us (9%)
    pallas_call x1, Pallas kernels, attention_core(): pl.pallas_call(lambda *refs: attention_kernel(width, *refs), out_shape=(j...  17.4 us
    ppermute x1, waiting for transfers between devices, on_device(): from_right = lax.ppermute(kv[:, :, :r], 'lon', left_pairs)  10.8 us
    ppermute x1, waiting for transfers between devices, on_device(): lax.ppermute(jnp.where(at_north, top_g, bottom_g), both, pole_pairs)  8.54 us
    ppermute x1, starting transfers between devices, on_device(): lax.ppermute(jnp.where(at_north, top_g, bottom_g), both, pole_pairs)  8.24 us
    ppermute x1, starting transfers between devices, on_device(): lax.ppermute(jnp.where(at_north, top_send, bottom_send), both, pole_pairs)  8.19 us
    unnamed x11, local copies, waits for them, and re-layouts  5.38 us
    ppermute x1, waiting for transfers between devices, on_device(): lax.ppermute(jnp.where(at_north, top_send, bottom_send), both, pole_pairs)  5.29 us
    ppermute x1, waiting for transfers between devices, on_device(): lax.ppermute(rowgrad[:, :, ext_w - r:].astype(jnp.bfloat16), 'lon', right...  4.92 us
  transfers between devices with their start and end apart: 10, of which 5 were waited for; matrix products, arithmetic and copies ran while one was open for 7% of the time, Pallas kernels for 0%

profile of v1, /device:TPU:32, one launch (start us, length us, event | category | flops | bytes accessed | tf_op | source)
XLA Modules:
  0.0 104.9 jit_solution(17329288876665040595)
XLA Ops:
  0.6 1.8 %copy_bitcast_fusion = (bf16[1,16,16,1024]{3,1,0,2:T(8,128)(2,1)S(1)}, bf16[1,16,16,1024]{3,1,0,2:T(8,128)(2,1)S(1)}) fusion(bf16[16,16,1024]{2,1,0:T(8,128)(2,1)} %param.11, bf16[16,16,1024]{2,1,0:T(8,128)(2,1)} %param.10), kind=kLoop, calls=%fused_computation.18 | loop fusion | bytes 2097152 | tf_op jit(solution)/shard_map/stack | solution.py:152
  2.5 1.2 %collective-permute-start.1 = (bf16[2,16,4,1024]{3,1,0,2:T(8,128)(2,1)S(1)}, bf16[2,16,4,1024]{3,1,0,2:T(8,128)(2,1)S(1)}, u32[]{:S(2)}, u32[]{:S(2)}) collective-permute-start(bf16[2,16,4,1024]{3,1,0,2:T(8,128)(2,1)S(1)} %get-tuple-element.33), channel_id=1, source_target_pairs={{0,15},{1,0},{2,1},{3,2},{4,3},{5,4},{6,5},{7,6},{8,7},{9,8},{10,9... | collective-permute-start | bytes 786440 | tf_op jit(solution)/shard_map/ppermute | solution.py:154
  3.7 0.9 collective-permute-start
  5.4 10.8 %collective-permute-done.1 = bf16[2,16,4,1024]{3,1,0,2:T(8,128)(2,1)S(1)} collective-permute-done((bf16[2,16,4,1024]{3,1,0,2:T(8,128)(2,1)S(1)}, bf16[2,16,4,1024]{3,1,0,2:T(8,128)(2,1)S(1)}, u32[]{:S(2)}, u32[]{:S(2)}) %collective-permute-start.1) | collective-permute-done | bytes 262176 | tf_op jit(solution)/shard_map/ppermute | solution.py:154
  16.2 1.4 %broadcast_select_fusion.4 = (bf16[2,4,24,1024]{3,1,0,2:T(4,128)(2,1)S(1)}, bf16[2,4,24,1024]{3,1,0,2:T(4,128)(2,1)}, bf16[2,4,24,1024]{3,1,0,2:T(4,128)(2,1)}) fusion(pred[]{:T(512)S(6)} %eq.13, bf16[2,16,4,1024]{3,1,0,2:T(8,128)(2,1)S(1)} %collective-permute-done.1, bf16[1,16,16,1024]{3,1,0,2:T(8,128)(2,1)S(1)} %get-tuple-element.36, ...), kind=kLoop, calls=%fused_computation.31 | loop fusion | flops 3342336 | bytes 2752513 | tf_op jit(solution)/shard_map/jit(_where)/select_n | solution.py:160
  17.6 8.2 %collective-permute-start.2 = (bf16[2,4,24,1024]{3,1,0,2:T(4,128)(2,1)S(1)}, bf16[2,4,24,1024]{3,1,0,2:T(4,128)(2,1)S(1)}, u32[]{:S(2)}, u32[]{:S(2)}) collective-permute-start(bf16[2,4,24,1024]{3,1,0,2:T(4,128)(2,1)S(1)} %get-tuple-element.16), channel_id=1, source_target_pairs={{0,8},{1,9},{2,10},{3,11},{4,12},{5,13},{6,14},{7,15},{8,0},{9,1},... | collective-permute-start | bytes 1179656 | tf_op jit(solution)/shard_map/ppermute | solution.py:160
  26.6 1.3 %collective-permute-start.3 = (bf16[2,4,24,1024]{3,1,0,2:T(4,128)(2,1)}, bf16[2,4,24,1024]{3,1,0,2:T(4,128)(2,1)S(1)}, u32[]{:S(2)}, u32[]{:S(2)}) collective-permute-start(bf16[2,4,24,1024]{3,1,0,2:T(4,128)(2,1)} %get-tuple-element.17), channel_id=1, source_target_pairs={{0,16},{1,17},{2,18},{3,19},{4,20},{5,21},{6,22},{7,23},{8,24},{9,... | collective-permute-start | bytes 1179656 | tf_op jit(solution)/shard_map/ppermute | solution.py:158
  27.9 1.3 %collective-permute-start.4 = (bf16[2,4,24,1024]{3,1,0,2:T(4,128)(2,1)}, bf16[2,4,24,1024]{3,1,0,2:T(4,128)(2,1)S(1)}, u32[]{:S(2)}, u32[]{:S(2)}) collective-permute-start(bf16[2,4,24,1024]{3,1,0,2:T(4,128)(2,1)} %get-tuple-element.18), channel_id=1, source_target_pairs={{16,0},{17,1},{18,2},{19,3},{20,4},{21,5},{22,6},{23,7},{24,8},{25... | collective-permute-start | bytes 1179656 | tf_op jit(solution)/shard_map/ppermute | solution.py:159
  29.2 0.8 scatter_custom_fusion
  30.1 5.3 %collective-permute-done.2 = bf16[2,4,24,1024]{3,1,0,2:T(4,128)(2,1)S(1)} collective-permute-done((bf16[2,4,24,1024]{3,1,0,2:T(4,128)(2,1)S(1)}, bf16[2,4,24,1024]{3,1,0,2:T(4,128)(2,1)S(1)}, u32[]{:S(2)}, u32[]{:S(2)}) %collective-permute-start.2) | collective-permute-done | bytes 393248 | tf_op jit(solution)/shard_map/ppermute | solution.py:160
  35.5 0.9 gather_fusion.1
  36.6 1.0 rev.6
  37.7 1.7 %pad_maximum_fusion.1 = bf16[2,24,24,1024]{3,1,0,2:T(8,128)(2,1)S(1)} fusion(bf16[2,4,24,1024]{3,1,0,2:T(4,128)(2,1)S(1)} %bitcast.35, bf16[2,16,4,1024]{3,1,0,2:T(8,128)(2,1)S(1)} %collective-permute-done.1, bf16[1,16,16,1024]{3,1,0,2:T(8,128)(2,1)S(1)} %get-tuple-element.36, bf16[1,16,16,1024]{3,1,0,2:T(8,128)(2,1)S(1)} %get-tuple-element.37, ...), kind=kLoop, calls=%fused_computation.6 | loop fusion | flops 14155776 | bytes 4718592 | tf_op jit(solution)/shard_map/concatenate | solution.py:164
  39.7 1.7 %copy.11 = bf16[1,24,24,1024]{3,2,1,0:T(8,128)(2,1)} copy(bf16[1,24,24,1024]{3,1,0,2:T(8,128)(2,1)S(1)} %get-tuple-element.27) | data formatting | bytes 2359296 | tf_op jit(solution)/shard_map/slice | solution.py:170
  41.4 1.7 %copy.12 = bf16[1,24,24,1024]{3,2,1,0:T(8,128)(2,1)} copy(bf16[1,24,24,1024]{3,1,0,2:T(8,128)(2,1)S(1)} %get-tuple-element.26) | data formatting | bytes 2359296 | tf_op jit(solution)/shard_map/slice | solution.py:171
  43.1 17.4 %neighbourhood_attention_bwd.1 = (bf16[256,1024]{1,0:T(8,128)(2,1)}, f32[576,1024]{1,0:T(8,128)}, f32[576,1024]{1,0:T(8,128)}) custom-call(bf16[256,1024]{1,0:T(8,128)(2,1)} %bitcast.41, bf16[256,1024]{1,0:T(8,128)(2,1)} %bitcast.42, bf16[576,1024]{1,0:T(8,128)(2,1)} %bitcast.37, bf16[576,1024]{1,0:T(8,128)(2,1)} %bitcast.38), custom_call_target="tpu_custom_call" | custom-call | flops 2013265920 | bytes 8650752 | tf_op jit(solution)/shard_map/neighbourhood_attention_bwd/pallas_call | solution.py:101
  60.5 3.2 %copy_dynamic-update-slice_fusion.1 = f32[2,24,24,1024]{3,1,0,2:T(8,128)S(1)} fusion(f32[1,24,24,1024]{3,2,1,0:T(8,128)} %bitcast.33), kind=kLoop, calls=%fused_computation.8 | loop fusion | bytes 4718592
  63.7 1.4 %copy_dynamic-update-slice_fusion = f32[2,24,24,1024]{3,1,0,2:T(8,128)S(1)} fusion(f32[2,24,24,1024]{3,1,0,2:T(8,128)S(1)} %copy_dynamic-update-slice_fusion.1, f32[1,24,24,1024]{3,2,1,0:T(8,128)S(1)} %bitcast.32), kind=kLoop, calls=%fused_computation.7 | loop fusion | bytes 4718592 | tf_op jit(solution)/shard_map/stack | solution.py:175
  65.4 1.7 %fusion.9 = (bf16[2,4,24,1024]{3,1,0,2:T(4,128)(2,1)}, bf16[2,4,24,1024]{3,1,0,2:T(4,128)(2,1)S(1)}, bf16[2,4,24,1024]{3,1,0,2:T(4,128)(2,1)S(1)}) fusion(bf16[2,24,24,1024]{3,1,0,2:T(8,128)(2,1)S(1)} %convert.16, pred[]{:T(512)S(6)} %eq.13), kind=kLoop, calls=%fused_computation.67 | loop fusion | flops 196608 | bytes 1966081 | tf_op jit(solution)/shard_map/slice | solution.py:177
  67.1 1.3 %collective-permute-start.6 = (bf16[2,4,24,1024]{3,1,0,2:T(4,128)(2,1)}, bf16[2,4,24,1024]{3,1,0,2:T(4,128)(2,1)S(1)}, u32[]{:S(2)}, u32[]{:S(2)}) collective-permute-start(bf16[2,4,24,1024]{3,1,0,2:T(4,128)(2,1)} %get-tuple-element.23), channel_id=1, source_target_pairs={{0,16},{1,17},{2,18},{3,19},{4,20},{5,21},{6,22},{7,23},{8,24},{9,... | collective-permute-start | bytes 1179656 | tf_op jit(solution)/shard_map/ppermute | solution.py:179
  68.4 8.2 %collective-permute-start.5 = (bf16[2,4,24,1024]{3,1,0,2:T(4,128)(2,1)S(1)}, bf16[2,4,24,1024]{3,1,0,2:T(4,128)(2,1)S(1)}, u32[]{:S(2)}, u32[]{:S(2)}) collective-permute-start(bf16[2,4,24,1024]{3,1,0,2:T(4,128)(2,1)S(1)} %get-tuple-element.24), channel_id=1, source_target_pairs={{0,8},{1,9},{2,10},{3,11},{4,12},{5,13},{6,14},{7,15},{8,0},{9,1},... | collective-permute-start | bytes 1179656 | tf_op jit(solution)/shard_map/ppermute | solution.py:180
  76.7 1.3 %collective-permute-start.7 = (bf16[2,4,24,1024]{3,1,0,2:T(4,128)(2,1)S(1)}, bf16[2,4,24,1024]{3,1,0,2:T(4,128)(2,1)S(1)}, u32[]{:S(2)}, u32[]{:S(2)}) collective-permute-start(bf16[2,4,24,1024]{3,1,0,2:T(4,128)(2,1)S(1)} %get-tuple-element.25), channel_id=1, source_target_pairs={{16,0},{17,1},{18,2},{19,3},{20,4},{21,5},{22,6},{23,7},{24,8},{25... | collective-permute-start | bytes 1179656 | tf_op jit(solution)/shard_map/ppermute | solution.py:178
  78.2 8.5 %collective-permute-done.5 = bf16[2,4,24,1024]{3,1,0,2:T(4,128)(2,1)S(1)} collective-permute-done((bf16[2,4,24,1024]{3,1,0,2:T(4,128)(2,1)S(1)}, bf16[2,4,24,1024]{3,1,0,2:T(4,128)(2,1)S(1)}, u32[]{:S(2)}, u32[]{:S(2)}) %collective-permute-start.5) | collective-permute-done | bytes 393248 | tf_op jit(solution)/shard_map/ppermute | solution.py:180
  86.7 1.0 rev.7
  87.8 0.9 gather_fusion.3
  88.7 2.6 %slice_add_fusion.1 = (f32[2,4,24,1024]{3,1,0,2:T(4,128)S(1)}, f32[2,4,24,1024]{3,1,0,2:T(4,128)S(1)}) fusion(f32[2,24,24,1024]{3,1,0,2:T(8,128)} %copy-done, bf16[2,4,24,1024]{3,1,0,2:T(4,128)(2,1)S(1)} %collective-permute-done.6, pred[]{:T(512)S(6)} %eq.13, bf16[24,2,4,1024]{3,2,1,0:T(4,128)(2,1)S(1)} %gather_fusion.3, ...), kind=kLoop, calls=%fused_computation.11 | loop fusion | flops 1376256 | bytes 4325402 | tf_op jit(solution)/shard_map/add | solution.py:186
  92.1 1.9 %collective-permute-start.8 = (bf16[2,16,4,1024]{3,1,0,2:T(8,128)(2,1)S(1)}, bf16[2,16,4,1024]{3,1,0,2:T(8,128)(2,1)S(1)}, u32[]{:S(2)}, u32[]{:S(2)}) collective-permute-start(bf16[2,16,4,1024]{3,1,0,2:T(8,128)(2,1)S(1)} %get-tuple-element.28), channel_id=1, source_target_pairs={{0,1},{1,2},{2,3},{3,4},{4,5},{5,6},{6,7},{7,8},{8,9},{9,10},{10,1... | collective-permute-start | bytes 786440 | tf_op jit(solution)/shard_map/ppermute | solution.py:193
  94.0 1.1 %collective-permute-start.9 = (bf16[2,16,4,1024]{3,1,0,2:T(8,128)(2,1)S(1)}, bf16[2,16,4,1024]{3,1,0,2:T(8,128)(2,1)S(1)}, u32[]{:S(2)}, u32[]{:S(2)}) collective-permute-start(bf16[2,16,4,1024]{3,1,0,2:T(8,128)(2,1)S(1)} %get-tuple-element.29), channel_id=1, source_target_pairs={{0,15},{1,0},{2,1},{3,2},{4,3},{5,4},{6,5},{7,6},{8,7},{9,8},{10,9... | collective-permute-start | bytes 786440 | tf_op jit(solution)/shard_map/ppermute | solution.py:192
  95.8 4.9 %collective-permute-done.8 = bf16[2,16,4,1024]{3,1,0,2:T(8,128)(2,1)S(1)} collective-permute-done((bf16[2,16,4,1024]{3,1,0,2:T(8,128)(2,1)S(1)}, bf16[2,16,4,1024]{3,1,0,2:T(8,128)(2,1)S(1)}, u32[]{:S(2)}, u32[]{:S(2)}) %collective-permute-start.8) | collective-permute-done | bytes 262176 | tf_op jit(solution)/shard_map/ppermute | solution.py:193
  100.7 1.6 %collective-permute-done.9 = bf16[2,16,4,1024]{3,1,0,2:T(8,128)(2,1)S(1)} collective-permute-done((bf16[2,16,4,1024]{3,1,0,2:T(8,128)(2,1)S(1)}, bf16[2,16,4,1024]{3,1,0,2:T(8,128)(2,1)S(1)}, u32[]{:S(2)}, u32[]{:S(2)}) %collective-permute-start.9) | collective-permute-done | bytes 262176 | tf_op jit(solution)/shard_map/ppermute | solution.py:192
  102.7 1.1 %copy.16 = bf16[16,16,1024]{2,1,0:T(8,128)(2,1)} copy(bf16[16,16,1024]{2,0,1:T(8,128)(2,1)S(1)} %get-tuple-element.31) | data formatting | bytes 1048576
  103.8 1.1 %copy.17 = bf16[16,16,1024]{2,1,0:T(8,128)(2,1)} copy(bf16[16,16,1024]{2,0,1:T(8,128)(2,1)S(1)} %get-tuple-element.30) | data formatting | bytes 1048576
  (42 shorter events, 4.6 us)
Async XLA Ops:
  0.6 4.0 %copy-start.3 = (s32[2,256]{1,0:T(2,128)S(1)}, s32[2,256]{1,0:T(2,128)}, u32[]{:S(2)}) copy-start(s32[2,256]{1,0:T(2,128)} %param.13) | copy-start | bytes 6148
  2.5 13.7 %collective-permute-start.1 = (bf16[2,16,4,1024]{3,1,0,2:T(8,128)(2,1)S(1)}, bf16[2,16,4,1024]{3,1,0,2:T(8,128)(2,1)S(1)}, u32[]{:S(2)}, u32[]{:S(2)}) collective-permute-start(bf16[2,16,4,1024]{3,1,0,2:T(8,128)(2,1)S(1)} %get-tuple-element.33), channel_id=1, source_target_pairs={{0,15},{1,0},{2,1},{3,2},{4,3},{5,4},{6,5},{7,6},{8,7},{9,8},{10,9... | collective-permute-start | bytes 786440 | tf_op jit(solution)/shard_map/ppermute | solution.py:154
  3.7 12.5 %collective-permute-start = (bf16[2,16,4,1024]{3,1,0,2:T(8,128)(2,1)S(1)}, bf16[2,16,4,1024]{3,1,0,2:T(8,128)(2,1)S(1)}, u32[]{:S(2)}, u32[]{:S(2)}) collective-permute-start(bf16[2,16,4,1024]{3,1,0,2:T(8,128)(2,1)S(1)} %get-tuple-element.32), channel_id=1, source_target_pairs={{0,1},{1,2},{2,3},{3,4},{4,5},{5,6},{6,7},{7,8},{8,9},{9,10},{10,1... | collective-permute-start | bytes 786440 | tf_op jit(solution)/shard_map/ppermute | solution.py:153
  17.6 17.7 %collective-permute-start.2 = (bf16[2,4,24,1024]{3,1,0,2:T(4,128)(2,1)S(1)}, bf16[2,4,24,1024]{3,1,0,2:T(4,128)(2,1)S(1)}, u32[]{:S(2)}, u32[]{:S(2)}) collective-permute-start(bf16[2,4,24,1024]{3,1,0,2:T(4,128)(2,1)S(1)} %get-tuple-element.16), channel_id=1, source_target_pairs={{0,8},{1,9},{2,10},{3,11},{4,12},{5,13},{6,14},{7,15},{8,0},{9,1},... | collective-permute-start | bytes 1179656 | tf_op jit(solution)/shard_map/ppermute | solution.py:160
  26.6 11.1 %collective-permute-start.3 = (bf16[2,4,24,1024]{3,1,0,2:T(4,128)(2,1)}, bf16[2,4,24,1024]{3,1,0,2:T(4,128)(2,1)S(1)}, u32[]{:S(2)}, u32[]{:S(2)}) collective-permute-start(bf16[2,4,24,1024]{3,1,0,2:T(4,128)(2,1)} %get-tuple-element.17), channel_id=1, source_target_pairs={{0,16},{1,17},{2,18},{3,19},{4,20},{5,21},{6,22},{7,23},{8,24},{9,... | collective-permute-start | bytes 1179656 | tf_op jit(solution)/shard_map/ppermute | solution.py:158
  27.9 9.8 %collective-permute-start.4 = (bf16[2,4,24,1024]{3,1,0,2:T(4,128)(2,1)}, bf16[2,4,24,1024]{3,1,0,2:T(4,128)(2,1)S(1)}, u32[]{:S(2)}, u32[]{:S(2)}) collective-permute-start(bf16[2,4,24,1024]{3,1,0,2:T(4,128)(2,1)} %get-tuple-element.18), channel_id=1, source_target_pairs={{16,0},{17,1},{18,2},{19,3},{20,4},{21,5},{22,6},{23,7},{24,8},{25... | collective-permute-start | bytes 1179656 | tf_op jit(solution)/shard_map/ppermute | solution.py:159
  60.5 3.2 %copy-start.2 = (f32[576,1024]{1,0:T(8,128)S(1)}, f32[576,1024]{1,0:T(8,128)}, u32[]{:S(2)}) copy-start(f32[576,1024]{1,0:T(8,128)} %get-tuple-element.10) | copy-start | bytes 7077892
  65.0 13.0 %copy-start = (f32[2,24,24,1024]{3,1,0,2:T(8,128)}, f32[2,24,24,1024]{3,1,0,2:T(8,128)S(1)}, u32[]{:S(2)}) copy-start(f32[2,24,24,1024]{3,1,0,2:T(8,128)S(1)} %copy_dynamic-update-slice_fusion) | copy-start | bytes 14155780
  67.1 21.6 %collective-permute-start.6 = (bf16[2,4,24,1024]{3,1,0,2:T(4,128)(2,1)}, bf16[2,4,24,1024]{3,1,0,2:T(4,128)(2,1)S(1)}, u32[]{:S(2)}, u32[]{:S(2)}) collective-permute-start(bf16[2,4,24,1024]{3,1,0,2:T(4,128)(2,1)} %get-tuple-element.23), channel_id=1, source_target_pairs={{0,16},{1,17},{2,18},{3,19},{4,20},{5,21},{6,22},{7,23},{8,24},{9,... | collective-permute-start | bytes 1179656 | tf_op jit(solution)/shard_map/ppermute | solution.py:179
  68.4 18.2 %collective-permute-start.5 = (bf16[2,4,24,1024]{3,1,0,2:T(4,128)(2,1)S(1)}, bf16[2,4,24,1024]{3,1,0,2:T(4,128)(2,1)S(1)}, u32[]{:S(2)}, u32[]{:S(2)}) collective-permute-start(bf16[2,4,24,1024]{3,1,0,2:T(4,128)(2,1)S(1)} %get-tuple-element.24), channel_id=1, source_target_pairs={{0,8},{1,9},{2,10},{3,11},{4,12},{5,13},{6,14},{7,15},{8,0},{9,1},... | collective-permute-start | bytes 1179656 | tf_op jit(solution)/shard_map/ppermute | solution.py:180
  76.7 12.0 %collective-permute-start.7 = (bf16[2,4,24,1024]{3,1,0,2:T(4,128)(2,1)S(1)}, bf16[2,4,24,1024]{3,1,0,2:T(4,128)(2,1)S(1)}, u32[]{:S(2)}, u32[]{:S(2)}) collective-permute-start(bf16[2,4,24,1024]{3,1,0,2:T(4,128)(2,1)S(1)} %get-tuple-element.25), channel_id=1, source_target_pairs={{16,0},{17,1},{18,2},{19,3},{20,4},{21,5},{22,6},{23,7},{24,8},{25... | collective-permute-start | bytes 1179656 | tf_op jit(solution)/shard_map/ppermute | solution.py:178
  92.1 3.7 %copy-start.1 = (bf16[2,16,24,1024]{3,1,0,2:T(8,128)(2,1)}, bf16[2,16,24,1024]{3,1,0,2:T(8,128)(2,1)S(1)}, u32[]{:S(2)}) copy-start(bf16[2,16,24,1024]{3,1,0,2:T(8,128)(2,1)S(1)} %fusion.8) | copy-start | bytes 4718596
  92.1 8.6 %collective-permute-start.8 = (bf16[2,16,4,1024]{3,1,0,2:T(8,128)(2,1)S(1)}, bf16[2,16,4,1024]{3,1,0,2:T(8,128)(2,1)S(1)}, u32[]{:S(2)}, u32[]{:S(2)}) collective-permute-start(bf16[2,16,4,1024]{3,1,0,2:T(8,128)(2,1)S(1)} %get-tuple-element.28), channel_id=1, source_target_pairs={{0,1},{1,2},{2,3},{3,4},{4,5},{5,6},{6,7},{7,8},{8,9},{9,10},{10,1... | collective-permute-start | bytes 786440 | tf_op jit(solution)/shard_map/ppermute | solution.py:193
  94.0 8.3 %collective-permute-start.9 = (bf16[2,16,4,1024]{3,1,0,2:T(8,128)(2,1)S(1)}, bf16[2,16,4,1024]{3,1,0,2:T(8,128)(2,1)S(1)}, u32[]{:S(2)}, u32[]{:S(2)}) collective-permute-start(bf16[2,16,4,1024]{3,1,0,2:T(8,128)(2,1)S(1)} %get-tuple-element.29), channel_id=1, source_target_pairs={{0,15},{1,0},{2,1},{3,2},{4,3},{5,4},{6,5},{7,6},{8,7},{9,8},{10,9... | collective-permute-start | bytes 786440 | tf_op jit(solution)/shard_map/ppermute | solution.py:192
  100.7 1.7 %slice-start = ((bf16[2,16,24,1024]{3,1,0,2:T(8,128)(2,1)}), bf16[2,16,8,1024]{3,1,0,2:T(8,128)(2,1)S(1)}, s32[]{:S(2)}) async-start(bf16[2,16,24,1024]{3,1,0,2:T(8,128)(2,1)} %copy-done.1), calls=%async_computation | async-start | bytes 1048576 | tf_op jit(solution)/shard_map/slice | solution.py:197

commit v2 on v1

--- a/solution.py
+++ b/solution.py
@@ -53,8 +53,8 @@
         for t in range(tiles):
             qp = q_ref[pl.ds(t * tq, tq), lanes]
             gp = g_ref[pl.ds(t * tq, tq), lanes]
-            kp = k_ref[pl.ds(t * step_k, tk), lanes]
-            vp = v_ref[pl.ds(t * step_k, tk), lanes]
+            kp = k_ref[pl.ds(t * step_k, tk), lanes].astype(jnp.bfloat16)
+            vp = v_ref[pl.ds(t * step_k, tk), lanes].astype(jnp.bfloat16)
             lo = lax.broadcasted_iota(jnp.int32, qp.shape, 1) < HEAD_DIM
             zero = jnp.zeros_like(qp)
             qa = jnp.where(lo, qp, zero)
@@ -111,7 +111,7 @@
         cost_estimate=pl.CostEstimate(
             flops=flops,
             transcendentals=2 * tq * tk * HEADS * tiles,
-            bytes_accessed=2 * (2 * cells * features) + 2 * (2 * ext_cells * features)
+            bytes_accessed=2 * (2 * cells * features) + 2 * (4 * ext_cells * features)
             + 2 * cells * features + 2 * 4 * ext_cells * features,
         ),
         name="neighbourhood_attention_bwd",
@@ -129,77 +129,123 @@
     at_south = i == n_lat - 1
     partner_j = (j + half) % n_lon
     r = RADIUS
+    f32 = jnp.float32
+    bf16 = jnp.bfloat16
 
     def flat(a, b):
         return a * n_lon + b
 
+    poles = (0, n_lat - 1)
     down_pairs = [(flat(a, b), flat(a + 1, b)) for a in range(n_lat - 1) for b in range(n_lon)]
     up_pairs = [(flat(a + 1, b), flat(a, b)) for a in range(n_lat - 1) for b in range(n_lon)]
-    pole_pairs = [(flat(a, b), flat(a, (b + half) % n_lon)) for a in (0, n_lat - 1) for b in range(n_lon)]
+    pole_pairs = [(flat(a, b), flat(a, (b + half) % n_lon)) for a in poles for b in range(n_lon)]
+    pole_right = [(flat(a, b), flat(a, (b + 1) % n_lon)) for a in poles for b in range(n_lon)]
+    pole_left = [(flat(a, b), flat(a, (b - 1) % n_lon)) for a in poles for b in range(n_lon)]
     right_pairs = [(b, (b + 1) % n_lon) for b in range(n_lon)]
     left_pairs = [(b, (b - 1) % n_lon) for b in range(n_lon)]
     both = ("lat", "lon")
 
     ext_rows = height + 2 * r
     ext_w = width + 2 * r
-    my_ext_cols = (j * width - r + jnp.arange(ext_w)) % (n_lon * width)
-    partner_ext_cols = (partner_j * width - r + jnp.arange(ext_w)) % (n_lon * width)
+    own_cols = j * width + jnp.arange(width)
+    partner_cols = partner_j * width + jnp.arange(width)
     fold_row = jnp.where(at_north, fold_cols[0], fold_cols[1])
-    fold_idx = (jnp.take(fold_row, my_ext_cols) - (partner_j * width - r)) % (n_lon * width)
-    landing = (jnp.take(fold_row, partner_ext_cols) - (j * width - r)) % (n_lon * width)
-    unfold_idx = jnp.zeros((ext_w,), jnp.int32).at[landing].set(jnp.arange(ext_w, dtype=jnp.int32))
-
-    kv = jnp.stack([keys, values])
-    from_left = lax.ppermute(kv[:, :, width - r :], "lon", right_pairs)
-    from_right = lax.ppermute(kv[:, :, :r], "lon", left_pairs)
-    rowfield = jnp.concatenate([from_left, kv, from_right], axis=2)
-    top_send = rowfield[:, :r]
-    bottom_send = rowfield[:, height - r :]
+    fold_idx = jnp.take(fold_row, own_cols) - partner_j * width
+    landing = jnp.take(fold_row, partner_cols) - j * width
+    unfold_idx = jnp.zeros((width,), jnp.int32).at[landing].set(jnp.arange(width, dtype=jnp.int32))
+
+    def pair(a, b):
+        return jnp.stack([a, b])
+
+    from_left = lax.ppermute(pair(keys[:, width - r :], values[:, width - r :]), "lon", right_pairs)
+    from_right = lax.ppermute(pair(keys[:, :r], values[:, :r]), "lon", left_pairs)
+    top_own = pair(keys[:r], values[:r])
+    bottom_own = pair(keys[height - r :], values[height - r :])
+    pole_recv = lax.ppermute(jnp.where(at_north, top_own, bottom_own), both, pole_pairs)
+    pole_rows = jnp.take(pole_recv, fold_idx, axis=2)[:, ::-1]
+
+    top_send = jnp.concatenate([from_left[:, :r], top_own, from_right[:, :r]], axis=2)
+    bottom_send = jnp.concatenate(
+        [from_left[:, height - r :], bottom_own, from_right[:, height - r :]], axis=2
+    )
     from_above = lax.ppermute(bottom_send, both, down_pairs)
     from_below = lax.ppermute(top_send, both, up_pairs)
-    pole_recv = lax.ppermute(jnp.where(at_north, top_send, bottom_send), both, pole_pairs)
-    pole_rows = jnp.take(pole_recv, fold_idx, axis=2)[:, ::-1]
-    top = jnp.where(at_north, pole_rows, from_above)
-    bottom = jnp.where(at_south, pole_rows, from_below)
-    ext = jnp.concatenate([top, rowfield, bottom], axis=1)
-    ext = ext.reshape(2, ext_rows * ext_w, features)
+    corner_left = lax.ppermute(pole_rows[:, :, width - r :], both, pole_right)
+    corner_right = lax.ppermute(pole_rows[:, :, :r], both, pole_left)
+    pole_full = jnp.concatenate([corner_left, pole_rows, corner_right], axis=2)
+    top = jnp.where(at_north, pole_full, from_above)
+    bottom = jnp.where(at_south, pole_full, from_below)
+
+    def ext_of(c, own):
+        middle = jnp.concatenate([from_left[c], own, from_right[c]], axis=1)
+        whole = jnp.concatenate([top[c], middle, bottom[c]], axis=0).astype(f32)
+        return whole.reshape(ext_rows * ext_w, features)
 
     dq, dk, dv = attention_core(
         queries.reshape(height * width, features),
         grad_out.reshape(height * width, features),
-        ext[0],
-        ext[1],
+        ext_of(0, keys),
+        ext_of(1, values),
         width,
     )
-
-    dkv = jnp.stack([dk, dv]).reshape(2, ext_rows, ext_w, features)
-    top_g = dkv[:, :r].astype(jnp.bfloat16)
-    bottom_g = dkv[:, ext_rows - r :].astype(jnp.bfloat16)
+    dk = dk.reshape(ext_rows, ext_w, features)
+    dv = dv.reshape(ext_rows, ext_w, features)
+
+    top_g = pair(dk[:r], dv[:r]).astype(bf16)
+    bottom_g = pair(dk[ext_rows - r :], dv[ext_rows - r :]).astype(bf16)
     up_recv = lax.ppermute(top_g, both, up_pairs)
     down_recv = lax.ppermute(bottom_g, both, down_pairs)
-    pole_g = lax.ppermute(jnp.where(at_north, top_g, bottom_g), both, pole_pairs)
-    unfolded = jnp.take(pole_g[:, ::-1], unfold_idx, axis=2)
-    add_top = jnp.where(at_north, unfolded, down_recv).astype(jnp.float32)
-    add_bottom = jnp.where(at_south, unfolded, up_recv).astype(jnp.float32)
-    rowgrad = jnp.concatenate(
+    pole_g = jnp.where(at_north, top_g, bottom_g)
+    corner_back_right = lax.ppermute(pole_g[:, :, :r], both, pole_left)
+    corner_back_left = lax.ppermute(pole_g[:, :, ext_w - r :], both, pole_right)
+    pole_own = jnp.concatenate(
         [
-            dkv[:, r : 2 * r] + add_top,
-            dkv[:, 2 * r : height],
-            dkv[:, height : height + r] + add_bottom,
-        ],
-        axis=1,
-    )
-    back_right = lax.ppermute(rowgrad[:, :, :r].astype(jnp.bfloat16), "lon", left_pairs)
-    back_left = lax.ppermute(rowgrad[:, :, ext_w - r :].astype(jnp.bfloat16), "lon", right_pairs)
-    grads = jnp.concatenate(
-        [
-            rowgrad[:, :, r : 2 * r] + back_left.astype(jnp.float32),
-            rowgrad[:, :, 2 * r : width],
-            rowgrad[:, :, width : width + r] + back_right.astype(jnp.float32),
+            pole_g[:, :, r : 2 * r].astype(f32) + corner_back_left.astype(f32),
+            pole_g[:, :, 2 * r : width].astype(f32),
+            pole_g[:, :, width : width + r].astype(f32) + corner_back_right.astype(f32),
         ],
         axis=2,
-    ).astype(jnp.bfloat16)
-    return (dq.reshape(height, width, features), grads[0], grads[1])
+    )
+
+    def rows_of(c, d):
+        return jnp.concatenate(
+            [
+                d[r : 2 * r] + down_recv[c].astype(f32),
+                d[2 * r : height],
+                d[height : height + r] + up_recv[c].astype(f32),
+            ],
+            axis=0,
+        )
+
+    rows_k = rows_of(0, dk)
+    rows_v = rows_of(1, dv)
+
+    back_right = lax.ppermute(
+        pair(rows_k[:, :r], rows_v[:, :r]).astype(bf16), "lon", left_pairs
+    )
+    back_left = lax.ppermute(
+        pair(rows_k[:, ext_w - r :], rows_v[:, ext_w - r :]).astype(bf16), "lon", right_pairs
+    )
+    pole_back = lax.ppermute(pole_own.astype(bf16), both, pole_pairs)
+    unfolded = jnp.take(pole_back[:, ::-1], unfold_idx, axis=2).astype(f32)
+    north_add = jnp.where(at_north, unfolded, 0.0)
+    south_add = jnp.where(at_south, unfolded, 0.0)
+
+    def final_of(c, rows):
+        middle = jnp.concatenate(
+            [
+                rows[:, r : 2 * r] + back_left[c].astype(f32),
+                rows[:, 2 * r : width],
+                rows[:, width : width + r] + back_right[c].astype(f32),
+            ],
+            axis=1,
+        )
+        return jnp.concatenate(
+            [middle[:r] + north_add[c], middle[r : height - r], middle[height - r :] + south_add[c]],
+            axis=0,
+        ).astype(bf16)
+
+    return (dq.reshape(height, width, features), final_of(0, rows_k), final_of(1, rows_v))
 
 
 def solution(mesh):

time: 106 us -> 125 us (1.18)
  starting transfers between devices: 26.7 us -> 42.8 us
  waiting for transfers between devices: 31.2 us -> 18.1 us
  other arithmetic: 9.92 us -> 17.8 us
  local copies, waits for them, and re-layouts: 18.6 us -> 25.7 us
    ppermute x6 -> x10, starting transfers between devices: 21.5 us -> 35 us  [the longest x1 8.32 us: on_device(): lax.ppermute(jnp.where(at_north, top_own, bottom_own), both, pole_pairs)]
    ppermute x6 -> x10, waiting for transfers between devices: 31.2 us -> 17.8 us  [the longest x1 7.57 us: on_device(): lax.ppermute(pair(rows_k[:, :r], rows_v[:, :r]).astype(bf16), 'lon', left...]
    slice x7 -> x23, local copies, waits for them, and re-layouts: 3.76 us -> 9.13 us  [the longest x2 2.6 us: on_device(): corner_left = lax.ppermute(pole_rows[:, :, width - r:], both, pole_right)]
    convert_element_type x0 -> x2, other arithmetic: none -> 3.58 us  [ext_of(): whole = jnp.concatenate([top[c], middle, bottom[c]], axis=0).astype(f32)]
    rev x2, local copies, waits for them, and re-layouts: 1.09 us -> 4.22 us  [on_device(): unfolded = jnp.take(pole_back[:, ::-1], unfold_idx, axis=2).astype(f32)]
    another operation x3 -> x11, other arithmetic: 1.2 us -> 3.3 us
    concatenate x3 -> x11, other arithmetic: 2.49 us -> 4.38 us  [the longest x1 1.04 us: on_device(): jnp.concatenate([from_left[:, :r], top_own, from_right[:, :r]], axis=2)]
    slice x2 -> x0, other arithmetic: 1.74 us -> none  [the longest x1 1.7 us: on_device(): bottom_g = dkv[:, ext_rows - r:].astype(jnp.bfloat16)]
  transfers between devices with their start and end apart: 10 -> 14, of which waited for: 5 -> 5; matrix products, arithmetic and copies ran while one was open for 7% -> 18% of each run, Pallas kernels for 0% -> 0%
where the time goes in v2:
time: 125 us; the launch traced here: 124 us
  starting transfers between devices  42.8 us (34%)
  local copies, waits for them, and re-layouts  25.7 us (21%)
  Pallas kernels  18.2 us (15%)
  waiting for transfers between devices  18.1 us (14%)
  other arithmetic  17.8 us (14%)
  between operations  1.39 us (1%)
    pallas_call x1, Pallas kernels, attention_core(): pl.pallas_call(lambda *refs: attention_kernel(width, *refs), out_shape=(j...  18.2 us
    ppermute x1, starting transfers between devices, on_device(): lax.ppermute(jnp.where(at_north, top_own, bottom_own), both, pole_pairs)  8.32 us
    ppermute x1, starting transfers between devices, on_device(): pole_back = lax.ppermute(pole_own.astype(bf16), both, pole_pairs)  7.96 us
    ppermute x1, waiting for transfers between devices, on_device(): lax.ppermute(pair(rows_k[:, :r], rows_v[:, :r]).astype(bf16), 'lon', left...  7.57 us
    ppermute x1, starting transfers between devices, on_device(): corner_back_right = lax.ppermute(pole_g[:, :, :r], both, pole_left)  4.82 us
    ppermute x1, waiting for transfers between devices, on_device(): pole_back = lax.ppermute(pole_own.astype(bf16), both, pole_pairs)  4.55 us
    rev x2, local copies, waits for them, and re-layouts, on_device(): unfolded = jnp.take(pole_back[:, ::-1], unfold_idx, axis=2).astype(f32)  4.22 us
    ppermute x1, starting transfers between devices, on_device(): corner_right = lax.ppermute(pole_rows[:, :, :r], both, pole_left)  4.05 us
  transfers between devices with their start and end apart: 14, of which 5 were waited for; matrix products, arithmetic and copies ran while one was open for 18% of the time, Pallas kernels for 0%

profile of v2, /device:TPU:32, one launch (start us, length us, event | category | flops | bytes accessed | tf_op | source)
XLA Modules:
  0.0 124.0 jit_solution(6684154081764767635)
XLA Ops:
  1.7 1.0 fusion.17
  4.2 8.3 %collective-permute-start = (bf16[2,4,16,1024]{3,1,0,2:T(4,128)(2,1)}, bf16[2,4,16,1024]{3,1,0,2:T(4,128)(2,1)S(1)}, u32[]{:S(2)}, u32[]{:S(2)}) collective-permute-start(bf16[2,4,16,1024]{3,1,0,2:T(4,128)(2,1)} %maximum_select_fusion), channel_id=1, source_target_pairs={{0,8},{1,9},{2,10},{3,11},{4,12},{5,13},{6,14},{7,15},{8,0},{9,1},... | collective-permute-start | bytes 786440 | tf_op jit(solution)/shard_map/ppermute | solution.py:164
  12.9 1.7 %collective-permute-start.3 = (bf16[2,16,4,1024]{3,1,0,2:T(8,128)(2,1)S(1)}, bf16[2,16,4,1024]{3,1,0,2:T(8,128)(2,1)S(1)}, u32[]{:S(2)}, u32[]{:S(2)}) collective-permute-start(bf16[2,16,4,1024]{3,1,0,2:T(8,128)(2,1)S(1)} %pad_maximum_fusion.11), channel_id=1, source_target_pairs={{0,1},{1,2},{2,3},{3,4},{4,5},{5,6},{6,7},{7,8},{8,9},{9,10},{10,1... | collective-permute-start | bytes 786440 | tf_op jit(solution)/shard_map/ppermute | solution.py:160
  14.7 1.4 %collective-permute-start.4 = (bf16[2,16,4,1024]{3,1,0,2:T(8,128)(2,1)S(1)}, bf16[2,16,4,1024]{3,1,0,2:T(8,128)(2,1)S(1)}, u32[]{:S(2)}, u32[]{:S(2)}) collective-permute-start(bf16[2,16,4,1024]{3,1,0,2:T(8,128)(2,1)S(1)} %pad_maximum_fusion.12), channel_id=1, source_target_pairs={{0,15},{1,0},{2,1},{3,2},{4,3},{5,4},{6,5},{7,6},{8,7},{9,8},{10,9... | collective-permute-start | bytes 786440 | tf_op jit(solution)/shard_map/ppermute | solution.py:161
  18.2 2.5 %collective-permute-done = bf16[2,4,16,1024]{3,1,0,2:T(4,128)(2,1)S(1)} collective-permute-done((bf16[2,4,16,1024]{3,1,0,2:T(4,128)(2,1)}, bf16[2,4,16,1024]{3,1,0,2:T(4,128)(2,1)S(1)}, u32[]{:S(2)}, u32[]{:S(2)}) %collective-permute-start) | collective-permute-done | bytes 262176 | tf_op jit(solution)/shard_map/ppermute | solution.py:164
  21.8 2.6 %slice.246 = bf16[2,4,4,1024]{3,1,0,2:T(4,128)(2,1)} reverse(bf16[2,4,4,1024]{3,1,0,2:T(4,128)(2,1)S(1)} %get-tuple-element.68), dimensions={1} | reverse | bytes 131072 | tf_op jit(solution)/shard_map/slice | solution.py:173
  24.4 2.7 %collective-permute-start.1 = (bf16[2,4,4,1024]{3,1,0,2:T(4,128)(2,1)}, bf16[2,4,4,1024]{3,1,0,2:T(4,128)(2,1)S(1)}, u32[]{:S(2)}, u32[]{:S(2)}) collective-permute-start(bf16[2,4,4,1024]{3,1,0,2:T(4,128)(2,1)} %slice.246), channel_id=1, source_target_pairs={{0,1},{1,2},{2,3},{3,4},{4,5},{5,6},{6,7},{7,8},{8,9},{9,10},{10,1... | collective-permute-start | bytes 196616 | tf_op jit(solution)/shard_map/ppermute | solution.py:173
  27.1 2.6 %slice.248 = bf16[2,4,4,1024]{3,1,0,2:T(4,128)(2,1)} reverse(bf16[2,4,4,1024]{3,1,0,2:T(4,128)(2,1)S(1)} %get-tuple-element.69), dimensions={1} | reverse | bytes 131072 | tf_op jit(solution)/shard_map/slice | solution.py:174
  29.6 4.0 %collective-permute-start.2 = (bf16[2,4,4,1024]{3,1,0,2:T(4,128)(2,1)}, bf16[2,4,4,1024]{3,1,0,2:T(4,128)(2,1)S(1)}, u32[]{:S(2)}, u32[]{:S(2)}) collective-permute-start(bf16[2,4,4,1024]{3,1,0,2:T(4,128)(2,1)} %slice.248), channel_id=1, source_target_pairs={{0,15},{1,0},{2,1},{3,2},{4,3},{5,4},{6,5},{7,6},{8,7},{9,8},{10,9... | collective-permute-start | bytes 196616 | tf_op jit(solution)/shard_map/ppermute | solution.py:174
  33.8 1.0 pad_maximum_fusion.10
  34.9 1.3 %collective-permute-start.6 = (bf16[2,4,24,1024]{3,1,0,2:T(4,128)(2,1)}, bf16[2,4,24,1024]{3,1,0,2:T(4,128)(2,1)S(1)}, u32[]{:S(2)}, u32[]{:S(2)}) collective-permute-start(bf16[2,4,24,1024]{3,1,0,2:T(4,128)(2,1)} %pad_maximum_fusion.10), channel_id=1, source_target_pairs={{16,0},{17,1},{18,2},{19,3},{20,4},{21,5},{22,6},{23,7},{24,8},{25... | collective-permute-start | bytes 1179656 | tf_op jit(solution)/shard_map/ppermute | solution.py:172
  36.2 1.0 pad_maximum_fusion.9
  37.2 3.0 %collective-permute-start.5 = (bf16[2,4,24,1024]{3,1,0,2:T(4,128)(2,1)}, bf16[2,4,24,1024]{3,1,0,2:T(4,128)(2,1)S(1)}, u32[]{:S(2)}, u32[]{:S(2)}) collective-permute-start(bf16[2,4,24,1024]{3,1,0,2:T(4,128)(2,1)} %pad_maximum_fusion.9), channel_id=1, source_target_pairs={{0,16},{1,17},{2,18},{3,19},{4,20},{5,21},{6,22},{7,23},{8,24},{9,... | collective-permute-start | bytes 1179656 | tf_op jit(solution)/shard_map/ppermute | solution.py:171
  43.1 1.8 %bitcast_convert_fusion.refs_3_ = f32[576,1024]{1,0:T(8,128)} fusion(bf16[24,24,1024]{2,1,0:T(8,128)(2,1)S(1)} %pad_maximum_fusion.3), kind=kLoop, calls=%fused_computation.9 | loop fusion | flops 589824 | bytes 3538944 | tf_op jit(solution)/shard_map/convert_element_type | solution.py:181
  45.4 1.8 %bitcast_convert_fusion.1.refs_2_ = f32[576,1024]{1,0:T(8,128)} fusion(bf16[24,24,1024]{2,1,0:T(8,128)(2,1)S(1)} %pad_maximum_fusion.2), kind=kLoop, calls=%fused_computation.10 | loop fusion | flops 589824 | bytes 3538944 | tf_op jit(solution)/shard_map/convert_element_type | solution.py:181
  47.2 18.2 %neighbourhood_attention_bwd.1 = (bf16[256,1024]{1,0:T(8,128)(2,1)}, f32[576,1024]{1,0:T(8,128)}, f32[576,1024]{1,0:T(8,128)}) custom-call(bf16[256,1024]{1,0:T(8,128)(2,1)} %bitcast.151, bf16[256,1024]{1,0:T(8,128)(2,1)} %bitcast.152, f32[576,1024]{1,0:T(8,128)} %bitcast_convert_fusion.1.refs_2_, f32[576,1024]{1,0:T(8,128)} %bitcast_convert_fusion.refs_3_), custom_call_target="tpu_custom_call" | custom-call | flops 2013265920 | bytes 11010048 | tf_op jit(solution)/shard_map/neighbourhood_attention_bwd/pallas_call | solution.py:101
  65.4 2.0 %convert.69 = bf16[576,1024]{1,0:T(8,128)(2,1)S(1)} convert(f32[576,1024]{1,0:T(8,128)} %get-tuple-element.9) | non-fusion elementwise | flops 589824 | bytes 3538944 | tf_op jit(solution)/shard_map/convert.44
  72.1 1.9 %collective-permute-start.11 = (bf16[2,4,4,1024]{3,1,0,2:T(4,128)(2,1)S(1)}, bf16[2,4,4,1024]{3,1,0,2:T(4,128)(2,1)S(1)}, u32[]{:S(2)}, u32[]{:S(2)}) collective-permute-start(bf16[2,4,4,1024]{3,1,0,2:T(4,128)(2,1)S(1)} %get-tuple-element.52), channel_id=1, source_target_pairs={{0,1},{1,2},{2,3},{3,4},{4,5},{5,6},{6,7},{7,8},{8,9},{9,10},{10,1... | collective-permute-start | bytes 196616 | tf_op jit(solution)/shard_map/ppermute | solution.py:200
  74.0 4.8 %collective-permute-start.12 = (bf16[2,4,4,1024]{3,1,0,2:T(4,128)(2,1)S(1)}, bf16[2,4,4,1024]{3,1,0,2:T(4,128)(2,1)S(1)}, u32[]{:S(2)}, u32[]{:S(2)}) collective-permute-start(bf16[2,4,4,1024]{3,1,0,2:T(4,128)(2,1)S(1)} %get-tuple-element.53), channel_id=1, source_target_pairs={{0,15},{1,0},{2,1},{3,2},{4,3},{5,4},{6,5},{7,6},{8,7},{9,8},{10,9... | collective-permute-start | bytes 196616 | tf_op jit(solution)/shard_map/ppermute | solution.py:199
  78.9 2.1 %collective-permute-start.7 = (bf16[2,4,24,1024]{3,1,0,2:T(4,128)(2,1)}, bf16[2,4,24,1024]{3,1,0,2:T(4,128)(2,1)}, u32[]{:S(2)}, u32[]{:S(2)}) collective-permute-start(bf16[2,4,24,1024]{3,1,0,2:T(4,128)(2,1)} %copy_dynamic-update-slice_fusion.2), channel_id=1, source_target_pairs={{0,16},{1,17},{2,18},{3,19},{4,20},{5,21},{6,22},{7,23},{8,24},{9,... | collective-permute-start | bytes 1179656 | tf_op jit(solution)/shard_map/ppermute | solution.py:197
  81.0 3.1 %collective-permute-done.12 = bf16[2,4,4,1024]{3,1,0,2:T(4,128)(2,1)S(1)} collective-permute-done((bf16[2,4,4,1024]{3,1,0,2:T(4,128)(2,1)S(1)}, bf16[2,4,4,1024]{3,1,0,2:T(4,128)(2,1)S(1)}, u32[]{:S(2)}, u32[]{:S(2)}) %collective-permute-start.12) | collective-permute-done | bytes 65568 | tf_op jit(solution)/shard_map/ppermute | solution.py:199
  84.3 8.0 %collective-permute-start.13 = (bf16[2,4,16,1024]{3,1,0,2:T(4,128)(2,1)S(1)}, bf16[2,4,16,1024]{3,1,0,2:T(4,128)(2,1)}, u32[]{:S(2)}, u32[]{:S(2)}) collective-permute-start(bf16[2,4,16,1024]{3,1,0,2:T(4,128)(2,1)S(1)} %pad_maximum_fusion.15), channel_id=1, source_target_pairs={{0,8},{1,9},{2,10},{3,11},{4,12},{5,13},{6,14},{7,15},{8,0},{9,1},... | collective-permute-start | bytes 786440 | tf_op jit(solution)/shard_map/ppermute | solution.py:229
  92.4 1.5 %collective-permute-start.8 = (bf16[2,4,24,1024]{3,1,0,2:T(4,128)(2,1)}, bf16[2,4,24,1024]{3,1,0,2:T(4,128)(2,1)}, u32[]{:S(2)}, u32[]{:S(2)}) collective-permute-start(bf16[2,4,24,1024]{3,1,0,2:T(4,128)(2,1)} %copy_dynamic-update-slice_fusion), channel_id=1, source_target_pairs={{16,0},{17,1},{18,2},{19,3},{20,4},{21,5},{22,6},{23,7},{24,8},{25... | collective-permute-start | bytes 1179656 | tf_op jit(solution)/shard_map/ppermute | solution.py:196
  95.0 4.6 %collective-permute-done.13 = bf16[2,4,16,1024]{3,1,0,2:T(4,128)(2,1)} collective-permute-done((bf16[2,4,16,1024]{3,1,0,2:T(4,128)(2,1)S(1)}, bf16[2,4,16,1024]{3,1,0,2:T(4,128)(2,1)}, u32[]{:S(2)}, u32[]{:S(2)}) %collective-permute-start.13) | collective-permute-done | bytes 262176 | tf_op jit(solution)/shard_map/ppermute | solution.py:229
  99.6 3.4 %rev.7 = bf16[2,4,16,1024]{3,1,0,2:T(4,128)(2,1)S(1)} reverse(bf16[2,4,16,1024]{3,1,0,2:T(4,128)(2,1)} %collective-permute-done.13), dimensions={1} | reverse | bytes 524288 | tf_op jit(solution)/shard_map/rev | solution.py:230
  103.8 1.7 %gather_fusion.3 = bf16[16,2,4,1024]{3,2,1,0:T(4,128)(2,1)S(1)} fusion(bf16[2,4,16,1024]{3,1,2,0:T(4,128)(2,1)} %copy.35, s32[1024]{0:T(1024)S(1)} %pad_clamp_fusion), kind=kCustom, calls=%fused_computation.3.clone | custom fusion | bytes 524352 | tf_op jit(solution)/shard_map/jit(_take)/gather | solution.py:230
  105.9 1.6 %convert_add_fusion.1 = (f32[4,24,1024]{2,0,1:T(4,128)S(1)}, f32[4,24,1024]{2,0,1:T(4,128)S(1)}) fusion(f32[4,24,1024]{2,1,0:T(8,128)S(1)} %bitcast.146, bf16[2,4,24,1024]{3,1,0,2:T(4,128)(2,1)} %collective-permute-done.7, f32[4,24,1024]{2,1,0:T(8,128)S(1)} %bitcast.144), kind=kLoop, calls=%fused_computation.22 | loop fusion | flops 393216 | bytes 1966080 | tf_op jit(solution)/shard_map/add | solution.py:213
  107.6 1.6 %convert_add_fusion = (f32[4,24,1024]{2,0,1:T(4,128)S(1)}, f32[4,24,1024]{2,0,1:T(4,128)S(1)}) fusion(f32[4,24,1024]{2,1,0:T(8,128)S(1)} %bitcast.145, bf16[2,4,24,1024]{3,1,0,2:T(4,128)(2,1)} %collective-permute-done.8, f32[4,24,1024]{2,1,0:T(8,128)S(1)} %bitcast.143), kind=kLoop, calls=%fused_computation.21 | loop fusion | flops 393216 | bytes 1966080 | tf_op jit(solution)/shard_map/add | solution.py:215
  110.0 2.1 %collective-permute-start.9 = (bf16[2,16,4,1024]{3,1,2,0:T(8,128)(2,1)S(1)}, bf16[2,16,4,1024]{3,1,2,0:T(8,128)(2,1)S(1)}, u32[]{:S(2)}, u32[]{:S(2)}) collective-permute-start(bf16[2,16,4,1024]{3,1,2,0:T(8,128)(2,1)S(1)} %pad_maximum_fusion.13), channel_id=1, source_target_pairs={{0,1},{1,2},{2,3},{3,4},{4,5},{5,6},{6,7},{7,8},{8,9},{9,10},{10,1... | collective-permute-start | bytes 786440 | tf_op jit(solution)/shard_map/ppermute | solution.py:226
  112.8 7.6 %collective-permute-done.10 = bf16[2,16,4,1024]{3,1,2,0:T(8,128)(2,1)S(1)} collective-permute-done((bf16[2,16,4,1024]{3,1,2,0:T(8,128)(2,1)S(1)}, bf16[2,16,4,1024]{3,1,2,0:T(8,128)(2,1)S(1)}, u32[]{:S(2)}, u32[]{:S(2)}) %collective-permute-start.10) | collective-permute-done | bytes 262176 | tf_op jit(solution)/shard_map/ppermute | solution.py:223
  121.6 1.1 copy.41
  122.9 1.1 copy.40
  (107 shorter events, 19.5 us)
Async XLA Ops:
  0.6 11.9 %copy-start.3 = (bf16[16,16,1024]{2,1,0:T(8,128)(2,1)S(1)}, bf16[16,16,1024]{2,1,0:T(8,128)(2,1)}, u32[]{:S(2)}) copy-start(bf16[16,16,1024]{2,1,0:T(8,128)(2,1)} %param.10) | copy-start | bytes 1572868
  1.7 10.9 %copy-start.2 = (bf16[16,16,1024]{2,1,0:T(8,128)(2,1)S(1)}, bf16[16,16,1024]{2,1,0:T(8,128)(2,1)}, u32[]{:S(2)}) copy-start(bf16[16,16,1024]{2,1,0:T(8,128)(2,1)} %param.11) | copy-start | bytes 1572868
  4.2 11.9 %copy-start.4 = (s32[2,256]{1,0:T(2,128)S(1)}, s32[2,256]{1,0:T(2,128)}, u32[]{:S(2)}) copy-start(s32[2,256]{1,0:T(2,128)} %param.13) | copy-start | bytes 6148
  4.2 16.5 %collective-permute-start = (bf16[2,4,16,1024]{3,1,0,2:T(4,128)(2,1)}, bf16[2,4,16,1024]{3,1,0,2:T(4,128)(2,1)S(1)}, u32[]{:S(2)}, u32[]{:S(2)}) collective-permute-start(bf16[2,4,16,1024]{3,1,0,2:T(4,128)(2,1)} %maximum_select_fusion), channel_id=1, source_target_pairs={{0,8},{1,9},{2,10},{3,11},{4,12},{5,13},{6,14},{7,15},{8,0},{9,1},... | collective-permute-start | bytes 786440 | tf_op jit(solution)/shard_map/ppermute | solution.py:164
  12.9 20.8 %collective-permute-start.3 = (bf16[2,16,4,1024]{3,1,0,2:T(8,128)(2,1)S(1)}, bf16[2,16,4,1024]{3,1,0,2:T(8,128)(2,1)S(1)}, u32[]{:S(2)}, u32[]{:S(2)}) collective-permute-start(bf16[2,16,4,1024]{3,1,0,2:T(8,128)(2,1)S(1)} %pad_maximum_fusion.11), channel_id=1, source_target_pairs={{0,1},{1,2},{2,3},{3,4},{4,5},{5,6},{6,7},{7,8},{8,9},{9,10},{10,1... | collective-permute-start | bytes 786440 | tf_op jit(solution)/shard_map/ppermute | solution.py:160
  14.7 19.1 %collective-permute-start.4 = (bf16[2,16,4,1024]{3,1,0,2:T(8,128)(2,1)S(1)}, bf16[2,16,4,1024]{3,1,0,2:T(8,128)(2,1)S(1)}, u32[]{:S(2)}, u32[]{:S(2)}) collective-permute-start(bf16[2,16,4,1024]{3,1,0,2:T(8,128)(2,1)S(1)} %pad_maximum_fusion.12), channel_id=1, source_target_pairs={{0,15},{1,0},{2,1},{3,2},{4,3},{5,4},{6,5},{7,6},{8,7},{9,8},{10,9... | collective-permute-start | bytes 786440 | tf_op jit(solution)/shard_map/ppermute | solution.py:161
  24.4 17.1 %collective-permute-start.1 = (bf16[2,4,4,1024]{3,1,0,2:T(4,128)(2,1)}, bf16[2,4,4,1024]{3,1,0,2:T(4,128)(2,1)S(1)}, u32[]{:S(2)}, u32[]{:S(2)}) collective-permute-start(bf16[2,4,4,1024]{3,1,0,2:T(4,128)(2,1)} %slice.246), channel_id=1, source_target_pairs={{0,1},{1,2},{2,3},{3,4},{4,5},{5,6},{6,7},{7,8},{8,9},{9,10},{10,1... | collective-permute-start | bytes 196616 | tf_op jit(solution)/shard_map/ppermute | solution.py:173
  29.6 11.8 %collective-permute-start.2 = (bf16[2,4,4,1024]{3,1,0,2:T(4,128)(2,1)}, bf16[2,4,4,1024]{3,1,0,2:T(4,128)(2,1)S(1)}, u32[]{:S(2)}, u32[]{:S(2)}) collective-permute-start(bf16[2,4,4,1024]{3,1,0,2:T(4,128)(2,1)} %slice.248), channel_id=1, source_target_pairs={{0,15},{1,0},{2,1},{3,2},{4,3},{5,4},{6,5},{7,6},{8,7},{9,8},{10,9... | collective-permute-start | bytes 196616 | tf_op jit(solution)/shard_map/ppermute | solution.py:174
  34.9 6.6 %collective-permute-start.6 = (bf16[2,4,24,1024]{3,1,0,2:T(4,128)(2,1)}, bf16[2,4,24,1024]{3,1,0,2:T(4,128)(2,1)S(1)}, u32[]{:S(2)}, u32[]{:S(2)}) collective-permute-start(bf16[2,4,24,1024]{3,1,0,2:T(4,128)(2,1)} %pad_maximum_fusion.10), channel_id=1, source_target_pairs={{16,0},{17,1},{18,2},{19,3},{20,4},{21,5},{22,6},{23,7},{24,8},{25... | collective-permute-start | bytes 1179656 | tf_op jit(solution)/shard_map/ppermute | solution.py:172
  37.2 4.6 %collective-permute-start.5 = (bf16[2,4,24,1024]{3,1,0,2:T(4,128)(2,1)}, bf16[2,4,24,1024]{3,1,0,2:T(4,128)(2,1)S(1)}, u32[]{:S(2)}, u32[]{:S(2)}) collective-permute-start(bf16[2,4,24,1024]{3,1,0,2:T(4,128)(2,1)} %pad_maximum_fusion.9), channel_id=1, source_target_pairs={{0,16},{1,17},{2,18},{3,19},{4,20},{5,21},{6,22},{7,23},{8,24},{9,... | collective-permute-start | bytes 1179656 | tf_op jit(solution)/shard_map/ppermute | solution.py:171
  65.4 2.9 %copy-start = (f32[576,1024]{1,0:T(8,128)S(1)}, f32[576,1024]{1,0:T(8,128)}, u32[]{:S(2)}) copy-start(f32[576,1024]{1,0:T(8,128)} %get-tuple-element.10) | copy-start | bytes 7077892
  70.2 22.2 %copy-start.1 = (f32[576,1024]{1,0:T(8,128)S(1)}, f32[576,1024]{1,0:T(8,128)}, u32[]{:S(2)}) copy-start(f32[576,1024]{1,0:T(8,128)} %get-tuple-element.9) | copy-start | bytes 7077892
  72.1 8.9 %collective-permute-start.11 = (bf16[2,4,4,1024]{3,1,0,2:T(4,128)(2,1)S(1)}, bf16[2,4,4,1024]{3,1,0,2:T(4,128)(2,1)S(1)}, u32[]{:S(2)}, u32[]{:S(2)}) collective-permute-start(bf16[2,4,4,1024]{3,1,0,2:T(4,128)(2,1)S(1)} %get-tuple-element.52), channel_id=1, source_target_pairs={{0,1},{1,2},{2,3},{3,4},{4,5},{5,6},{6,7},{7,8},{8,9},{9,10},{10,1... | collective-permute-start | bytes 196616 | tf_op jit(solution)/shard_map/ppermute | solution.py:200
  74.0 10.0 %collective-permute-start.12 = (bf16[2,4,4,1024]{3,1,0,2:T(4,128)(2,1)S(1)}, bf16[2,4,4,1024]{3,1,0,2:T(4,128)(2,1)S(1)}, u32[]{:S(2)}, u32[]{:S(2)}) collective-permute-start(bf16[2,4,4,1024]{3,1,0,2:T(4,128)(2,1)S(1)} %get-tuple-element.53), channel_id=1, source_target_pairs={{0,15},{1,0},{2,1},{3,2},{4,3},{5,4},{6,5},{7,6},{8,7},{9,8},{10,9... | collective-permute-start | bytes 196616 | tf_op jit(solution)/shard_map/ppermute | solution.py:199
  78.9 27.0 %collective-permute-start.7 = (bf16[2,4,24,1024]{3,1,0,2:T(4,128)(2,1)}, bf16[2,4,24,1024]{3,1,0,2:T(4,128)(2,1)}, u32[]{:S(2)}, u32[]{:S(2)}) collective-permute-start(bf16[2,4,24,1024]{3,1,0,2:T(4,128)(2,1)} %copy_dynamic-update-slice_fusion.2), channel_id=1, source_target_pairs={{0,16},{1,17},{2,18},{3,19},{4,20},{5,21},{6,22},{7,23},{8,24},{9,... | collective-permute-start | bytes 1179656 | tf_op jit(solution)/shard_map/ppermute | solution.py:197
  84.3 15.2 %collective-permute-start.13 = (bf16[2,4,16,1024]{3,1,0,2:T(4,128)(2,1)S(1)}, bf16[2,4,16,1024]{3,1,0,2:T(4,128)(2,1)}, u32[]{:S(2)}, u32[]{:S(2)}) collective-permute-start(bf16[2,4,16,1024]{3,1,0,2:T(4,128)(2,1)S(1)} %pad_maximum_fusion.15), channel_id=1, source_target_pairs={{0,8},{1,9},{2,10},{3,11},{4,12},{5,13},{6,14},{7,15},{8,0},{9,1},... | collective-permute-start | bytes 786440 | tf_op jit(solution)/shard_map/ppermute | solution.py:229
  92.4 15.1 %collective-permute-start.8 = (bf16[2,4,24,1024]{3,1,0,2:T(4,128)(2,1)}, bf16[2,4,24,1024]{3,1,0,2:T(4,128)(2,1)}, u32[]{:S(2)}, u32[]{:S(2)}) collective-permute-start(bf16[2,4,24,1024]{3,1,0,2:T(4,128)(2,1)} %copy_dynamic-update-slice_fusion), channel_id=1, source_target_pairs={{16,0},{17,1},{18,2},{19,3},{20,4},{21,5},{22,6},{23,7},{24,8},{25... | collective-permute-start | bytes 1179656 | tf_op jit(solution)/shard_map/ppermute | solution.py:196
  109.9 10.5 %collective-permute-start.10 = (bf16[2,16,4,1024]{3,1,2,0:T(8,128)(2,1)S(1)}, bf16[2,16,4,1024]{3,1,2,0:T(8,128)(2,1)S(1)}, u32[]{:S(2)}, u32[]{:S(2)}) collective-permute-start(bf16[2,16,4,1024]{3,1,2,0:T(8,128)(2,1)S(1)} %pad_maximum_fusion.14), channel_id=1, source_target_pairs={{0,15},{1,0},{2,1},{3,2},{4,3},{5,4},{6,5},{7,6},{8,7},{9,8},{10,9... | collective-permute-start | bytes 786440 | tf_op jit(solution)/shard_map/ppermute | solution.py:223
  110.0 10.4 %collective-permute-start.9 = (bf16[2,16,4,1024]{3,1,2,0:T(8,128)(2,1)S(1)}, bf16[2,16,4,1024]{3,1,2,0:T(8,128)(2,1)S(1)}, u32[]{:S(2)}, u32[]{:S(2)}) collective-permute-start(bf16[2,16,4,1024]{3,1,2,0:T(8,128)(2,1)S(1)} %pad_maximum_fusion.13), channel_id=1, source_target_pairs={{0,1},{1,2},{2,3},{3,4},{4,5},{5,6},{6,7},{7,8},{8,9},{9,10},{10,1... | collective-permute-start | bytes 786440 | tf_op jit(solution)/shard_map/ppermute | solution.py:226

commit v3 on v1

v3 whole, which is shorter than its diff:
```python
import jax
import jax.numpy as jnp
from jax import lax
from jax.experimental import pallas as pl
from jax.experimental.pallas import tpu as pltpu
from jax.sharding import PartitionSpec as P

HEADS = 16
HEAD_DIM = 64
RADIUS = 4

SPAN = 2 * RADIUS + 1
TILE_ROWS = 8
LANES = 128


def attention_kernel(width, *refs):
    (q_ref, g_ref, k_own, k_top, k_bot, k_left, k_right, v_own, v_top, v_bot, v_left, v_right) = refs[:12]
    (dq_ref, dk_own, dk_top, dk_bot, dk_left, dk_right, dv_own, dv_top, dv_bot, dv_left, dv_right) = refs[12:23]
    bias_ref = refs[23]
    scale = HEAD_DIM ** (-0.5)
    r = RADIUS
    tq = TILE_ROWS * width
    main = 2 * TILE_ROWS * width
    side = 2 * TILE_ROWS * r
    tk = main + 2 * side
    edge = r * width
    pairs = q_ref.shape[1] // LANES

    qi = lax.broadcasted_iota(jnp.int32, (tq, tk), 0).astype(jnp.float32)
    ki = lax.broadcasted_iota(jnp.int32, (tq, tk), 1).astype(jnp.float32)
    qr = jnp.floor((qi + 0.5) * (1.0 / width))
    qc = qi - width * qr
    in_main = ki < main
    in_left = (ki >= main) & (ki < main + side)
    kk = jnp.where(in_main, ki, jnp.where(in_left, ki - main, ki - main - side))
    per_row = jnp.where(in_main, float(width), float(r))
    kr = jnp.floor((kk + 0.5) / per_row)
    kc = kk - per_row * kr + jnp.where(in_main, float(r), jnp.where(in_left, 0.0, float(width + r)))
    dr = kr - qr
    dc = kc - qc
    ok = (dr >= 0) & (dr <= 2 * r) & (dc >= 0) & (dc <= 2 * r)
    bias_ref[...] = jnp.where(ok, 0.0, -jnp.inf).astype(jnp.float32)

    nt = (((1,), (1,)), ((), ()))
    tn = (((0,), (0,)), ((), ()))

    def head(qh, gh, kp, vp):
        s = lax.dot_general(qh, kp, nt, preferred_element_type=jnp.float32) * scale + bias_ref[...]
        m = jnp.max(s, axis=1, keepdims=True)
        e = jnp.exp(s - m)
        total = jnp.sum(e, axis=1, keepdims=True)
        w = e * (1.0 / total)
        dw = lax.dot_general(gh, vp, nt, preferred_element_type=jnp.float32)
        corr = jnp.sum(w * dw, axis=1, keepdims=True)
        ds = (w * (dw - corr)).astype(jnp.bfloat16)
        return ds, w.astype(jnp.bfloat16)

    def gather_keys(own, top, bot, left, right, t, lanes):
        if t == 0:
            middle = [top[pl.ds(0, edge), lanes], own[pl.ds(0, main - edge), lanes]]
        else:
            middle = [own[pl.ds(edge, main - edge), lanes], bot[pl.ds(0, edge), lanes]]
        sides = [left[pl.ds(t * side // 2, side), lanes], right[pl.ds(t * side // 2, side), lanes]]
        return jnp.concatenate(middle + sides, axis=0)

    def scatter_grads(d, own, top, bot, left, right, t, lanes):
        half = side // 2
        if t == 0:
            top[pl.ds(0, edge), lanes] = d[:edge]
            own[pl.ds(0, main - edge), lanes] = d[edge:main]
            left[pl.ds(0, side), lanes] = d[main : main + side]
            right[pl.ds(0, side), lanes] = d[main + side :]
        else:
            shared = main - 2 * edge
            own[pl.ds(edge, shared), lanes] += d[:shared]
            own[pl.ds(edge + shared, edge), lanes] = d[shared : main - edge]
            bot[pl.ds(0, edge), lanes] = d[main - edge : main]
            left[pl.ds(half, half), lanes] += d[main : main + half]
            left[pl.ds(side, half), lanes] = d[main + half : main + side]
            right[pl.ds(half, half), lanes] += d[main + side : main + side + half]
            right[pl.ds(side, half), lanes] = d[main + side + half :]

    def body(p, carry):
        lanes = pl.ds(pl.multiple_of(p * LANES, LANES), LANES)
        for t in range(2):
            qp = q_ref[pl.ds(t * tq, tq), lanes]
            gp = g_ref[pl.ds(t * tq, tq), lanes]
            kp = gather_keys(k_own, k_top, k_bot, k_left, k_right, t, lanes)
            vp = gather_keys(v_own, v_top, v_bot, v_left, v_right, t, lanes)
            lo = lax.broadcasted_iota(jnp.int32, qp.shape, 1) < HEAD_DIM
            zero = jnp.zeros_like(qp)
            qa = jnp.where(lo, qp, zero)
            qb = jnp.where(lo, zero, qp)
            ga = jnp.where(lo, gp, zero)
            gb = jnp.where(lo, zero, gp)
            dsa, wa = head(qa, ga, kp, vp)
            dsb, wb = head(qb, gb, kp, vp)
            dqa = jnp.dot(dsa, kp, preferred_element_type=jnp.float32)
            dqb = jnp.dot(dsb, kp, preferred_element_type=jnp.float32)
            dq = jnp.where(lo, dqa, dqb) * scale
            dq_ref[pl.ds(t * tq, tq), lanes] = dq.astype(dq_ref.dtype)
            dk = (
                lax.dot_general(dsa, qa, tn, preferred_element_type=jnp.float32)
                + lax.dot_general(dsb, qb, tn, preferred_element_type=jnp.float32)
            ) * scale
            dv = lax.dot_general(wa, ga, tn, preferred_element_type=jnp.float32) + lax.dot_general(
                wb, gb, tn, preferred_element_type=jnp.float32
            )
            scatter_grads(dk, dk_own, dk_top, dk_bot, dk_left, dk_right, t, lanes)
            scatter_grads(dv, dv_own, dv_top, dv_bot, dv_left, dv_right, t, lanes)
        return carry

    lax.fori_loop(0, pairs, body, 0)


def attention_core(q2, g2, k_parts, v_parts, width):
    cells, features = q2.shape
    r = RADIUS
    tq = TILE_ROWS * width
    tk = 2 * TILE_ROWS * (width + 2 * r)
    tiles = cells // tq
    assert tiles == 2
    part_shapes = [p.shape for p in k_parts]
    key_cells = sum(s[0] for s in part_shapes)
    flops = 10 * 2 * tq * tk * LANES * (features // LANES) * tiles
    vmem = pl.BlockSpec(memory_space=pltpu.VMEM)
    outs = [jax.ShapeDtypeStruct((cells, features), jnp.bfloat16)]
    outs += [jax.ShapeDtypeStruct(s, jnp.float32) for s in part_shapes] * 2
    results = pl.pallas_call(
        lambda *refs: attention_kernel(width, *refs),
        out_shape=tuple(outs),
        in_specs=[vmem] * 12,
        out_specs=tuple([vmem] * 11),
        scratch_shapes=[pltpu.VMEM((tq, tk), jnp.float32)],
        cost_estimate=pl.CostEstimate(
            flops=flops,
            transcendentals=2 * tq * tk * HEADS * tiles,
            bytes_accessed=2 * (3 * cells * features) + 2 * (2 * key_cells * features)
            + 4 * (2 * key_cells * features),
        ),
        name="neighbourhood_attention_bwd",
    )(q2, g2, *k_parts, *v_parts)
    return results[0], results[1:6], results[6:11]


def on_device(queries, keys, values, grad_out, fold_cols):
    height, width, features = queries.shape
    n_lat = lax.axis_size("lat")
    n_lon = lax.axis_size("lon")
    half = n_lon // 2
    i = lax.axis_index("lat")
    j = lax.axis_index("lon")
    at_north = i == 0
    at_south = i == n_lat - 1
    partner_j = (j + half) % n_lon
    r = RADIUS

    def flat(a, b):
        return a * n_lon + b

    down_pairs = [(flat(a, b), flat(a + 1, b)) for a in range(n_lat - 1) for b in range(n_lon)]
    up_pairs = [(flat(a + 1, b), flat(a, b)) for a in range(n_lat - 1) for b in range(n_lon)]
    pole_pairs = [(flat(a, b), flat(a, (b + half) % n_lon)) for a in (0, n_lat - 1) for b in range(n_lon)]
    right_pairs = [(b, (b + 1) % n_lon) for b in range(n_lon)]
    left_pairs = [(b, (b - 1) % n_lon) for b in range(n_lon)]
    both = ("lat", "lon")

    ext_rows = height + 2 * r
    ext_w = width + 2 * r
    my_ext_cols = (j * width - r + jnp.arange(ext_w)) % (n_lon * width)
    partner_ext_cols = (partner_j * width - r + jnp.arange(ext_w)) % (n_lon * width)
    fold_row = jnp.where(at_north, fold_cols[0], fold_cols[1])
    fold_idx = (jnp.take(fold_row, my_ext_cols) - (partner_j * width - r)) % (n_lon * width)
    landing = (jnp.take(fold_row, partner_ext_cols) - (j * width - r)) % (n_lon * width)
    unfold_idx = jnp.zeros((ext_w,), jnp.int32).at[landing].set(jnp.arange(ext_w, dtype=jnp.int32))

    f32 = jnp.float32
    bf16 = jnp.bfloat16

    def pair(a, b):
        return jnp.stack([a, b])

    from_left = lax.ppermute(pair(keys[:, width - r :], values[:, width - r :]), "lon", right_pairs)
    from_right = lax.ppermute(pair(keys[:, :r], values[:, :r]), "lon", left_pairs)
    top_send = jnp.concatenate([from_left[:, :r], pair(keys[:r], values[:r]), from_right[:, :r]], axis=2)
    bottom_send = jnp.concatenate(
        [from_left[:, height - r :], pair(keys[height - r :], values[height - r :]), from_right[:, height - r :]],
        axis=2,
    )
    from_above = lax.ppermute(bottom_send, both, down_pairs)
    from_below = lax.ppermute(top_send, both, up_pairs)
    pole_recv = lax.ppermute(jnp.where(at_north, top_send, bottom_send), both, pole_pairs)
    pole_rows = jnp.take(pole_recv, fold_idx, axis=2)[:, ::-1]
    top = jnp.where(at_north, pole_rows, from_above)
    bottom = jnp.where(at_south, pole_rows, from_below)

    def parts_of(c, own):
        side_l = jnp.concatenate([top[c, :, :r], from_left[c], bottom[c, :, :r]], axis=0)
        side_r = jnp.concatenate([top[c, :, ext_w - r :], from_right[c], bottom[c, :, ext_w - r :]], axis=0)
        return (
            own.reshape(height * width, features),
            top[c, :, r : ext_w - r].reshape(r * width, features),
            bottom[c, :, r : ext_w - r].reshape(r * width, features),
            side_l.reshape(ext_rows * r, features),
            side_r.reshape(ext_rows * r, features),
        )

    dq, dk, dv = attention_core(
        queries.reshape(height * width, features),
        grad_out.reshape(height * width, features),
        parts_of(0, keys),
        parts_of(1, values),
        width,
    )

    def strip(d, which):
        own, top_p, bot_p, left_p, right_p = d
        rows = slice(0, r) if which == 0 else slice(ext_rows - r, ext_rows)
        middle = top_p if which == 0 else bot_p
        return jnp.concatenate(
            [
                left_p.reshape(ext_rows, r, features)[rows],
                middle.reshape(r, width, features),
                right_p.reshape(ext_rows, r, features)[rows],
            ],
            axis=1,
        )

    top_g = pair(strip(dk, 0), strip(dv, 0)).astype(bf16)
    bottom_g = pair(strip(dk, 1), strip(dv, 1)).astype(bf16)
    up_recv = lax.ppermute(top_g, both, up_pairs)
    down_recv = lax.ppermute(bottom_g, both, down_pairs)
    pole_g = lax.ppermute(jnp.where(at_north, top_g, bottom_g), both, pole_pairs)
    unfolded = jnp.take(pole_g[:, ::-1], unfold_idx, axis=2)
    add_top = jnp.where(at_north, unfolded, down_recv).astype(f32)
    add_bottom = jnp.where(at_south, unfolded, up_recv).astype(f32)

    def rows_added(c, block, cols):
        return jnp.concatenate(
            [block[:r] + add_top[c, :, cols], block[r : height - r], block[height - r :] + add_bottom[c, :, cols]],
            axis=0,
        )

    def sides_of(c, d):
        left_p = d[3].reshape(ext_rows, r, features)[r : ext_rows - r]
        right_p = d[4].reshape(ext_rows, r, features)[r : ext_rows - r]
        return (
            rows_added(c, left_p, slice(0, r)),
            rows_added(c, right_p, slice(ext_w - r, ext_w)),
        )

    left_k, right_k = sides_of(0, dk)
    left_v, right_v = sides_of(1, dv)
    back_right = lax.ppermute(pair(left_k, left_v).astype(bf16), "lon", left_pairs)
    back_left = lax.ppermute(pair(right_k, right_v).astype(bf16), "lon", right_pairs)

    def final_of(c, d):
        own = rows_added(c, d[0].reshape(height, width, features), slice(r, ext_w - r))
        return jnp.concatenate(
            [
                own[:, :r] + back_left[c].astype(f32),
                own[:, r : width - r],
                own[:, width - r :] + back_right[c].astype(f32),
            ],
            axis=1,
        ).astype(bf16)

    return (dq.reshape(height, width, features), final_of(0, dk), final_of(1, dv))


def solution(mesh):
    placed = (
        P("lat", "lon", None),
        P("lat", "lon", None),
        P("lat", "lon", None),
        P("lat", "lon", None),
        P(),
    )
    return jax.shard_map(
        on_device,
        mesh=mesh,
        in_specs=placed,
        out_specs=(P("lat", "lon", None), P("lat", "lon", None), P("lat", "lon", None)),
        check_vma=False,
    )
```

time: 106 us -> 113 us (1.066)
  local copies, waits for them, and re-layouts: 18.6 us -> 24.9 us
    slice x7 -> x42, local copies, waits for them, and re-layouts: 3.76 us -> 8.35 us  [the longest x10 2.71 us: rows_added(): block[r:height - r]]
    ppermute x4, waiting for transfers between devices: 17.4 us -> 13.8 us  [the longest x1 8.38 us: on_device(): lax.ppermute(pair(keys[:, :r], values[:, :r]), 'lon', left_pairs)]
    reshape x0 -> x4, local copies, waits for them, and re-layouts: none -> 2.94 us  [the longest x2 1.48 us: parts_of(): side_r.reshape(ext_rows * r, features)]
    another operation x3 -> x25, other arithmetic: 1.2 us -> 3.96 us  [the longest x13 2.27 us: pair(): return jnp.stack([a, b])]
    ppermute x1, waiting for transfers between devices: 5.29 us -> 7.99 us  [on_device(): lax.ppermute(jnp.where(at_north, top_send, bottom_send), both, pole_pairs)]
    add x1 -> x2, other arithmetic: 2.65 us -> 0.19 us  [the longest x1 0.1 us: rows_added(): block[height - r:] + add_bottom[c, :, cols]]
    unnamed x11 -> x40, local copies, waits for them, and re-layouts: 5.38 us -> 7.45 us
    slice x2 -> x0, other arithmetic: 1.74 us -> none  [the longest x1 1.7 us: on_device(): bottom_g = dkv[:, ext_rows - r:].astype(jnp.bfloat16)]
  transfers between devices with their start and end apart: 10 -> 10, of which waited for: 5 -> 4; matrix products, arithmetic and copies ran while one was open for 7% -> 6% of each run, Pallas kernels for 0% -> 0%
where the time goes in v3:
time: 113 us; the launch traced here: 111 us
  waiting for transfers between devices  30.3 us (27%)
  starting transfers between devices  27.8 us (25%)
  local copies, waits for them, and re-layouts  24.9 us (22%)
  Pallas kernels  17.4 us (15%)
  other arithmetic  9.64 us (9%)
  between operations  1.45 us (1%)
    pallas_call x1, Pallas kernels, attention_core(): pl.pallas_call(lambda *refs: attention_kernel(width, *refs), out_shape=tu...  17.4 us
    ppermute x1, waiting for transfers between devices, on_device(): lax.ppermute(jnp.where(at_north, top_g, bottom_g), both, pole_pairs)  8.5 us
    ppermute x1, waiting for transfers between devices, on_device(): lax.ppermute(pair(keys[:, :r], values[:, :r]), 'lon', left_pairs)  8.38 us
    ppermute x1, starting transfers between devices, on_device(): lax.ppermute(jnp.where(at_north, top_g, bottom_g), both, pole_pairs)  8.26 us
    ppermute x1, starting transfers between devices, on_device(): lax.ppermute(jnp.where(at_north, top_send, bottom_send), both, pole_pairs)  8.2 us
    ppermute x1, waiting for transfers between devices, on_device(): lax.ppermute(jnp.where(at_north, top_send, bottom_send), both, pole_pairs)  7.99 us
    unnamed x40, local copies, waits for them, and re-layouts  7.45 us
    ppermute x1, waiting for transfers between devices, on_device(): lax.ppermute(pair(left_k, left_v).astype(bf16), 'lon', left_pairs)  5.37 us
  transfers between devices with their start and end apart: 10, of which 4 were waited for; matrix products, arithmetic and copies ran while one was open for 6% of the time, Pallas kernels for 0%

profile of v3, /device:TPU:32, one launch (start us, length us, event | category | flops | bytes accessed | tf_op | source)
XLA Modules:
  0.0 111.5 jit_solution(8220535550320248039)
XLA Ops:
  0.6 1.4 %slice_bitcast_fusion.18 = (bf16[1,16,4,1024]{3,2,1,0:T(4,128)(2,1)S(1)}, bf16[1,16,4,1024]{3,2,1,0:T(4,128)(2,1)S(1)}, bf16[1,16,4,1024]{3,2,1,0:T(4,128)(2,1)S(1)}, bf16[1,16,4,1024]{3,2,1,0:T(4,128)(2,1)S(1)}) fusion(bf16[16,16,1024]{2,1,0:T(8,128)(2,1)} %param.11, bf16[16,16,1024]{2,1,0:T(8,128)(2,1)} %param.10), kind=kLoop, calls=%fused_computation.72 | loop fusion | bytes 1048576 | tf_op jit(solution)/shard_map/stack | solution.py:182
  2.3 1.2 %collective-permute-start.1 = (bf16[2,16,4,1024]{3,2,1,0:T(4,128)(2,1)S(1)}, bf16[2,16,4,1024]{3,2,1,0:T(4,128)(2,1)S(1)}, u32[]{:S(2)}, u32[]{:S(2)}) collective-permute-start(bf16[2,16,4,1024]{3,2,1,0:T(4,128)(2,1)S(1)} %pad_maximum_fusion.9), channel_id=1, source_target_pairs={{0,15},{1,0},{2,1},{3,2},{4,3},{5,4},{6,5},{7,6},{8,7},{9,8},{10,9... | collective-permute-start | bytes 786440 | tf_op jit(solution)/shard_map/ppermute | solution.py:185
  3.6 1.0 collective-permute-start
  7.6 8.4 %collective-permute-done.1 = bf16[2,16,4,1024]{3,2,1,0:T(4,128)(2,1)S(1)} collective-permute-done((bf16[2,16,4,1024]{3,2,1,0:T(4,128)(2,1)S(1)}, bf16[2,16,4,1024]{3,2,1,0:T(4,128)(2,1)S(1)}, u32[]{:S(2)}, u32[]{:S(2)}) %collective-permute-start.1) | collective-permute-done | bytes 262176 | tf_op jit(solution)/shard_map/ppermute | solution.py:185
  16.6 1.3 %collective-permute-start.4 = (bf16[2,4,24,1024]{3,2,1,0:T(8,128)(2,1)S(1)}, bf16[2,4,24,1024]{3,2,1,0:T(8,128)(2,1)S(1)}, u32[]{:S(2)}, u32[]{:S(2)}) collective-permute-start(bf16[2,4,24,1024]{3,2,1,0:T(8,128)(2,1)S(1)} %get-tuple-element.80), channel_id=1, source_target_pairs={{16,0},{17,1},{18,2},{19,3},{20,4},{21,5},{22,6},{23,7},{24,8},{25... | collective-permute-start | bytes 1179656 | tf_op jit(solution)/shard_map/ppermute | solution.py:192
  17.9 8.2 %collective-permute-start.2 = (bf16[2,4,24,1024]{3,2,1,0:T(8,128)(2,1)S(1)}, bf16[2,4,24,1024]{3,2,1,0:T(8,128)(2,1)S(1)}, u32[]{:S(2)}, u32[]{:S(2)}) collective-permute-start(bf16[2,4,24,1024]{3,2,1,0:T(8,128)(2,1)S(1)} %get-tuple-element.81), channel_id=1, source_target_pairs={{0,8},{1,9},{2,10},{3,11},{4,12},{5,13},{6,14},{7,15},{8,0},{9,1},... | collective-permute-start | bytes 1179656 | tf_op jit(solution)/shard_map/ppermute | solution.py:193
  26.1 1.3 %collective-permute-start.3 = (bf16[2,4,24,1024]{3,2,1,0:T(8,128)(2,1)S(1)}, bf16[2,4,24,1024]{3,2,1,0:T(8,128)(2,1)S(1)}, u32[]{:S(2)}, u32[]{:S(2)}) collective-permute-start(bf16[2,4,24,1024]{3,2,1,0:T(8,128)(2,1)S(1)} %get-tuple-element.82), channel_id=1, source_target_pairs={{0,16},{1,17},{2,18},{3,19},{4,20},{5,21},{6,22},{7,23},{8,24},{9,... | collective-permute-start | bytes 1179656 | tf_op jit(solution)/shard_map/ppermute | solution.py:191
  27.6 8.0 %collective-permute-done.2 = bf16[2,4,24,1024]{3,2,1,0:T(8,128)(2,1)S(1)} collective-permute-done((bf16[2,4,24,1024]{3,2,1,0:T(8,128)(2,1)S(1)}, bf16[2,4,24,1024]{3,2,1,0:T(8,128)(2,1)S(1)}, u32[]{:S(2)}, u32[]{:S(2)}) %collective-permute-start.2) | collective-permute-done | bytes 393248 | tf_op jit(solution)/shard_map/ppermute | solution.py:193
  35.9 0.9 gather_fusion.1
  37.4 0.8 fusion.39
  38.2 0.8 fusion.40
  39.2 0.7 reshape.132.refs_11_
  42.6 17.4 %neighbourhood_attention_bwd.1 = (bf16[256,1024]{1,0:T(8,128)(2,1)}, f32[256,1024]{1,0:T(8,128)}, f32[64,1024]{1,0:T(8,128)}, f32[64,1024]{1,0:T(8,128)}, f32[96...) custom-call(bf16[256,1024]{1,0:T(8,128)(2,1)} %bitcast.190, ...), custom_call_target="tpu_custom_call" | custom-call | flops 2013265920 | bytes 8650752 | tf_op jit(solution)/shard_map/neighbourhood_attention_bwd/pallas_call | solution.py:130
  59.9 0.9 fusion.37
  60.8 1.1 convert.124
  62.0 0.9 copy-done.3
  63.0 0.9 copy-done.2
  64.0 0.9 copy-done.14
  65.1 0.9 copy-done.12
  71.9 0.8 pad_maximum_fusion.7
  72.7 2.0 %collective-permute-start.6 = (bf16[2,4,24,1024]{3,2,1,0:T(8,128)(2,1)}, bf16[2,4,24,1024]{3,2,1,0:T(8,128)(2,1)}, u32[]{:S(2)}, u32[]{:S(2)}) collective-permute-start(bf16[2,4,24,1024]{3,2,1,0:T(8,128)(2,1)} %get-tuple-element.63), channel_id=1, source_target_pairs={{0,16},{1,17},{2,18},{3,19},{4,20},{5,21},{6,22},{7,23},{8,24},{9,... | collective-permute-start | bytes 1179656 | tf_op jit(solution)/shard_map/ppermute | solution.py:233
  74.7 8.3 %collective-permute-start.5 = (bf16[2,4,24,1024]{3,2,1,0:T(8,128)(2,1)S(1)}, bf16[2,4,24,1024]{3,2,1,0:T(8,128)(2,1)S(1)}, u32[]{:S(2)}, u32[]{:S(2)}) collective-permute-start(bf16[2,4,24,1024]{3,2,1,0:T(8,128)(2,1)S(1)} %get-tuple-element.64), channel_id=1, source_target_pairs={{0,8},{1,9},{2,10},{3,11},{4,12},{5,13},{6,14},{7,15},{8,0},{9,1},... | collective-permute-start | bytes 1179656 | tf_op jit(solution)/shard_map/ppermute | solution.py:234
  83.0 1.3 %collective-permute-start.7 = (bf16[2,4,24,1024]{3,2,1,0:T(8,128)(2,1)S(1)}, bf16[2,4,24,1024]{3,2,1,0:T(8,128)(2,1)}, u32[]{:S(2)}, u32[]{:S(2)}) collective-permute-start(bf16[2,4,24,1024]{3,2,1,0:T(8,128)(2,1)S(1)} %get-tuple-element.65), channel_id=1, source_target_pairs={{16,0},{17,1},{18,2},{19,3},{20,4},{21,5},{22,6},{23,7},{24,8},{25... | collective-permute-start | bytes 1179656 | tf_op jit(solution)/shard_map/ppermute | solution.py:232
  84.5 8.5 %collective-permute-done.5 = bf16[2,4,24,1024]{3,2,1,0:T(8,128)(2,1)S(1)} collective-permute-done((bf16[2,4,24,1024]{3,2,1,0:T(8,128)(2,1)S(1)}, bf16[2,4,24,1024]{3,2,1,0:T(8,128)(2,1)S(1)}, u32[]{:S(2)}, u32[]{:S(2)}) %collective-permute-start.5) | collective-permute-done | bytes 393248 | tf_op jit(solution)/shard_map/ppermute | solution.py:234
  93.4 0.9 gather_fusion.3
  94.3 1.6 %fusion = (f32[2,4,24,1024]{3,2,1,0:T(8,128)S(1)}, f32[2,4,24,1024]{3,2,1,0:T(8,128)S(1)}) fusion(bf16[2,4,24,1024]{3,2,1,0:T(8,128)(2,1)} %collective-permute-done.6, pred[]{:T(512)S(6)} %eq.13, bf16[24,2,4,1024]{3,2,1,0:T(4,128)(2,1)S(1)} %gather_fusion.3, pred[24]{0:T(512)(128)(4,1)S(1)} %compare_and_fusion, ...), kind=kLoop, calls=%fused_computation.17 | loop fusion | flops 983040 | bytes 2752538 | tf_op jit(solution)/shard_map/convert_element_type | solution.py:236
  96.8 0.8 copy-done.17
  98.7 2.2 %collective-permute-start.8 = (bf16[2,16,4,1024]{3,2,1,0:T(4,128)(2,1)S(1)}, bf16[2,16,4,1024]{3,2,1,0:T(4,128)(2,1)S(1)}, u32[]{:S(2)}, u32[]{:S(2)}) collective-permute-start(bf16[2,16,4,1024]{3,2,1,0:T(4,128)(2,1)S(1)} %pad_maximum_fusion.10), channel_id=1, source_target_pairs={{0,1},{1,2},{2,3},{3,4},{4,5},{5,6},{6,7},{7,8},{8,9},{9,10},{10,1... | collective-permute-start | bytes 786440 | tf_op jit(solution)/shard_map/ppermute | solution.py:256
  102.1 1.0 collective-permute-start.9
  103.7 5.4 %collective-permute-done.9 = bf16[2,16,4,1024]{3,2,1,0:T(4,128)(2,1)S(1)} collective-permute-done((bf16[2,16,4,1024]{3,2,1,0:T(4,128)(2,1)S(1)}, bf16[2,16,4,1024]{3,2,1,0:T(4,128)(2,1)S(1)}, u32[]{:S(2)}, u32[]{:S(2)}) %collective-permute-start.9) | collective-permute-done | bytes 262176 | tf_op jit(solution)/shard_map/ppermute | solution.py:255
  109.4 1.0 pad_maximum_fusion.3
  110.4 1.0 pad_maximum_fusion.2
  (139 shorter events, 18.3 us)
Async XLA Ops:
  2.0 2.6 %copy-start.5 = (bf16[16,16,1024]{2,1,0:T(8,128)(2,1)S(1)}, bf16[16,16,1024]{2,1,0:T(8,128)(2,1)}, u32[]{:S(2)}) copy-start(bf16[16,16,1024]{2,1,0:T(8,128)(2,1)} %param.10) | copy-start | bytes 1572868
  2.0 2.6 %copy-start.6 = (bf16[16,16,1024]{2,1,0:T(8,128)(2,1)S(1)}, bf16[16,16,1024]{2,1,0:T(8,128)(2,1)}, u32[]{:S(2)}) copy-start(bf16[16,16,1024]{2,1,0:T(8,128)(2,1)} %param.11) | copy-start | bytes 1572868
  2.3 13.7 %collective-permute-start.1 = (bf16[2,16,4,1024]{3,2,1,0:T(4,128)(2,1)S(1)}, bf16[2,16,4,1024]{3,2,1,0:T(4,128)(2,1)S(1)}, u32[]{:S(2)}, u32[]{:S(2)}) collective-permute-start(bf16[2,16,4,1024]{3,2,1,0:T(4,128)(2,1)S(1)} %pad_maximum_fusion.9), channel_id=1, source_target_pairs={{0,15},{1,0},{2,1},{3,2},{4,3},{5,4},{6,5},{7,6},{8,7},{9,8},{10,9... | collective-permute-start | bytes 786440 | tf_op jit(solution)/shard_map/ppermute | solution.py:185
  3.6 12.4 %collective-permute-start = (bf16[2,16,4,1024]{3,2,1,0:T(4,128)(2,1)S(1)}, bf16[2,16,4,1024]{3,2,1,0:T(4,128)(2,1)S(1)}, u32[]{:S(2)}, u32[]{:S(2)}) collective-permute-start(bf16[2,16,4,1024]{3,2,1,0:T(4,128)(2,1)S(1)} %pad_maximum_fusion.8), channel_id=1, source_target_pairs={{0,1},{1,2},{2,3},{3,4},{4,5},{5,6},{6,7},{7,8},{8,9},{9,10},{10,1... | collective-permute-start | bytes 786440 | tf_op jit(solution)/shard_map/ppermute | solution.py:184
  4.7 0.7 copy-start.19
  16.6 20.5 %collective-permute-start.4 = (bf16[2,4,24,1024]{3,2,1,0:T(8,128)(2,1)S(1)}, bf16[2,4,24,1024]{3,2,1,0:T(8,128)(2,1)S(1)}, u32[]{:S(2)}, u32[]{:S(2)}) collective-permute-start(bf16[2,4,24,1024]{3,2,1,0:T(8,128)(2,1)S(1)} %get-tuple-element.80), channel_id=1, source_target_pairs={{16,0},{17,1},{18,2},{19,3},{20,4},{21,5},{22,6},{23,7},{24,8},{25... | collective-permute-start | bytes 1179656 | tf_op jit(solution)/shard_map/ppermute | solution.py:192
  17.9 17.7 %collective-permute-start.2 = (bf16[2,4,24,1024]{3,2,1,0:T(8,128)(2,1)S(1)}, bf16[2,4,24,1024]{3,2,1,0:T(8,128)(2,1)S(1)}, u32[]{:S(2)}, u32[]{:S(2)}) collective-permute-start(bf16[2,4,24,1024]{3,2,1,0:T(8,128)(2,1)S(1)} %get-tuple-element.81), channel_id=1, source_target_pairs={{0,8},{1,9},{2,10},{3,11},{4,12},{5,13},{6,14},{7,15},{8,0},{9,1},... | collective-permute-start | bytes 1179656 | tf_op jit(solution)/shard_map/ppermute | solution.py:193
  26.1 11.0 %collective-permute-start.3 = (bf16[2,4,24,1024]{3,2,1,0:T(8,128)(2,1)S(1)}, bf16[2,4,24,1024]{3,2,1,0:T(8,128)(2,1)S(1)}, u32[]{:S(2)}, u32[]{:S(2)}) collective-permute-start(bf16[2,4,24,1024]{3,2,1,0:T(8,128)(2,1)S(1)} %get-tuple-element.82), channel_id=1, source_target_pairs={{0,16},{1,17},{2,18},{3,19},{4,20},{5,21},{6,22},{7,23},{8,24},{9,... | collective-permute-start | bytes 1179656 | tf_op jit(solution)/shard_map/ppermute | solution.py:191
  60.8 1.1 %copy-start.4 = (f32[96,1024]{1,0:T(8,128)S(1)}, f32[96,1024]{1,0:T(8,128)}, u32[]{:S(2)}) copy-start(f32[96,1024]{1,0:T(8,128)} %get-tuple-element.20) | copy-start | bytes 1179652
  61.9 1.0 copy-start.3
  63.0 1.0 copy-start.2
  64.0 1.0 copy-start.14
  64.0 1.0 copy-start.13
  65.0 1.0 copy-start.12
  65.0 1.0 copy-start.11
  71.8 12.5 %copy-start.1 = (f32[256,1024]{1,0:T(8,128)S(1)}, f32[256,1024]{1,0:T(8,128)}, u32[]{:S(2)}) copy-start(f32[256,1024]{1,0:T(8,128)} %get-tuple-element.17) | copy-start | bytes 3145732
  71.9 12.5 %copy-start = (f32[256,1024]{1,0:T(8,128)S(1)}, f32[256,1024]{1,0:T(8,128)}, u32[]{:S(2)}) copy-start(f32[256,1024]{1,0:T(8,128)} %get-tuple-element.26) | copy-start | bytes 3145732
  72.7 21.6 %collective-permute-start.6 = (bf16[2,4,24,1024]{3,2,1,0:T(8,128)(2,1)}, bf16[2,4,24,1024]{3,2,1,0:T(8,128)(2,1)}, u32[]{:S(2)}, u32[]{:S(2)}) collective-permute-start(bf16[2,4,24,1024]{3,2,1,0:T(8,128)(2,1)} %get-tuple-element.63), channel_id=1, source_target_pairs={{0,16},{1,17},{2,18},{3,19},{4,20},{5,21},{6,22},{7,23},{8,24},{9,... | collective-permute-start | bytes 1179656 | tf_op jit(solution)/shard_map/ppermute | solution.py:233
  74.7 18.3 %collective-permute-start.5 = (bf16[2,4,24,1024]{3,2,1,0:T(8,128)(2,1)S(1)}, bf16[2,4,24,1024]{3,2,1,0:T(8,128)(2,1)S(1)}, u32[]{:S(2)}, u32[]{:S(2)}) collective-permute-start(bf16[2,4,24,1024]{3,2,1,0:T(8,128)(2,1)S(1)} %get-tuple-element.64), channel_id=1, source_target_pairs={{0,8},{1,9},{2,10},{3,11},{4,12},{5,13},{6,14},{7,15},{8,0},{9,1},... | collective-permute-start | bytes 1179656 | tf_op jit(solution)/shard_map/ppermute | solution.py:234
  83.0 11.3 %collective-permute-start.7 = (bf16[2,4,24,1024]{3,2,1,0:T(8,128)(2,1)S(1)}, bf16[2,4,24,1024]{3,2,1,0:T(8,128)(2,1)}, u32[]{:S(2)}, u32[]{:S(2)}) collective-permute-start(bf16[2,4,24,1024]{3,2,1,0:T(8,128)(2,1)S(1)} %get-tuple-element.65), channel_id=1, source_target_pairs={{16,0},{17,1},{18,2},{19,3},{20,4},{21,5},{22,6},{23,7},{24,8},{25... | collective-permute-start | bytes 1179656 | tf_op jit(solution)/shard_map/ppermute | solution.py:232
  94.2 1.6 %copy-start.7 = (f32[4,4,1024]{2,1,0:T(4,128)S(1)}, f32[4,4,1024]{2,1,0:T(4,128)}, u32[]{:S(2)}) copy-start(f32[4,4,1024]{2,1,0:T(4,128)} %slice.407) | copy-start | bytes 196612
  94.3 1.6 %copy-start.9 = (f32[4,4,1024]{2,1,0:T(4,128)S(1)}, f32[4,4,1024]{2,1,0:T(4,128)}, u32[]{:S(2)}) copy-start(f32[4,4,1024]{2,1,0:T(4,128)} %slice.434) | copy-start | bytes 196612
  94.3 1.6 %copy-start.10 = (f32[4,4,1024]{2,1,0:T(4,128)S(1)}, f32[4,4,1024]{2,1,0:T(4,128)}, u32[]{:S(2)}) copy-start(f32[4,4,1024]{2,1,0:T(4,128)} %slice.415) | copy-start | bytes 196612
  95.9 0.8 copy-start.8
  96.7 0.8 copy-start.17
  97.6 0.8 copy-start.18
  98.5 2.4 %copy-start.16 = (bf16[8,4,1024]{2,1,0:T(4,128)(2,1)S(1)}, bf16[8,4,1024]{2,1,0:T(4,128)(2,1)}, u32[]{:S(2)}) copy-start(bf16[8,4,1024]{2,1,0:T(4,128)(2,1)} %slice.432) | copy-start | bytes 196612
  98.7 10.5 %collective-permute-start.8 = (bf16[2,16,4,1024]{3,2,1,0:T(4,128)(2,1)S(1)}, bf16[2,16,4,1024]{3,2,1,0:T(4,128)(2,1)S(1)}, u32[]{:S(2)}, u32[]{:S(2)}) collective-permute-start(bf16[2,16,4,1024]{3,2,1,0:T(4,128)(2,1)S(1)} %pad_maximum_fusion.10), channel_id=1, source_target_pairs={{0,1},{1,2},{2,3},{3,4},{4,5},{5,6},{6,7},{7,8},{8,9},{9,10},{10,1... | collective-permute-start | bytes 786440 | tf_op jit(solution)/shard_map/ppermute | solution.py:256
  100.9 0.8 copy-start.15
  102.1 7.0 %collective-permute-start.9 = (bf16[2,16,4,1024]{3,2,1,0:T(4,128)(2,1)S(1)}, bf16[2,16,4,1024]{3,2,1,0:T(4,128)(2,1)S(1)}, u32[]{:S(2)}, u32[]{:S(2)}) collective-permute-start(bf16[2,16,4,1024]{3,2,1,0:T(4,128)(2,1)S(1)} %pad_maximum_fusion.11), channel_id=1, source_target_pairs={{0,15},{1,0},{2,1},{3,2},{4,3},{5,4},{6,5},{7,6},{8,7},{9,8},{10,9... | collective-permute-start | bytes 786440 | tf_op jit(solution)/shard_map/ppermute | solution.py:255

commit v4 on v3

v4 whole, which is shorter than its diff:
```python
import jax
import jax.numpy as jnp
import numpy as np
from jax import lax
from jax.experimental import pallas as pl
from jax.experimental.pallas import tpu as pltpu
from jax.sharding import PartitionSpec as P

HEADS = 16
HEAD_DIM = 64
RADIUS = 4

SPAN = 2 * RADIUS + 1
TILE_ROWS = 8
LANES = 128


def attention_kernel(width, *refs):
    (q_ref, g_ref, k_own, v_own, top_in, bot_in, left_in, right_in) = refs[:8]
    (dq_ref, dk_own, dv_own, top_out, bot_out, left_out, right_out) = refs[8:15]
    bias_ref = refs[15]
    scale = HEAD_DIM ** (-0.5)
    r = RADIUS
    tq = TILE_ROWS * width
    main = 2 * TILE_ROWS * width
    side = 2 * TILE_ROWS * r
    tk = main + 2 * side
    edge = r * width
    corner = r * r
    pairs = q_ref.shape[1] // LANES

    qi = lax.broadcasted_iota(jnp.int32, (tq, tk), 0).astype(jnp.float32)
    ki = lax.broadcasted_iota(jnp.int32, (tq, tk), 1).astype(jnp.float32)
    qr = jnp.floor((qi + 0.5) * (1.0 / width))
    qc = qi - width * qr
    in_main = ki < main
    in_left = (ki >= main) & (ki < main + side)
    kk = jnp.where(in_main, ki, jnp.where(in_left, ki - main, ki - main - side))
    per_row = jnp.where(in_main, float(width), float(r))
    kr = jnp.floor((kk + 0.5) / per_row)
    kc = kk - per_row * kr + jnp.where(in_main, float(r), jnp.where(in_left, 0.0, float(width + r)))
    dr = kr - qr
    dc = kc - qc
    ok = (dr >= 0) & (dr <= 2 * r) & (dc >= 0) & (dc <= 2 * r)
    bias_ref[...] = jnp.where(ok, 0.0, -jnp.inf).astype(jnp.float32)

    nt = (((1,), (1,)), ((), ()))
    tn = (((0,), (0,)), ((), ()))

    def head(qh, gh, kp, vp):
        s = lax.dot_general(qh, kp, nt, preferred_element_type=jnp.float32) * scale + bias_ref[...]
        m = jnp.max(s, axis=1, keepdims=True)
        e = jnp.exp(s - m)
        total = jnp.sum(e, axis=1, keepdims=True)
        w = e * (1.0 / total)
        dw = lax.dot_general(gh, vp, nt, preferred_element_type=jnp.float32)
        corr = jnp.sum(w * dw, axis=1, keepdims=True)
        ds = (w * (dw - corr)).astype(jnp.bfloat16)
        return ds, w.astype(jnp.bfloat16)

    def gather_keys(own, c, t, lanes):
        rows = side - corner
        if t == 0:
            parts = [
                top_in[c, pl.ds(0, edge), lanes],
                own[pl.ds(0, main - edge), lanes],
                top_in[c, pl.ds(edge, corner), lanes],
                left_in[c, pl.ds(0, rows), lanes],
                top_in[c, pl.ds(edge + corner, corner), lanes],
                right_in[c, pl.ds(0, rows), lanes],
            ]
        else:
            start = left_in.shape[1] - rows
            parts = [
                own[pl.ds(edge, main - edge), lanes],
                bot_in[c, pl.ds(0, edge), lanes],
                left_in[c, pl.ds(start, rows), lanes],
                bot_in[c, pl.ds(edge, corner), lanes],
                right_in[c, pl.ds(start, rows), lanes],
                bot_in[c, pl.ds(edge + corner, corner), lanes],
            ]
        return jnp.concatenate(parts, axis=0)

    def scatter_grads(d, own, c, t, lanes):
        bf = jnp.bfloat16
        rows = side - corner
        n_side = left_out.shape[1]
        if t == 0:
            top_out[c, pl.ds(0, edge), lanes] = d[:edge].astype(bf)
            own[pl.ds(0, main - edge), lanes] = d[edge:main]
            top_out[c, pl.ds(edge, corner), lanes] = d[main : main + corner].astype(bf)
            left_out[c, pl.ds(0, rows), lanes] = d[main + corner : main + side]
            top_out[c, pl.ds(edge + corner, corner), lanes] = d[main + side : main + side + corner].astype(bf)
            right_out[c, pl.ds(0, rows), lanes] = d[main + side + corner :]
        else:
            shared = main - 2 * edge
            own[pl.ds(edge, shared), lanes] += d[:shared]
            own[pl.ds(edge + shared, edge), lanes] = d[shared : main - edge]
            bot_out[c, pl.ds(0, edge), lanes] = d[main - edge : main].astype(bf)
            start = n_side - rows
            overlap = rows - start
            left_out[c, pl.ds(start, overlap), lanes] += d[main : main + overlap]
            left_out[c, pl.ds(rows, n_side - rows), lanes] = d[main + overlap : main + rows]
            bot_out[c, pl.ds(edge, corner), lanes] = d[main + rows : main + side].astype(bf)
            right_out[c, pl.ds(start, overlap), lanes] += d[main + side : main + side + overlap]
            right_out[c, pl.ds(rows, n_side - rows), lanes] = d[main + side + overlap : main + side + rows]
            bot_out[c, pl.ds(edge + corner, corner), lanes] = d[main + side + rows :].astype(bf)

    def body(p, carry):
        lanes = pl.ds(pl.multiple_of(p * LANES, LANES), LANES)
        for t in range(2):
            qp = q_ref[pl.ds(t * tq, tq), lanes]
            gp = g_ref[pl.ds(t * tq, tq), lanes]
            kp = gather_keys(k_own, 0, t, lanes)
            vp = gather_keys(v_own, 1, t, lanes)
            lo = lax.broadcasted_iota(jnp.int32, qp.shape, 1) < HEAD_DIM
            zero = jnp.zeros_like(qp)
            qa = jnp.where(lo, qp, zero)
            qb = jnp.where(lo, zero, qp)
            ga = jnp.where(lo, gp, zero)
            gb = jnp.where(lo, zero, gp)
            dsa, wa = head(qa, ga, kp, vp)
            dsb, wb = head(qb, gb, kp, vp)
            dqa = jnp.dot(dsa, kp, preferred_element_type=jnp.float32)
            dqb = jnp.dot(dsb, kp, preferred_element_type=jnp.float32)
            dq = jnp.where(lo, dqa, dqb) * scale
            dq_ref[pl.ds(t * tq, tq), lanes] = dq.astype(dq_ref.dtype)
            dk = (
                lax.dot_general(dsa, qa, tn, preferred_element_type=jnp.float32)
                + lax.dot_general(dsb, qb, tn, preferred_element_type=jnp.float32)
            ) * scale
            dv = lax.dot_general(wa, ga, tn, preferred_element_type=jnp.float32) + lax.dot_general(
                wb, gb, tn, preferred_element_type=jnp.float32
            )
            scatter_grads(dk, dk_own, 0, t, lanes)
            scatter_grads(dv, dv_own, 1, t, lanes)
        return carry

    lax.fori_loop(0, pairs, body, 0)


def attention_core(q2, g2, k2, v2, top_in, bot_in, left_in, right_in, width):
    cells, features = q2.shape
    r = RADIUS
    tq = TILE_ROWS * width
    tk = 2 * TILE_ROWS * (width + 2 * r)
    tiles = cells // tq
    assert tiles == 2
    flops = 10 * 2 * tq * tk * LANES * (features // LANES) * tiles
    vmem = pl.BlockSpec(memory_space=pltpu.VMEM)
    f32 = jnp.float32
    outs = (
        jax.ShapeDtypeStruct((cells, features), jnp.bfloat16),
        jax.ShapeDtypeStruct((cells, features), f32),
        jax.ShapeDtypeStruct((cells, features), f32),
        jax.ShapeDtypeStruct(top_in.shape, jnp.bfloat16),
        jax.ShapeDtypeStruct(bot_in.shape, jnp.bfloat16),
        jax.ShapeDtypeStruct(left_in.shape, f32),
        jax.ShapeDtypeStruct(right_in.shape, f32),
    )
    in_bytes = 2 * (4 * cells * features + top_in.size + bot_in.size + left_in.size + right_in.size)
    out_bytes = 2 * cells * features + 8 * cells * features + 2 * (top_in.size + bot_in.size) + 4 * (
        left_in.size + right_in.size
    )
    return pl.pallas_call(
        lambda *refs: attention_kernel(width, *refs),
        out_shape=outs,
        in_specs=[vmem] * 8,
        out_specs=tuple([vmem] * 7),
        scratch_shapes=[pltpu.VMEM((tq, tk), jnp.float32)],
        cost_estimate=pl.CostEstimate(
            flops=flops,
            transcendentals=2 * tq * tk * HEADS * tiles,
            bytes_accessed=in_bytes + out_bytes,
        ),
        name="neighbourhood_attention_bwd",
    )(q2, g2, k2, v2, top_in, bot_in, left_in, right_in)


def on_device(queries, keys, values, grad_out, fold_cols):
    height, width, features = queries.shape
    n_lat = lax.axis_size("lat")
    n_lon = lax.axis_size("lon")
    half = n_lon // 2
    i = lax.axis_index("lat")
    j = lax.axis_index("lon")
    at_north = i == 0
    at_south = i == n_lat - 1
    partner_j = (j + half) % n_lon
    r = RADIUS
    f32 = jnp.float32
    bf16 = jnp.bfloat16
    cells = height * width
    edge = r * width
    corner = r * r

    def flat(a, b):
        return a * n_lon + b

    down_pairs = [(flat(a, b), flat(a + 1, b)) for a in range(n_lat - 1) for b in range(n_lon)]
    up_pairs = [(flat(a + 1, b), flat(a, b)) for a in range(n_lat - 1) for b in range(n_lon)]
    pole_pairs = [(flat(a, b), flat(a, (b + half) % n_lon)) for a in (0, n_lat - 1) for b in range(n_lon)]
    right_pairs = [(b, (b + 1) % n_lon) for b in range(n_lon)]
    left_pairs = [(b, (b - 1) % n_lon) for b in range(n_lon)]
    both = ("lat", "lon")

    ext_w = width + 2 * r
    n_cols = n_lon * width
    my_ext_cols = (j * width - r + jnp.arange(ext_w)) % n_cols
    partner_ext_cols = (partner_j * width - r + jnp.arange(ext_w)) % n_cols
    fold_row = jnp.where(at_north, fold_cols[0], fold_cols[1])
    fold_idx = (jnp.take(fold_row, my_ext_cols) - (partner_j * width - r)) % n_cols
    landing = (jnp.take(fold_row, partner_ext_cols) - (j * width - r)) % n_cols
    unfold_idx = jnp.zeros((ext_w,), jnp.int32).at[landing].set(jnp.arange(ext_w, dtype=jnp.int32))

    strip_row = np.concatenate([np.arange(edge) // width, np.arange(corner) // r, np.arange(corner) // r])
    strip_col = np.concatenate(
        [r + np.arange(edge) % width, np.arange(corner) % r, width + r + np.arange(corner) % r]
    )

    def strip_cell(row, col):
        return jnp.where(
            col < r,
            edge + row * r + col,
            jnp.where(col >= width + r, edge + corner + row * r + col - width - r, row * width + col - r),
        )

    pole_src = strip_cell(r - 1 - strip_row, jnp.take(fold_idx, strip_col))
    pole_dst = strip_cell(r - 1 - strip_row, jnp.take(unfold_idx, strip_col))

    def pair(a, b):
        return jnp.stack([a, b])

    kf = keys.reshape(cells, features)
    vf = values.reshape(cells, features)

    def cols(x, a, b):
        return x[:, a:b].reshape(height * (b - a), features)

    from_left = lax.ppermute(pair(cols(keys, width - r, width), cols(values, width - r, width)), "lon", right_pairs)
    from_right = lax.ppermute(pair(cols(keys, 0, r), cols(values, 0, r)), "lon", left_pairs)
    n_side = height * r
    top_send = jnp.concatenate(
        [pair(kf[:edge], vf[:edge]), from_left[:, :corner], from_right[:, :corner]], axis=1
    )
    bottom_send = jnp.concatenate(
        [pair(kf[cells - edge :], vf[cells - edge :]), from_left[:, n_side - corner :], from_right[:, n_side - corner :]],
        axis=1,
    )
    from_above = lax.ppermute(bottom_send, both, down_pairs)
    from_below = lax.ppermute(top_send, both, up_pairs)
    pole_recv = lax.ppermute(jnp.where(at_north, top_send, bottom_send), both, pole_pairs)
    pole_strip = jnp.take(pole_recv, pole_src, axis=1)
    top = jnp.where(at_north, pole_strip, from_above)
    bottom = jnp.where(at_south, pole_strip, from_below)

    dq, dk_own, dv_own, top_g, bottom_g, left_g, right_g = attention_core(
        queries.reshape(cells, features),
        grad_out.reshape(cells, features),
        kf,
        vf,
        top,
        bottom,
        from_left,
        from_right,
        width,
    )

    up_recv = lax.ppermute(top_g, both, up_pairs)
    down_recv = lax.ppermute(bottom_g, both, down_pairs)
    pole_g = lax.ppermute(jnp.where(at_north, top_g, bottom_g), both, pole_pairs)
    unfolded = jnp.take(pole_g, pole_dst, axis=1)
    add_top = jnp.where(at_north, unfolded, down_recv).astype(f32)
    add_bottom = jnp.where(at_south, unfolded, up_recv).astype(f32)

    def side_send(g, first):
        pads_top = [(0, 0), (0, n_side - corner), (0, 0)]
        pads_bottom = [(0, 0), (n_side - corner, 0), (0, 0)]
        return (
            g
            + jnp.pad(add_top[:, first : first + corner], pads_top)
            + jnp.pad(add_bottom[:, first : first + corner], pads_bottom)
        ).astype(bf16)

    back_right = lax.ppermute(side_send(left_g, edge), "lon", left_pairs)
    back_left = lax.ppermute(side_send(right_g, edge + corner), "lon", right_pairs)

    def final_of(c, own):
        block = own.reshape(height, width, features)
        row_pad = [(0, 0), (0, 0)]
        block = (
            block
            + jnp.pad(add_top[c, :edge].reshape(r, width, features), [(0, height - r)] + row_pad)
            + jnp.pad(add_bottom[c, :edge].reshape(r, width, features), [(height - r, 0)] + row_pad)
            + jnp.pad(
                back_left[c].reshape(height, r, features).astype(f32), [(0, 0), (0, width - r), (0, 0)]
            )
            + jnp.pad(
                back_right[c].reshape(height, r, features).astype(f32), [(0, 0), (width - r, 0), (0, 0)]
            )
        )
        return block.astype(bf16)

    return (dq.reshape(height, width, features), final_of(0, dk_own), final_of(1, dv_own))


def solution(mesh):
    placed = (
        P("lat", "lon", None),
        P("lat", "lon", None),
        P("lat", "lon", None),
        P("lat", "lon", None),
        P(),
    )
    return jax.shard_map(
        on_device,
        mesh=mesh,
        in_specs=placed,
        out_specs=(P("lat", "lon", None), P("lat", "lon", None), P("lat", "lon", None)),
        check_vma=False,
    )
```

time: 113 us -> 94.9 us (0.84)
  the two profiles are of different devices: /device:TPU:32 before, /device:TPU:1 now
where the time goes in v4:
time: 94.9 us; the launch traced here: 94.5 us
  starting transfers between devices  38.3 us (40%)
  waiting for transfers between devices  19.8 us (21%)
  Pallas kernels  16.9 us (18%)
  local copies, waits for them, and re-layouts  13.4 us (14%)
  other arithmetic  4.93 us (5%)
  between operations  1.15 us (1%)
    ppermute x1, starting transfers between devices, on_device(): up_recv = lax.ppermute(top_g, both, up_pairs)  17 us
    pallas_call x1, Pallas kernels, attention_core(): pl.pallas_call(lambda *refs: attention_kernel(width, *refs), out_shape=ou...  16.9 us
    ppermute x1, waiting for transfers between devices, on_device(): lax.ppermute(side_send(right_g, edge + corner), 'lon', right_pairs)  7.68 us
    ppermute x1, starting transfers between devices, on_device(): lax.ppermute(pair(cols(keys, 0, r), cols(values, 0, r)), 'lon', left_pairs)  7.48 us
    ppermute x1, waiting for transfers between devices, on_device(): lax.ppermute(pair(cols(keys, width - r, width), cols(values, width - r, w...  4.16 us
    ppermute x1, waiting for transfers between devices, on_device(): back_right = lax.ppermute(side_send(left_g, edge), 'lon', left_pairs)  3.72 us
    ppermute x1, starting transfers between devices, on_device(): from_below = lax.ppermute(top_send, both, up_pairs)  3.71 us
    unnamed x30, local copies, waits for them, and re-layouts  3.45 us
  transfers between devices with their start and end apart: 10, of which 6 were waited for; matrix products, arithmetic and copies ran while one was open for 9% of the time, Pallas kernels for 0%

profile of v4, /device:TPU:1, one launch (start us, length us, event | category | flops | bytes accessed | tf_op | source)
XLA Modules:
  0.0 94.5 jit_solution(2735052151021439436)
XLA Ops:
  0.6 1.2 %fusion.14 = (bf16[16,4,1024]{2,1,0:T(4,128)(2,1)S(1)}, bf16[16,4,1024]{2,1,0:T(4,128)(2,1)S(1)}) fusion(bf16[16,16,1024]{2,1,0:T(8,128)(2,1)} %param.19), kind=kLoop, calls=%fused_computation.72 | loop fusion | bytes 524288 | tf_op jit(solution)/shard_map/slice | solution.py:238
  2.1 7.5 %collective-permute-start.1 = (bf16[2,64,1024]{2,1,0:T(8,128)(2,1)S(1)}, bf16[2,64,1024]{2,1,0:T(8,128)(2,1)S(1)}, u32[]{:S(2)}, u32[]{:S(2)}) collective-permute-start(bf16[2,64,1024]{2,1,0:T(8,128)(2,1)S(1)} %pad_maximum_fusion.3), channel_id=1, source_target_pairs={{0,15},{1,0},{2,1},{3,2},{4,3},{5,4},{6,5},{7,6},{8,7},{9,8},{10,9... | collective-permute-start | bytes 786440 | tf_op jit(solution)/shard_map/ppermute | solution.py:241
  9.8 0.8 copy-done.2
  10.7 0.7 copy-done.10
  11.4 0.7 gather_fusion
  12.1 0.7 gather_fusion.3
  12.9 0.6 scatter_custom_fusion
  13.5 1.1 %collective-permute-done.1.refs_7_ = bf16[2,64,1024]{2,1,0:T(8,128)(2,1)S(1)} collective-permute-done((bf16[2,64,1024]{2,1,0:T(8,128)(2,1)S(1)}, bf16[2,64,1024]{2,1,0:T(8,128)(2,1)S(1)}, u32[]{:S(2)}, u32[]{:S(2)}) %collective-permute-start.1) | collective-permute-done | bytes 262176 | tf_op jit(solution)/shard_map/ppermute | solution.py:241
  14.6 4.2 %collective-permute-done.refs_6_ = bf16[2,64,1024]{2,1,0:T(8,128)(2,1)S(1)} collective-permute-done((bf16[2,64,1024]{2,1,0:T(8,128)(2,1)S(1)}, bf16[2,64,1024]{2,1,0:T(8,128)(2,1)S(1)}, u32[]{:S(2)}, u32[]{:S(2)}) %collective-permute-start) | collective-permute-done | bytes 262176 | tf_op jit(solution)/shard_map/ppermute | solution.py:240
  19.0 0.5 copy-done.9
  19.5 3.7 %collective-permute-start.4 = (bf16[2,96,1024]{2,1,0:T(8,128)(2,1)S(1)}, bf16[2,96,1024]{2,1,0:T(8,128)(2,1)S(1)}, u32[]{:S(2)}, u32[]{:S(2)}) collective-permute-start(bf16[2,96,1024]{2,1,0:T(8,128)(2,1)S(1)} %get-tuple-element.44), channel_id=1, source_target_pairs={{16,0},{17,1},{18,2},{19,3},{20,4},{21,5},{22,6},{23,7},{24,8},{25... | collective-permute-start | bytes 1179656 | tf_op jit(solution)/shard_map/ppermute | solution.py:251
  23.2 0.7 collective-permute-start.2
  23.9 3.0 %collective-permute-start.3 = (bf16[2,96,1024]{2,1,0:T(8,128)(2,1)S(1)}, bf16[2,96,1024]{2,1,0:T(8,128)(2,1)S(1)}, u32[]{:S(2)}, u32[]{:S(2)}) collective-permute-start(bf16[2,96,1024]{2,1,0:T(8,128)(2,1)S(1)} %get-tuple-element.46), channel_id=1, source_target_pairs={{0,16},{1,17},{2,18},{3,19},{4,20},{5,21},{6,22},{7,23},{8,24},{9,... | collective-permute-start | bytes 1179656 | tf_op jit(solution)/shard_map/ppermute | solution.py:250
  26.9 1.2 %gather_fusion.4 = s32[96]{0:T(128)S(1)} fusion(s32[24]{0:T(128)S(1)} %scatter_custom_fusion, s32[1024]{0:T(1024)S(1)} %pad_clamp_fusion.3), kind=kCustom, calls=%fused_computation.4.clone | custom fusion | bytes 1152 | tf_op jit(solution)/shard_map/jit(_take)/gather | solution.py:229
  28.2 1.2 %gather_fusion.1 = s32[96]{0:T(128)S(1)} fusion(s32[24]{0:T(128)S(1)} %get-tuple-element.58, s32[1024]{0:T(1024)S(1)} %pad_clamp_fusion.3), kind=kCustom, calls=%fused_computation.1.clone | custom fusion | bytes 1152 | tf_op jit(solution)/shard_map/jit(_take)/gather | solution.py:228
  29.5 0.4 copy.15
  29.9 1.4 %gather_fusion.2 = bf16[96,2,1024]{2,1,0:T(2,128)(2,1)S(1)} fusion(bf16[2,96,1024]{2,0,1:T(2,128)(2,1)S(1)} %copy.15, s32[1024]{0:T(1024)S(1)} %pad_clamp_fusion.2), kind=kCustom, calls=%fused_computation.2.clone | custom fusion | bytes 786816 | tf_op jit(solution)/shard_map/jit(_take)/gather | solution.py:253
  31.6 1.1 %bitcast_select_fusion.2 = (bf16[2,96,1024]{2,1,0:T(8,128)(2,1)}, bf16[2,96,1024]{2,1,0:T(8,128)(2,1)}) fusion(bf16[2,96,1024]{2,1,0:T(8,128)(2,1)S(1)} %collective-permute-done.4, pred[]{:T(512)S(6)} %eq.14, bf16[96,2,1024]{2,1,0:T(2,128)(2,1)S(1)} %gather_fusion.2, pred[96]{0:T(512)(128)(4,1)S(1)} %get-tuple-element.55, ...), kind=kLoop, calls=%fused_computation.17 | loop fusion | flops 589824 | bytes 1966178 | tf_op jit(solution)/shard_map/jit(_where)/select_n | solution.py:255
  32.7 16.9 %neighbourhood_attention_bwd.1 = (bf16[256,1024]{1,0:T(8,128)(2,1)}, f32[256,1024]{1,0:T(8,128)}, f32[256,1024]{1,0:T(8,128)}, bf16[2,96,1024]{2,1,0:T(8,128)(2,...) custom-call(bf16[256,1024]{1,0:T(8,128)(2,1)} %bitcast.41, ...), custom_call_target="tpu_custom_call" | custom-call | flops 2013265920 | bytes 7864320 | tf_op jit(solution)/shard_map/neighbourhood_attention_bwd/pallas_call | solution.py:165
  49.6 1.1 %broadcast_select_fusion = bf16[2,96,1024]{2,1,0:T(8,128)(2,1)S(1)} fusion(bf16[2,96,1024]{2,1,0:T(8,128)(2,1)} %get-tuple-element.15, bf16[2,96,1024]{2,1,0:T(8,128)(2,1)} %get-tuple-element.16, pred[]{:T(512)S(6)} %eq.13), kind=kLoop, calls=%fused_computation.21 | loop fusion | flops 196608 | bytes 1179649 | tf_op jit(solution)/shard_map/jit(_where)/select_n | solution.py:271
  50.8 0.7 collective-permute-start.5
  51.5 17.0 %collective-permute-start.7 = (bf16[2,96,1024]{2,1,0:T(8,128)(2,1)S(1)}, bf16[2,96,1024]{2,1,0:T(8,128)(2,1)S(1)}, u32[]{:S(2)}, u32[]{:S(2)}) collective-permute-start(bf16[2,96,1024]{2,1,0:T(8,128)(2,1)S(1)} %copy-done.7), channel_id=1, source_target_pairs={{16,0},{17,1},{18,2},{19,3},{20,4},{21,5},{22,6},{23,7},{24,8},{25... | collective-permute-start | bytes 1179656 | tf_op jit(solution)/shard_map/ppermute | solution.py:269
  68.4 1.9 %collective-permute-start.6 = (bf16[2,96,1024]{2,1,0:T(8,128)(2,1)S(1)}, bf16[2,96,1024]{2,1,0:T(8,128)(2,1)S(1)}, u32[]{:S(2)}, u32[]{:S(2)}) collective-permute-start(bf16[2,96,1024]{2,1,0:T(8,128)(2,1)S(1)} %copy-done.6), channel_id=1, source_target_pairs={{0,16},{1,17},{2,18},{3,19},{4,20},{5,21},{6,22},{7,23},{8,24},{9,... | collective-permute-start | bytes 1179656 | tf_op jit(solution)/shard_map/ppermute | solution.py:270
  70.8 1.4 %gather_fusion.5 = bf16[96,2,1024]{2,1,0:T(2,128)(2,1)S(1)} fusion(bf16[2,96,1024]{2,0,1:T(2,128)(2,1)S(1)} %copy.17, s32[1024]{0:T(1024)S(1)} %pad_clamp_fusion), kind=kCustom, calls=%fused_computation.5.clone | custom fusion | bytes 786816 | tf_op jit(solution)/shard_map/jit(_take)/gather | solution.py:272
  72.2 2.9 %collective-permute-done.6 = bf16[2,96,1024]{2,1,0:T(8,128)(2,1)S(1)} collective-permute-done((bf16[2,96,1024]{2,1,0:T(8,128)(2,1)S(1)}, bf16[2,96,1024]{2,1,0:T(8,128)(2,1)S(1)}, u32[]{:S(2)}, u32[]{:S(2)}) %collective-permute-start.6) | collective-permute-done | bytes 393248 | tf_op jit(solution)/shard_map/ppermute | solution.py:270
  75.4 1.0 %copy-done.5 = f32[2,64,1024]{2,1,0:T(8,128)S(1)} copy-done((f32[2,64,1024]{2,1,0:T(8,128)S(1)}, f32[2,64,1024]{2,1,0:T(8,128)}, u32[]{:S(2)}) %copy-start.5) | copy-done | bytes 524312
  76.5 2.0 %collective-permute-start.8 = (bf16[2,64,1024]{2,1,0:T(8,128)(2,1)S(1)}, bf16[2,64,1024]{2,1,0:T(8,128)(2,1)S(1)}, u32[]{:S(2)}, u32[]{:S(2)}) collective-permute-start(bf16[2,64,1024]{2,1,0:T(8,128)(2,1)S(1)} %add_convert_fusion.3), channel_id=1, source_target_pairs={{0,1},{1,2},{2,3},{3,4},{4,5},{5,6},{6,7},{7,8},{8,9},{9,10},{10,1... | collective-permute-start | bytes 786440 | tf_op jit(solution)/shard_map/ppermute | solution.py:286
  78.5 1.8 %collective-permute-start.9 = (bf16[2,64,1024]{2,1,0:T(8,128)(2,1)S(1)}, bf16[2,64,1024]{2,1,0:T(8,128)(2,1)S(1)}, u32[]{:S(2)}, u32[]{:S(2)}) collective-permute-start(bf16[2,64,1024]{2,1,0:T(8,128)(2,1)S(1)} %add_convert_fusion.2), channel_id=1, source_target_pairs={{0,15},{1,0},{2,1},{3,2},{4,3},{5,4},{6,5},{7,6},{8,7},{9,8},{10,9... | collective-permute-start | bytes 786440 | tf_op jit(solution)/shard_map/ppermute | solution.py:285
  80.3 7.7 %collective-permute-done.8 = bf16[2,64,1024]{2,1,0:T(8,128)(2,1)S(1)} collective-permute-done((bf16[2,64,1024]{2,1,0:T(8,128)(2,1)S(1)}, bf16[2,64,1024]{2,1,0:T(8,128)(2,1)S(1)}, u32[]{:S(2)}, u32[]{:S(2)}) %collective-permute-start.8) | collective-permute-done | bytes 262176 | tf_op jit(solution)/shard_map/ppermute | solution.py:286
  88.2 3.7 %collective-permute-done.9 = bf16[2,64,1024]{2,1,0:T(8,128)(2,1)S(1)} collective-permute-done((bf16[2,64,1024]{2,1,0:T(8,128)(2,1)S(1)}, bf16[2,64,1024]{2,1,0:T(8,128)(2,1)S(1)}, u32[]{:S(2)}, u32[]{:S(2)}) %collective-permute-start.9) | collective-permute-done | bytes 262176 | tf_op jit(solution)/shard_map/ppermute | solution.py:285
  92.0 1.0 %add_convert_fusion = bf16[16,16,1024]{2,1,0:T(8,128)(2,1)} fusion(f32[4,16,1024]{2,1,0:T(8,128)S(1)} %bitcast.34, f32[16,16,1024]{2,1,0:T(8,128)S(1)} %bitcast.30, f32[4,16,1024]{2,1,0:T(8,128)S(1)} %bitcast.32, bf16[16,4,1024]{2,1,0:T(4,128)(2,1)S(1)} %convert_element_type.60, bf16[16,4,1024]{2,1,0:T(4,128)(2,1)S(1)} %convert_element_type.59), kind=kLoop, calls=%fused_computation.7 | loop fusion | flops 1835008 | bytes 2359296 | tf_op jit(solution)/shard_map/convert_element_type | solution.py:302
  93.4 1.0 %add_convert_fusion.1 = bf16[16,16,1024]{2,1,0:T(8,128)(2,1)} fusion(f32[4,16,1024]{2,1,0:T(8,128)S(1)} %bitcast.33, f32[16,16,1024]{2,1,0:T(8,128)S(1)} %bitcast.29, f32[4,16,1024]{2,1,0:T(8,128)S(1)} %bitcast.31, bf16[16,4,1024]{2,1,0:T(4,128)(2,1)S(1)} %convert_element_type.57, bf16[16,4,1024]{2,1,0:T(4,128)(2,1)S(1)} %convert_element_type.55), kind=kLoop, calls=%fused_computation.8 | loop fusion | flops 1835008 | bytes 2359296 | tf_op jit(solution)/shard_map/convert_element_type | solution.py:302
  (69 shorter events, 2.6 us)
Async XLA Ops:
  0.6 1.2 %copy-start.3 = (bf16[16,16,1024]{2,1,0:T(8,128)(2,1)S(1)}, bf16[16,16,1024]{2,1,0:T(8,128)(2,1)}, u32[]{:S(2)}) copy-start(bf16[16,16,1024]{2,1,0:T(8,128)(2,1)} %param.20) | copy-start | bytes 1572868
  2.1 12.5 %collective-permute-start.1 = (bf16[2,64,1024]{2,1,0:T(8,128)(2,1)S(1)}, bf16[2,64,1024]{2,1,0:T(8,128)(2,1)S(1)}, u32[]{:S(2)}, u32[]{:S(2)}) collective-permute-start(bf16[2,64,1024]{2,1,0:T(8,128)(2,1)S(1)} %pad_maximum_fusion.3), channel_id=1, source_target_pairs={{0,15},{1,0},{2,1},{3,2},{4,3},{5,4},{6,5},{7,6},{8,7},{9,8},{10,9... | collective-permute-start | bytes 786440 | tf_op jit(solution)/shard_map/ppermute | solution.py:241
  9.6 1.0 %copy-start.2 = (bf16[16,16,1024]{2,1,0:T(8,128)(2,1)S(1)}, bf16[16,16,1024]{2,1,0:T(8,128)(2,1)}, u32[]{:S(2)}) copy-start(bf16[16,16,1024]{2,1,0:T(8,128)(2,1)} %param.19) | copy-start | bytes 1572868
  9.7 9.1 %collective-permute-start = (bf16[2,64,1024]{2,1,0:T(8,128)(2,1)S(1)}, bf16[2,64,1024]{2,1,0:T(8,128)(2,1)S(1)}, u32[]{:S(2)}, u32[]{:S(2)}) collective-permute-start(bf16[2,64,1024]{2,1,0:T(8,128)(2,1)S(1)} %pad_maximum_fusion.2), channel_id=1, source_target_pairs={{0,1},{1,2},{2,3},{3,4},{4,5},{5,6},{6,7},{7,8},{8,9},{9,10},{10,1... | collective-permute-start | bytes 786440 | tf_op jit(solution)/shard_map/ppermute | solution.py:240
  10.7 0.7 copy-start.10
  14.6 4.2 %copy-start.8 = (bf16[2,64,1024]{2,1,0:T(8,128)(2,1)}, bf16[2,64,1024]{2,1,0:T(8,128)(2,1)S(1)}, u32[]{:S(2)}) copy-start(bf16[2,64,1024]{2,1,0:T(8,128)(2,1)S(1)} %collective-permute-done.1.refs_7_) | copy-start | bytes 786436
  18.8 0.7 copy-start.9
  19.5 11.8 %collective-permute-start.4 = (bf16[2,96,1024]{2,1,0:T(8,128)(2,1)S(1)}, bf16[2,96,1024]{2,1,0:T(8,128)(2,1)S(1)}, u32[]{:S(2)}, u32[]{:S(2)}) collective-permute-start(bf16[2,96,1024]{2,1,0:T(8,128)(2,1)S(1)} %get-tuple-element.44), channel_id=1, source_target_pairs={{16,0},{17,1},{18,2},{19,3},{20,4},{21,5},{22,6},{23,7},{24,8},{25... | collective-permute-start | bytes 1179656 | tf_op jit(solution)/shard_map/ppermute | solution.py:251
  23.2 3.7 %copy-start.14 = (s32[96]{0:T(128)S(1)}, s32[96]{0:T(128)}, u32[]{:S(2)}) copy-start(s32[96]{0:T(128)} %constant.162) | copy-start | bytes 1156
  23.2 6.3 %collective-permute-start.2 = (bf16[2,96,1024]{2,1,0:T(8,128)(2,1)S(1)}, bf16[2,96,1024]{2,1,0:T(8,128)(2,1)S(1)}, u32[]{:S(2)}, u32[]{:S(2)}) collective-permute-start(bf16[2,96,1024]{2,1,0:T(8,128)(2,1)S(1)} %get-tuple-element.45), channel_id=1, source_target_pairs={{0,8},{1,9},{2,10},{3,11},{4,12},{5,13},{6,14},{7,15},{8,0},{9,1},... | collective-permute-start | bytes 1179656 | tf_op jit(solution)/shard_map/ppermute | solution.py:252
  23.9 7.7 %collective-permute-start.3 = (bf16[2,96,1024]{2,1,0:T(8,128)(2,1)S(1)}, bf16[2,96,1024]{2,1,0:T(8,128)(2,1)S(1)}, u32[]{:S(2)}, u32[]{:S(2)}) collective-permute-start(bf16[2,96,1024]{2,1,0:T(8,128)(2,1)S(1)} %get-tuple-element.46), channel_id=1, source_target_pairs={{0,16},{1,17},{2,18},{3,19},{4,20},{5,21},{6,22},{7,23},{8,24},{9,... | collective-permute-start | bytes 1179656 | tf_op jit(solution)/shard_map/ppermute | solution.py:250
  28.2 1.3 %copy-start.11 = (s32[96]{0:T(128)S(1)}, s32[96]{0:T(128)}, u32[]{:S(2)}) copy-start(s32[96]{0:T(128)} %constant.119.clone) | copy-start | bytes 1156
  28.2 1.3 %copy-start.12 = (s32[96]{0:T(128)S(1)}, s32[96]{0:T(128)}, u32[]{:S(2)}) copy-start(s32[96]{0:T(128)} %constant.118.clone) | copy-start | bytes 1156
  28.2 1.3 %copy-start.13 = (s32[96]{0:T(128)S(1)}, s32[96]{0:T(128)}, u32[]{:S(2)}) copy-start(s32[96]{0:T(128)} %constant.117.clone) | copy-start | bytes 1156
  49.6 1.8 %copy-start.7 = (bf16[2,96,1024]{2,1,0:T(8,128)(2,1)S(1)}, bf16[2,96,1024]{2,1,0:T(8,128)(2,1)}, u32[]{:S(2)}) copy-start(bf16[2,96,1024]{2,1,0:T(8,128)(2,1)} %get-tuple-element.15) | copy-start | bytes 1179652
  49.6 18.8 %copy-start.6 = (bf16[2,96,1024]{2,1,0:T(8,128)(2,1)S(1)}, bf16[2,96,1024]{2,1,0:T(8,128)(2,1)}, u32[]{:S(2)}) copy-start(bf16[2,96,1024]{2,1,0:T(8,128)(2,1)} %get-tuple-element.16) | copy-start | bytes 1179652
  50.8 19.6 %collective-permute-start.5 = (bf16[2,96,1024]{2,1,0:T(8,128)(2,1)S(1)}, bf16[2,96,1024]{2,1,0:T(8,128)(2,1)S(1)}, u32[]{:S(2)}, u32[]{:S(2)}) collective-permute-start(bf16[2,96,1024]{2,1,0:T(8,128)(2,1)S(1)} %broadcast_select_fusion), channel_id=1, source_target_pairs={{0,8},{1,9},{2,10},{3,11},{4,12},{5,13},{6,14},{7,15},{8,0},{9,1},... | collective-permute-start | bytes 1179656 | tf_op jit(solution)/shard_map/ppermute | solution.py:271
  51.5 20.7 %collective-permute-start.7 = (bf16[2,96,1024]{2,1,0:T(8,128)(2,1)S(1)}, bf16[2,96,1024]{2,1,0:T(8,128)(2,1)S(1)}, u32[]{:S(2)}, u32[]{:S(2)}) collective-permute-start(bf16[2,96,1024]{2,1,0:T(8,128)(2,1)S(1)} %copy-done.7), channel_id=1, source_target_pairs={{16,0},{17,1},{18,2},{19,3},{20,4},{21,5},{22,6},{23,7},{24,8},{25... | collective-permute-start | bytes 1179656 | tf_op jit(solution)/shard_map/ppermute | solution.py:269
  68.4 6.6 %collective-permute-start.6 = (bf16[2,96,1024]{2,1,0:T(8,128)(2,1)S(1)}, bf16[2,96,1024]{2,1,0:T(8,128)(2,1)S(1)}, u32[]{:S(2)}, u32[]{:S(2)}) collective-permute-start(bf16[2,96,1024]{2,1,0:T(8,128)(2,1)S(1)} %copy-done.6), channel_id=1, source_target_pairs={{0,16},{1,17},{2,18},{3,19},{4,20},{5,21},{6,22},{7,23},{8,24},{9,... | collective-permute-start | bytes 1179656 | tf_op jit(solution)/shard_map/ppermute | solution.py:270
  75.4 1.0 %copy-start.5 = (f32[2,64,1024]{2,1,0:T(8,128)S(1)}, f32[2,64,1024]{2,1,0:T(8,128)}, u32[]{:S(2)}) copy-start(f32[2,64,1024]{2,1,0:T(8,128)} %get-tuple-element.17) | copy-start | bytes 1572868
  76.4 2.0 %copy-start.4 = (f32[2,64,1024]{2,1,0:T(8,128)S(1)}, f32[2,64,1024]{2,1,0:T(8,128)}, u32[]{:S(2)}) copy-start(f32[2,64,1024]{2,1,0:T(8,128)} %get-tuple-element.18) | copy-start | bytes 1572868
  76.5 11.5 %collective-permute-start.8 = (bf16[2,64,1024]{2,1,0:T(8,128)(2,1)S(1)}, bf16[2,64,1024]{2,1,0:T(8,128)(2,1)S(1)}, u32[]{:S(2)}, u32[]{:S(2)}) collective-permute-start(bf16[2,64,1024]{2,1,0:T(8,128)(2,1)S(1)} %add_convert_fusion.3), channel_id=1, source_target_pairs={{0,1},{1,2},{2,3},{3,4},{4,5},{5,6},{6,7},{7,8},{8,9},{9,10},{10,1... | collective-permute-start | bytes 786440 | tf_op jit(solution)/shard_map/ppermute | solution.py:286
  78.5 13.4 %collective-permute-start.9 = (bf16[2,64,1024]{2,1,0:T(8,128)(2,1)S(1)}, bf16[2,64,1024]{2,1,0:T(8,128)(2,1)S(1)}, u32[]{:S(2)}, u32[]{:S(2)}) collective-permute-start(bf16[2,64,1024]{2,1,0:T(8,128)(2,1)S(1)} %add_convert_fusion.2), channel_id=1, source_target_pairs={{0,15},{1,0},{2,1},{3,2},{4,3},{5,4},{6,5},{7,6},{8,7},{9,8},{10,9... | collective-permute-start | bytes 786440 | tf_op jit(solution)/shard_map/ppermute | solution.py:285
  80.3 11.7 %copy-start.1 = (f32[256,1024]{1,0:T(8,128)S(1)}, f32[256,1024]{1,0:T(8,128)}, u32[]{:S(2)}) copy-start(f32[256,1024]{1,0:T(8,128)} %get-tuple-element.19) | copy-start | bytes 3145732
  92.0 1.4 %copy-start = (f32[256,1024]{1,0:T(8,128)S(1)}, f32[256,1024]{1,0:T(8,128)}, u32[]{:S(2)}) copy-start(f32[256,1024]{1,0:T(8,128)} %get-tuple-element.14) | copy-start | bytes 3145732

commit v5 on v4

--- a/solution.py
+++ b/solution.py
@@ -239,18 +239,23 @@
 
     from_left = lax.ppermute(pair(cols(keys, width - r, width), cols(values, width - r, width)), "lon", right_pairs)
     from_right = lax.ppermute(pair(cols(keys, 0, r), cols(values, 0, r)), "lon", left_pairs)
+    top_mid = pair(kf[:edge], vf[:edge])
+    bottom_mid = pair(kf[cells - edge :], vf[cells - edge :])
+    pole_mid = lax.ppermute(jnp.where(at_north, top_mid, bottom_mid), both, pole_pairs)
     n_side = height * r
-    top_send = jnp.concatenate(
-        [pair(kf[:edge], vf[:edge]), from_left[:, :corner], from_right[:, :corner]], axis=1
-    )
+    top_send = jnp.concatenate([top_mid, from_left[:, :corner], from_right[:, :corner]], axis=1)
     bottom_send = jnp.concatenate(
-        [pair(kf[cells - edge :], vf[cells - edge :]), from_left[:, n_side - corner :], from_right[:, n_side - corner :]],
-        axis=1,
+        [bottom_mid, from_left[:, n_side - corner :], from_right[:, n_side - corner :]], axis=1
     )
     from_above = lax.ppermute(bottom_send, both, down_pairs)
     from_below = lax.ppermute(top_send, both, up_pairs)
-    pole_recv = lax.ppermute(jnp.where(at_north, top_send, bottom_send), both, pole_pairs)
-    pole_strip = jnp.take(pole_recv, pole_src, axis=1)
+    pole_corners = lax.ppermute(
+        jnp.where(at_north, top_send[:, edge:], bottom_send[:, edge:]), both, pole_pairs
+    )
+    pole_strip = jnp.concatenate(
+        [jnp.take(pole_mid, pole_src[:edge], axis=1), jnp.take(pole_corners, pole_src[edge:] - edge, axis=1)],
+        axis=1,
+    )
     top = jnp.where(at_north, pole_strip, from_above)
     bottom = jnp.where(at_south, pole_strip, from_below)
 
@@ -268,10 +273,16 @@
 
     up_recv = lax.ppermute(top_g, both, up_pairs)
     down_recv = lax.ppermute(bottom_g, both, down_pairs)
-    pole_g = lax.ppermute(jnp.where(at_north, top_g, bottom_g), both, pole_pairs)
-    unfolded = jnp.take(pole_g, pole_dst, axis=1)
-    add_top = jnp.where(at_north, unfolded, down_recv).astype(f32)
-    add_bottom = jnp.where(at_south, unfolded, up_recv).astype(f32)
+    pole_g = jnp.where(at_north, top_g, bottom_g)
+    pole_g_corners = lax.ppermute(pole_g[:, edge:], both, pole_pairs)
+    unfolded_corners = jnp.take(pole_g_corners, pole_dst[edge:] - edge, axis=1)
+    zero_mid = jnp.zeros_like(up_recv[:, :edge])
+    add_top = jnp.where(
+        at_north, jnp.concatenate([zero_mid, unfolded_corners], axis=1), down_recv
+    ).astype(f32)
+    add_bottom = jnp.where(
+        at_south, jnp.concatenate([zero_mid, unfolded_corners], axis=1), up_recv
+    ).astype(f32)
 
     def side_send(g, first):
         pads_top = [(0, 0), (0, n_side - corner), (0, 0)]
@@ -284,14 +295,18 @@
 
     back_right = lax.ppermute(side_send(left_g, edge), "lon", left_pairs)
     back_left = lax.ppermute(side_send(right_g, edge + corner), "lon", right_pairs)
+    pole_g_mid = lax.ppermute(pole_g[:, :edge], both, pole_pairs)
+    unfolded_mid = jnp.take(pole_g_mid, pole_dst[:edge], axis=1).astype(f32)
+    north_mid = jnp.where(at_north, unfolded_mid, 0.0)
+    south_mid = jnp.where(at_south, unfolded_mid, 0.0)
 
     def final_of(c, own):
         block = own.reshape(height, width, features)
         row_pad = [(0, 0), (0, 0)]
         block = (
             block
-            + jnp.pad(add_top[c, :edge].reshape(r, width, features), [(0, height - r)] + row_pad)
-            + jnp.pad(add_bottom[c, :edge].reshape(r, width, features), [(height - r, 0)] + row_pad)
+            + jnp.pad((add_top[c, :edge] + north_mid[c]).reshape(r, width, features), [(0, height - r)] + row_pad)
+            + jnp.pad((add_bottom[c, :edge] + south_mid[c]).reshape(r, width, features), [(height - r, 0)] + row_pad)
             + jnp.pad(
                 back_left[c].reshape(height, r, features).astype(f32), [(0, 0), (0, width - r), (0, 0)]
             )

time: 94.9 us -> 94.7 us (level)
  waiting for transfers between devices: 19.8 us -> 13 us
  starting transfers between devices: 38.3 us -> 41.4 us
  local copies, waits for them, and re-layouts: 13.4 us -> 16.1 us
    ppermute x1, starting transfers between devices: 3.71 us -> 7.09 us  [on_device(): from_below = lax.ppermute(top_send, both, up_pairs)]
    ppermute x1, waiting for transfers between devices: 4.16 us -> 1.07 us  [on_device(): lax.ppermute(pair(cols(keys, width - r, width), cols(values, width - r, w...]
    ppermute x1, starting transfers between devices: 17 us -> 14.3 us  [on_device(): up_recv = lax.ppermute(top_g, both, up_pairs)]
    ppermute x1, starting transfers between devices: 1.97 us -> 0.08 us  [on_device(): lax.ppermute(side_send(right_g, edge + corner), 'lon', right_pairs)]
    ppermute x1, starting transfers between devices: 3.02 us -> 4.81 us  [on_device(): from_above = lax.ppermute(bottom_send, both, down_pairs)]
    ppermute x1, waiting for transfers between devices: 3.72 us -> 2.04 us  [on_device(): back_right = lax.ppermute(side_send(left_g, edge), 'lon', left_pairs)]
    unnamed x30, local copies, waits for them, and re-layouts: 3.45 us -> 5.09 us
    ppermute x2 -> x4, starting transfers between devices: 1.37 us -> 2.81 us  [the longest x1 0.8 us: on_device(): pole_g_corners = lax.ppermute(pole_g[:, edge:], both, pole_pairs)]
  transfers between devices with their start and end apart: 10 -> 12, of which waited for: 6 -> 4; matrix products, arithmetic and copies ran while one was open for 9% -> 11% of each run, Pallas kernels for 0% -> 0%
where the time goes in v5:
time: 94.7 us; the launch traced here: 94.2 us
  starting transfers between devices  41.4 us (44%)
  Pallas kernels  16.9 us (18%)
  local copies, waits for them, and re-layouts  16.1 us (17%)
  waiting for transfers between devices  13 us (14%)
  other arithmetic  5.55 us (6%)
  between operations  1.3 us (1%)
    pallas_call x1, Pallas kernels, attention_core(): pl.pallas_call(lambda *refs: attention_kernel(width, *refs), out_shape=ou...  16.9 us
    ppermute x1, starting transfers between devices, on_device(): up_recv = lax.ppermute(top_g, both, up_pairs)  14.3 us
    ppermute x1, waiting for transfers between devices, on_device(): lax.ppermute(side_send(right_g, edge + corner), 'lon', right_pairs)  7.78 us
    ppermute x1, starting transfers between devices, on_device(): lax.ppermute(pair(cols(keys, 0, r), cols(values, 0, r)), 'lon', left_pairs)  7.48 us
    ppermute x1, starting transfers between devices, on_device(): from_below = lax.ppermute(top_send, both, up_pairs)  7.09 us
    unnamed x30, local copies, waits for them, and re-layouts  5.09 us
    ppermute x1, starting transfers between devices, on_device(): from_above = lax.ppermute(bottom_send, both, down_pairs)  4.81 us
    ppermute x1, starting transfers between devices, on_device(): back_right = lax.ppermute(side_send(left_g, edge), 'lon', left_pairs)  2.74 us
  transfers between devices with their start and end apart: 12, of which 4 were waited for; matrix products, arithmetic and copies ran while one was open for 11% of the time, Pallas kernels for 0%

profile of v5, /device:TPU:1, one launch (start us, length us, event | category | flops | bytes accessed | tf_op | source)
XLA Modules:
  0.0 94.2 jit_solution(16042123615259839362)
XLA Ops:
  0.6 1.2 %fusion.15 = (bf16[16,4,1024]{2,1,0:T(4,128)(2,1)S(1)}, bf16[16,4,1024]{2,1,0:T(4,128)(2,1)S(1)}) fusion(bf16[16,16,1024]{2,1,0:T(8,128)(2,1)} %param.21), kind=kLoop, calls=%fused_computation.91 | loop fusion | bytes 524288 | tf_op jit(solution)/shard_map/slice | solution.py:238
  2.1 7.5 %collective-permute-start.2 = (bf16[2,64,1024]{2,1,0:T(8,128)(2,1)S(1)}, bf16[2,64,1024]{2,1,0:T(8,128)(2,1)S(1)}, u32[]{:S(2)}, u32[]{:S(2)}) collective-permute-start(bf16[2,64,1024]{2,1,0:T(8,128)(2,1)S(1)} %pad_maximum_fusion.4), channel_id=1, source_target_pairs={{0,15},{1,0},{2,1},{3,2},{4,3},{5,4},{6,5},{7,6},{8,7},{9,8},{10,9... | collective-permute-start | bytes 786440 | tf_op jit(solution)/shard_map/ppermute | solution.py:241
  9.8 0.8 copy-done.2
  10.7 0.7 collective-permute-start
  11.4 0.7 copy-done.10
  12.1 0.7 gather_fusion
  12.9 0.7 gather_fusion.4
  14.9 1.2 %gather_fusion.5 = s32[96]{0:T(128)S(1)} fusion(s32[24]{0:T(128)S(1)} %scatter_custom_fusion, s32[1024]{0:T(1024)S(1)} %pad_clamp_fusion.5), kind=kCustom, calls=%fused_computation.5.clone | custom fusion | bytes 1152 | tf_op jit(solution)/shard_map/jit(_take)/gather | solution.py:229
  16.2 1.2 %gather_fusion.1 = s32[96]{0:T(128)S(1)} fusion(s32[24]{0:T(128)S(1)} %get-tuple-element.62, s32[1024]{0:T(1024)S(1)} %pad_clamp_fusion.5), kind=kCustom, calls=%fused_computation.1.clone | custom fusion | bytes 1152 | tf_op jit(solution)/shard_map/jit(_take)/gather | solution.py:228
  17.7 1.1 %collective-permute-done.1.refs_6_ = bf16[2,64,1024]{2,1,0:T(8,128)(2,1)S(1)} collective-permute-done((bf16[2,64,1024]{2,1,0:T(8,128)(2,1)S(1)}, bf16[2,64,1024]{2,1,0:T(8,128)(2,1)S(1)}, u32[]{:S(2)}, u32[]{:S(2)}) %collective-permute-start.1) | collective-permute-done | bytes 262176 | tf_op jit(solution)/shard_map/ppermute | solution.py:240
  19.5 0.7 collective-permute-start.3
  20.2 4.8 %collective-permute-start.4 = (bf16[2,96,1024]{2,1,0:T(8,128)(2,1)S(1)}, bf16[2,96,1024]{2,1,0:T(8,128)(2,1)S(1)}, u32[]{:S(2)}, u32[]{:S(2)}) collective-permute-start(bf16[2,96,1024]{2,1,0:T(8,128)(2,1)S(1)} %pad_maximum_fusion.1), channel_id=1, source_target_pairs={{0,16},{1,17},{2,18},{3,19},{4,20},{5,21},{6,22},{7,23},{8,24},{9,... | collective-permute-start | bytes 1179656 | tf_op jit(solution)/shard_map/ppermute | solution.py:250
  25.0 7.1 %collective-permute-start.5 = (bf16[2,96,1024]{2,1,0:T(8,128)(2,1)S(1)}, bf16[2,96,1024]{2,1,0:T(8,128)(2,1)S(1)}, u32[]{:S(2)}, u32[]{:S(2)}) collective-permute-start(bf16[2,96,1024]{2,1,0:T(8,128)(2,1)S(1)} %pad_maximum_fusion.2), channel_id=1, source_target_pairs={{16,0},{17,1},{18,2},{19,3},{20,4},{21,5},{22,6},{23,7},{24,8},{25... | collective-permute-start | bytes 1179656 | tf_op jit(solution)/shard_map/ppermute | solution.py:251
  32.4 1.1 %gather_fusion.2 = bf16[64,2,1024]{2,1,0:T(2,128)(2,1)S(1)} fusion(bf16[2,64,1024]{2,0,1:T(2,128)(2,1)S(1)} %copy.15, s32[1024]{0:T(1024)S(1)} %pad_clamp_fusion.4), kind=kCustom, calls=%fused_computation.2.clone | custom fusion | bytes 524544 | tf_op jit(solution)/shard_map/jit(_take)/gather | solution.py:256
  33.8 0.8 gather_fusion.3
  34.7 1.1 %broadcast_select_fusion = (bf16[2,96,1024]{2,1,0:T(8,128)(2,1)}, bf16[2,96,1024]{2,1,0:T(8,128)(2,1)}) fusion(bf16[2,96,1024]{2,1,0:T(8,128)(2,1)S(1)} %collective-permute-done.5, pred[]{:T(512)S(6)} %eq.14, bf16[2,32,1024]{2,1,0:T(8,128)(2,1)S(1)} %fusion.4, bf16[2,64,1024]{2,1,0:T(8,128)(2,1)S(1)} %fusion.2, ...), kind=kLoop, calls=%fused_computation.22 | loop fusion | flops 1179648 | bytes 1966082 | tf_op jit(solution)/shard_map/jit(_where)/select_n | solution.py:260
  35.8 16.9 %neighbourhood_attention_bwd.1 = (bf16[256,1024]{1,0:T(8,128)(2,1)}, f32[256,1024]{1,0:T(8,128)}, f32[256,1024]{1,0:T(8,128)}, bf16[2,96,1024]{2,1,0:T(8,128)(2,...) custom-call(bf16[256,1024]{1,0:T(8,128)(2,1)} %bitcast.44, ...), custom_call_target="tpu_custom_call" | custom-call | flops 2013265920 | bytes 7864320 | tf_op jit(solution)/shard_map/neighbourhood_attention_bwd/pallas_call | solution.py:165
  52.7 1.0 %broadcast_select_fusion.1 = bf16[2,96,1024]{2,1,0:T(8,128)(2,1)S(1)} fusion(bf16[2,96,1024]{2,1,0:T(8,128)(2,1)} %get-tuple-element.16, bf16[2,96,1024]{2,1,0:T(8,128)(2,1)} %get-tuple-element.17, pred[]{:T(512)S(6)} %eq.13), kind=kLoop, calls=%fused_computation.23 | loop fusion | flops 196608 | bytes 1179649 | tf_op jit(solution)/shard_map/jit(_where)/select_n | solution.py:276
  53.8 0.8 collective-permute-start.6
  54.7 0.7 collective-permute-start.8
  55.4 14.3 %collective-permute-start.9 = (bf16[2,96,1024]{2,1,0:T(8,128)(2,1)S(1)}, bf16[2,96,1024]{2,1,0:T(8,128)(2,1)S(1)}, u32[]{:S(2)}, u32[]{:S(2)}) collective-permute-start(bf16[2,96,1024]{2,1,0:T(8,128)(2,1)S(1)} %copy-done.7), channel_id=1, source_target_pairs={{16,0},{17,1},{18,2},{19,3},{20,4},{21,5},{22,6},{23,7},{24,8},{25... | collective-permute-start | bytes 1179656 | tf_op jit(solution)/shard_map/ppermute | solution.py:274
  69.7 1.9 %collective-permute-start.7 = (bf16[2,96,1024]{2,1,0:T(8,128)(2,1)S(1)}, bf16[2,96,1024]{2,1,0:T(8,128)(2,1)S(1)}, u32[]{:S(2)}, u32[]{:S(2)}) collective-permute-start(bf16[2,96,1024]{2,1,0:T(8,128)(2,1)S(1)} %copy-done.6), channel_id=1, source_target_pairs={{0,16},{1,17},{2,18},{3,19},{4,20},{5,21},{6,22},{7,23},{8,24},{9,... | collective-permute-start | bytes 1179656 | tf_op jit(solution)/shard_map/ppermute | solution.py:275
  71.8 0.8 gather_fusion.6
  73.0 1.1 %gather_fusion.7 = bf16[64,2,1024]{2,1,0:T(2,128)(2,1)S(1)} fusion(bf16[2,64,1024]{2,0,1:T(2,128)(2,1)S(1)} %copy.21, s32[1024]{0:T(1024)S(1)} %pad_clamp_fusion), kind=kCustom, calls=%fused_computation.6.clone | custom fusion | bytes 524544 | tf_op jit(solution)/shard_map/jit(_take)/gather | solution.py:299
  74.3 2.0 %collective-permute-done.7 = bf16[2,96,1024]{2,1,0:T(8,128)(2,1)S(1)} collective-permute-done((bf16[2,96,1024]{2,1,0:T(8,128)(2,1)S(1)}, bf16[2,96,1024]{2,1,0:T(8,128)(2,1)S(1)}, u32[]{:S(2)}, u32[]{:S(2)}) %collective-permute-start.7) | collective-permute-done | bytes 393248 | tf_op jit(solution)/shard_map/ppermute | solution.py:275
  76.6 1.0 %copy-done.5 = f32[2,64,1024]{2,1,0:T(8,128)S(1)} copy-done((f32[2,64,1024]{2,1,0:T(8,128)S(1)}, f32[2,64,1024]{2,1,0:T(8,128)}, u32[]{:S(2)}) %copy-start.5) | copy-done | bytes 524312
  77.8 0.9 copy-done.4
  78.7 2.7 %collective-permute-start.11 = (bf16[2,64,1024]{2,1,0:T(8,128)(2,1)S(1)}, bf16[2,64,1024]{2,1,0:T(8,128)(2,1)S(1)}, u32[]{:S(2)}, u32[]{:S(2)}) collective-permute-start(bf16[2,64,1024]{2,1,0:T(8,128)(2,1)S(1)} %add_convert_fusion.2), channel_id=1, source_target_pairs={{0,15},{1,0},{2,1},{3,2},{4,3},{5,4},{6,5},{7,6},{8,7},{9,8},{10,9... | collective-permute-start | bytes 786440 | tf_op jit(solution)/shard_map/ppermute | solution.py:296
  81.6 7.8 %collective-permute-done.10 = bf16[2,64,1024]{2,1,0:T(8,128)(2,1)S(1)} collective-permute-done((bf16[2,64,1024]{2,1,0:T(8,128)(2,1)S(1)}, bf16[2,64,1024]{2,1,0:T(8,128)(2,1)S(1)}, u32[]{:S(2)}, u32[]{:S(2)}) %collective-permute-start.10) | collective-permute-done | bytes 262176 | tf_op jit(solution)/shard_map/ppermute | solution.py:297
  89.5 2.0 %collective-permute-done.11 = bf16[2,64,1024]{2,1,0:T(8,128)(2,1)S(1)} collective-permute-done((bf16[2,64,1024]{2,1,0:T(8,128)(2,1)S(1)}, bf16[2,64,1024]{2,1,0:T(8,128)(2,1)S(1)}, u32[]{:S(2)}, u32[]{:S(2)}) %collective-permute-start.11) | collective-permute-done | bytes 262176 | tf_op jit(solution)/shard_map/ppermute | solution.py:296
  91.7 1.0 %add_convert_fusion = bf16[16,16,1024]{2,1,0:T(8,128)(2,1)} fusion(f32[4,16,1024]{2,1,0:T(8,128)S(1)} %bitcast.40, f32[16,16,1024]{2,1,0:T(8,128)S(1)} %bitcast.37, f32[4,16,1024]{2,1,0:T(8,128)S(1)} %bitcast.41, bf16[16,4,1024]{2,1,0:T(4,128)(2,1)S(1)} %convert_element_type.64, bf16[16,4,1024]{2,1,0:T(4,128)(2,1)S(1)} %convert_element_type.63), kind=kLoop, calls=%fused_computation.9 | loop fusion | flops 1835008 | bytes 2359296 | tf_op jit(solution)/shard_map/convert_element_type | solution.py:317
  93.1 1.0 %add_convert_fusion.1 = bf16[16,16,1024]{2,1,0:T(8,128)(2,1)} fusion(f32[4,16,1024]{2,1,0:T(8,128)S(1)} %bitcast.38, f32[16,16,1024]{2,1,0:T(8,128)S(1)} %bitcast.36, f32[4,16,1024]{2,1,0:T(8,128)S(1)} %bitcast.39, bf16[16,4,1024]{2,1,0:T(4,128)(2,1)S(1)} %convert_element_type.61, bf16[16,4,1024]{2,1,0:T(4,128)(2,1)S(1)} %convert_element_type.59), kind=kLoop, calls=%fused_computation.10 | loop fusion | flops 1835008 | bytes 2359296 | tf_op jit(solution)/shard_map/convert_element_type | solution.py:317
  (92 shorter events, 5.4 us)
Async XLA Ops:
  0.6 1.2 %copy-start.3 = (bf16[16,16,1024]{2,1,0:T(8,128)(2,1)S(1)}, bf16[16,16,1024]{2,1,0:T(8,128)(2,1)}, u32[]{:S(2)}) copy-start(bf16[16,16,1024]{2,1,0:T(8,128)(2,1)} %param.22) | copy-start | bytes 1572868
  2.1 15.6 %collective-permute-start.2 = (bf16[2,64,1024]{2,1,0:T(8,128)(2,1)S(1)}, bf16[2,64,1024]{2,1,0:T(8,128)(2,1)S(1)}, u32[]{:S(2)}, u32[]{:S(2)}) collective-permute-start(bf16[2,64,1024]{2,1,0:T(8,128)(2,1)S(1)} %pad_maximum_fusion.4), channel_id=1, source_target_pairs={{0,15},{1,0},{2,1},{3,2},{4,3},{5,4},{6,5},{7,6},{8,7},{9,8},{10,9... | collective-permute-start | bytes 786440 | tf_op jit(solution)/shard_map/ppermute | solution.py:241
  9.6 1.0 %copy-start.2 = (bf16[16,16,1024]{2,1,0:T(8,128)(2,1)S(1)}, bf16[16,16,1024]{2,1,0:T(8,128)(2,1)}, u32[]{:S(2)}) copy-start(bf16[16,16,1024]{2,1,0:T(8,128)(2,1)} %param.21) | copy-start | bytes 1572868
  9.7 9.1 %collective-permute-start.1 = (bf16[2,64,1024]{2,1,0:T(8,128)(2,1)S(1)}, bf16[2,64,1024]{2,1,0:T(8,128)(2,1)S(1)}, u32[]{:S(2)}, u32[]{:S(2)}) collective-permute-start(bf16[2,64,1024]{2,1,0:T(8,128)(2,1)S(1)} %pad_maximum_fusion.3), channel_id=1, source_target_pairs={{0,1},{1,2},{2,3},{3,4},{4,5},{5,6},{6,7},{7,8},{8,9},{9,10},{10,1... | collective-permute-start | bytes 786440 | tf_op jit(solution)/shard_map/ppermute | solution.py:240
  10.7 21.4 %collective-permute-start = (bf16[2,64,1024]{2,1,0:T(8,128)(2,1)S(1)}, bf16[2,64,1024]{2,1,0:T(8,128)(2,1)S(1)}, u32[]{:S(2)}, u32[]{:S(2)}) collective-permute-start(bf16[2,64,1024]{2,1,0:T(8,128)(2,1)S(1)} %maximum_select_fusion), channel_id=1, source_target_pairs={{0,8},{1,9},{2,10},{3,11},{4,12},{5,13},{6,14},{7,15},{8,0},{9,1},... | collective-permute-start | bytes 786440 | tf_op jit(solution)/shard_map/ppermute | solution.py:244
  11.4 0.7 copy-start.10
  13.6 0.7 copy-start.14
  16.1 1.3 %copy-start.11 = (s32[96]{0:T(128)S(1)}, s32[96]{0:T(128)}, u32[]{:S(2)}) copy-start(s32[96]{0:T(128)} %constant.135.clone) | copy-start | bytes 1156
  16.1 1.3 %copy-start.12 = (s32[96]{0:T(128)S(1)}, s32[96]{0:T(128)}, u32[]{:S(2)}) copy-start(s32[96]{0:T(128)} %constant.134.clone) | copy-start | bytes 1156
  16.1 1.3 %copy-start.13 = (s32[96]{0:T(128)S(1)}, s32[96]{0:T(128)}, u32[]{:S(2)}) copy-start(s32[96]{0:T(128)} %constant.133.clone) | copy-start | bytes 1156
  17.7 1.1 %copy-start.8 = (bf16[2,64,1024]{2,1,0:T(8,128)(2,1)}, bf16[2,64,1024]{2,1,0:T(8,128)(2,1)S(1)}, u32[]{:S(2)}) copy-start(bf16[2,64,1024]{2,1,0:T(8,128)(2,1)S(1)} %collective-permute-done.2.refs_7_) | copy-start | bytes 786436
  18.8 0.7 copy-start.9
  19.5 14.1 %collective-permute-start.3 = (bf16[2,32,1024]{2,1,0:T(8,128)(2,1)S(1)}, bf16[2,32,1024]{2,1,0:T(8,128)(2,1)S(1)}, u32[]{:S(2)}, u32[]{:S(2)}) collective-permute-start(bf16[2,32,1024]{2,1,0:T(8,128)(2,1)S(1)} %maximum_select_fusion.1), channel_id=1, source_target_pairs={{0,8},{1,9},{2,10},{3,11},{4,12},{5,13},{6,14},{7,15},{8,0},{9,1},... | collective-permute-start | bytes 393224 | tf_op jit(solution)/shard_map/ppermute | solution.py:252
  20.2 14.5 %collective-permute-start.4 = (bf16[2,96,1024]{2,1,0:T(8,128)(2,1)S(1)}, bf16[2,96,1024]{2,1,0:T(8,128)(2,1)S(1)}, u32[]{:S(2)}, u32[]{:S(2)}) collective-permute-start(bf16[2,96,1024]{2,1,0:T(8,128)(2,1)S(1)} %pad_maximum_fusion.1), channel_id=1, source_target_pairs={{0,16},{1,17},{2,18},{3,19},{4,20},{5,21},{6,22},{7,23},{8,24},{9,... | collective-permute-start | bytes 1179656 | tf_op jit(solution)/shard_map/ppermute | solution.py:250
  25.0 9.7 %collective-permute-start.5 = (bf16[2,96,1024]{2,1,0:T(8,128)(2,1)S(1)}, bf16[2,96,1024]{2,1,0:T(8,128)(2,1)S(1)}, u32[]{:S(2)}, u32[]{:S(2)}) collective-permute-start(bf16[2,96,1024]{2,1,0:T(8,128)(2,1)S(1)} %pad_maximum_fusion.2), channel_id=1, source_target_pairs={{16,0},{17,1},{18,2},{19,3},{20,4},{21,5},{22,6},{23,7},{24,8},{25... | collective-permute-start | bytes 1179656 | tf_op jit(solution)/shard_map/ppermute | solution.py:251
  53.8 1.6 %copy-start.7 = (bf16[2,96,1024]{2,1,0:T(8,128)(2,1)S(1)}, bf16[2,96,1024]{2,1,0:T(8,128)(2,1)}, u32[]{:S(2)}) copy-start(bf16[2,96,1024]{2,1,0:T(8,128)(2,1)} %get-tuple-element.16) | copy-start | bytes 1179652
  53.8 15.9 %copy-start.6 = (bf16[2,96,1024]{2,1,0:T(8,128)(2,1)S(1)}, bf16[2,96,1024]{2,1,0:T(8,128)(2,1)}, u32[]{:S(2)}) copy-start(bf16[2,96,1024]{2,1,0:T(8,128)(2,1)} %get-tuple-element.17) | copy-start | bytes 1179652
  53.8 17.9 %collective-permute-start.6 = (bf16[2,32,1024]{2,1,0:T(8,128)(2,1)S(1)}, bf16[2,32,1024]{2,1,0:T(8,128)(2,1)S(1)}, u32[]{:S(2)}, u32[]{:S(2)}) collective-permute-start(bf16[2,32,1024]{2,1,0:T(8,128)(2,1)S(1)} %slice.172), channel_id=1, source_target_pairs={{0,8},{1,9},{2,10},{3,11},{4,12},{5,13},{6,14},{7,15},{8,0},{9,1},... | collective-permute-start | bytes 393224 | tf_op jit(solution)/shard_map/ppermute | solution.py:277
  54.7 18.1 %collective-permute-start.8 = (bf16[2,64,1024]{2,1,0:T(8,128)(2,1)S(1)}, bf16[2,64,1024]{2,1,0:T(8,128)(2,1)S(1)}, u32[]{:S(2)}, u32[]{:S(2)}) collective-permute-start(bf16[2,64,1024]{2,1,0:T(8,128)(2,1)S(1)} %slice.174), channel_id=1, source_target_pairs={{0,8},{1,9},{2,10},{3,11},{4,12},{5,13},{6,14},{7,15},{8,0},{9,1},... | collective-permute-start | bytes 786440 | tf_op jit(solution)/shard_map/ppermute | solution.py:298
  55.4 18.9 %collective-permute-start.9 = (bf16[2,96,1024]{2,1,0:T(8,128)(2,1)S(1)}, bf16[2,96,1024]{2,1,0:T(8,128)(2,1)S(1)}, u32[]{:S(2)}, u32[]{:S(2)}) collective-permute-start(bf16[2,96,1024]{2,1,0:T(8,128)(2,1)S(1)} %copy-done.7), channel_id=1, source_target_pairs={{16,0},{17,1},{18,2},{19,3},{20,4},{21,5},{22,6},{23,7},{24,8},{25... | collective-permute-start | bytes 1179656 | tf_op jit(solution)/shard_map/ppermute | solution.py:274
  69.7 6.6 %collective-permute-start.7 = (bf16[2,96,1024]{2,1,0:T(8,128)(2,1)S(1)}, bf16[2,96,1024]{2,1,0:T(8,128)(2,1)S(1)}, u32[]{:S(2)}, u32[]{:S(2)}) collective-permute-start(bf16[2,96,1024]{2,1,0:T(8,128)(2,1)S(1)} %copy-done.6), channel_id=1, source_target_pairs={{0,16},{1,17},{2,18},{3,19},{4,20},{5,21},{6,22},{7,23},{8,24},{9,... | collective-permute-start | bytes 1179656 | tf_op jit(solution)/shard_map/ppermute | solution.py:275
  76.6 1.0 %copy-start.5 = (f32[2,64,1024]{2,1,0:T(8,128)S(1)}, f32[2,64,1024]{2,1,0:T(8,128)}, u32[]{:S(2)}) copy-start(f32[2,64,1024]{2,1,0:T(8,128)} %get-tuple-element.18) | copy-start | bytes 1572868
  77.6 1.0 %copy-start.4 = (f32[2,64,1024]{2,1,0:T(8,128)S(1)}, f32[2,64,1024]{2,1,0:T(8,128)}, u32[]{:S(2)}) copy-start(f32[2,64,1024]{2,1,0:T(8,128)} %get-tuple-element.19) | copy-start | bytes 1572868
  77.7 11.7 %collective-permute-start.10 = (bf16[2,64,1024]{2,1,0:T(8,128)(2,1)S(1)}, bf16[2,64,1024]{2,1,0:T(8,128)(2,1)S(1)}, u32[]{:S(2)}, u32[]{:S(2)}) collective-permute-start(bf16[2,64,1024]{2,1,0:T(8,128)(2,1)S(1)} %add_convert_fusion.3), channel_id=1, source_target_pairs={{0,1},{1,2},{2,3},{3,4},{4,5},{5,6},{6,7},{7,8},{8,9},{9,10},{10,1... | collective-permute-start | bytes 786440 | tf_op jit(solution)/shard_map/ppermute | solution.py:297
  78.7 12.9 %collective-permute-start.11 = (bf16[2,64,1024]{2,1,0:T(8,128)(2,1)S(1)}, bf16[2,64,1024]{2,1,0:T(8,128)(2,1)S(1)}, u32[]{:S(2)}, u32[]{:S(2)}) collective-permute-start(bf16[2,64,1024]{2,1,0:T(8,128)(2,1)S(1)} %add_convert_fusion.2), channel_id=1, source_target_pairs={{0,15},{1,0},{2,1},{3,2},{4,3},{5,4},{6,5},{7,6},{8,7},{9,8},{10,9... | collective-permute-start | bytes 786440 | tf_op jit(solution)/shard_map/ppermute | solution.py:296
  81.6 10.1 %copy-start.1 = (f32[256,1024]{1,0:T(8,128)S(1)}, f32[256,1024]{1,0:T(8,128)}, u32[]{:S(2)}) copy-start(f32[256,1024]{1,0:T(8,128)} %get-tuple-element.20) | copy-start | bytes 3145732
  91.7 1.4 %copy-start = (f32[256,1024]{1,0:T(8,128)S(1)}, f32[256,1024]{1,0:T(8,128)}, u32[]{:S(2)}) copy-start(f32[256,1024]{1,0:T(8,128)} %get-tuple-element.15) | copy-start | bytes 3145732

commit v6 on v5

--- a/solution.py
+++ b/solution.py
@@ -11,7 +11,7 @@
 RADIUS = 4
 
 SPAN = 2 * RADIUS + 1
-TILE_ROWS = 8
+TILE_ROWS = 4
 LANES = 128
 
 
@@ -22,11 +22,15 @@
     scale = HEAD_DIM ** (-0.5)
     r = RADIUS
     tq = TILE_ROWS * width
-    main = 2 * TILE_ROWS * width
-    side = 2 * TILE_ROWS * r
+    win = TILE_ROWS + 2 * r
+    main = win * width
+    side = win * r
     tk = main + 2 * side
     edge = r * width
     corner = r * r
+    tiles = q_ref.shape[0] // tq
+    groups_per_tile = win // r
+    last_group = (tiles * TILE_ROWS + 2 * r) // r - 1
     pairs = q_ref.shape[1] // LANES
 
     qi = lax.broadcasted_iota(jnp.int32, (tq, tk), 0).astype(jnp.float32)
@@ -58,57 +62,36 @@
         ds = (w * (dw - corr)).astype(jnp.bfloat16)
         return ds, w.astype(jnp.bfloat16)
 
+    def places(g, own, top, bot, left, right, c):
+        if g == 0:
+            return [(top, (c,), 0, edge), (top, (c,), edge, corner), (top, (c,), edge + corner, corner)]
+        if g == last_group:
+            return [(bot, (c,), 0, edge), (bot, (c,), edge, corner), (bot, (c,), edge + corner, corner)]
+        return [(own, (), (g - 1) * edge, edge), (left, (c,), (g - 1) * corner, corner),
+                (right, (c,), (g - 1) * corner, corner)]
+
     def gather_keys(own, c, t, lanes):
-        rows = side - corner
-        if t == 0:
-            parts = [
-                top_in[c, pl.ds(0, edge), lanes],
-                own[pl.ds(0, main - edge), lanes],
-                top_in[c, pl.ds(edge, corner), lanes],
-                left_in[c, pl.ds(0, rows), lanes],
-                top_in[c, pl.ds(edge + corner, corner), lanes],
-                right_in[c, pl.ds(0, rows), lanes],
-            ]
-        else:
-            start = left_in.shape[1] - rows
-            parts = [
-                own[pl.ds(edge, main - edge), lanes],
-                bot_in[c, pl.ds(0, edge), lanes],
-                left_in[c, pl.ds(start, rows), lanes],
-                bot_in[c, pl.ds(edge, corner), lanes],
-                right_in[c, pl.ds(start, rows), lanes],
-                bot_in[c, pl.ds(edge + corner, corner), lanes],
-            ]
-        return jnp.concatenate(parts, axis=0)
+        parts = [[], [], []]
+        for g in range(t, t + groups_per_tile):
+            for kind, (ref, pre, start, size) in enumerate(places(g, own, top_in, bot_in, left_in, right_in, c)):
+                parts[kind].append(ref[pre + (pl.ds(start, size), lanes)])
+        return jnp.concatenate(parts[0] + parts[1] + parts[2], axis=0)
 
     def scatter_grads(d, own, c, t, lanes):
-        bf = jnp.bfloat16
-        rows = side - corner
-        n_side = left_out.shape[1]
-        if t == 0:
-            top_out[c, pl.ds(0, edge), lanes] = d[:edge].astype(bf)
-            own[pl.ds(0, main - edge), lanes] = d[edge:main]
-            top_out[c, pl.ds(edge, corner), lanes] = d[main : main + corner].astype(bf)
-            left_out[c, pl.ds(0, rows), lanes] = d[main + corner : main + side]
-            top_out[c, pl.ds(edge + corner, corner), lanes] = d[main + side : main + side + corner].astype(bf)
-            right_out[c, pl.ds(0, rows), lanes] = d[main + side + corner :]
-        else:
-            shared = main - 2 * edge
-            own[pl.ds(edge, shared), lanes] += d[:shared]
-            own[pl.ds(edge + shared, edge), lanes] = d[shared : main - edge]
-            bot_out[c, pl.ds(0, edge), lanes] = d[main - edge : main].astype(bf)
-            start = n_side - rows
-            overlap = rows - start
-            left_out[c, pl.ds(start, overlap), lanes] += d[main : main + overlap]
-            left_out[c, pl.ds(rows, n_side - rows), lanes] = d[main + overlap : main + rows]
-            bot_out[c, pl.ds(edge, corner), lanes] = d[main + rows : main + side].astype(bf)
-            right_out[c, pl.ds(start, overlap), lanes] += d[main + side : main + side + overlap]
-            right_out[c, pl.ds(rows, n_side - rows), lanes] = d[main + side + overlap : main + side + rows]
-            bot_out[c, pl.ds(edge + corner, corner), lanes] = d[main + side + rows :].astype(bf)
+        offsets = [0, main, main + side]
+        for n, g in enumerate(range(t, t + groups_per_tile)):
+            first = t == max(0, g - (groups_per_tile - 1))
+            for kind, (ref, pre, start, size) in enumerate(places(g, own, top_out, bot_out, left_out, right_out, c)):
+                piece = d[offsets[kind] + n * size : offsets[kind] + (n + 1) * size]
+                index = pre + (pl.ds(start, size), lanes)
+                if first:
+                    ref[index] = piece.astype(ref.dtype)
+                else:
+                    ref[index] += piece
 
     def body(p, carry):
         lanes = pl.ds(pl.multiple_of(p * LANES, LANES), LANES)
-        for t in range(2):
+        for t in range(tiles):
             qp = q_ref[pl.ds(t * tq, tq), lanes]
             gp = g_ref[pl.ds(t * tq, tq), lanes]
             kp = gather_keys(k_own, 0, t, lanes)
@@ -143,9 +126,9 @@
     cells, features = q2.shape
     r = RADIUS
     tq = TILE_ROWS * width
-    tk = 2 * TILE_ROWS * (width + 2 * r)
+    tk = (TILE_ROWS + 2 * r) * (width + 2 * r)
     tiles = cells // tq
-    assert tiles == 2
+    assert TILE_ROWS % r == 0 and tiles * TILE_ROWS == cells // width
     flops = 10 * 2 * tq * tk * LANES * (features // LANES) * tiles
     vmem = pl.BlockSpec(memory_space=pltpu.VMEM)
     f32 = jnp.float32

time: 94.7 us -> 102 us (1.077)
  Pallas kernels: 16.9 us -> 23.7 us
    pallas_call x1, Pallas kernels: 16.9 us -> 23.7 us  [attention_core(): pl.pallas_call(lambda *refs: attention_kernel(width, *refs), out_shape=ou...]
  transfers between devices with their start and end apart: 12 -> 12, of which waited for: 4 -> 4; matrix products, arithmetic and copies ran while one was open for 11% -> 10% of each run, Pallas kernels for 0% -> 0%
where the time goes in v6:
time: 102 us; the launch traced here: 101 us
  starting transfers between devices  41.4 us (41%)
  Pallas kernels  23.7 us (23%)
  local copies, waits for them, and re-layouts  16.1 us (16%)
  waiting for transfers between devices  13 us (13%)
  other arithmetic  5.55 us (5%)
  between operations  1.3 us (1%)
    pallas_call x1, Pallas kernels, attention_core(): pl.pallas_call(lambda *refs: attention_kernel(width, *refs), out_shape=ou...  23.7 us
    ppermute x1, starting transfers between devices, on_device(): up_recv = lax.ppermute(top_g, both, up_pairs)  14.3 us
    ppermute x1, waiting for transfers between devices, on_device(): lax.ppermute(side_send(right_g, edge + corner), 'lon', right_pairs)  7.77 us
    ppermute x1, starting transfers between devices, on_device(): lax.ppermute(pair(cols(keys, 0, r), cols(values, 0, r)), 'lon', left_pairs)  7.48 us
    ppermute x1, starting transfers between devices, on_device(): from_below = lax.ppermute(top_send, both, up_pairs)  7.09 us
    unnamed x30, local copies, waits for them, and re-layouts  5.09 us
    ppermute x1, starting transfers between devices, on_device(): from_above = lax.ppermute(bottom_send, both, down_pairs)  4.81 us
    ppermute x1, starting transfers between devices, on_device(): back_right = lax.ppermute(side_send(left_g, edge), 'lon', left_pairs)  2.74 us
  transfers between devices with their start and end apart: 12, of which 4 were waited for; matrix products, arithmetic and copies ran while one was open for 10% of the time, Pallas kernels for 0%

profile of v6, /device:TPU:1, one launch (start us, length us, event | category | flops | bytes accessed | tf_op | source)
XLA Modules:
  0.0 101.0 jit_solution(18438055298745078909)
XLA Ops:
  0.6 1.2 %fusion.15 = (bf16[16,4,1024]{2,1,0:T(4,128)(2,1)S(1)}, bf16[16,4,1024]{2,1,0:T(4,128)(2,1)S(1)}) fusion(bf16[16,16,1024]{2,1,0:T(8,128)(2,1)} %param.21), kind=kLoop, calls=%fused_computation.91 | loop fusion | bytes 524288 | tf_op jit(solution)/shard_map/slice | solution.py:221
  2.1 7.5 %collective-permute-start.2 = (bf16[2,64,1024]{2,1,0:T(8,128)(2,1)S(1)}, bf16[2,64,1024]{2,1,0:T(8,128)(2,1)S(1)}, u32[]{:S(2)}, u32[]{:S(2)}) collective-permute-start(bf16[2,64,1024]{2,1,0:T(8,128)(2,1)S(1)} %pad_maximum_fusion.4), channel_id=1, source_target_pairs={{0,15},{1,0},{2,1},{3,2},{4,3},{5,4},{6,5},{7,6},{8,7},{9,8},{10,9... | collective-permute-start | bytes 786440 | tf_op jit(solution)/shard_map/ppermute | solution.py:224
  9.8 0.8 copy-done.2
  10.7 0.7 collective-permute-start
  11.4 0.7 copy-done.10
  12.1 0.7 gather_fusion
  12.9 0.7 gather_fusion.4
  14.9 1.2 %gather_fusion.5 = s32[96]{0:T(128)S(1)} fusion(s32[24]{0:T(128)S(1)} %scatter_custom_fusion, s32[1024]{0:T(1024)S(1)} %pad_clamp_fusion.5), kind=kCustom, calls=%fused_computation.5.clone | custom fusion | bytes 1152 | tf_op jit(solution)/shard_map/jit(_take)/gather | solution.py:212
  16.2 1.2 %gather_fusion.1 = s32[96]{0:T(128)S(1)} fusion(s32[24]{0:T(128)S(1)} %get-tuple-element.62, s32[1024]{0:T(1024)S(1)} %pad_clamp_fusion.5), kind=kCustom, calls=%fused_computation.1.clone | custom fusion | bytes 1152 | tf_op jit(solution)/shard_map/jit(_take)/gather | solution.py:211
  17.7 1.1 %collective-permute-done.1.refs_6_ = bf16[2,64,1024]{2,1,0:T(8,128)(2,1)S(1)} collective-permute-done((bf16[2,64,1024]{2,1,0:T(8,128)(2,1)S(1)}, bf16[2,64,1024]{2,1,0:T(8,128)(2,1)S(1)}, u32[]{:S(2)}, u32[]{:S(2)}) %collective-permute-start.1) | collective-permute-done | bytes 262176 | tf_op jit(solution)/shard_map/ppermute | solution.py:223
  19.5 0.7 collective-permute-start.3
  20.2 4.8 %collective-permute-start.4 = (bf16[2,96,1024]{2,1,0:T(8,128)(2,1)S(1)}, bf16[2,96,1024]{2,1,0:T(8,128)(2,1)S(1)}, u32[]{:S(2)}, u32[]{:S(2)}) collective-permute-start(bf16[2,96,1024]{2,1,0:T(8,128)(2,1)S(1)} %pad_maximum_fusion.1), channel_id=1, source_target_pairs={{0,16},{1,17},{2,18},{3,19},{4,20},{5,21},{6,22},{7,23},{8,24},{9,... | collective-permute-start | bytes 1179656 | tf_op jit(solution)/shard_map/ppermute | solution.py:233
  25.0 7.1 %collective-permute-start.5 = (bf16[2,96,1024]{2,1,0:T(8,128)(2,1)S(1)}, bf16[2,96,1024]{2,1,0:T(8,128)(2,1)S(1)}, u32[]{:S(2)}, u32[]{:S(2)}) collective-permute-start(bf16[2,96,1024]{2,1,0:T(8,128)(2,1)S(1)} %pad_maximum_fusion.2), channel_id=1, source_target_pairs={{16,0},{17,1},{18,2},{19,3},{20,4},{21,5},{22,6},{23,7},{24,8},{25... | collective-permute-start | bytes 1179656 | tf_op jit(solution)/shard_map/ppermute | solution.py:234
  32.4 1.1 %gather_fusion.2 = bf16[64,2,1024]{2,1,0:T(2,128)(2,1)S(1)} fusion(bf16[2,64,1024]{2,0,1:T(2,128)(2,1)S(1)} %copy.15, s32[1024]{0:T(1024)S(1)} %pad_clamp_fusion.4), kind=kCustom, calls=%fused_computation.2.clone | custom fusion | bytes 524544 | tf_op jit(solution)/shard_map/jit(_take)/gather | solution.py:239
  33.8 0.8 gather_fusion.3
  34.7 1.1 %broadcast_select_fusion = (bf16[2,96,1024]{2,1,0:T(8,128)(2,1)}, bf16[2,96,1024]{2,1,0:T(8,128)(2,1)}) fusion(bf16[2,96,1024]{2,1,0:T(8,128)(2,1)S(1)} %collective-permute-done.5, pred[]{:T(512)S(6)} %eq.14, bf16[2,32,1024]{2,1,0:T(8,128)(2,1)S(1)} %fusion.4, bf16[2,64,1024]{2,1,0:T(8,128)(2,1)S(1)} %fusion.2, ...), kind=kLoop, calls=%fused_computation.22 | loop fusion | flops 1179648 | bytes 1966082 | tf_op jit(solution)/shard_map/jit(_where)/select_n | solution.py:243
  35.8 23.7 %neighbourhood_attention_bwd.1 = (bf16[256,1024]{1,0:T(8,128)(2,1)}, f32[256,1024]{1,0:T(8,128)}, f32[256,1024]{1,0:T(8,128)}, bf16[2,96,1024]{2,1,0:T(8,128)(2,...) custom-call(bf16[256,1024]{1,0:T(8,128)(2,1)} %bitcast.44, ...), custom_call_target="tpu_custom_call" | custom-call | flops 1509949440 | bytes 7864320 | tf_op jit(solution)/shard_map/neighbourhood_attention_bwd/pallas_call | solution.py:148
  59.5 1.0 %broadcast_select_fusion.1 = bf16[2,96,1024]{2,1,0:T(8,128)(2,1)S(1)} fusion(bf16[2,96,1024]{2,1,0:T(8,128)(2,1)} %get-tuple-element.16, bf16[2,96,1024]{2,1,0:T(8,128)(2,1)} %get-tuple-element.17, pred[]{:T(512)S(6)} %eq.13), kind=kLoop, calls=%fused_computation.23 | loop fusion | flops 196608 | bytes 1179649 | tf_op jit(solution)/shard_map/jit(_where)/select_n | solution.py:259
  60.6 0.8 collective-permute-start.6
  61.5 0.7 collective-permute-start.8
  62.2 14.3 %collective-permute-start.9 = (bf16[2,96,1024]{2,1,0:T(8,128)(2,1)S(1)}, bf16[2,96,1024]{2,1,0:T(8,128)(2,1)S(1)}, u32[]{:S(2)}, u32[]{:S(2)}) collective-permute-start(bf16[2,96,1024]{2,1,0:T(8,128)(2,1)S(1)} %copy-done.7), channel_id=1, source_target_pairs={{16,0},{17,1},{18,2},{19,3},{20,4},{21,5},{22,6},{23,7},{24,8},{25... | collective-permute-start | bytes 1179656 | tf_op jit(solution)/shard_map/ppermute | solution.py:257
  76.6 1.9 %collective-permute-start.7 = (bf16[2,96,1024]{2,1,0:T(8,128)(2,1)S(1)}, bf16[2,96,1024]{2,1,0:T(8,128)(2,1)S(1)}, u32[]{:S(2)}, u32[]{:S(2)}) collective-permute-start(bf16[2,96,1024]{2,1,0:T(8,128)(2,1)S(1)} %copy-done.6), channel_id=1, source_target_pairs={{0,16},{1,17},{2,18},{3,19},{4,20},{5,21},{6,22},{7,23},{8,24},{9,... | collective-permute-start | bytes 1179656 | tf_op jit(solution)/shard_map/ppermute | solution.py:258
  78.6 0.8 gather_fusion.6
  79.8 1.1 %gather_fusion.7 = bf16[64,2,1024]{2,1,0:T(2,128)(2,1)S(1)} fusion(bf16[2,64,1024]{2,0,1:T(2,128)(2,1)S(1)} %copy.21, s32[1024]{0:T(1024)S(1)} %pad_clamp_fusion), kind=kCustom, calls=%fused_computation.6.clone | custom fusion | bytes 524544 | tf_op jit(solution)/shard_map/jit(_take)/gather | solution.py:282
  81.1 2.0 %collective-permute-done.7 = bf16[2,96,1024]{2,1,0:T(8,128)(2,1)S(1)} collective-permute-done((bf16[2,96,1024]{2,1,0:T(8,128)(2,1)S(1)}, bf16[2,96,1024]{2,1,0:T(8,128)(2,1)S(1)}, u32[]{:S(2)}, u32[]{:S(2)}) %collective-permute-start.7) | collective-permute-done | bytes 393248 | tf_op jit(solution)/shard_map/ppermute | solution.py:258
  83.5 1.0 copy-done.5
  84.6 0.9 copy-done.4
  85.5 2.7 %collective-permute-start.11 = (bf16[2,64,1024]{2,1,0:T(8,128)(2,1)S(1)}, bf16[2,64,1024]{2,1,0:T(8,128)(2,1)S(1)}, u32[]{:S(2)}, u32[]{:S(2)}) collective-permute-start(bf16[2,64,1024]{2,1,0:T(8,128)(2,1)S(1)} %add_convert_fusion.2), channel_id=1, source_target_pairs={{0,15},{1,0},{2,1},{3,2},{4,3},{5,4},{6,5},{7,6},{8,7},{9,8},{10,9... | collective-permute-start | bytes 786440 | tf_op jit(solution)/shard_map/ppermute | solution.py:279
  88.4 7.8 %collective-permute-done.10 = bf16[2,64,1024]{2,1,0:T(8,128)(2,1)S(1)} collective-permute-done((bf16[2,64,1024]{2,1,0:T(8,128)(2,1)S(1)}, bf16[2,64,1024]{2,1,0:T(8,128)(2,1)S(1)}, u32[]{:S(2)}, u32[]{:S(2)}) %collective-permute-start.10) | collective-permute-done | bytes 262176 | tf_op jit(solution)/shard_map/ppermute | solution.py:280
  96.3 2.0 %collective-permute-done.11 = bf16[2,64,1024]{2,1,0:T(8,128)(2,1)S(1)} collective-permute-done((bf16[2,64,1024]{2,1,0:T(8,128)(2,1)S(1)}, bf16[2,64,1024]{2,1,0:T(8,128)(2,1)S(1)}, u32[]{:S(2)}, u32[]{:S(2)}) %collective-permute-start.11) | collective-permute-done | bytes 262176 | tf_op jit(solution)/shard_map/ppermute | solution.py:279
  98.5 1.0 add_convert_fusion
  100.0 1.0 %add_convert_fusion.1 = bf16[16,16,1024]{2,1,0:T(8,128)(2,1)} fusion(f32[4,16,1024]{2,1,0:T(8,128)S(1)} %bitcast.38, f32[16,16,1024]{2,1,0:T(8,128)S(1)} %bitcast.36, f32[4,16,1024]{2,1,0:T(8,128)S(1)} %bitcast.39, bf16[16,4,1024]{2,1,0:T(4,128)(2,1)S(1)} %convert_element_type.61, bf16[16,4,1024]{2,1,0:T(4,128)(2,1)S(1)} %convert_element_type.59), kind=kLoop, calls=%fused_computation.10 | loop fusion | flops 1835008 | bytes 2359296 | tf_op jit(solution)/shard_map/convert_element_type | solution.py:300
  (92 shorter events, 5.4 us)
Async XLA Ops:
  0.6 1.2 %copy-start.3 = (bf16[16,16,1024]{2,1,0:T(8,128)(2,1)S(1)}, bf16[16,16,1024]{2,1,0:T(8,128)(2,1)}, u32[]{:S(2)}) copy-start(bf16[16,16,1024]{2,1,0:T(8,128)(2,1)} %param.22) | copy-start | bytes 1572868
  2.1 15.6 %collective-permute-start.2 = (bf16[2,64,1024]{2,1,0:T(8,128)(2,1)S(1)}, bf16[2,64,1024]{2,1,0:T(8,128)(2,1)S(1)}, u32[]{:S(2)}, u32[]{:S(2)}) collective-permute-start(bf16[2,64,1024]{2,1,0:T(8,128)(2,1)S(1)} %pad_maximum_fusion.4), channel_id=1, source_target_pairs={{0,15},{1,0},{2,1},{3,2},{4,3},{5,4},{6,5},{7,6},{8,7},{9,8},{10,9... | collective-permute-start | bytes 786440 | tf_op jit(solution)/shard_map/ppermute | solution.py:224
  9.6 1.0 %copy-start.2 = (bf16[16,16,1024]{2,1,0:T(8,128)(2,1)S(1)}, bf16[16,16,1024]{2,1,0:T(8,128)(2,1)}, u32[]{:S(2)}) copy-start(bf16[16,16,1024]{2,1,0:T(8,128)(2,1)} %param.21) | copy-start | bytes 1572868
  9.7 9.1 %collective-permute-start.1 = (bf16[2,64,1024]{2,1,0:T(8,128)(2,1)S(1)}, bf16[2,64,1024]{2,1,0:T(8,128)(2,1)S(1)}, u32[]{:S(2)}, u32[]{:S(2)}) collective-permute-start(bf16[2,64,1024]{2,1,0:T(8,128)(2,1)S(1)} %pad_maximum_fusion.3), channel_id=1, source_target_pairs={{0,1},{1,2},{2,3},{3,4},{4,5},{5,6},{6,7},{7,8},{8,9},{9,10},{10,1... | collective-permute-start | bytes 786440 | tf_op jit(solution)/shard_map/ppermute | solution.py:223
  10.7 21.4 %collective-permute-start = (bf16[2,64,1024]{2,1,0:T(8,128)(2,1)S(1)}, bf16[2,64,1024]{2,1,0:T(8,128)(2,1)S(1)}, u32[]{:S(2)}, u32[]{:S(2)}) collective-permute-start(bf16[2,64,1024]{2,1,0:T(8,128)(2,1)S(1)} %maximum_select_fusion), channel_id=1, source_target_pairs={{0,8},{1,9},{2,10},{3,11},{4,12},{5,13},{6,14},{7,15},{8,0},{9,1},... | collective-permute-start | bytes 786440 | tf_op jit(solution)/shard_map/ppermute | solution.py:227
  11.4 0.7 copy-start.10
  13.6 0.7 copy-start.14
  16.1 1.3 %copy-start.11 = (s32[96]{0:T(128)S(1)}, s32[96]{0:T(128)}, u32[]{:S(2)}) copy-start(s32[96]{0:T(128)} %constant.135.clone) | copy-start | bytes 1156
  16.1 1.3 %copy-start.12 = (s32[96]{0:T(128)S(1)}, s32[96]{0:T(128)}, u32[]{:S(2)}) copy-start(s32[96]{0:T(128)} %constant.134.clone) | copy-start | bytes 1156
  16.1 1.3 %copy-start.13 = (s32[96]{0:T(128)S(1)}, s32[96]{0:T(128)}, u32[]{:S(2)}) copy-start(s32[96]{0:T(128)} %constant.133.clone) | copy-start | bytes 1156
  17.7 1.1 %copy-start.8 = (bf16[2,64,1024]{2,1,0:T(8,128)(2,1)}, bf16[2,64,1024]{2,1,0:T(8,128)(2,1)S(1)}, u32[]{:S(2)}) copy-start(bf16[2,64,1024]{2,1,0:T(8,128)(2,1)S(1)} %collective-permute-done.2.refs_7_) | copy-start | bytes 786436
  18.8 0.7 copy-start.9
  19.5 14.1 %collective-permute-start.3 = (bf16[2,32,1024]{2,1,0:T(8,128)(2,1)S(1)}, bf16[2,32,1024]{2,1,0:T(8,128)(2,1)S(1)}, u32[]{:S(2)}, u32[]{:S(2)}) collective-permute-start(bf16[2,32,1024]{2,1,0:T(8,128)(2,1)S(1)} %maximum_select_fusion.1), channel_id=1, source_target_pairs={{0,8},{1,9},{2,10},{3,11},{4,12},{5,13},{6,14},{7,15},{8,0},{9,1},... | collective-permute-start | bytes 393224 | tf_op jit(solution)/shard_map/ppermute | solution.py:235
  20.2 14.5 %collective-permute-start.4 = (bf16[2,96,1024]{2,1,0:T(8,128)(2,1)S(1)}, bf16[2,96,1024]{2,1,0:T(8,128)(2,1)S(1)}, u32[]{:S(2)}, u32[]{:S(2)}) collective-permute-start(bf16[2,96,1024]{2,1,0:T(8,128)(2,1)S(1)} %pad_maximum_fusion.1), channel_id=1, source_target_pairs={{0,16},{1,17},{2,18},{3,19},{4,20},{5,21},{6,22},{7,23},{8,24},{9,... | collective-permute-start | bytes 1179656 | tf_op jit(solution)/shard_map/ppermute | solution.py:233
  25.0 9.7 %collective-permute-start.5 = (bf16[2,96,1024]{2,1,0:T(8,128)(2,1)S(1)}, bf16[2,96,1024]{2,1,0:T(8,128)(2,1)S(1)}, u32[]{:S(2)}, u32[]{:S(2)}) collective-permute-start(bf16[2,96,1024]{2,1,0:T(8,128)(2,1)S(1)} %pad_maximum_fusion.2), channel_id=1, source_target_pairs={{16,0},{17,1},{18,2},{19,3},{20,4},{21,5},{22,6},{23,7},{24,8},{25... | collective-permute-start | bytes 1179656 | tf_op jit(solution)/shard_map/ppermute | solution.py:234
  60.6 1.6 %copy-start.7 = (bf16[2,96,1024]{2,1,0:T(8,128)(2,1)S(1)}, bf16[2,96,1024]{2,1,0:T(8,128)(2,1)}, u32[]{:S(2)}) copy-start(bf16[2,96,1024]{2,1,0:T(8,128)(2,1)} %get-tuple-element.16) | copy-start | bytes 1179652
  60.6 15.9 %copy-start.6 = (bf16[2,96,1024]{2,1,0:T(8,128)(2,1)S(1)}, bf16[2,96,1024]{2,1,0:T(8,128)(2,1)}, u32[]{:S(2)}) copy-start(bf16[2,96,1024]{2,1,0:T(8,128)(2,1)} %get-tuple-element.17) | copy-start | bytes 1179652
  60.6 17.9 %collective-permute-start.6 = (bf16[2,32,1024]{2,1,0:T(8,128)(2,1)S(1)}, bf16[2,32,1024]{2,1,0:T(8,128)(2,1)S(1)}, u32[]{:S(2)}, u32[]{:S(2)}) collective-permute-start(bf16[2,32,1024]{2,1,0:T(8,128)(2,1)S(1)} %slice.172), channel_id=1, source_target_pairs={{0,8},{1,9},{2,10},{3,11},{4,12},{5,13},{6,14},{7,15},{8,0},{9,1},... | collective-permute-start | bytes 393224 | tf_op jit(solution)/shard_map/ppermute | solution.py:260
  61.5 18.1 %collective-permute-start.8 = (bf16[2,64,1024]{2,1,0:T(8,128)(2,1)S(1)}, bf16[2,64,1024]{2,1,0:T(8,128)(2,1)S(1)}, u32[]{:S(2)}, u32[]{:S(2)}) collective-permute-start(bf16[2,64,1024]{2,1,0:T(8,128)(2,1)S(1)} %slice.174), channel_id=1, source_target_pairs={{0,8},{1,9},{2,10},{3,11},{4,12},{5,13},{6,14},{7,15},{8,0},{9,1},... | collective-permute-start | bytes 786440 | tf_op jit(solution)/shard_map/ppermute | solution.py:281
  62.2 18.9 %collective-permute-start.9 = (bf16[2,96,1024]{2,1,0:T(8,128)(2,1)S(1)}, bf16[2,96,1024]{2,1,0:T(8,128)(2,1)S(1)}, u32[]{:S(2)}, u32[]{:S(2)}) collective-permute-start(bf16[2,96,1024]{2,1,0:T(8,128)(2,1)S(1)} %copy-done.7), channel_id=1, source_target_pairs={{16,0},{17,1},{18,2},{19,3},{20,4},{21,5},{22,6},{23,7},{24,8},{25... | collective-permute-start | bytes 1179656 | tf_op jit(solution)/shard_map/ppermute | solution.py:257
  76.6 6.6 %collective-permute-start.7 = (bf16[2,96,1024]{2,1,0:T(8,128)(2,1)S(1)}, bf16[2,96,1024]{2,1,0:T(8,128)(2,1)S(1)}, u32[]{:S(2)}, u32[]{:S(2)}) collective-permute-start(bf16[2,96,1024]{2,1,0:T(8,128)(2,1)S(1)} %copy-done.6), channel_id=1, source_target_pairs={{0,16},{1,17},{2,18},{3,19},{4,20},{5,21},{6,22},{7,23},{8,24},{9,... | collective-permute-start | bytes 1179656 | tf_op jit(solution)/shard_map/ppermute | solution.py:258
  83.4 1.0 %copy-start.5 = (f32[2,64,1024]{2,1,0:T(8,128)S(1)}, f32[2,64,1024]{2,1,0:T(8,128)}, u32[]{:S(2)}) copy-start(f32[2,64,1024]{2,1,0:T(8,128)} %get-tuple-element.18) | copy-start | bytes 1572868
  84.4 1.0 %copy-start.4 = (f32[2,64,1024]{2,1,0:T(8,128)S(1)}, f32[2,64,1024]{2,1,0:T(8,128)}, u32[]{:S(2)}) copy-start(f32[2,64,1024]{2,1,0:T(8,128)} %get-tuple-element.19) | copy-start | bytes 1572868
  84.5 11.7 %collective-permute-start.10 = (bf16[2,64,1024]{2,1,0:T(8,128)(2,1)S(1)}, bf16[2,64,1024]{2,1,0:T(8,128)(2,1)S(1)}, u32[]{:S(2)}, u32[]{:S(2)}) collective-permute-start(bf16[2,64,1024]{2,1,0:T(8,128)(2,1)S(1)} %add_convert_fusion.3), channel_id=1, source_target_pairs={{0,1},{1,2},{2,3},{3,4},{4,5},{5,6},{6,7},{7,8},{8,9},{9,10},{10,1... | collective-permute-start | bytes 786440 | tf_op jit(solution)/shard_map/ppermute | solution.py:280
  85.5 12.9 %collective-permute-start.11 = (bf16[2,64,1024]{2,1,0:T(8,128)(2,1)S(1)}, bf16[2,64,1024]{2,1,0:T(8,128)(2,1)S(1)}, u32[]{:S(2)}, u32[]{:S(2)}) collective-permute-start(bf16[2,64,1024]{2,1,0:T(8,128)(2,1)S(1)} %add_convert_fusion.2), channel_id=1, source_target_pairs={{0,15},{1,0},{2,1},{3,2},{4,3},{5,4},{6,5},{7,6},{8,7},{9,8},{10,9... | collective-permute-start | bytes 786440 | tf_op jit(solution)/shard_map/ppermute | solution.py:279
  88.4 10.1 %copy-start.1 = (f32[256,1024]{1,0:T(8,128)S(1)}, f32[256,1024]{1,0:T(8,128)}, u32[]{:S(2)}) copy-start(f32[256,1024]{1,0:T(8,128)} %get-tuple-element.20) | copy-start | bytes 3145732
  98.5 1.4 %copy-start = (f32[256,1024]{1,0:T(8,128)S(1)}, f32[256,1024]{1,0:T(8,128)}, u32[]{:S(2)}) copy-start(f32[256,1024]{1,0:T(8,128)} %get-tuple-element.15) | copy-start | bytes 3145732

commit v7 on v5

--- a/solution.py
+++ b/solution.py
@@ -29,8 +29,9 @@
     corner = r * r
     pairs = q_ref.shape[1] // LANES
 
-    qi = lax.broadcasted_iota(jnp.int32, (tq, tk), 0).astype(jnp.float32)
-    ki = lax.broadcasted_iota(jnp.int32, (tq, tk), 1).astype(jnp.float32)
+    qi = lax.broadcasted_iota(jnp.int32, (2 * tq, tk), 0).astype(jnp.float32)
+    ki = lax.broadcasted_iota(jnp.int32, (2 * tq, tk), 1).astype(jnp.float32)
+    qi = jnp.where(qi >= tq, qi - tq, qi)
     qr = jnp.floor((qi + 0.5) * (1.0 / width))
     qc = qi - width * qr
     in_main = ki < main
@@ -47,13 +48,13 @@
     nt = (((1,), (1,)), ((), ()))
     tn = (((0,), (0,)), ((), ()))
 
-    def head(qh, gh, kp, vp):
-        s = lax.dot_general(qh, kp, nt, preferred_element_type=jnp.float32) * scale + bias_ref[...]
+    def both_heads(qab, gab, kp, vp):
+        s = lax.dot_general(qab, kp, nt, preferred_element_type=jnp.float32) * scale + bias_ref[...]
         m = jnp.max(s, axis=1, keepdims=True)
         e = jnp.exp(s - m)
         total = jnp.sum(e, axis=1, keepdims=True)
         w = e * (1.0 / total)
-        dw = lax.dot_general(gh, vp, nt, preferred_element_type=jnp.float32)
+        dw = lax.dot_general(gab, vp, nt, preferred_element_type=jnp.float32)
         corr = jnp.sum(w * dw, axis=1, keepdims=True)
         ds = (w * (dw - corr)).astype(jnp.bfloat16)
         return ds, w.astype(jnp.bfloat16)
@@ -115,23 +116,14 @@
             vp = gather_keys(v_own, 1, t, lanes)
             lo = lax.broadcasted_iota(jnp.int32, qp.shape, 1) < HEAD_DIM
             zero = jnp.zeros_like(qp)
-            qa = jnp.where(lo, qp, zero)
-            qb = jnp.where(lo, zero, qp)
-            ga = jnp.where(lo, gp, zero)
-            gb = jnp.where(lo, zero, gp)
-            dsa, wa = head(qa, ga, kp, vp)
-            dsb, wb = head(qb, gb, kp, vp)
-            dqa = jnp.dot(dsa, kp, preferred_element_type=jnp.float32)
-            dqb = jnp.dot(dsb, kp, preferred_element_type=jnp.float32)
-            dq = jnp.where(lo, dqa, dqb) * scale
+            qab = jnp.concatenate([jnp.where(lo, qp, zero), jnp.where(lo, zero, qp)], axis=0)
+            gab = jnp.concatenate([jnp.where(lo, gp, zero), jnp.where(lo, zero, gp)], axis=0)
+            ds, w = both_heads(qab, gab, kp, vp)
+            dq_ab = jnp.dot(ds, kp, preferred_element_type=jnp.float32)
+            dq = jnp.where(lo, dq_ab[:tq], dq_ab[tq:]) * scale
             dq_ref[pl.ds(t * tq, tq), lanes] = dq.astype(dq_ref.dtype)
-            dk = (
-                lax.dot_general(dsa, qa, tn, preferred_element_type=jnp.float32)
-                + lax.dot_general(dsb, qb, tn, preferred_element_type=jnp.float32)
-            ) * scale
-            dv = lax.dot_general(wa, ga, tn, preferred_element_type=jnp.float32) + lax.dot_general(
-                wb, gb, tn, preferred_element_type=jnp.float32
-            )
+            dk = lax.dot_general(ds, qab, tn, preferred_element_type=jnp.float32) * scale
+            dv = lax.dot_general(w, gab, tn, preferred_element_type=jnp.float32)
             scatter_grads(dk, dk_own, 0, t, lanes)
             scatter_grads(dv, dv_own, 1, t, lanes)
         return carry
@@ -167,7 +159,7 @@
         out_shape=outs,
         in_specs=[vmem] * 8,
         out_specs=tuple([vmem] * 7),
-        scratch_shapes=[pltpu.VMEM((tq, tk), jnp.float32)],
+        scratch_shapes=[pltpu.VMEM((2 * tq, tk), jnp.float32)],
         cost_estimate=pl.CostEstimate(
             flops=flops,
             transcendentals=2 * tq * tk * HEADS * tiles,

time: 94.7 us -> 94.2 us (level)
  no operation moved by 1% of the time
where the time goes in v7:
time: 94.2 us; the launch traced here: 93.7 us
  starting transfers between devices  41.4 us (44%)
  Pallas kernels  16.4 us (17%)
  local copies, waits for them, and re-layouts  16.1 us (17%)
  waiting for transfers between devices  13 us (14%)
  other arithmetic  5.55 us (6%)
  between operations  1.3 us (1%)
    pallas_call x1, Pallas kernels, attention_core(): pl.pallas_call(lambda *refs: attention_kernel(width, *refs), out_shape=ou...  16.4 us
    ppermute x1, starting transfers between devices, on_device(): up_recv = lax.ppermute(top_g, both, up_pairs)  14.4 us
    ppermute x1, waiting for transfers between devices, on_device(): lax.ppermute(side_send(right_g, edge + corner), 'lon', right_pairs)  7.76 us
    ppermute x1, starting transfers between devices, on_device(): lax.ppermute(pair(cols(keys, 0, r), cols(values, 0, r)), 'lon', left_pairs)  7.48 us
    ppermute x1, starting transfers between devices, on_device(): from_below = lax.ppermute(top_send, both, up_pairs)  7.09 us
    unnamed x30, local copies, waits for them, and re-layouts  5.09 us
    ppermute x1, starting transfers between devices, on_device(): from_above = lax.ppermute(bottom_send, both, down_pairs)  4.81 us
    ppermute x1, starting transfers between devices, on_device(): back_right = lax.ppermute(side_send(left_g, edge), 'lon', left_pairs)  2.74 us
  transfers between devices with their start and end apart: 12, of which 4 were waited for; matrix products, arithmetic and copies ran while one was open for 11% of the time, Pallas kernels for 0%

profile of v7, /device:TPU:1, one launch (start us, length us, event | category | flops | bytes accessed | tf_op | source)
XLA Modules:
  0.0 93.7 jit_solution(6417788101367259940)
XLA Ops:
  0.6 1.2 %fusion.15 = (bf16[16,4,1024]{2,1,0:T(4,128)(2,1)S(1)}, bf16[16,4,1024]{2,1,0:T(4,128)(2,1)S(1)}) fusion(bf16[16,16,1024]{2,1,0:T(8,128)(2,1)} %param.21), kind=kLoop, calls=%fused_computation.91 | loop fusion | bytes 524288 | tf_op jit(solution)/shard_map/slice | solution.py:230
  2.1 7.5 %collective-permute-start.2 = (bf16[2,64,1024]{2,1,0:T(8,128)(2,1)S(1)}, bf16[2,64,1024]{2,1,0:T(8,128)(2,1)S(1)}, u32[]{:S(2)}, u32[]{:S(2)}) collective-permute-start(bf16[2,64,1024]{2,1,0:T(8,128)(2,1)S(1)} %pad_maximum_fusion.4), channel_id=1, source_target_pairs={{0,15},{1,0},{2,1},{3,2},{4,3},{5,4},{6,5},{7,6},{8,7},{9,8},{10,9... | collective-permute-start | bytes 786440 | tf_op jit(solution)/shard_map/ppermute | solution.py:233
  9.8 0.8 copy-done.2
  10.7 0.7 collective-permute-start
  11.4 0.7 copy-done.10
  12.1 0.7 gather_fusion
  12.9 0.7 gather_fusion.4
  14.9 1.2 %gather_fusion.5 = s32[96]{0:T(128)S(1)} fusion(s32[24]{0:T(128)S(1)} %scatter_custom_fusion, s32[1024]{0:T(1024)S(1)} %pad_clamp_fusion.5), kind=kCustom, calls=%fused_computation.5.clone | custom fusion | bytes 1152 | tf_op jit(solution)/shard_map/jit(_take)/gather | solution.py:221
  16.2 1.2 %gather_fusion.1 = s32[96]{0:T(128)S(1)} fusion(s32[24]{0:T(128)S(1)} %get-tuple-element.62, s32[1024]{0:T(1024)S(1)} %pad_clamp_fusion.5), kind=kCustom, calls=%fused_computation.1.clone | custom fusion | bytes 1152 | tf_op jit(solution)/shard_map/jit(_take)/gather | solution.py:220
  17.7 1.1 %collective-permute-done.1.refs_6_ = bf16[2,64,1024]{2,1,0:T(8,128)(2,1)S(1)} collective-permute-done((bf16[2,64,1024]{2,1,0:T(8,128)(2,1)S(1)}, bf16[2,64,1024]{2,1,0:T(8,128)(2,1)S(1)}, u32[]{:S(2)}, u32[]{:S(2)}) %collective-permute-start.1) | collective-permute-done | bytes 262176 | tf_op jit(solution)/shard_map/ppermute | solution.py:232
  19.5 0.7 collective-permute-start.3
  20.2 4.8 %collective-permute-start.4 = (bf16[2,96,1024]{2,1,0:T(8,128)(2,1)S(1)}, bf16[2,96,1024]{2,1,0:T(8,128)(2,1)S(1)}, u32[]{:S(2)}, u32[]{:S(2)}) collective-permute-start(bf16[2,96,1024]{2,1,0:T(8,128)(2,1)S(1)} %pad_maximum_fusion.1), channel_id=1, source_target_pairs={{0,16},{1,17},{2,18},{3,19},{4,20},{5,21},{6,22},{7,23},{8,24},{9,... | collective-permute-start | bytes 1179656 | tf_op jit(solution)/shard_map/ppermute | solution.py:242
  25.0 7.1 %collective-permute-start.5 = (bf16[2,96,1024]{2,1,0:T(8,128)(2,1)S(1)}, bf16[2,96,1024]{2,1,0:T(8,128)(2,1)S(1)}, u32[]{:S(2)}, u32[]{:S(2)}) collective-permute-start(bf16[2,96,1024]{2,1,0:T(8,128)(2,1)S(1)} %pad_maximum_fusion.2), channel_id=1, source_target_pairs={{16,0},{17,1},{18,2},{19,3},{20,4},{21,5},{22,6},{23,7},{24,8},{25... | collective-permute-start | bytes 1179656 | tf_op jit(solution)/shard_map/ppermute | solution.py:243
  32.4 1.1 %gather_fusion.2 = bf16[64,2,1024]{2,1,0:T(2,128)(2,1)S(1)} fusion(bf16[2,64,1024]{2,0,1:T(2,128)(2,1)S(1)} %copy.15, s32[1024]{0:T(1024)S(1)} %pad_clamp_fusion.4), kind=kCustom, calls=%fused_computation.2.clone | custom fusion | bytes 524544 | tf_op jit(solution)/shard_map/jit(_take)/gather | solution.py:248
  33.8 0.8 gather_fusion.3
  34.7 1.1 %broadcast_select_fusion = (bf16[2,96,1024]{2,1,0:T(8,128)(2,1)}, bf16[2,96,1024]{2,1,0:T(8,128)(2,1)}) fusion(bf16[2,96,1024]{2,1,0:T(8,128)(2,1)S(1)} %collective-permute-done.5, pred[]{:T(512)S(6)} %eq.14, bf16[2,32,1024]{2,1,0:T(8,128)(2,1)S(1)} %fusion.4, bf16[2,64,1024]{2,1,0:T(8,128)(2,1)S(1)} %fusion.2, ...), kind=kLoop, calls=%fused_computation.22 | loop fusion | flops 1179648 | bytes 1966082 | tf_op jit(solution)/shard_map/jit(_where)/select_n | solution.py:252
  35.8 16.4 %neighbourhood_attention_bwd.1 = (bf16[256,1024]{1,0:T(8,128)(2,1)}, f32[256,1024]{1,0:T(8,128)}, f32[256,1024]{1,0:T(8,128)}, bf16[2,96,1024]{2,1,0:T(8,128)(2,...) custom-call(bf16[256,1024]{1,0:T(8,128)(2,1)} %bitcast.44, ...), custom_call_target="tpu_custom_call" | custom-call | flops 2013265920 | bytes 7864320 | tf_op jit(solution)/shard_map/neighbourhood_attention_bwd/pallas_call | solution.py:157
  52.2 1.0 %broadcast_select_fusion.1 = bf16[2,96,1024]{2,1,0:T(8,128)(2,1)S(1)} fusion(bf16[2,96,1024]{2,1,0:T(8,128)(2,1)} %get-tuple-element.16, bf16[2,96,1024]{2,1,0:T(8,128)(2,1)} %get-tuple-element.17, pred[]{:T(512)S(6)} %eq.13), kind=kLoop, calls=%fused_computation.23 | loop fusion | flops 196608 | bytes 1179649 | tf_op jit(solution)/shard_map/jit(_where)/select_n | solution.py:268
  53.3 0.8 collective-permute-start.6
  54.1 0.7 collective-permute-start.8
  54.9 14.4 %collective-permute-start.9 = (bf16[2,96,1024]{2,1,0:T(8,128)(2,1)S(1)}, bf16[2,96,1024]{2,1,0:T(8,128)(2,1)S(1)}, u32[]{:S(2)}, u32[]{:S(2)}) collective-permute-start(bf16[2,96,1024]{2,1,0:T(8,128)(2,1)S(1)} %copy-done.7), channel_id=1, source_target_pairs={{16,0},{17,1},{18,2},{19,3},{20,4},{21,5},{22,6},{23,7},{24,8},{25... | collective-permute-start | bytes 1179656 | tf_op jit(solution)/shard_map/ppermute | solution.py:266
  69.2 1.9 %collective-permute-start.7 = (bf16[2,96,1024]{2,1,0:T(8,128)(2,1)S(1)}, bf16[2,96,1024]{2,1,0:T(8,128)(2,1)S(1)}, u32[]{:S(2)}, u32[]{:S(2)}) collective-permute-start(bf16[2,96,1024]{2,1,0:T(8,128)(2,1)S(1)} %copy-done.6), channel_id=1, source_target_pairs={{0,16},{1,17},{2,18},{3,19},{4,20},{5,21},{6,22},{7,23},{8,24},{9,... | collective-permute-start | bytes 1179656 | tf_op jit(solution)/shard_map/ppermute | solution.py:267
  71.3 0.8 gather_fusion.6
  72.5 1.1 %gather_fusion.7 = bf16[64,2,1024]{2,1,0:T(2,128)(2,1)S(1)} fusion(bf16[2,64,1024]{2,0,1:T(2,128)(2,1)S(1)} %copy.21, s32[1024]{0:T(1024)S(1)} %pad_clamp_fusion), kind=kCustom, calls=%fused_computation.6.clone | custom fusion | bytes 524544 | tf_op jit(solution)/shard_map/jit(_take)/gather | solution.py:291
  73.8 2.0 %collective-permute-done.7 = bf16[2,96,1024]{2,1,0:T(8,128)(2,1)S(1)} collective-permute-done((bf16[2,96,1024]{2,1,0:T(8,128)(2,1)S(1)}, bf16[2,96,1024]{2,1,0:T(8,128)(2,1)S(1)}, u32[]{:S(2)}, u32[]{:S(2)}) %collective-permute-start.7) | collective-permute-done | bytes 393248 | tf_op jit(solution)/shard_map/ppermute | solution.py:267
  76.1 1.0 %copy-done.5 = f32[2,64,1024]{2,1,0:T(8,128)S(1)} copy-done((f32[2,64,1024]{2,1,0:T(8,128)S(1)}, f32[2,64,1024]{2,1,0:T(8,128)}, u32[]{:S(2)}) %copy-start.5) | copy-done | bytes 524312
  77.3 0.9 copy-done.4
  78.2 2.7 %collective-permute-start.11 = (bf16[2,64,1024]{2,1,0:T(8,128)(2,1)S(1)}, bf16[2,64,1024]{2,1,0:T(8,128)(2,1)S(1)}, u32[]{:S(2)}, u32[]{:S(2)}) collective-permute-start(bf16[2,64,1024]{2,1,0:T(8,128)(2,1)S(1)} %add_convert_fusion.2), channel_id=1, source_target_pairs={{0,15},{1,0},{2,1},{3,2},{4,3},{5,4},{6,5},{7,6},{8,7},{9,8},{10,9... | collective-permute-start | bytes 786440 | tf_op jit(solution)/shard_map/ppermute | solution.py:288
  81.1 7.8 %collective-permute-done.10 = bf16[2,64,1024]{2,1,0:T(8,128)(2,1)S(1)} collective-permute-done((bf16[2,64,1024]{2,1,0:T(8,128)(2,1)S(1)}, bf16[2,64,1024]{2,1,0:T(8,128)(2,1)S(1)}, u32[]{:S(2)}, u32[]{:S(2)}) %collective-permute-start.10) | collective-permute-done | bytes 262176 | tf_op jit(solution)/shard_map/ppermute | solution.py:289
  89.0 2.1 %collective-permute-done.11 = bf16[2,64,1024]{2,1,0:T(8,128)(2,1)S(1)} collective-permute-done((bf16[2,64,1024]{2,1,0:T(8,128)(2,1)S(1)}, bf16[2,64,1024]{2,1,0:T(8,128)(2,1)S(1)}, u32[]{:S(2)}, u32[]{:S(2)}) %collective-permute-start.11) | collective-permute-done | bytes 262176 | tf_op jit(solution)/shard_map/ppermute | solution.py:288
  91.2 1.0 %add_convert_fusion = bf16[16,16,1024]{2,1,0:T(8,128)(2,1)} fusion(f32[4,16,1024]{2,1,0:T(8,128)S(1)} %bitcast.40, f32[16,16,1024]{2,1,0:T(8,128)S(1)} %bitcast.37, f32[4,16,1024]{2,1,0:T(8,128)S(1)} %bitcast.41, bf16[16,4,1024]{2,1,0:T(4,128)(2,1)S(1)} %convert_element_type.64, bf16[16,4,1024]{2,1,0:T(4,128)(2,1)S(1)} %convert_element_type.63), kind=kLoop, calls=%fused_computation.9 | loop fusion | flops 1835008 | bytes 2359296 | tf_op jit(solution)/shard_map/convert_element_type | solution.py:309
  92.6 1.0 %add_convert_fusion.1 = bf16[16,16,1024]{2,1,0:T(8,128)(2,1)} fusion(f32[4,16,1024]{2,1,0:T(8,128)S(1)} %bitcast.38, f32[16,16,1024]{2,1,0:T(8,128)S(1)} %bitcast.36, f32[4,16,1024]{2,1,0:T(8,128)S(1)} %bitcast.39, bf16[16,4,1024]{2,1,0:T(4,128)(2,1)S(1)} %convert_element_type.61, bf16[16,4,1024]{2,1,0:T(4,128)(2,1)S(1)} %convert_element_type.59), kind=kLoop, calls=%fused_computation.10 | loop fusion | flops 1835008 | bytes 2359296 | tf_op jit(solution)/shard_map/convert_element_type | solution.py:309
  (92 shorter events, 5.4 us)
Async XLA Ops:
  0.6 1.2 %copy-start.3 = (bf16[16,16,1024]{2,1,0:T(8,128)(2,1)S(1)}, bf16[16,16,1024]{2,1,0:T(8,128)(2,1)}, u32[]{:S(2)}) copy-start(bf16[16,16,1024]{2,1,0:T(8,128)(2,1)} %param.22) | copy-start | bytes 1572868
  2.1 15.6 %collective-permute-start.2 = (bf16[2,64,1024]{2,1,0:T(8,128)(2,1)S(1)}, bf16[2,64,1024]{2,1,0:T(8,128)(2,1)S(1)}, u32[]{:S(2)}, u32[]{:S(2)}) collective-permute-start(bf16[2,64,1024]{2,1,0:T(8,128)(2,1)S(1)} %pad_maximum_fusion.4), channel_id=1, source_target_pairs={{0,15},{1,0},{2,1},{3,2},{4,3},{5,4},{6,5},{7,6},{8,7},{9,8},{10,9... | collective-permute-start | bytes 786440 | tf_op jit(solution)/shard_map/ppermute | solution.py:233
  9.6 1.0 %copy-start.2 = (bf16[16,16,1024]{2,1,0:T(8,128)(2,1)S(1)}, bf16[16,16,1024]{2,1,0:T(8,128)(2,1)}, u32[]{:S(2)}) copy-start(bf16[16,16,1024]{2,1,0:T(8,128)(2,1)} %param.21) | copy-start | bytes 1572868
  9.7 9.1 %collective-permute-start.1 = (bf16[2,64,1024]{2,1,0:T(8,128)(2,1)S(1)}, bf16[2,64,1024]{2,1,0:T(8,128)(2,1)S(1)}, u32[]{:S(2)}, u32[]{:S(2)}) collective-permute-start(bf16[2,64,1024]{2,1,0:T(8,128)(2,1)S(1)} %pad_maximum_fusion.3), channel_id=1, source_target_pairs={{0,1},{1,2},{2,3},{3,4},{4,5},{5,6},{6,7},{7,8},{8,9},{9,10},{10,1... | collective-permute-start | bytes 786440 | tf_op jit(solution)/shard_map/ppermute | solution.py:232
  10.7 21.4 %collective-permute-start = (bf16[2,64,1024]{2,1,0:T(8,128)(2,1)S(1)}, bf16[2,64,1024]{2,1,0:T(8,128)(2,1)S(1)}, u32[]{:S(2)}, u32[]{:S(2)}) collective-permute-start(bf16[2,64,1024]{2,1,0:T(8,128)(2,1)S(1)} %maximum_select_fusion), channel_id=1, source_target_pairs={{0,8},{1,9},{2,10},{3,11},{4,12},{5,13},{6,14},{7,15},{8,0},{9,1},... | collective-permute-start | bytes 786440 | tf_op jit(solution)/shard_map/ppermute | solution.py:236
  11.4 0.7 copy-start.10
  13.6 0.7 copy-start.14
  16.1 1.3 %copy-start.11 = (s32[96]{0:T(128)S(1)}, s32[96]{0:T(128)}, u32[]{:S(2)}) copy-start(s32[96]{0:T(128)} %constant.135.clone) | copy-start | bytes 1156
  16.1 1.3 %copy-start.12 = (s32[96]{0:T(128)S(1)}, s32[96]{0:T(128)}, u32[]{:S(2)}) copy-start(s32[96]{0:T(128)} %constant.134.clone) | copy-start | bytes 1156
  16.1 1.3 %copy-start.13 = (s32[96]{0:T(128)S(1)}, s32[96]{0:T(128)}, u32[]{:S(2)}) copy-start(s32[96]{0:T(128)} %constant.133.clone) | copy-start | bytes 1156
  17.7 1.1 %copy-start.8 = (bf16[2,64,1024]{2,1,0:T(8,128)(2,1)}, bf16[2,64,1024]{2,1,0:T(8,128)(2,1)S(1)}, u32[]{:S(2)}) copy-start(bf16[2,64,1024]{2,1,0:T(8,128)(2,1)S(1)} %collective-permute-done.2.refs_7_) | copy-start | bytes 786436
  18.8 0.7 copy-start.9
  19.5 14.1 %collective-permute-start.3 = (bf16[2,32,1024]{2,1,0:T(8,128)(2,1)S(1)}, bf16[2,32,1024]{2,1,0:T(8,128)(2,1)S(1)}, u32[]{:S(2)}, u32[]{:S(2)}) collective-permute-start(bf16[2,32,1024]{2,1,0:T(8,128)(2,1)S(1)} %maximum_select_fusion.1), channel_id=1, source_target_pairs={{0,8},{1,9},{2,10},{3,11},{4,12},{5,13},{6,14},{7,15},{8,0},{9,1},... | collective-permute-start | bytes 393224 | tf_op jit(solution)/shard_map/ppermute | solution.py:244
  20.2 14.5 %collective-permute-start.4 = (bf16[2,96,1024]{2,1,0:T(8,128)(2,1)S(1)}, bf16[2,96,1024]{2,1,0:T(8,128)(2,1)S(1)}, u32[]{:S(2)}, u32[]{:S(2)}) collective-permute-start(bf16[2,96,1024]{2,1,0:T(8,128)(2,1)S(1)} %pad_maximum_fusion.1), channel_id=1, source_target_pairs={{0,16},{1,17},{2,18},{3,19},{4,20},{5,21},{6,22},{7,23},{8,24},{9,... | collective-permute-start | bytes 1179656 | tf_op jit(solution)/shard_map/ppermute | solution.py:242
  25.0 9.7 %collective-permute-start.5 = (bf16[2,96,1024]{2,1,0:T(8,128)(2,1)S(1)}, bf16[2,96,1024]{2,1,0:T(8,128)(2,1)S(1)}, u32[]{:S(2)}, u32[]{:S(2)}) collective-permute-start(bf16[2,96,1024]{2,1,0:T(8,128)(2,1)S(1)} %pad_maximum_fusion.2), channel_id=1, source_target_pairs={{16,0},{17,1},{18,2},{19,3},{20,4},{21,5},{22,6},{23,7},{24,8},{25... | collective-permute-start | bytes 1179656 | tf_op jit(solution)/shard_map/ppermute | solution.py:243
  53.3 1.6 %copy-start.7 = (bf16[2,96,1024]{2,1,0:T(8,128)(2,1)S(1)}, bf16[2,96,1024]{2,1,0:T(8,128)(2,1)}, u32[]{:S(2)}) copy-start(bf16[2,96,1024]{2,1,0:T(8,128)(2,1)} %get-tuple-element.16) | copy-start | bytes 1179652
  53.3 15.9 %copy-start.6 = (bf16[2,96,1024]{2,1,0:T(8,128)(2,1)S(1)}, bf16[2,96,1024]{2,1,0:T(8,128)(2,1)}, u32[]{:S(2)}) copy-start(bf16[2,96,1024]{2,1,0:T(8,128)(2,1)} %get-tuple-element.17) | copy-start | bytes 1179652
  53.3 17.9 %collective-permute-start.6 = (bf16[2,32,1024]{2,1,0:T(8,128)(2,1)S(1)}, bf16[2,32,1024]{2,1,0:T(8,128)(2,1)S(1)}, u32[]{:S(2)}, u32[]{:S(2)}) collective-permute-start(bf16[2,32,1024]{2,1,0:T(8,128)(2,1)S(1)} %slice.172), channel_id=1, source_target_pairs={{0,8},{1,9},{2,10},{3,11},{4,12},{5,13},{6,14},{7,15},{8,0},{9,1},... | collective-permute-start | bytes 393224 | tf_op jit(solution)/shard_map/ppermute | solution.py:269
  54.1 18.1 %collective-permute-start.8 = (bf16[2,64,1024]{2,1,0:T(8,128)(2,1)S(1)}, bf16[2,64,1024]{2,1,0:T(8,128)(2,1)S(1)}, u32[]{:S(2)}, u32[]{:S(2)}) collective-permute-start(bf16[2,64,1024]{2,1,0:T(8,128)(2,1)S(1)} %slice.174), channel_id=1, source_target_pairs={{0,8},{1,9},{2,10},{3,11},{4,12},{5,13},{6,14},{7,15},{8,0},{9,1},... | collective-permute-start | bytes 786440 | tf_op jit(solution)/shard_map/ppermute | solution.py:290
  54.9 18.9 %collective-permute-start.9 = (bf16[2,96,1024]{2,1,0:T(8,128)(2,1)S(1)}, bf16[2,96,1024]{2,1,0:T(8,128)(2,1)S(1)}, u32[]{:S(2)}, u32[]{:S(2)}) collective-permute-start(bf16[2,96,1024]{2,1,0:T(8,128)(2,1)S(1)} %copy-done.7), channel_id=1, source_target_pairs={{16,0},{17,1},{18,2},{19,3},{20,4},{21,5},{22,6},{23,7},{24,8},{25... | collective-permute-start | bytes 1179656 | tf_op jit(solution)/shard_map/ppermute | solution.py:266
  69.2 6.6 %collective-permute-start.7 = (bf16[2,96,1024]{2,1,0:T(8,128)(2,1)S(1)}, bf16[2,96,1024]{2,1,0:T(8,128)(2,1)S(1)}, u32[]{:S(2)}, u32[]{:S(2)}) collective-permute-start(bf16[2,96,1024]{2,1,0:T(8,128)(2,1)S(1)} %copy-done.6), channel_id=1, source_target_pairs={{0,16},{1,17},{2,18},{3,19},{4,20},{5,21},{6,22},{7,23},{8,24},{9,... | collective-permute-start | bytes 1179656 | tf_op jit(solution)/shard_map/ppermute | solution.py:267
  76.1 1.0 %copy-start.5 = (f32[2,64,1024]{2,1,0:T(8,128)S(1)}, f32[2,64,1024]{2,1,0:T(8,128)}, u32[]{:S(2)}) copy-start(f32[2,64,1024]{2,1,0:T(8,128)} %get-tuple-element.18) | copy-start | bytes 1572868
  77.1 1.0 %copy-start.4 = (f32[2,64,1024]{2,1,0:T(8,128)S(1)}, f32[2,64,1024]{2,1,0:T(8,128)}, u32[]{:S(2)}) copy-start(f32[2,64,1024]{2,1,0:T(8,128)} %get-tuple-element.19) | copy-start | bytes 1572868
  77.2 11.7 %collective-permute-start.10 = (bf16[2,64,1024]{2,1,0:T(8,128)(2,1)S(1)}, bf16[2,64,1024]{2,1,0:T(8,128)(2,1)S(1)}, u32[]{:S(2)}, u32[]{:S(2)}) collective-permute-start(bf16[2,64,1024]{2,1,0:T(8,128)(2,1)S(1)} %add_convert_fusion.3), channel_id=1, source_target_pairs={{0,1},{1,2},{2,3},{3,4},{4,5},{5,6},{6,7},{7,8},{8,9},{9,10},{10,1... | collective-permute-start | bytes 786440 | tf_op jit(solution)/shard_map/ppermute | solution.py:289
  78.2 12.9 %collective-permute-start.11 = (bf16[2,64,1024]{2,1,0:T(8,128)(2,1)S(1)}, bf16[2,64,1024]{2,1,0:T(8,128)(2,1)S(1)}, u32[]{:S(2)}, u32[]{:S(2)}) collective-permute-start(bf16[2,64,1024]{2,1,0:T(8,128)(2,1)S(1)} %add_convert_fusion.2), channel_id=1, source_target_pairs={{0,15},{1,0},{2,1},{3,2},{4,3},{5,4},{6,5},{7,6},{8,7},{9,8},{10,9... | collective-permute-start | bytes 786440 | tf_op jit(solution)/shard_map/ppermute | solution.py:288
  81.1 10.1 %copy-start.1 = (f32[256,1024]{1,0:T(8,128)S(1)}, f32[256,1024]{1,0:T(8,128)}, u32[]{:S(2)}) copy-start(f32[256,1024]{1,0:T(8,128)} %get-tuple-element.20) | copy-start | bytes 3145732
  91.2 1.4 %copy-start = (f32[256,1024]{1,0:T(8,128)S(1)}, f32[256,1024]{1,0:T(8,128)}, u32[]{:S(2)}) copy-start(f32[256,1024]{1,0:T(8,128)} %get-tuple-element.15) | copy-start | bytes 3145732

commit v8 on v7

--- a/solution.py
+++ b/solution.py
@@ -16,9 +16,28 @@
 
 
 def attention_kernel(width, *refs):
-    (q_ref, g_ref, k_own, v_own, top_in, bot_in, left_in, right_in) = refs[:8]
-    (dq_ref, dk_own, dv_own, top_out, bot_out, left_out, right_out) = refs[8:15]
-    bias_ref = refs[15]
+    (q_ref, g_ref, k_own, v_own, above_in, below_in, pole_mid_in, pole_corner_in, left_in, right_in, flag_ref) = refs[:11]
+    (dq_ref, dk_own, dv_own, top_out, bot_out, left_out, right_out, pole_mid_out, pole_corner_out) = refs[11:20]
+    bias_ref = refs[20]
+    north = flag_ref[0:1, :] > 0.5
+    south = flag_ref[1:2, :] > 0.5
+
+    class Strip:
+        def __init__(self, neighbour, pole):
+            self.neighbour, self.pole = neighbour, pole
+
+        def __getitem__(self, index):
+            c, cells, lanes = index
+            if cells.start >= edge:
+                pole = self.pole_corner_ref[c, pl.ds(cells.start - edge, cells.size), lanes]
+            else:
+                pole = pole_mid_in[c, cells, lanes]
+            return jnp.where(self.pole, pole, self.neighbour[c, cells, lanes])
+
+    top_in = Strip(above_in, north)
+    bot_in = Strip(below_in, south)
+    top_in.pole_corner_ref = pole_corner_in
+    bot_in.pole_corner_ref = pole_corner_in
     scale = HEAD_DIM ** (-0.5)
     r = RADIUS
     tq = TILE_ROWS * width
@@ -82,30 +101,46 @@
             ]
         return jnp.concatenate(parts, axis=0)
 
+    def put_strip(out, c, start, piece, t):
+        bf = jnp.bfloat16
+        piece = piece.astype(bf)
+        out[c, pl.ds(start, piece.shape[0]), lanes_now[0]] = piece
+        if start < edge:
+            pole_ref, pole_start = pole_mid_out, start
+        else:
+            pole_ref, pole_start = pole_corner_out, start - edge
+        index = (c, pl.ds(pole_start, piece.shape[0]), lanes_now[0])
+        if t == 0:
+            pole_ref[index] = piece
+        else:
+            pole_ref[index] = jnp.where(south, piece, pole_ref[index])
+
+    lanes_now = [None]
+
     def scatter_grads(d, own, c, t, lanes):
-        bf = jnp.bfloat16
         rows = side - corner
         n_side = left_out.shape[1]
+        lanes_now[0] = lanes
         if t == 0:
-            top_out[c, pl.ds(0, edge), lanes] = d[:edge].astype(bf)
+            put_strip(top_out, c, 0, d[:edge], t)
             own[pl.ds(0, main - edge), lanes] = d[edge:main]
-            top_out[c, pl.ds(edge, corner), lanes] = d[main : main + corner].astype(bf)
+            put_strip(top_out, c, edge, d[main : main + corner], t)
             left_out[c, pl.ds(0, rows), lanes] = d[main + corner : main + side]
-            top_out[c, pl.ds(edge + corner, corner), lanes] = d[main + side : main + side + corner].astype(bf)
+            put_strip(top_out, c, edge + corner, d[main + side : main + side + corner], t)
             right_out[c, pl.ds(0, rows), lanes] = d[main + side + corner :]
         else:
             shared = main - 2 * edge
             own[pl.ds(edge, shared), lanes] += d[:shared]
             own[pl.ds(edge + shared, edge), lanes] = d[shared : main - edge]
-            bot_out[c, pl.ds(0, edge), lanes] = d[main - edge : main].astype(bf)
+            put_strip(bot_out, c, 0, d[main - edge : main], t)
             start = n_side - rows
             overlap = rows - start
             left_out[c, pl.ds(start, overlap), lanes] += d[main : main + overlap]
             left_out[c, pl.ds(rows, n_side - rows), lanes] = d[main + overlap : main + rows]
-            bot_out[c, pl.ds(edge, corner), lanes] = d[main + rows : main + side].astype(bf)
+            put_strip(bot_out, c, edge, d[main + rows : main + side], t)
             right_out[c, pl.ds(start, overlap), lanes] += d[main + side : main + side + overlap]
             right_out[c, pl.ds(rows, n_side - rows), lanes] = d[main + side + overlap : main + side + rows]
-            bot_out[c, pl.ds(edge + corner, corner), lanes] = d[main + side + rows :].astype(bf)
+            put_strip(bot_out, c, edge + corner, d[main + side + rows :], t)
 
     def body(p, carry):
         lanes = pl.ds(pl.multiple_of(p * LANES, LANES), LANES)
@@ -131,7 +166,7 @@
     lax.fori_loop(0, pairs, body, 0)
 
 
-def attention_core(q2, g2, k2, v2, top_in, bot_in, left_in, right_in, width):
+def attention_core(q2, g2, k2, v2, above, below, pole_mid, pole_corner, left_in, right_in, flags, width):
     cells, features = q2.shape
     r = RADIUS
     tq = TILE_ROWS * width
@@ -145,20 +180,21 @@
         jax.ShapeDtypeStruct((cells, features), jnp.bfloat16),
         jax.ShapeDtypeStruct((cells, features), f32),
         jax.ShapeDtypeStruct((cells, features), f32),
-        jax.ShapeDtypeStruct(top_in.shape, jnp.bfloat16),
-        jax.ShapeDtypeStruct(bot_in.shape, jnp.bfloat16),
+        jax.ShapeDtypeStruct(above.shape, jnp.bfloat16),
+        jax.ShapeDtypeStruct(below.shape, jnp.bfloat16),
         jax.ShapeDtypeStruct(left_in.shape, f32),
         jax.ShapeDtypeStruct(right_in.shape, f32),
-    )
-    in_bytes = 2 * (4 * cells * features + top_in.size + bot_in.size + left_in.size + right_in.size)
-    out_bytes = 2 * cells * features + 8 * cells * features + 2 * (top_in.size + bot_in.size) + 4 * (
-        left_in.size + right_in.size
-    )
+        jax.ShapeDtypeStruct(pole_mid.shape, jnp.bfloat16),
+        jax.ShapeDtypeStruct(pole_corner.shape, jnp.bfloat16),
+    )
+    strips = above.size + below.size + pole_mid.size + pole_corner.size
+    in_bytes = 2 * (4 * cells * features + strips + left_in.size + right_in.size)
+    out_bytes = 10 * cells * features + 2 * strips + 4 * (left_in.size + right_in.size)
     return pl.pallas_call(
         lambda *refs: attention_kernel(width, *refs),
         out_shape=outs,
-        in_specs=[vmem] * 8,
-        out_specs=tuple([vmem] * 7),
+        in_specs=[vmem] * 11,
+        out_specs=tuple([vmem] * 9),
         scratch_shapes=[pltpu.VMEM((2 * tq, tk), jnp.float32)],
         cost_estimate=pl.CostEstimate(
             flops=flops,
@@ -166,7 +202,7 @@
             bytes_accessed=in_bytes + out_bytes,
         ),
         name="neighbourhood_attention_bwd",
-    )(q2, g2, k2, v2, top_in, bot_in, left_in, right_in)
+    )(q2, g2, k2, v2, above, below, pole_mid, pole_corner, left_in, right_in, flags)
 
 
 def on_device(queries, keys, values, grad_out, fold_cols):
@@ -244,29 +280,22 @@
     pole_corners = lax.ppermute(
         jnp.where(at_north, top_send[:, edge:], bottom_send[:, edge:]), both, pole_pairs
     )
-    pole_strip = jnp.concatenate(
-        [jnp.take(pole_mid, pole_src[:edge], axis=1), jnp.take(pole_corners, pole_src[edge:] - edge, axis=1)],
-        axis=1,
-    )
-    top = jnp.where(at_north, pole_strip, from_above)
-    bottom = jnp.where(at_south, pole_strip, from_below)
-
-    dq, dk_own, dv_own, top_g, bottom_g, left_g, right_g = attention_core(
-        queries.reshape(cells, features),
-        grad_out.reshape(cells, features),
-        kf,
-        vf,
-        top,
-        bottom,
-        from_left,
-        from_right,
-        width,
+    pole_mid_rows = jnp.take(pole_mid, pole_src[:edge], axis=1)
+    pole_corner_rows = jnp.take(pole_corners, pole_src[edge:] - edge, axis=1)
+    flags = jnp.stack(
+        [jnp.full((LANES,), at_north, f32), jnp.full((LANES,), at_south, f32)]
+        + [jnp.zeros((LANES,), f32)] * 6
+    )
+
+    q2 = queries.reshape(cells, features)
+    g2 = grad_out.reshape(cells, features)
+    dq, dk_own, dv_own, top_g, bottom_g, left_g, right_g, pole_g_mid_send, pole_g_corner_send = attention_core(
+        q2, g2, kf, vf, from_above, from_below, pole_mid_rows, pole_corner_rows, from_left, from_right, flags, width
     )
 
     up_recv = lax.ppermute(top_g, both, up_pairs)
     down_recv = lax.ppermute(bottom_g, both, down_pairs)
-    pole_g = jnp.where(at_north, top_g, bottom_g)
-    pole_g_corners = lax.ppermute(pole_g[:, edge:], both, pole_pairs)
+    pole_g_corners = lax.ppermute(pole_g_corner_send, both, pole_pairs)
     unfolded_corners = jnp.take(pole_g_corners, pole_dst[edge:] - edge, axis=1)
     zero_mid = jnp.zeros_like(up_recv[:, :edge])
     add_top = jnp.where(
@@ -287,7 +316,7 @@
 
     back_right = lax.ppermute(side_send(left_g, edge), "lon", left_pairs)
     back_left = lax.ppermute(side_send(right_g, edge + corner), "lon", right_pairs)
-    pole_g_mid = lax.ppermute(pole_g[:, :edge], both, pole_pairs)
+    pole_g_mid = lax.ppermute(pole_g_mid_send, both, pole_pairs)
     unfolded_mid = jnp.take(pole_g_mid, pole_dst[:edge], axis=1).astype(f32)
     north_mid = jnp.where(at_north, unfolded_mid, 0.0)
     south_mid = jnp.where(at_south, unfolded_mid, 0.0)

time: 94.2 us -> 90.5 us (0.961)
  the two profiles are of different devices: /device:TPU:1 before, /device:TPU:23 now
where the time goes in v8:
time: 90.5 us; the launch traced here: 90 us
  starting transfers between devices  35.2 us (39%)
  Pallas kernels  16.9 us (19%)
  local copies, waits for them, and re-layouts  16.2 us (18%)
  waiting for transfers between devices  15.6 us (17%)
  other arithmetic  4.84 us (5%)
  between operations  1.22 us (1%)
    pallas_call x1, Pallas kernels, attention_core(): pl.pallas_call(lambda *refs: attention_kernel(width, *refs), out_shape=ou...  16.9 us
    ppermute x1, waiting for transfers between devices, on_device(): lax.ppermute(side_send(right_g, edge + corner), 'lon', right_pairs)  7.88 us
    ppermute x1, starting transfers between devices, on_device(): lax.ppermute(jnp.where(at_north, top_mid, bottom_mid), both, pole_pairs)  6.07 us
    ppermute x1, starting transfers between devices, on_device(): lax.ppermute(pair(cols(keys, 0, r), cols(values, 0, r)), 'lon', left_pairs)  5.39 us
    ppermute x1, starting transfers between devices, on_device(): pole_g_corners = lax.ppermute(pole_g_corner_send, both, pole_pairs)  4.83 us
    unnamed x30, local copies, waits for them, and re-layouts  4.51 us
    ppermute x1, starting transfers between devices, on_device(): pole_g_mid = lax.ppermute(pole_g_mid_send, both, pole_pairs)  4.35 us
    ppermute x1, starting transfers between devices, on_device(): lax.ppermute(jnp.where(at_north, top_send[:, edge:], bottom_send[:, edge:...  3.73 us
  transfers between devices with their start and end apart: 12, of which 4 were waited for; matrix products, arithmetic and copies ran while one was open for 13% of the time, Pallas kernels for 0%

profile of v8, /device:TPU:23, one launch (start us, length us, event | category | flops | bytes accessed | tf_op | source)
XLA Modules:
  0.0 90.0 jit_solution(8716401398972204091)
XLA Ops:
  0.6 1.2 %fusion.15 = (bf16[16,4,1024]{2,1,0:T(4,128)(2,1)S(1)}, bf16[16,4,1024]{2,1,0:T(4,128)(2,1)S(1)}) fusion(bf16[16,16,1024]{2,1,0:T(8,128)(2,1)} %param.21), kind=kLoop, calls=%fused_computation.88 | loop fusion | bytes 524288 | tf_op jit(solution)/shard_map/slice | solution.py:266
  2.1 1.1 %collective-permute-start = (bf16[2,64,1024]{2,1,0:T(8,128)(2,1)S(1)}, bf16[2,64,1024]{2,1,0:T(8,128)(2,1)S(1)}, u32[]{:S(2)}, u32[]{:S(2)}) collective-permute-start(bf16[2,64,1024]{2,1,0:T(8,128)(2,1)S(1)} %pad_maximum_fusion.2), channel_id=1, source_target_pairs={{0,1},{1,2},{2,3},{3,4},{4,5},{5,6},{6,7},{7,8},{8,9},{9,10},{10,1... | collective-permute-start | bytes 786440 | tf_op jit(solution)/shard_map/ppermute | solution.py:268
  3.3 5.4 %collective-permute-start.1 = (bf16[2,64,1024]{2,1,0:T(8,128)(2,1)S(1)}, bf16[2,64,1024]{2,1,0:T(8,128)(2,1)S(1)}, u32[]{:S(2)}, u32[]{:S(2)}) collective-permute-start(bf16[2,64,1024]{2,1,0:T(8,128)(2,1)S(1)} %pad_maximum_fusion.3), channel_id=1, source_target_pairs={{0,15},{1,0},{2,1},{3,2},{4,3},{5,4},{6,5},{7,6},{8,7},{9,8},{10,9... | collective-permute-start | bytes 786440 | tf_op jit(solution)/shard_map/ppermute | solution.py:269
  8.8 6.1 %collective-permute-start.4 = (bf16[2,64,1024]{2,1,0:T(8,128)(2,1)S(1)}, bf16[2,64,1024]{2,1,0:T(8,128)(2,1)S(1)}, u32[]{:S(2)}, u32[]{:S(2)}) collective-permute-start(bf16[2,64,1024]{2,1,0:T(8,128)(2,1)S(1)} %maximum_select_fusion), channel_id=1, source_target_pairs={{0,8},{1,9},{2,10},{3,11},{4,12},{5,13},{6,14},{7,15},{8,0},{9,1},... | collective-permute-start | bytes 786440 | tf_op jit(solution)/shard_map/ppermute | solution.py:272
  15.6 0.7 gather_fusion
  16.3 0.7 gather_fusion.4
  18.4 1.2 %gather_fusion.5 = s32[96]{0:T(128)S(1)} fusion(s32[24]{0:T(128)S(1)} %scatter_custom_fusion, s32[1024]{0:T(1024)S(1)} %pad_clamp_fusion.5), kind=kCustom, calls=%fused_computation.5.clone | custom fusion | bytes 1152 | tf_op jit(solution)/shard_map/jit(_take)/gather | solution.py:257
  19.6 1.2 %gather_fusion.1 = s32[96]{0:T(128)S(1)} fusion(s32[24]{0:T(128)S(1)} %get-tuple-element.64, s32[1024]{0:T(1024)S(1)} %pad_clamp_fusion.5), kind=kCustom, calls=%fused_computation.1.clone | custom fusion | bytes 1152 | tf_op jit(solution)/shard_map/jit(_take)/gather | solution.py:256
  22.1 3.7 %collective-permute-start.5 = (bf16[2,32,1024]{2,1,0:T(8,128)(2,1)S(1)}, bf16[2,32,1024]{2,1,0:T(8,128)(2,1)S(1)}, u32[]{:S(2)}, u32[]{:S(2)}) collective-permute-start(bf16[2,32,1024]{2,1,0:T(8,128)(2,1)S(1)} %maximum_select_fusion.1), channel_id=1, source_target_pairs={{0,8},{1,9},{2,10},{3,11},{4,12},{5,13},{6,14},{7,15},{8,0},{9,1},... | collective-permute-start | bytes 393224 | tf_op jit(solution)/shard_map/ppermute | solution.py:280
  25.8 1.3 %collective-permute-start.3 = (bf16[2,96,1024]{2,1,0:T(8,128)(2,1)S(1)}, bf16[2,96,1024]{2,1,0:T(8,128)(2,1)S(1)}, u32[]{:S(2)}, u32[]{:S(2)}) collective-permute-start(bf16[2,96,1024]{2,1,0:T(8,128)(2,1)S(1)} %pad_maximum_fusion.1), channel_id=1, source_target_pairs={{16,0},{17,1},{18,2},{19,3},{20,4},{21,5},{22,6},{23,7},{24,8},{25... | collective-permute-start | bytes 1179656 | tf_op jit(solution)/shard_map/ppermute | solution.py:279
  27.2 1.3 %collective-permute-start.2 = (bf16[2,96,1024]{2,1,0:T(8,128)(2,1)S(1)}, bf16[2,96,1024]{2,1,0:T(8,128)(2,1)S(1)}, u32[]{:S(2)}, u32[]{:S(2)}) collective-permute-start(bf16[2,96,1024]{2,1,0:T(8,128)(2,1)S(1)} %pad_maximum_fusion), channel_id=1, source_target_pairs={{0,16},{1,17},{2,18},{3,19},{4,20},{5,21},{6,22},{7,23},{8,24},{9,... | collective-permute-start | bytes 1179656 | tf_op jit(solution)/shard_map/ppermute | solution.py:278
  28.8 1.1 %gather_fusion.2 = bf16[64,2,1024]{2,1,0:T(2,128)(2,1)S(1)} fusion(bf16[2,64,1024]{2,0,1:T(2,128)(2,1)S(1)} %copy.15, s32[1024]{0:T(1024)S(1)} %pad_clamp_fusion.4), kind=kCustom, calls=%fused_computation.2.clone | custom fusion | bytes 524544 | tf_op jit(solution)/shard_map/jit(_take)/gather | solution.py:283
  29.9 0.8 fusion.2.refs_6_
  30.7 1.3 %collective-permute-done.5 = bf16[2,32,1024]{2,1,0:T(8,128)(2,1)S(1)} collective-permute-done((bf16[2,32,1024]{2,1,0:T(8,128)(2,1)S(1)}, bf16[2,32,1024]{2,1,0:T(8,128)(2,1)S(1)}, u32[]{:S(2)}, u32[]{:S(2)}) %collective-permute-start.5) | collective-permute-done | bytes 131104 | tf_op jit(solution)/shard_map/ppermute | solution.py:280
  32.2 0.8 gather_fusion.3
  33.0 0.8 fusion.4.refs_7_
  33.8 0.8 broadcast.157.refs_10_
  34.7 16.9 %neighbourhood_attention_bwd.1 = (bf16[256,1024]{1,0:T(8,128)(2,1)}, f32[256,1024]{1,0:T(8,128)}, f32[256,1024]{1,0:T(8,128)}, bf16[2,96,1024]{2,1,0:T(8,128)(2,...) custom-call(bf16[256,1024]{1,0:T(8,128)(2,1)} %bitcast.45, ...), custom_call_target="tpu_custom_call" | custom-call | flops 2013265920 | bytes 8650752 | tf_op jit(solution)/shard_map/neighbourhood_attention_bwd/pallas_call | solution.py:193
  51.5 4.8 %collective-permute-start.6 = (bf16[2,32,1024]{2,1,0:T(8,128)(2,1)}, bf16[2,32,1024]{2,1,0:T(8,128)(2,1)S(1)}, u32[]{:S(2)}, u32[]{:S(2)}) collective-permute-start(bf16[2,32,1024]{2,1,0:T(8,128)(2,1)} %get-tuple-element.18), channel_id=1, source_target_pairs={{0,8},{1,9},{2,10},{3,11},{4,12},{5,13},{6,14},{7,15},{8,0},{9,1},... | collective-permute-start | bytes 393224 | tf_op jit(solution)/shard_map/ppermute | solution.py:298
  56.4 4.4 %collective-permute-start.8 = (bf16[2,64,1024]{2,1,0:T(8,128)(2,1)}, bf16[2,64,1024]{2,1,0:T(8,128)(2,1)S(1)}, u32[]{:S(2)}, u32[]{:S(2)}) collective-permute-start(bf16[2,64,1024]{2,1,0:T(8,128)(2,1)} %get-tuple-element.20), channel_id=1, source_target_pairs={{0,8},{1,9},{2,10},{3,11},{4,12},{5,13},{6,14},{7,15},{8,0},{9,1},... | collective-permute-start | bytes 786440 | tf_op jit(solution)/shard_map/ppermute | solution.py:319
  60.8 1.3 %collective-permute-start.7 = (bf16[2,96,1024]{2,1,0:T(8,128)(2,1)}, bf16[2,96,1024]{2,1,0:T(8,128)(2,1)S(1)}, u32[]{:S(2)}, u32[]{:S(2)}) collective-permute-start(bf16[2,96,1024]{2,1,0:T(8,128)(2,1)} %get-tuple-element.19), channel_id=1, source_target_pairs={{0,16},{1,17},{2,18},{3,19},{4,20},{5,21},{6,22},{7,23},{8,24},{9,... | collective-permute-start | bytes 1179656 | tf_op jit(solution)/shard_map/ppermute | solution.py:297
  62.1 3.1 %collective-permute-start.9 = (bf16[2,96,1024]{2,1,0:T(8,128)(2,1)}, bf16[2,96,1024]{2,1,0:T(8,128)(2,1)S(1)}, u32[]{:S(2)}, u32[]{:S(2)}) collective-permute-start(bf16[2,96,1024]{2,1,0:T(8,128)(2,1)} %get-tuple-element.21), channel_id=1, source_target_pairs={{16,0},{17,1},{18,2},{19,3},{20,4},{21,5},{22,6},{23,7},{24,8},{25... | collective-permute-start | bytes 1179656 | tf_op jit(solution)/shard_map/ppermute | solution.py:296
  65.3 0.8 gather_fusion.6
  66.2 3.2 %collective-permute-done.8 = bf16[2,64,1024]{2,1,0:T(8,128)(2,1)S(1)} collective-permute-done((bf16[2,64,1024]{2,1,0:T(8,128)(2,1)}, bf16[2,64,1024]{2,1,0:T(8,128)(2,1)S(1)}, u32[]{:S(2)}, u32[]{:S(2)}) %collective-permute-start.8) | collective-permute-done | bytes 262176 | tf_op jit(solution)/shard_map/ppermute | solution.py:319
  69.7 1.1 %gather_fusion.7 = bf16[64,2,1024]{2,1,0:T(2,128)(2,1)S(1)} fusion(bf16[2,64,1024]{2,0,1:T(2,128)(2,1)S(1)} %copy.21, s32[1024]{0:T(1024)S(1)} %pad_clamp_fusion), kind=kCustom, calls=%fused_computation.6.clone | custom fusion | bytes 524544 | tf_op jit(solution)/shard_map/jit(_take)/gather | solution.py:320
  71.2 1.0 %copy-done.5 = f32[2,64,1024]{2,1,0:T(8,128)S(1)} copy-done((f32[2,64,1024]{2,1,0:T(8,128)S(1)}, f32[2,64,1024]{2,1,0:T(8,128)}, u32[]{:S(2)}) %copy-start.5) | copy-done | bytes 524312
  72.4 0.9 copy-done.4
  73.3 2.7 %collective-permute-start.11 = (bf16[2,64,1024]{2,1,0:T(8,128)(2,1)S(1)}, bf16[2,64,1024]{2,1,0:T(8,128)(2,1)S(1)}, u32[]{:S(2)}, u32[]{:S(2)}) collective-permute-start(bf16[2,64,1024]{2,1,0:T(8,128)(2,1)S(1)} %add_convert_fusion.2), channel_id=1, source_target_pairs={{0,15},{1,0},{2,1},{3,2},{4,3},{5,4},{6,5},{7,6},{8,7},{9,8},{10,9... | collective-permute-start | bytes 786440 | tf_op jit(solution)/shard_map/ppermute | solution.py:317
  76.2 7.9 %collective-permute-done.10 = bf16[2,64,1024]{2,1,0:T(8,128)(2,1)S(1)} collective-permute-done((bf16[2,64,1024]{2,1,0:T(8,128)(2,1)S(1)}, bf16[2,64,1024]{2,1,0:T(8,128)(2,1)S(1)}, u32[]{:S(2)}, u32[]{:S(2)}) %collective-permute-start.10) | collective-permute-done | bytes 262176 | tf_op jit(solution)/shard_map/ppermute | solution.py:318
  84.2 3.2 %collective-permute-done.11 = bf16[2,64,1024]{2,1,0:T(8,128)(2,1)S(1)} collective-permute-done((bf16[2,64,1024]{2,1,0:T(8,128)(2,1)S(1)}, bf16[2,64,1024]{2,1,0:T(8,128)(2,1)S(1)}, u32[]{:S(2)}, u32[]{:S(2)}) %collective-permute-start.11) | collective-permute-done | bytes 262176 | tf_op jit(solution)/shard_map/ppermute | solution.py:317
  87.6 1.0 %add_convert_fusion = bf16[16,16,1024]{2,1,0:T(8,128)(2,1)} fusion(f32[4,16,1024]{2,1,0:T(8,128)S(1)} %bitcast.42, f32[16,16,1024]{2,1,0:T(8,128)S(1)} %bitcast.38, f32[4,16,1024]{2,1,0:T(8,128)S(1)} %bitcast.41, bf16[16,4,1024]{2,1,0:T(4,128)(2,1)S(1)} %convert_element_type.72, bf16[16,4,1024]{2,1,0:T(4,128)(2,1)S(1)} %convert_element_type.71), kind=kLoop, calls=%fused_computation.9 | loop fusion | flops 1835008 | bytes 2359296 | tf_op jit(solution)/shard_map/convert_element_type | solution.py:338
  89.0 1.0 %add_convert_fusion.1 = bf16[16,16,1024]{2,1,0:T(8,128)(2,1)} fusion(f32[4,16,1024]{2,1,0:T(8,128)S(1)} %bitcast.40, f32[16,16,1024]{2,1,0:T(8,128)S(1)} %bitcast.37, f32[4,16,1024]{2,1,0:T(8,128)S(1)} %bitcast.39, bf16[16,4,1024]{2,1,0:T(4,128)(2,1)S(1)} %convert_element_type.69, bf16[16,4,1024]{2,1,0:T(4,128)(2,1)S(1)} %convert_element_type.67), kind=kLoop, calls=%fused_computation.10 | loop fusion | flops 1835008 | bytes 2359296 | tf_op jit(solution)/shard_map/convert_element_type | solution.py:338
  (92 shorter events, 6.1 us)
Async XLA Ops:
  0.6 1.2 %copy-start.3 = (bf16[16,16,1024]{2,1,0:T(8,128)(2,1)S(1)}, bf16[16,16,1024]{2,1,0:T(8,128)(2,1)}, u32[]{:S(2)}) copy-start(bf16[16,16,1024]{2,1,0:T(8,128)(2,1)} %param.22) | copy-start | bytes 1572868
  2.1 19.2 %collective-permute-start = (bf16[2,64,1024]{2,1,0:T(8,128)(2,1)S(1)}, bf16[2,64,1024]{2,1,0:T(8,128)(2,1)S(1)}, u32[]{:S(2)}, u32[]{:S(2)}) collective-permute-start(bf16[2,64,1024]{2,1,0:T(8,128)(2,1)S(1)} %pad_maximum_fusion.2), channel_id=1, source_target_pairs={{0,1},{1,2},{2,3},{3,4},{4,5},{5,6},{6,7},{7,8},{8,9},{9,10},{10,1... | collective-permute-start | bytes 786440 | tf_op jit(solution)/shard_map/ppermute | solution.py:268
  3.2 5.5 %copy-start.2 = (bf16[16,16,1024]{2,1,0:T(8,128)(2,1)S(1)}, bf16[16,16,1024]{2,1,0:T(8,128)(2,1)}, u32[]{:S(2)}) copy-start(bf16[16,16,1024]{2,1,0:T(8,128)(2,1)} %param.21) | copy-start | bytes 1572868
  3.3 18.0 %collective-permute-start.1 = (bf16[2,64,1024]{2,1,0:T(8,128)(2,1)S(1)}, bf16[2,64,1024]{2,1,0:T(8,128)(2,1)S(1)}, u32[]{:S(2)}, u32[]{:S(2)}) collective-permute-start(bf16[2,64,1024]{2,1,0:T(8,128)(2,1)S(1)} %pad_maximum_fusion.3), channel_id=1, source_target_pairs={{0,15},{1,0},{2,1},{3,2},{4,3},{5,4},{6,5},{7,6},{8,7},{9,8},{10,9... | collective-permute-start | bytes 786440 | tf_op jit(solution)/shard_map/ppermute | solution.py:269
  8.8 19.7 %collective-permute-start.4 = (bf16[2,64,1024]{2,1,0:T(8,128)(2,1)S(1)}, bf16[2,64,1024]{2,1,0:T(8,128)(2,1)S(1)}, u32[]{:S(2)}, u32[]{:S(2)}) collective-permute-start(bf16[2,64,1024]{2,1,0:T(8,128)(2,1)S(1)} %maximum_select_fusion), channel_id=1, source_target_pairs={{0,8},{1,9},{2,10},{3,11},{4,12},{5,13},{6,14},{7,15},{8,0},{9,1},... | collective-permute-start | bytes 786440 | tf_op jit(solution)/shard_map/ppermute | solution.py:272
  14.9 0.7 copy-start.8
  17.0 0.7 copy-start.12
  19.6 1.3 %copy-start.9 = (s32[96]{0:T(128)S(1)}, s32[96]{0:T(128)}, u32[]{:S(2)}) copy-start(s32[96]{0:T(128)} %constant.135.clone) | copy-start | bytes 1156
  19.6 1.3 %copy-start.10 = (s32[96]{0:T(128)S(1)}, s32[96]{0:T(128)}, u32[]{:S(2)}) copy-start(s32[96]{0:T(128)} %constant.136.clone) | copy-start | bytes 1156
  19.6 1.3 %copy-start.11 = (s32[96]{0:T(128)S(1)}, s32[96]{0:T(128)}, u32[]{:S(2)}) copy-start(s32[96]{0:T(128)} %constant.137.clone) | copy-start | bytes 1156
  21.2 0.7 copy-start.6
  21.3 0.8 copy-start.7
  22.1 10.0 %collective-permute-start.5 = (bf16[2,32,1024]{2,1,0:T(8,128)(2,1)S(1)}, bf16[2,32,1024]{2,1,0:T(8,128)(2,1)S(1)}, u32[]{:S(2)}, u32[]{:S(2)}) collective-permute-start(bf16[2,32,1024]{2,1,0:T(8,128)(2,1)S(1)} %maximum_select_fusion.1), channel_id=1, source_target_pairs={{0,8},{1,9},{2,10},{3,11},{4,12},{5,13},{6,14},{7,15},{8,0},{9,1},... | collective-permute-start | bytes 393224 | tf_op jit(solution)/shard_map/ppermute | solution.py:280
  25.8 7.9 %collective-permute-start.3 = (bf16[2,96,1024]{2,1,0:T(8,128)(2,1)S(1)}, bf16[2,96,1024]{2,1,0:T(8,128)(2,1)S(1)}, u32[]{:S(2)}, u32[]{:S(2)}) collective-permute-start(bf16[2,96,1024]{2,1,0:T(8,128)(2,1)S(1)} %pad_maximum_fusion.1), channel_id=1, source_target_pairs={{16,0},{17,1},{18,2},{19,3},{20,4},{21,5},{22,6},{23,7},{24,8},{25... | collective-permute-start | bytes 1179656 | tf_op jit(solution)/shard_map/ppermute | solution.py:279
  27.2 6.6 %collective-permute-start.2 = (bf16[2,96,1024]{2,1,0:T(8,128)(2,1)S(1)}, bf16[2,96,1024]{2,1,0:T(8,128)(2,1)S(1)}, u32[]{:S(2)}, u32[]{:S(2)}) collective-permute-start(bf16[2,96,1024]{2,1,0:T(8,128)(2,1)S(1)} %pad_maximum_fusion), channel_id=1, source_target_pairs={{0,16},{1,17},{2,18},{3,19},{4,20},{5,21},{6,22},{7,23},{8,24},{9,... | collective-permute-start | bytes 1179656 | tf_op jit(solution)/shard_map/ppermute | solution.py:278
  33.7 0.8 copy-start.13
  33.8 0.9 %copy-start.14 = (bf16[2,96,1024]{2,1,0:T(8,128)(2,1)}, bf16[2,96,1024]{2,1,0:T(8,128)(2,1)S(1)}, u32[]{:S(2)}) copy-start(bf16[2,96,1024]{2,1,0:T(8,128)(2,1)S(1)} %collective-permute-done.2.refs_4_) | copy-start | bytes 1179652
  51.5 13.6 %collective-permute-start.6 = (bf16[2,32,1024]{2,1,0:T(8,128)(2,1)}, bf16[2,32,1024]{2,1,0:T(8,128)(2,1)S(1)}, u32[]{:S(2)}, u32[]{:S(2)}) collective-permute-start(bf16[2,32,1024]{2,1,0:T(8,128)(2,1)} %get-tuple-element.18), channel_id=1, source_target_pairs={{0,8},{1,9},{2,10},{3,11},{4,12},{5,13},{6,14},{7,15},{8,0},{9,1},... | collective-permute-start | bytes 393224 | tf_op jit(solution)/shard_map/ppermute | solution.py:298
  56.4 13.0 %collective-permute-start.8 = (bf16[2,64,1024]{2,1,0:T(8,128)(2,1)}, bf16[2,64,1024]{2,1,0:T(8,128)(2,1)S(1)}, u32[]{:S(2)}, u32[]{:S(2)}) collective-permute-start(bf16[2,64,1024]{2,1,0:T(8,128)(2,1)} %get-tuple-element.20), channel_id=1, source_target_pairs={{0,8},{1,9},{2,10},{3,11},{4,12},{5,13},{6,14},{7,15},{8,0},{9,1},... | collective-permute-start | bytes 786440 | tf_op jit(solution)/shard_map/ppermute | solution.py:319
  60.8 10.2 %collective-permute-start.7 = (bf16[2,96,1024]{2,1,0:T(8,128)(2,1)}, bf16[2,96,1024]{2,1,0:T(8,128)(2,1)S(1)}, u32[]{:S(2)}, u32[]{:S(2)}) collective-permute-start(bf16[2,96,1024]{2,1,0:T(8,128)(2,1)} %get-tuple-element.19), channel_id=1, source_target_pairs={{0,16},{1,17},{2,18},{3,19},{4,20},{5,21},{6,22},{7,23},{8,24},{9,... | collective-permute-start | bytes 1179656 | tf_op jit(solution)/shard_map/ppermute | solution.py:297
  62.1 8.9 %collective-permute-start.9 = (bf16[2,96,1024]{2,1,0:T(8,128)(2,1)}, bf16[2,96,1024]{2,1,0:T(8,128)(2,1)S(1)}, u32[]{:S(2)}, u32[]{:S(2)}) collective-permute-start(bf16[2,96,1024]{2,1,0:T(8,128)(2,1)} %get-tuple-element.21), channel_id=1, source_target_pairs={{16,0},{17,1},{18,2},{19,3},{20,4},{21,5},{22,6},{23,7},{24,8},{25... | collective-permute-start | bytes 1179656 | tf_op jit(solution)/shard_map/ppermute | solution.py:296
  71.2 1.0 %copy-start.5 = (f32[2,64,1024]{2,1,0:T(8,128)S(1)}, f32[2,64,1024]{2,1,0:T(8,128)}, u32[]{:S(2)}) copy-start(f32[2,64,1024]{2,1,0:T(8,128)} %get-tuple-element.22) | copy-start | bytes 1572868
  72.2 1.0 %copy-start.4 = (f32[2,64,1024]{2,1,0:T(8,128)S(1)}, f32[2,64,1024]{2,1,0:T(8,128)}, u32[]{:S(2)}) copy-start(f32[2,64,1024]{2,1,0:T(8,128)} %get-tuple-element.23) | copy-start | bytes 1572868
  72.3 11.8 %collective-permute-start.10 = (bf16[2,64,1024]{2,1,0:T(8,128)(2,1)S(1)}, bf16[2,64,1024]{2,1,0:T(8,128)(2,1)S(1)}, u32[]{:S(2)}, u32[]{:S(2)}) collective-permute-start(bf16[2,64,1024]{2,1,0:T(8,128)(2,1)S(1)} %add_convert_fusion.3), channel_id=1, source_target_pairs={{0,1},{1,2},{2,3},{3,4},{4,5},{5,6},{6,7},{7,8},{8,9},{9,10},{10,1... | collective-permute-start | bytes 786440 | tf_op jit(solution)/shard_map/ppermute | solution.py:318
  73.3 14.0 %collective-permute-start.11 = (bf16[2,64,1024]{2,1,0:T(8,128)(2,1)S(1)}, bf16[2,64,1024]{2,1,0:T(8,128)(2,1)S(1)}, u32[]{:S(2)}, u32[]{:S(2)}) collective-permute-start(bf16[2,64,1024]{2,1,0:T(8,128)(2,1)S(1)} %add_convert_fusion.2), channel_id=1, source_target_pairs={{0,15},{1,0},{2,1},{3,2},{4,3},{5,4},{6,5},{7,6},{8,7},{9,8},{10,9... | collective-permute-start | bytes 786440 | tf_op jit(solution)/shard_map/ppermute | solution.py:317
  76.2 11.3 %copy-start.1 = (f32[256,1024]{1,0:T(8,128)S(1)}, f32[256,1024]{1,0:T(8,128)}, u32[]{:S(2)}) copy-start(f32[256,1024]{1,0:T(8,128)} %get-tuple-element.24) | copy-start | bytes 3145732
  87.5 1.4 %copy-start = (f32[256,1024]{1,0:T(8,128)S(1)}, f32[256,1024]{1,0:T(8,128)}, u32[]{:S(2)}) copy-start(f32[256,1024]{1,0:T(8,128)} %get-tuple-element.17) | copy-start | bytes 3145732

commit v9 on v8

--- a/solution.py
+++ b/solution.py
@@ -15,12 +15,13 @@
 LANES = 128
 
 
-def attention_kernel(width, *refs):
-    (q_ref, g_ref, k_own, v_own, above_in, below_in, pole_mid_in, pole_corner_in, left_in, right_in, flag_ref) = refs[:11]
-    (dq_ref, dk_own, dv_own, top_out, bot_out, left_out, right_out, pole_mid_out, pole_corner_out) = refs[11:20]
-    bias_ref = refs[20]
-    north = flag_ref[0:1, :] > 0.5
-    south = flag_ref[1:2, :] > 0.5
+def attention_kernel(width, n_lat, *refs):
+    (q_ref, g_ref, k_own, v_own, above_in, below_in, pole_mid_in, pole_corner_in, left_in, right_in) = refs[:10]
+    (dq_ref, dk_own, dv_own, top_out, bot_out, left_out, right_out, pole_mid_out, pole_corner_out) = refs[10:19]
+    bias_ref = refs[19]
+    lat = lax.axis_index("lat")
+    north = lat == 0
+    south = lat == n_lat - 1
 
     class Strip:
         def __init__(self, neighbour, pole):
@@ -166,7 +167,7 @@
     lax.fori_loop(0, pairs, body, 0)
 
 
-def attention_core(q2, g2, k2, v2, above, below, pole_mid, pole_corner, left_in, right_in, flags, width):
+def attention_core(q2, g2, k2, v2, above, below, pole_mid, pole_corner, left_in, right_in, width, n_lat):
     cells, features = q2.shape
     r = RADIUS
     tq = TILE_ROWS * width
@@ -191,9 +192,9 @@
     in_bytes = 2 * (4 * cells * features + strips + left_in.size + right_in.size)
     out_bytes = 10 * cells * features + 2 * strips + 4 * (left_in.size + right_in.size)
     return pl.pallas_call(
-        lambda *refs: attention_kernel(width, *refs),
+        lambda *refs: attention_kernel(width, n_lat, *refs),
         out_shape=outs,
-        in_specs=[vmem] * 11,
+        in_specs=[vmem] * 10,
         out_specs=tuple([vmem] * 9),
         scratch_shapes=[pltpu.VMEM((2 * tq, tk), jnp.float32)],
         cost_estimate=pl.CostEstimate(
@@ -202,7 +203,7 @@
             bytes_accessed=in_bytes + out_bytes,
         ),
         name="neighbourhood_attention_bwd",
-    )(q2, g2, k2, v2, above, below, pole_mid, pole_corner, left_in, right_in, flags)
+    )(q2, g2, k2, v2, above, below, pole_mid, pole_corner, left_in, right_in)
 
 
 def on_device(queries, keys, values, grad_out, fold_cols):
@@ -282,15 +283,11 @@
     )
     pole_mid_rows = jnp.take(pole_mid, pole_src[:edge], axis=1)
     pole_corner_rows = jnp.take(pole_corners, pole_src[edge:] - edge, axis=1)
-    flags = jnp.stack(
-        [jnp.full((LANES,), at_north, f32), jnp.full((LANES,), at_south, f32)]
-        + [jnp.zeros((LANES,), f32)] * 6
-    )
 
     q2 = queries.reshape(cells, features)
     g2 = grad_out.reshape(cells, features)
     dq, dk_own, dv_own, top_g, bottom_g, left_g, right_g, pole_g_mid_send, pole_g_corner_send = attention_core(
-        q2, g2, kf, vf, from_above, from_below, pole_mid_rows, pole_corner_rows, from_left, from_right, flags, width
+        q2, g2, kf, vf, from_above, from_below, pole_mid_rows, pole_corner_rows, from_left, from_right, width, n_lat
     )
 
     up_recv = lax.ppermute(top_g, both, up_pairs)

time: 90.5 us -> 89.9 us (level)
  the two profiles are of different devices: /device:TPU:23 before, /device:TPU:32 now
where the time goes in v9:
time: 89.9 us; the launch traced here: 88.2 us
  starting transfers between devices  35.1 us (39%)
  Pallas kernels  16.9 us (19%)
  local copies, waits for them, and re-layouts  16.2 us (18%)
  waiting for transfers between devices  14.1 us (16%)
  other arithmetic  4.76 us (5%)
  between operations  1.21 us (1%)
    pallas_call x1, Pallas kernels, attention_core(): pl.pallas_call(lambda *refs: attention_kernel(width, n_lat, *refs), out_s...  16.9 us
    ppermute x1, starting transfers between devices, on_device(): lax.ppermute(jnp.where(at_north, top_mid, bottom_mid), both, pole_pairs)  8.2 us
    ppermute x1, waiting for transfers between devices, on_device(): pole_g_mid = lax.ppermute(pole_g_mid_send, both, pole_pairs)  6.68 us
    unnamed x30, local copies, waits for them, and re-layouts  5.25 us
    ppermute x1, starting transfers between devices, on_device(): lax.ppermute(jnp.where(at_north, top_send[:, edge:], bottom_send[:, edge:...  4.94 us
    ppermute x1, starting transfers between devices, on_device(): pole_g_corners = lax.ppermute(pole_g_corner_send, both, pole_pairs)  4.94 us
    ppermute x1, starting transfers between devices, on_device(): pole_g_mid = lax.ppermute(pole_g_mid_send, both, pole_pairs)  4.8 us
    ppermute x1, waiting for transfers between devices, on_device(): lax.ppermute(side_send(right_g, edge + corner), 'lon', right_pairs)  4.16 us
  transfers between devices with their start and end apart: 12, of which 4 were waited for; matrix products, arithmetic and copies ran while one was open for 13% of the time, Pallas kernels for 0%

profile of v9, /device:TPU:32, one launch (start us, length us, event | category | flops | bytes accessed | tf_op | source)
XLA Modules:
  0.0 88.2 jit_solution(18436073882999701397)
XLA Ops:
  0.6 1.2 %fusion.15 = (bf16[16,4,1024]{2,1,0:T(4,128)(2,1)S(1)}, bf16[16,4,1024]{2,1,0:T(4,128)(2,1)S(1)}) fusion(bf16[16,16,1024]{2,1,0:T(8,128)(2,1)} %param.21), kind=kLoop, calls=%fused_computation.87 | loop fusion | bytes 524288 | tf_op jit(solution)/shard_map/slice | solution.py:267
  2.1 1.7 %collective-permute-start = (bf16[2,64,1024]{2,1,0:T(8,128)(2,1)S(1)}, bf16[2,64,1024]{2,1,0:T(8,128)(2,1)S(1)}, u32[]{:S(2)}, u32[]{:S(2)}) collective-permute-start(bf16[2,64,1024]{2,1,0:T(8,128)(2,1)S(1)} %pad_maximum_fusion.2), channel_id=1, source_target_pairs={{0,1},{1,2},{2,3},{3,4},{4,5},{5,6},{6,7},{7,8},{8,9},{9,10},{10,1... | collective-permute-start | bytes 786440 | tf_op jit(solution)/shard_map/ppermute | solution.py:269
  3.8 1.4 %collective-permute-start.1 = (bf16[2,64,1024]{2,1,0:T(8,128)(2,1)S(1)}, bf16[2,64,1024]{2,1,0:T(8,128)(2,1)S(1)}, u32[]{:S(2)}, u32[]{:S(2)}) collective-permute-start(bf16[2,64,1024]{2,1,0:T(8,128)(2,1)S(1)} %pad_maximum_fusion.3), channel_id=1, source_target_pairs={{0,15},{1,0},{2,1},{3,2},{4,3},{5,4},{6,5},{7,6},{8,7},{9,8},{10,9... | collective-permute-start | bytes 786440 | tf_op jit(solution)/shard_map/ppermute | solution.py:270
  5.4 8.2 %collective-permute-start.4 = (bf16[2,64,1024]{2,1,0:T(8,128)(2,1)S(1)}, bf16[2,64,1024]{2,1,0:T(8,128)(2,1)S(1)}, u32[]{:S(2)}, u32[]{:S(2)}) collective-permute-start(bf16[2,64,1024]{2,1,0:T(8,128)(2,1)S(1)} %maximum_select_fusion), channel_id=1, source_target_pairs={{0,8},{1,9},{2,10},{3,11},{4,12},{5,13},{6,14},{7,15},{8,0},{9,1},... | collective-permute-start | bytes 786440 | tf_op jit(solution)/shard_map/ppermute | solution.py:273
  13.6 0.7 copy-done.8
  14.3 0.7 gather_fusion
  15.1 0.7 gather_fusion.4
  17.1 1.2 %gather_fusion.5 = s32[96]{0:T(128)S(1)} fusion(s32[24]{0:T(128)S(1)} %scatter_custom_fusion, s32[1024]{0:T(1024)S(1)} %pad_clamp_fusion.5), kind=kCustom, calls=%fused_computation.5.clone | custom fusion | bytes 1152 | tf_op jit(solution)/shard_map/jit(_take)/gather | solution.py:258
  18.4 1.2 %gather_fusion.1 = s32[96]{0:T(128)S(1)} fusion(s32[24]{0:T(128)S(1)} %get-tuple-element.64, s32[1024]{0:T(1024)S(1)} %pad_clamp_fusion.5), kind=kCustom, calls=%fused_computation.1.clone | custom fusion | bytes 1152 | tf_op jit(solution)/shard_map/jit(_take)/gather | solution.py:257
  20.7 4.9 %collective-permute-start.5 = (bf16[2,32,1024]{2,1,0:T(8,128)(2,1)S(1)}, bf16[2,32,1024]{2,1,0:T(8,128)(2,1)S(1)}, u32[]{:S(2)}, u32[]{:S(2)}) collective-permute-start(bf16[2,32,1024]{2,1,0:T(8,128)(2,1)S(1)} %maximum_select_fusion.1), channel_id=1, source_target_pairs={{0,8},{1,9},{2,10},{3,11},{4,12},{5,13},{6,14},{7,15},{8,0},{9,1},... | collective-permute-start | bytes 393224 | tf_op jit(solution)/shard_map/ppermute | solution.py:281
  25.7 1.3 %collective-permute-start.3 = (bf16[2,96,1024]{2,1,0:T(8,128)(2,1)S(1)}, bf16[2,96,1024]{2,1,0:T(8,128)(2,1)S(1)}, u32[]{:S(2)}, u32[]{:S(2)}) collective-permute-start(bf16[2,96,1024]{2,1,0:T(8,128)(2,1)S(1)} %pad_maximum_fusion.1), channel_id=1, source_target_pairs={{16,0},{17,1},{18,2},{19,3},{20,4},{21,5},{22,6},{23,7},{24,8},{25... | collective-permute-start | bytes 1179656 | tf_op jit(solution)/shard_map/ppermute | solution.py:280
  27.0 3.1 %collective-permute-start.2 = (bf16[2,96,1024]{2,1,0:T(8,128)(2,1)S(1)}, bf16[2,96,1024]{2,1,0:T(8,128)(2,1)S(1)}, u32[]{:S(2)}, u32[]{:S(2)}) collective-permute-start(bf16[2,96,1024]{2,1,0:T(8,128)(2,1)S(1)} %pad_maximum_fusion), channel_id=1, source_target_pairs={{0,16},{1,17},{2,18},{3,19},{4,20},{5,21},{6,22},{7,23},{8,24},{9,... | collective-permute-start | bytes 1179656 | tf_op jit(solution)/shard_map/ppermute | solution.py:279
  30.4 1.1 %gather_fusion.2 = bf16[64,2,1024]{2,1,0:T(2,128)(2,1)S(1)} fusion(bf16[2,64,1024]{2,0,1:T(2,128)(2,1)S(1)} %copy.15, s32[1024]{0:T(1024)S(1)} %pad_clamp_fusion.4), kind=kCustom, calls=%fused_computation.2.clone | custom fusion | bytes 524544 | tf_op jit(solution)/shard_map/jit(_take)/gather | solution.py:284
  31.4 0.8 fusion.2.refs_6_
  33.0 0.8 gather_fusion.3
  33.8 0.8 fusion.4.refs_7_
  34.6 0.7 copy-done.13
  35.5 16.9 %neighbourhood_attention_bwd.1 = (bf16[256,1024]{1,0:T(8,128)(2,1)}, f32[256,1024]{1,0:T(8,128)}, f32[256,1024]{1,0:T(8,128)}, bf16[2,96,1024]{2,1,0:T(8,128)(2,...) custom-call(bf16[256,1024]{1,0:T(8,128)(2,1)} %bitcast.43, ...), custom_call_target="tpu_custom_call" | custom-call | flops 2013265920 | bytes 8650752 | tf_op jit(solution)/shard_map/neighbourhood_attention_bwd/pallas_call | solution.py:194
  52.4 4.9 %collective-permute-start.6 = (bf16[2,32,1024]{2,1,0:T(8,128)(2,1)}, bf16[2,32,1024]{2,1,0:T(8,128)(2,1)S(1)}, u32[]{:S(2)}, u32[]{:S(2)}) collective-permute-start(bf16[2,32,1024]{2,1,0:T(8,128)(2,1)} %get-tuple-element.18), channel_id=1, source_target_pairs={{0,8},{1,9},{2,10},{3,11},{4,12},{5,13},{6,14},{7,15},{8,0},{9,1},... | collective-permute-start | bytes 393224 | tf_op jit(solution)/shard_map/ppermute | solution.py:295
  57.3 4.8 %collective-permute-start.8 = (bf16[2,64,1024]{2,1,0:T(8,128)(2,1)}, bf16[2,64,1024]{2,1,0:T(8,128)(2,1)S(1)}, u32[]{:S(2)}, u32[]{:S(2)}) collective-permute-start(bf16[2,64,1024]{2,1,0:T(8,128)(2,1)} %get-tuple-element.20), channel_id=1, source_target_pairs={{0,8},{1,9},{2,10},{3,11},{4,12},{5,13},{6,14},{7,15},{8,0},{9,1},... | collective-permute-start | bytes 786440 | tf_op jit(solution)/shard_map/ppermute | solution.py:316
  62.1 1.3 %collective-permute-start.7 = (bf16[2,96,1024]{2,1,0:T(8,128)(2,1)}, bf16[2,96,1024]{2,1,0:T(8,128)(2,1)S(1)}, u32[]{:S(2)}, u32[]{:S(2)}) collective-permute-start(bf16[2,96,1024]{2,1,0:T(8,128)(2,1)} %get-tuple-element.19), channel_id=1, source_target_pairs={{0,16},{1,17},{2,18},{3,19},{4,20},{5,21},{6,22},{7,23},{8,24},{9,... | collective-permute-start | bytes 1179656 | tf_op jit(solution)/shard_map/ppermute | solution.py:294
  63.5 1.3 %collective-permute-start.9 = (bf16[2,96,1024]{2,1,0:T(8,128)(2,1)}, bf16[2,96,1024]{2,1,0:T(8,128)(2,1)S(1)}, u32[]{:S(2)}, u32[]{:S(2)}) collective-permute-start(bf16[2,96,1024]{2,1,0:T(8,128)(2,1)} %get-tuple-element.21), channel_id=1, source_target_pairs={{16,0},{17,1},{18,2},{19,3},{20,4},{21,5},{22,6},{23,7},{24,8},{25... | collective-permute-start | bytes 1179656 | tf_op jit(solution)/shard_map/ppermute | solution.py:293
  64.9 0.8 gather_fusion.6
  65.8 6.7 %collective-permute-done.8 = bf16[2,64,1024]{2,1,0:T(8,128)(2,1)S(1)} collective-permute-done((bf16[2,64,1024]{2,1,0:T(8,128)(2,1)}, bf16[2,64,1024]{2,1,0:T(8,128)(2,1)S(1)}, u32[]{:S(2)}, u32[]{:S(2)}) %collective-permute-start.8) | collective-permute-done | bytes 262176 | tf_op jit(solution)/shard_map/ppermute | solution.py:316
  72.8 1.1 %gather_fusion.7 = bf16[64,2,1024]{2,1,0:T(2,128)(2,1)S(1)} fusion(bf16[2,64,1024]{2,0,1:T(2,128)(2,1)S(1)} %copy.21, s32[1024]{0:T(1024)S(1)} %pad_clamp_fusion), kind=kCustom, calls=%fused_computation.6.clone | custom fusion | bytes 524544 | tf_op jit(solution)/shard_map/jit(_take)/gather | solution.py:317
  74.4 1.0 %copy-done.5 = f32[2,64,1024]{2,1,0:T(8,128)S(1)} copy-done((f32[2,64,1024]{2,1,0:T(8,128)S(1)}, f32[2,64,1024]{2,1,0:T(8,128)}, u32[]{:S(2)}) %copy-start.5) | copy-done | bytes 524312
  75.5 0.9 %copy-done.4 = f32[2,64,1024]{2,1,0:T(8,128)S(1)} copy-done((f32[2,64,1024]{2,1,0:T(8,128)S(1)}, f32[2,64,1024]{2,1,0:T(8,128)}, u32[]{:S(2)}) %copy-start.4) | copy-done | bytes 524312
  76.4 2.1 %collective-permute-start.11 = (bf16[2,64,1024]{2,1,0:T(8,128)(2,1)S(1)}, bf16[2,64,1024]{2,1,0:T(8,128)(2,1)S(1)}, u32[]{:S(2)}, u32[]{:S(2)}) collective-permute-start(bf16[2,64,1024]{2,1,0:T(8,128)(2,1)S(1)} %add_convert_fusion.2), channel_id=1, source_target_pairs={{0,15},{1,0},{2,1},{3,2},{4,3},{5,4},{6,5},{7,6},{8,7},{9,8},{10,9... | collective-permute-start | bytes 786440 | tf_op jit(solution)/shard_map/ppermute | solution.py:314
  78.7 4.2 %collective-permute-done.10 = bf16[2,64,1024]{2,1,0:T(8,128)(2,1)S(1)} collective-permute-done((bf16[2,64,1024]{2,1,0:T(8,128)(2,1)S(1)}, bf16[2,64,1024]{2,1,0:T(8,128)(2,1)S(1)}, u32[]{:S(2)}, u32[]{:S(2)}) %collective-permute-start.10) | collective-permute-done | bytes 262176 | tf_op jit(solution)/shard_map/ppermute | solution.py:315
  82.9 2.6 %collective-permute-done.11 = bf16[2,64,1024]{2,1,0:T(8,128)(2,1)S(1)} collective-permute-done((bf16[2,64,1024]{2,1,0:T(8,128)(2,1)S(1)}, bf16[2,64,1024]{2,1,0:T(8,128)(2,1)S(1)}, u32[]{:S(2)}, u32[]{:S(2)}) %collective-permute-start.11) | collective-permute-done | bytes 262176 | tf_op jit(solution)/shard_map/ppermute | solution.py:314
  85.8 1.0 %add_convert_fusion = bf16[16,16,1024]{2,1,0:T(8,128)(2,1)} fusion(f32[4,16,1024]{2,1,0:T(8,128)S(1)} %bitcast.40, f32[16,16,1024]{2,1,0:T(8,128)S(1)} %bitcast.36, f32[4,16,1024]{2,1,0:T(8,128)S(1)} %bitcast.39, bf16[16,4,1024]{2,1,0:T(4,128)(2,1)S(1)} %convert_element_type.64, bf16[16,4,1024]{2,1,0:T(4,128)(2,1)S(1)} %convert_element_type.63), kind=kLoop, calls=%fused_computation.9 | loop fusion | flops 1835008 | bytes 2359296 | tf_op jit(solution)/shard_map/convert_element_type | solution.py:335
  87.2 1.0 %add_convert_fusion.1 = bf16[16,16,1024]{2,1,0:T(8,128)(2,1)} fusion(f32[4,16,1024]{2,1,0:T(8,128)S(1)} %bitcast.38, f32[16,16,1024]{2,1,0:T(8,128)S(1)} %bitcast.35, f32[4,16,1024]{2,1,0:T(8,128)S(1)} %bitcast.37, bf16[16,4,1024]{2,1,0:T(4,128)(2,1)S(1)} %convert_element_type.61, bf16[16,4,1024]{2,1,0:T(4,128)(2,1)S(1)} %convert_element_type.59), kind=kLoop, calls=%fused_computation.10 | loop fusion | flops 1835008 | bytes 2359296 | tf_op jit(solution)/shard_map/convert_element_type | solution.py:335
  (88 shorter events, 5.9 us)
Async XLA Ops:
  0.6 1.2 %copy-start.3 = (bf16[16,16,1024]{2,1,0:T(8,128)(2,1)S(1)}, bf16[16,16,1024]{2,1,0:T(8,128)(2,1)}, u32[]{:S(2)}) copy-start(bf16[16,16,1024]{2,1,0:T(8,128)(2,1)} %param.22) | copy-start | bytes 1572868
  2.1 17.8 %collective-permute-start = (bf16[2,64,1024]{2,1,0:T(8,128)(2,1)S(1)}, bf16[2,64,1024]{2,1,0:T(8,128)(2,1)S(1)}, u32[]{:S(2)}, u32[]{:S(2)}) collective-permute-start(bf16[2,64,1024]{2,1,0:T(8,128)(2,1)S(1)} %pad_maximum_fusion.2), channel_id=1, source_target_pairs={{0,1},{1,2},{2,3},{3,4},{4,5},{5,6},{6,7},{7,8},{8,9},{9,10},{10,1... | collective-permute-start | bytes 786440 | tf_op jit(solution)/shard_map/ppermute | solution.py:269
  3.7 1.5 %copy-start.2 = (bf16[16,16,1024]{2,1,0:T(8,128)(2,1)S(1)}, bf16[16,16,1024]{2,1,0:T(8,128)(2,1)}, u32[]{:S(2)}) copy-start(bf16[16,16,1024]{2,1,0:T(8,128)(2,1)} %param.21) | copy-start | bytes 1572868
  3.8 16.1 %collective-permute-start.1 = (bf16[2,64,1024]{2,1,0:T(8,128)(2,1)S(1)}, bf16[2,64,1024]{2,1,0:T(8,128)(2,1)S(1)}, u32[]{:S(2)}, u32[]{:S(2)}) collective-permute-start(bf16[2,64,1024]{2,1,0:T(8,128)(2,1)S(1)} %pad_maximum_fusion.3), channel_id=1, source_target_pairs={{0,15},{1,0},{2,1},{3,2},{4,3},{5,4},{6,5},{7,6},{8,7},{9,8},{10,9... | collective-permute-start | bytes 786440 | tf_op jit(solution)/shard_map/ppermute | solution.py:270
  5.4 24.7 %collective-permute-start.4 = (bf16[2,64,1024]{2,1,0:T(8,128)(2,1)S(1)}, bf16[2,64,1024]{2,1,0:T(8,128)(2,1)S(1)}, u32[]{:S(2)}, u32[]{:S(2)}) collective-permute-start(bf16[2,64,1024]{2,1,0:T(8,128)(2,1)S(1)} %maximum_select_fusion), channel_id=1, source_target_pairs={{0,8},{1,9},{2,10},{3,11},{4,12},{5,13},{6,14},{7,15},{8,0},{9,1},... | collective-permute-start | bytes 786440 | tf_op jit(solution)/shard_map/ppermute | solution.py:273
  13.6 0.7 copy-start.8
  15.8 0.7 copy-start.12
  18.3 1.3 %copy-start.9 = (s32[96]{0:T(128)S(1)}, s32[96]{0:T(128)}, u32[]{:S(2)}) copy-start(s32[96]{0:T(128)} %constant.133.clone) | copy-start | bytes 1156
  18.3 1.3 %copy-start.10 = (s32[96]{0:T(128)S(1)}, s32[96]{0:T(128)}, u32[]{:S(2)}) copy-start(s32[96]{0:T(128)} %constant.134.clone) | copy-start | bytes 1156
  18.4 1.3 %copy-start.11 = (s32[96]{0:T(128)S(1)}, s32[96]{0:T(128)}, u32[]{:S(2)}) copy-start(s32[96]{0:T(128)} %constant.135.clone) | copy-start | bytes 1156
  19.9 0.7 copy-start.6
  19.9 0.8 copy-start.7
  20.7 12.2 %collective-permute-start.5 = (bf16[2,32,1024]{2,1,0:T(8,128)(2,1)S(1)}, bf16[2,32,1024]{2,1,0:T(8,128)(2,1)S(1)}, u32[]{:S(2)}, u32[]{:S(2)}) collective-permute-start(bf16[2,32,1024]{2,1,0:T(8,128)(2,1)S(1)} %maximum_select_fusion.1), channel_id=1, source_target_pairs={{0,8},{1,9},{2,10},{3,11},{4,12},{5,13},{6,14},{7,15},{8,0},{9,1},... | collective-permute-start | bytes 393224 | tf_op jit(solution)/shard_map/ppermute | solution.py:281
  25.7 8.9 %collective-permute-start.3 = (bf16[2,96,1024]{2,1,0:T(8,128)(2,1)S(1)}, bf16[2,96,1024]{2,1,0:T(8,128)(2,1)S(1)}, u32[]{:S(2)}, u32[]{:S(2)}) collective-permute-start(bf16[2,96,1024]{2,1,0:T(8,128)(2,1)S(1)} %pad_maximum_fusion.1), channel_id=1, source_target_pairs={{16,0},{17,1},{18,2},{19,3},{20,4},{21,5},{22,6},{23,7},{24,8},{25... | collective-permute-start | bytes 1179656 | tf_op jit(solution)/shard_map/ppermute | solution.py:280
  27.0 7.6 %collective-permute-start.2 = (bf16[2,96,1024]{2,1,0:T(8,128)(2,1)S(1)}, bf16[2,96,1024]{2,1,0:T(8,128)(2,1)S(1)}, u32[]{:S(2)}, u32[]{:S(2)}) collective-permute-start(bf16[2,96,1024]{2,1,0:T(8,128)(2,1)S(1)} %pad_maximum_fusion), channel_id=1, source_target_pairs={{0,16},{1,17},{2,18},{3,19},{4,20},{5,21},{6,22},{7,23},{8,24},{9,... | collective-permute-start | bytes 1179656 | tf_op jit(solution)/shard_map/ppermute | solution.py:279
  34.6 0.7 copy-start.13
  34.6 0.9 %copy-start.14 = (bf16[2,96,1024]{2,1,0:T(8,128)(2,1)}, bf16[2,96,1024]{2,1,0:T(8,128)(2,1)S(1)}, u32[]{:S(2)}) copy-start(bf16[2,96,1024]{2,1,0:T(8,128)(2,1)S(1)} %collective-permute-done.2.refs_4_) | copy-start | bytes 1179652
  52.4 12.4 %collective-permute-start.6 = (bf16[2,32,1024]{2,1,0:T(8,128)(2,1)}, bf16[2,32,1024]{2,1,0:T(8,128)(2,1)S(1)}, u32[]{:S(2)}, u32[]{:S(2)}) collective-permute-start(bf16[2,32,1024]{2,1,0:T(8,128)(2,1)} %get-tuple-element.18), channel_id=1, source_target_pairs={{0,8},{1,9},{2,10},{3,11},{4,12},{5,13},{6,14},{7,15},{8,0},{9,1},... | collective-permute-start | bytes 393224 | tf_op jit(solution)/shard_map/ppermute | solution.py:295
  57.3 15.2 %collective-permute-start.8 = (bf16[2,64,1024]{2,1,0:T(8,128)(2,1)}, bf16[2,64,1024]{2,1,0:T(8,128)(2,1)S(1)}, u32[]{:S(2)}, u32[]{:S(2)}) collective-permute-start(bf16[2,64,1024]{2,1,0:T(8,128)(2,1)} %get-tuple-element.20), channel_id=1, source_target_pairs={{0,8},{1,9},{2,10},{3,11},{4,12},{5,13},{6,14},{7,15},{8,0},{9,1},... | collective-permute-start | bytes 786440 | tf_op jit(solution)/shard_map/ppermute | solution.py:316
  62.1 11.9 %collective-permute-start.7 = (bf16[2,96,1024]{2,1,0:T(8,128)(2,1)}, bf16[2,96,1024]{2,1,0:T(8,128)(2,1)S(1)}, u32[]{:S(2)}, u32[]{:S(2)}) collective-permute-start(bf16[2,96,1024]{2,1,0:T(8,128)(2,1)} %get-tuple-element.19), channel_id=1, source_target_pairs={{0,16},{1,17},{2,18},{3,19},{4,20},{5,21},{6,22},{7,23},{8,24},{9,... | collective-permute-start | bytes 1179656 | tf_op jit(solution)/shard_map/ppermute | solution.py:294
  63.5 10.6 %collective-permute-start.9 = (bf16[2,96,1024]{2,1,0:T(8,128)(2,1)}, bf16[2,96,1024]{2,1,0:T(8,128)(2,1)S(1)}, u32[]{:S(2)}, u32[]{:S(2)}) collective-permute-start(bf16[2,96,1024]{2,1,0:T(8,128)(2,1)} %get-tuple-element.21), channel_id=1, source_target_pairs={{16,0},{17,1},{18,2},{19,3},{20,4},{21,5},{22,6},{23,7},{24,8},{25... | collective-permute-start | bytes 1179656 | tf_op jit(solution)/shard_map/ppermute | solution.py:293
  74.3 1.0 %copy-start.5 = (f32[2,64,1024]{2,1,0:T(8,128)S(1)}, f32[2,64,1024]{2,1,0:T(8,128)}, u32[]{:S(2)}) copy-start(f32[2,64,1024]{2,1,0:T(8,128)} %get-tuple-element.22) | copy-start | bytes 1572868
  75.3 1.0 %copy-start.4 = (f32[2,64,1024]{2,1,0:T(8,128)S(1)}, f32[2,64,1024]{2,1,0:T(8,128)}, u32[]{:S(2)}) copy-start(f32[2,64,1024]{2,1,0:T(8,128)} %get-tuple-element.23) | copy-start | bytes 1572868
  75.4 7.4 %collective-permute-start.10 = (bf16[2,64,1024]{2,1,0:T(8,128)(2,1)S(1)}, bf16[2,64,1024]{2,1,0:T(8,128)(2,1)S(1)}, u32[]{:S(2)}, u32[]{:S(2)}) collective-permute-start(bf16[2,64,1024]{2,1,0:T(8,128)(2,1)S(1)} %add_convert_fusion.3), channel_id=1, source_target_pairs={{0,1},{1,2},{2,3},{3,4},{4,5},{5,6},{6,7},{7,8},{8,9},{9,10},{10,1... | collective-permute-start | bytes 786440 | tf_op jit(solution)/shard_map/ppermute | solution.py:315
  76.4 9.1 %collective-permute-start.11 = (bf16[2,64,1024]{2,1,0:T(8,128)(2,1)S(1)}, bf16[2,64,1024]{2,1,0:T(8,128)(2,1)S(1)}, u32[]{:S(2)}, u32[]{:S(2)}) collective-permute-start(bf16[2,64,1024]{2,1,0:T(8,128)(2,1)S(1)} %add_convert_fusion.2), channel_id=1, source_target_pairs={{0,15},{1,0},{2,1},{3,2},{4,3},{5,4},{6,5},{7,6},{8,7},{9,8},{10,9... | collective-permute-start | bytes 786440 | tf_op jit(solution)/shard_map/ppermute | solution.py:314
  78.7 7.1 %copy-start.1 = (f32[256,1024]{1,0:T(8,128)S(1)}, f32[256,1024]{1,0:T(8,128)}, u32[]{:S(2)}) copy-start(f32[256,1024]{1,0:T(8,128)} %get-tuple-element.24) | copy-start | bytes 3145732
  85.8 1.4 %copy-start = (f32[256,1024]{1,0:T(8,128)S(1)}, f32[256,1024]{1,0:T(8,128)}, u32[]{:S(2)}) copy-start(f32[256,1024]{1,0:T(8,128)} %get-tuple-element.17) | copy-start | bytes 3145732

commit v10 on v9

--- a/solution.py
+++ b/solution.py
@@ -270,7 +270,10 @@
     from_right = lax.ppermute(pair(cols(keys, 0, r), cols(values, 0, r)), "lon", left_pairs)
     top_mid = pair(kf[:edge], vf[:edge])
     bottom_mid = pair(kf[cells - edge :], vf[cells - edge :])
-    pole_mid = lax.ppermute(jnp.where(at_north, top_mid, bottom_mid), both, pole_pairs)
+    partner_src = strip_cell(r - 1 - strip_row, jnp.take(landing, strip_col))
+    pole_mid_rows = lax.ppermute(
+        jnp.take(jnp.where(at_north, top_mid, bottom_mid), partner_src[:edge], axis=1), both, pole_pairs
+    )
     n_side = height * r
     top_send = jnp.concatenate([top_mid, from_left[:, :corner], from_right[:, :corner]], axis=1)
     bottom_send = jnp.concatenate(
@@ -278,11 +281,11 @@
     )
     from_above = lax.ppermute(bottom_send, both, down_pairs)
     from_below = lax.ppermute(top_send, both, up_pairs)
-    pole_corners = lax.ppermute(
-        jnp.where(at_north, top_send[:, edge:], bottom_send[:, edge:]), both, pole_pairs
-    )
-    pole_mid_rows = jnp.take(pole_mid, pole_src[:edge], axis=1)
-    pole_corner_rows = jnp.take(pole_corners, pole_src[edge:] - edge, axis=1)
+    pole_corner_rows = lax.ppermute(
+        jnp.take(jnp.where(at_north, top_send[:, edge:], bottom_send[:, edge:]), partner_src[edge:] - edge, axis=1),
+        both,
+        pole_pairs,
+    )
 
     q2 = queries.reshape(cells, features)
     g2 = grad_out.reshape(cells, features)

time: 89.9 us -> 91.8 us (1.021); the launches traced: 88.2 us -> 91 us
  waiting for transfers between devices: 14.1 us -> 20.4 us
  other arithmetic: 4.76 us -> 3.42 us
  starting transfers between devices: 35.1 us -> 34 us
  local copies, waits for them, and re-layouts: 16.2 us -> 15.1 us
    ppermute x2, waiting for transfers between devices: 0.59 us -> 7.4 us  [the longest x1 7.4 us: on_device(): lax.ppermute(jnp.take(jnp.where(at_north, top_send[:, edge:], bottom_send...]
    select_n x3 -> x2, other arithmetic: 1.57 us -> 0.18 us  [the longest x1 0.09 us: on_device(): jnp.take(jnp.where(at_north, top_mid, bottom_mid), partner_src[:edge], ax...]
    gather x4 -> x3, local copies, waits for them, and re-layouts: 3.84 us -> 3.13 us  [the longest x1 1.23 us: on_device(): partner_src = strip_cell(r - 1 - strip_row, jnp.take(landing, strip_col))]
    unnamed x30 -> x34, local copies, waits for them, and re-layouts: 5.25 us -> 4.85 us
  transfers between devices with their start and end apart: 12 -> 12, of which waited for: 4 -> 4; matrix products, arithmetic and copies ran while one was open for 13% -> 11% of each run, Pallas kernels for 0% -> 0%
where the time goes in v10:
time: 91.8 us; the launch traced here: 91 us
  starting transfers between devices  34 us (37%)
  waiting for transfers between devices  20.4 us (22%)
  Pallas kernels  16.8 us (18%)
  local copies, waits for them, and re-layouts  15.1 us (16%)
  other arithmetic  3.42 us (4%)
  between operations  1.2 us (1%)
    pallas_call x1, Pallas kernels, attention_core(): pl.pallas_call(lambda *refs: attention_kernel(width, n_lat, *refs), out_s...  16.8 us
    ppermute x1, starting transfers between devices, on_device(): lax.ppermute(jnp.take(jnp.where(at_north, top_mid, bottom_mid), partner_s...  8.23 us
    ppermute x1, waiting for transfers between devices, on_device(): lax.ppermute(jnp.take(jnp.where(at_north, top_send[:, edge:], bottom_send...  7.4 us
    ppermute x1, waiting for transfers between devices, on_device(): pole_g_mid = lax.ppermute(pole_g_mid_send, both, pole_pairs)  6.33 us
    ppermute x1, starting transfers between devices, on_device(): pole_g_mid = lax.ppermute(pole_g_mid_send, both, pole_pairs)  5.07 us
    unnamed x34, local copies, waits for them, and re-layouts  4.85 us
    ppermute x1, starting transfers between devices, on_device(): pole_g_corners = lax.ppermute(pole_g_corner_send, both, pole_pairs)  4.67 us
    ppermute x1, starting transfers between devices, on_device(): lax.ppermute(jnp.take(jnp.where(at_north, top_send[:, edge:], bottom_send...  4.36 us
  transfers between devices with their start and end apart: 12, of which 4 were waited for; matrix products, arithmetic and copies ran while one was open for 11% of the time, Pallas kernels for 0%

profile of v10, /device:TPU:32, one launch (start us, length us, event | category | flops | bytes accessed | tf_op | source)
XLA Modules:
  0.0 91.0 jit_solution(9313521191553264898)
XLA Ops:
  0.6 1.2 %fusion.17 = (bf16[16,4,1024]{2,1,0:T(4,128)(2,1)S(1)}, bf16[16,4,1024]{2,1,0:T(4,128)(2,1)S(1)}) fusion(bf16[16,16,1024]{2,1,0:T(8,128)(2,1)} %param.19), kind=kLoop, calls=%fused_computation.87 | loop fusion | bytes 524288 | tf_op jit(solution)/shard_map/slice | solution.py:267
  2.1 1.2 %collective-permute-start.1 = (bf16[2,64,1024]{2,1,0:T(8,128)(2,1)S(1)}, bf16[2,64,1024]{2,1,0:T(8,128)(2,1)S(1)}, u32[]{:S(2)}, u32[]{:S(2)}) collective-permute-start(bf16[2,64,1024]{2,1,0:T(8,128)(2,1)S(1)} %pad_maximum_fusion.3), channel_id=1, source_target_pairs={{0,15},{1,0},{2,1},{3,2},{4,3},{5,4},{6,5},{7,6},{8,7},{9,8},{10,9... | collective-permute-start | bytes 786440 | tf_op jit(solution)/shard_map/ppermute | solution.py:270
  3.4 1.0 %collective-permute-start = (bf16[2,64,1024]{2,1,0:T(8,128)(2,1)S(1)}, bf16[2,64,1024]{2,1,0:T(8,128)(2,1)S(1)}, u32[]{:S(2)}, u32[]{:S(2)}) collective-permute-start(bf16[2,64,1024]{2,1,0:T(8,128)(2,1)S(1)} %pad_maximum_fusion.2), channel_id=1, source_target_pairs={{0,1},{1,2},{2,3},{3,4},{4,5},{5,6},{6,7},{7,8},{8,9},{9,10},{10,1... | collective-permute-start | bytes 786440 | tf_op jit(solution)/shard_map/ppermute | solution.py:269
  4.4 0.7 copy-done.8
  5.1 0.7 gather_fusion
  5.9 0.6 copy-done.12
  6.5 0.6 scatter_custom_fusion
  7.2 1.2 %gather_fusion.4 = s32[96]{0:T(128)S(1)} fusion(s32[24]{0:T(128)S(1)} %scatter_custom_fusion, s32[1024]{0:T(1024)S(1)} %pad_clamp_fusion.4), kind=kCustom, calls=%fused_computation.3.clone | custom fusion | bytes 1152 | tf_op jit(solution)/shard_map/jit(_take)/gather | solution.py:258
  8.5 1.2 %gather_fusion.1 = s32[96]{0:T(128)S(1)} fusion(s32[24]{0:T(128)S(1)} %and_select_fusion.2, s32[1024]{0:T(1024)S(1)} %pad_clamp_fusion.4), kind=kCustom, calls=%fused_computation.clone | custom fusion | bytes 1152 | tf_op jit(solution)/shard_map/jit(_take)/gather | solution.py:273
  10.1 1.1 %gather_fusion.2 = bf16[64,2,1024]{2,1,0:T(2,128)(2,1)S(1)} fusion(bf16[2,64,1024]{2,0,1:T(2,128)(2,1)S(1)} %copy.15, s32[1024]{0:T(1024)S(1)} %pad_clamp_fusion.3), kind=kCustom, calls=%fused_computation.1.clone | custom fusion | bytes 524544 | tf_op jit(solution)/shard_map/jit(_take)/gather | solution.py:275
  11.3 8.2 %collective-permute-start.4 = (bf16[2,64,1024]{2,1,0:T(8,128)(2,1)S(1)}, bf16[2,64,1024]{2,1,0:T(8,128)(2,1)S(1)}, u32[]{:S(2)}, u32[]{:S(2)}) collective-permute-start(bf16[2,64,1024]{2,1,0:T(8,128)(2,1)S(1)} %fusion.2), channel_id=1, source_target_pairs={{0,8},{1,9},{2,10},{3,11},{4,12},{5,13},{6,14},{7,15},{8,0},{9,1},... | collective-permute-start | bytes 786440 | tf_op jit(solution)/shard_map/ppermute | solution.py:274
  19.7 0.6 copy-done.6
  20.7 1.3 %collective-permute-start.3 = (bf16[2,96,1024]{2,1,0:T(8,128)(2,1)S(1)}, bf16[2,96,1024]{2,1,0:T(8,128)(2,1)S(1)}, u32[]{:S(2)}, u32[]{:S(2)}) collective-permute-start(bf16[2,96,1024]{2,1,0:T(8,128)(2,1)S(1)} %pad_maximum_fusion.1), channel_id=1, source_target_pairs={{16,0},{17,1},{18,2},{19,3},{20,4},{21,5},{22,6},{23,7},{24,8},{25... | collective-permute-start | bytes 1179656 | tf_op jit(solution)/shard_map/ppermute | solution.py:283
  22.0 3.1 %collective-permute-start.2 = (bf16[2,96,1024]{2,1,0:T(8,128)(2,1)S(1)}, bf16[2,96,1024]{2,1,0:T(8,128)(2,1)S(1)}, u32[]{:S(2)}, u32[]{:S(2)}) collective-permute-start(bf16[2,96,1024]{2,1,0:T(8,128)(2,1)S(1)} %pad_maximum_fusion), channel_id=1, source_target_pairs={{0,16},{1,17},{2,18},{3,19},{4,20},{5,21},{6,22},{7,23},{8,24},{9,... | collective-permute-start | bytes 1179656 | tf_op jit(solution)/shard_map/ppermute | solution.py:282
  25.0 0.8 gather_fusion.3
  25.9 4.4 %collective-permute-start.5 = (bf16[2,32,1024]{2,1,0:T(8,128)(2,1)S(1)}, bf16[2,32,1024]{2,1,0:T(8,128)(2,1)S(1)}, u32[]{:S(2)}, u32[]{:S(2)}) collective-permute-start(bf16[2,32,1024]{2,1,0:T(8,128)(2,1)S(1)} %fusion.4), channel_id=1, source_target_pairs={{0,8},{1,9},{2,10},{3,11},{4,12},{5,13},{6,14},{7,15},{8,0},{9,1},... | collective-permute-start | bytes 393224 | tf_op jit(solution)/shard_map/ppermute | solution.py:284
  30.4 7.4 %collective-permute-done.5.refs_7_ = bf16[2,32,1024]{2,1,0:T(8,128)(2,1)S(1)} collective-permute-done((bf16[2,32,1024]{2,1,0:T(8,128)(2,1)S(1)}, bf16[2,32,1024]{2,1,0:T(8,128)(2,1)S(1)}, u32[]{:S(2)}, u32[]{:S(2)}) %collective-permute-start.5) | collective-permute-done | bytes 131104 | tf_op jit(solution)/shard_map/ppermute | solution.py:284
  37.8 0.6 copy-done.16
  38.8 16.8 %neighbourhood_attention_bwd.1 = (bf16[256,1024]{1,0:T(8,128)(2,1)}, f32[256,1024]{1,0:T(8,128)}, f32[256,1024]{1,0:T(8,128)}, bf16[2,96,1024]{2,1,0:T(8,128)(2,...) custom-call(bf16[256,1024]{1,0:T(8,128)(2,1)} %bitcast.51, ...), custom_call_target="tpu_custom_call" | custom-call | flops 2013265920 | bytes 8650752 | tf_op jit(solution)/shard_map/neighbourhood_attention_bwd/pallas_call | solution.py:194
  55.6 4.7 %collective-permute-start.6 = (bf16[2,32,1024]{2,1,0:T(8,128)(2,1)}, bf16[2,32,1024]{2,1,0:T(8,128)(2,1)S(1)}, u32[]{:S(2)}, u32[]{:S(2)}) collective-permute-start(bf16[2,32,1024]{2,1,0:T(8,128)(2,1)} %get-tuple-element.17), channel_id=1, source_target_pairs={{0,8},{1,9},{2,10},{3,11},{4,12},{5,13},{6,14},{7,15},{8,0},{9,1},... | collective-permute-start | bytes 393224 | tf_op jit(solution)/shard_map/ppermute | solution.py:298
  60.3 5.1 %collective-permute-start.8 = (bf16[2,64,1024]{2,1,0:T(8,128)(2,1)}, bf16[2,64,1024]{2,1,0:T(8,128)(2,1)S(1)}, u32[]{:S(2)}, u32[]{:S(2)}) collective-permute-start(bf16[2,64,1024]{2,1,0:T(8,128)(2,1)} %get-tuple-element.19), channel_id=1, source_target_pairs={{0,8},{1,9},{2,10},{3,11},{4,12},{5,13},{6,14},{7,15},{8,0},{9,1},... | collective-permute-start | bytes 786440 | tf_op jit(solution)/shard_map/ppermute | solution.py:319
  65.4 1.3 %collective-permute-start.7 = (bf16[2,96,1024]{2,1,0:T(8,128)(2,1)}, bf16[2,96,1024]{2,1,0:T(8,128)(2,1)S(1)}, u32[]{:S(2)}, u32[]{:S(2)}) collective-permute-start(bf16[2,96,1024]{2,1,0:T(8,128)(2,1)} %get-tuple-element.18), channel_id=1, source_target_pairs={{0,16},{1,17},{2,18},{3,19},{4,20},{5,21},{6,22},{7,23},{8,24},{9,... | collective-permute-start | bytes 1179656 | tf_op jit(solution)/shard_map/ppermute | solution.py:297
  66.7 1.3 %collective-permute-start.9 = (bf16[2,96,1024]{2,1,0:T(8,128)(2,1)}, bf16[2,96,1024]{2,1,0:T(8,128)(2,1)S(1)}, u32[]{:S(2)}, u32[]{:S(2)}) collective-permute-start(bf16[2,96,1024]{2,1,0:T(8,128)(2,1)} %get-tuple-element.20), channel_id=1, source_target_pairs={{16,0},{17,1},{18,2},{19,3},{20,4},{21,5},{22,6},{23,7},{24,8},{25... | collective-permute-start | bytes 1179656 | tf_op jit(solution)/shard_map/ppermute | solution.py:296
  68.2 0.8 gather_fusion.5
  69.1 6.3 %collective-permute-done.8 = bf16[2,64,1024]{2,1,0:T(8,128)(2,1)S(1)} collective-permute-done((bf16[2,64,1024]{2,1,0:T(8,128)(2,1)}, bf16[2,64,1024]{2,1,0:T(8,128)(2,1)S(1)}, u32[]{:S(2)}, u32[]{:S(2)}) %collective-permute-start.8) | collective-permute-done | bytes 262176 | tf_op jit(solution)/shard_map/ppermute | solution.py:319
  75.7 1.1 %gather_fusion.6 = bf16[64,2,1024]{2,1,0:T(2,128)(2,1)S(1)} fusion(bf16[2,64,1024]{2,0,1:T(2,128)(2,1)S(1)} %copy.21, s32[1024]{0:T(1024)S(1)} %pad_clamp_fusion), kind=kCustom, calls=%fused_computation.4.clone | custom fusion | bytes 524544 | tf_op jit(solution)/shard_map/jit(_take)/gather | solution.py:320
  77.2 1.0 %copy-done.5 = f32[2,64,1024]{2,1,0:T(8,128)S(1)} copy-done((f32[2,64,1024]{2,1,0:T(8,128)S(1)}, f32[2,64,1024]{2,1,0:T(8,128)}, u32[]{:S(2)}) %copy-start.5) | copy-done | bytes 524312
  79.3 2.1 %collective-permute-start.11 = (bf16[2,64,1024]{2,1,0:T(8,128)(2,1)S(1)}, bf16[2,64,1024]{2,1,0:T(8,128)(2,1)S(1)}, u32[]{:S(2)}, u32[]{:S(2)}) collective-permute-start(bf16[2,64,1024]{2,1,0:T(8,128)(2,1)S(1)} %add_convert_fusion.2), channel_id=1, source_target_pairs={{0,15},{1,0},{2,1},{3,2},{4,3},{5,4},{6,5},{7,6},{8,7},{9,8},{10,9... | collective-permute-start | bytes 786440 | tf_op jit(solution)/shard_map/ppermute | solution.py:317
  81.6 4.3 %collective-permute-done.10 = bf16[2,64,1024]{2,1,0:T(8,128)(2,1)S(1)} collective-permute-done((bf16[2,64,1024]{2,1,0:T(8,128)(2,1)S(1)}, bf16[2,64,1024]{2,1,0:T(8,128)(2,1)S(1)}, u32[]{:S(2)}, u32[]{:S(2)}) %collective-permute-start.10) | collective-permute-done | bytes 262176 | tf_op jit(solution)/shard_map/ppermute | solution.py:318
  86.0 2.4 %collective-permute-done.11 = bf16[2,64,1024]{2,1,0:T(8,128)(2,1)S(1)} collective-permute-done((bf16[2,64,1024]{2,1,0:T(8,128)(2,1)S(1)}, bf16[2,64,1024]{2,1,0:T(8,128)(2,1)S(1)}, u32[]{:S(2)}, u32[]{:S(2)}) %collective-permute-start.11) | collective-permute-done | bytes 262176 | tf_op jit(solution)/shard_map/ppermute | solution.py:317
  88.6 1.0 %add_convert_fusion = bf16[16,16,1024]{2,1,0:T(8,128)(2,1)} fusion(f32[4,16,1024]{2,1,0:T(8,128)S(1)} %bitcast.45, f32[16,16,1024]{2,1,0:T(8,128)S(1)} %bitcast.48, f32[4,16,1024]{2,1,0:T(8,128)S(1)} %bitcast.46, bf16[16,4,1024]{2,1,0:T(4,128)(2,1)S(1)} %convert_element_type.64, bf16[16,4,1024]{2,1,0:T(4,128)(2,1)S(1)} %convert_element_type.63), kind=kLoop, calls=%fused_computation.8 | loop fusion | flops 1835008 | bytes 2359296 | tf_op jit(solution)/shard_map/convert_element_type | solution.py:338
  90.0 1.0 %add_convert_fusion.1 = bf16[16,16,1024]{2,1,0:T(8,128)(2,1)} fusion(f32[4,16,1024]{2,1,0:T(8,128)S(1)} %bitcast.43, f32[16,16,1024]{2,1,0:T(8,128)S(1)} %bitcast.47, f32[4,16,1024]{2,1,0:T(8,128)S(1)} %bitcast.44, bf16[16,4,1024]{2,1,0:T(4,128)(2,1)S(1)} %convert_element_type.61, bf16[16,4,1024]{2,1,0:T(4,128)(2,1)S(1)} %convert_element_type.59), kind=kLoop, calls=%fused_computation.9 | loop fusion | flops 1835008 | bytes 2359296 | tf_op jit(solution)/shard_map/convert_element_type | solution.py:338
  (88 shorter events, 4.6 us)
Async XLA Ops:
  0.6 1.2 %copy-start.3 = (bf16[16,16,1024]{2,1,0:T(8,128)(2,1)S(1)}, bf16[16,16,1024]{2,1,0:T(8,128)(2,1)}, u32[]{:S(2)}) copy-start(bf16[16,16,1024]{2,1,0:T(8,128)(2,1)} %param.20) | copy-start | bytes 1572868
  2.1 17.6 %collective-permute-start.1 = (bf16[2,64,1024]{2,1,0:T(8,128)(2,1)S(1)}, bf16[2,64,1024]{2,1,0:T(8,128)(2,1)S(1)}, u32[]{:S(2)}, u32[]{:S(2)}) collective-permute-start(bf16[2,64,1024]{2,1,0:T(8,128)(2,1)S(1)} %pad_maximum_fusion.3), channel_id=1, source_target_pairs={{0,15},{1,0},{2,1},{3,2},{4,3},{5,4},{6,5},{7,6},{8,7},{9,8},{10,9... | collective-permute-start | bytes 786440 | tf_op jit(solution)/shard_map/ppermute | solution.py:270
  3.3 2.5 %copy-start.2 = (bf16[16,16,1024]{2,1,0:T(8,128)(2,1)S(1)}, bf16[16,16,1024]{2,1,0:T(8,128)(2,1)}, u32[]{:S(2)}) copy-start(bf16[16,16,1024]{2,1,0:T(8,128)(2,1)} %param.19) | copy-start | bytes 1572868
  3.4 16.3 %collective-permute-start = (bf16[2,64,1024]{2,1,0:T(8,128)(2,1)S(1)}, bf16[2,64,1024]{2,1,0:T(8,128)(2,1)S(1)}, u32[]{:S(2)}, u32[]{:S(2)}) collective-permute-start(bf16[2,64,1024]{2,1,0:T(8,128)(2,1)S(1)} %pad_maximum_fusion.2), channel_id=1, source_target_pairs={{0,1},{1,2},{2,3},{3,4},{4,5},{5,6},{6,7},{7,8},{8,9},{9,10},{10,1... | collective-permute-start | bytes 786440 | tf_op jit(solution)/shard_map/ppermute | solution.py:269
  4.4 0.7 copy-start.8
  5.9 0.7 copy-start.12
  8.4 1.3 %copy-start.9 = (s32[96]{0:T(128)S(1)}, s32[96]{0:T(128)}, u32[]{:S(2)}) copy-start(s32[96]{0:T(128)} %constant.132.clone) | copy-start | bytes 1156
  8.4 1.3 %copy-start.10 = (s32[96]{0:T(128)S(1)}, s32[96]{0:T(128)}, u32[]{:S(2)}) copy-start(s32[96]{0:T(128)} %constant.131.clone) | copy-start | bytes 1156
  8.5 1.3 %copy-start.11 = (s32[96]{0:T(128)S(1)}, s32[96]{0:T(128)}, u32[]{:S(2)}) copy-start(s32[96]{0:T(128)} %constant.130.clone) | copy-start | bytes 1156
  11.3 19.1 %collective-permute-start.4 = (bf16[2,64,1024]{2,1,0:T(8,128)(2,1)S(1)}, bf16[2,64,1024]{2,1,0:T(8,128)(2,1)S(1)}, u32[]{:S(2)}, u32[]{:S(2)}) collective-permute-start(bf16[2,64,1024]{2,1,0:T(8,128)(2,1)S(1)} %fusion.2), channel_id=1, source_target_pairs={{0,8},{1,9},{2,10},{3,11},{4,12},{5,13},{6,14},{7,15},{8,0},{9,1},... | collective-permute-start | bytes 786440 | tf_op jit(solution)/shard_map/ppermute | solution.py:274
  19.7 0.7 copy-start.6
  19.7 0.8 copy-start.7
  20.7 17.1 %collective-permute-start.3 = (bf16[2,96,1024]{2,1,0:T(8,128)(2,1)S(1)}, bf16[2,96,1024]{2,1,0:T(8,128)(2,1)S(1)}, u32[]{:S(2)}, u32[]{:S(2)}) collective-permute-start(bf16[2,96,1024]{2,1,0:T(8,128)(2,1)S(1)} %pad_maximum_fusion.1), channel_id=1, source_target_pairs={{16,0},{17,1},{18,2},{19,3},{20,4},{21,5},{22,6},{23,7},{24,8},{25... | collective-permute-start | bytes 1179656 | tf_op jit(solution)/shard_map/ppermute | solution.py:283
  22.0 15.8 %collective-permute-start.2 = (bf16[2,96,1024]{2,1,0:T(8,128)(2,1)S(1)}, bf16[2,96,1024]{2,1,0:T(8,128)(2,1)S(1)}, u32[]{:S(2)}, u32[]{:S(2)}) collective-permute-start(bf16[2,96,1024]{2,1,0:T(8,128)(2,1)S(1)} %pad_maximum_fusion), channel_id=1, source_target_pairs={{0,16},{1,17},{2,18},{3,19},{4,20},{5,21},{6,22},{7,23},{8,24},{9,... | collective-permute-start | bytes 1179656 | tf_op jit(solution)/shard_map/ppermute | solution.py:282
  25.9 11.9 %collective-permute-start.5 = (bf16[2,32,1024]{2,1,0:T(8,128)(2,1)S(1)}, bf16[2,32,1024]{2,1,0:T(8,128)(2,1)S(1)}, u32[]{:S(2)}, u32[]{:S(2)}) collective-permute-start(bf16[2,32,1024]{2,1,0:T(8,128)(2,1)S(1)} %fusion.4), channel_id=1, source_target_pairs={{0,8},{1,9},{2,10},{3,11},{4,12},{5,13},{6,14},{7,15},{8,0},{9,1},... | collective-permute-start | bytes 393224 | tf_op jit(solution)/shard_map/ppermute | solution.py:284
  30.4 7.4 %copy-start.15 = (bf16[2,64,1024]{2,1,0:T(8,128)(2,1)}, bf16[2,64,1024]{2,1,0:T(8,128)(2,1)S(1)}, u32[]{:S(2)}) copy-start(bf16[2,64,1024]{2,1,0:T(8,128)(2,1)S(1)} %collective-permute-done.4.refs_6_) | copy-start | bytes 786436
  37.8 0.7 copy-start.16
  37.8 0.8 copy-start.13
  37.8 0.9 %copy-start.14 = (bf16[2,96,1024]{2,1,0:T(8,128)(2,1)}, bf16[2,96,1024]{2,1,0:T(8,128)(2,1)S(1)}, u32[]{:S(2)}) copy-start(bf16[2,96,1024]{2,1,0:T(8,128)(2,1)S(1)} %collective-permute-done.2.refs_4_) | copy-start | bytes 1179652
  55.6 12.4 %collective-permute-start.6 = (bf16[2,32,1024]{2,1,0:T(8,128)(2,1)}, bf16[2,32,1024]{2,1,0:T(8,128)(2,1)S(1)}, u32[]{:S(2)}, u32[]{:S(2)}) collective-permute-start(bf16[2,32,1024]{2,1,0:T(8,128)(2,1)} %get-tuple-element.17), channel_id=1, source_target_pairs={{0,8},{1,9},{2,10},{3,11},{4,12},{5,13},{6,14},{7,15},{8,0},{9,1},... | collective-permute-start | bytes 393224 | tf_op jit(solution)/shard_map/ppermute | solution.py:298
  60.3 15.1 %collective-permute-start.8 = (bf16[2,64,1024]{2,1,0:T(8,128)(2,1)}, bf16[2,64,1024]{2,1,0:T(8,128)(2,1)S(1)}, u32[]{:S(2)}, u32[]{:S(2)}) collective-permute-start(bf16[2,64,1024]{2,1,0:T(8,128)(2,1)} %get-tuple-element.19), channel_id=1, source_target_pairs={{0,8},{1,9},{2,10},{3,11},{4,12},{5,13},{6,14},{7,15},{8,0},{9,1},... | collective-permute-start | bytes 786440 | tf_op jit(solution)/shard_map/ppermute | solution.py:319
  65.4 11.6 %collective-permute-start.7 = (bf16[2,96,1024]{2,1,0:T(8,128)(2,1)}, bf16[2,96,1024]{2,1,0:T(8,128)(2,1)S(1)}, u32[]{:S(2)}, u32[]{:S(2)}) collective-permute-start(bf16[2,96,1024]{2,1,0:T(8,128)(2,1)} %get-tuple-element.18), channel_id=1, source_target_pairs={{0,16},{1,17},{2,18},{3,19},{4,20},{5,21},{6,22},{7,23},{8,24},{9,... | collective-permute-start | bytes 1179656 | tf_op jit(solution)/shard_map/ppermute | solution.py:297
  66.7 10.3 %collective-permute-start.9 = (bf16[2,96,1024]{2,1,0:T(8,128)(2,1)}, bf16[2,96,1024]{2,1,0:T(8,128)(2,1)S(1)}, u32[]{:S(2)}, u32[]{:S(2)}) collective-permute-start(bf16[2,96,1024]{2,1,0:T(8,128)(2,1)} %get-tuple-element.20), channel_id=1, source_target_pairs={{16,0},{17,1},{18,2},{19,3},{20,4},{21,5},{22,6},{23,7},{24,8},{25... | collective-permute-start | bytes 1179656 | tf_op jit(solution)/shard_map/ppermute | solution.py:296
  77.2 1.0 %copy-start.5 = (f32[2,64,1024]{2,1,0:T(8,128)S(1)}, f32[2,64,1024]{2,1,0:T(8,128)}, u32[]{:S(2)}) copy-start(f32[2,64,1024]{2,1,0:T(8,128)} %get-tuple-element.21) | copy-start | bytes 1572868
  78.2 1.0 %copy-start.4 = (f32[2,64,1024]{2,1,0:T(8,128)S(1)}, f32[2,64,1024]{2,1,0:T(8,128)}, u32[]{:S(2)}) copy-start(f32[2,64,1024]{2,1,0:T(8,128)} %get-tuple-element.22) | copy-start | bytes 1572868
  78.3 7.6 %collective-permute-start.10 = (bf16[2,64,1024]{2,1,0:T(8,128)(2,1)S(1)}, bf16[2,64,1024]{2,1,0:T(8,128)(2,1)S(1)}, u32[]{:S(2)}, u32[]{:S(2)}) collective-permute-start(bf16[2,64,1024]{2,1,0:T(8,128)(2,1)S(1)} %add_convert_fusion.3), channel_id=1, source_target_pairs={{0,1},{1,2},{2,3},{3,4},{4,5},{5,6},{6,7},{7,8},{8,9},{9,10},{10,1... | collective-permute-start | bytes 786440 | tf_op jit(solution)/shard_map/ppermute | solution.py:318
  79.3 9.1 %collective-permute-start.11 = (bf16[2,64,1024]{2,1,0:T(8,128)(2,1)S(1)}, bf16[2,64,1024]{2,1,0:T(8,128)(2,1)S(1)}, u32[]{:S(2)}, u32[]{:S(2)}) collective-permute-start(bf16[2,64,1024]{2,1,0:T(8,128)(2,1)S(1)} %add_convert_fusion.2), channel_id=1, source_target_pairs={{0,15},{1,0},{2,1},{3,2},{4,3},{5,4},{6,5},{7,6},{8,7},{9,8},{10,9... | collective-permute-start | bytes 786440 | tf_op jit(solution)/shard_map/ppermute | solution.py:317
  81.6 7.0 %copy-start.1 = (f32[256,1024]{1,0:T(8,128)S(1)}, f32[256,1024]{1,0:T(8,128)}, u32[]{:S(2)}) copy-start(f32[256,1024]{1,0:T(8,128)} %get-tuple-element.23) | copy-start | bytes 3145732
  88.6 1.4 %copy-start = (f32[256,1024]{1,0:T(8,128)S(1)}, f32[256,1024]{1,0:T(8,128)}, u32[]{:S(2)}) copy-start(f32[256,1024]{1,0:T(8,128)} %get-tuple-element.16) | copy-start | bytes 3145732

commit v11 on v9

--- a/solution.py
+++ b/solution.py
@@ -69,7 +69,7 @@
     tn = (((0,), (0,)), ((), ()))
 
     def both_heads(qab, gab, kp, vp):
-        s = lax.dot_general(qab, kp, nt, preferred_element_type=jnp.float32) * scale + bias_ref[...]
+        s = lax.dot_general(qab, kp, nt, preferred_element_type=jnp.float32) + bias_ref[...]
         m = jnp.max(s, axis=1, keepdims=True)
         e = jnp.exp(s - m)
         total = jnp.sum(e, axis=1, keepdims=True)
@@ -152,13 +152,14 @@
             vp = gather_keys(v_own, 1, t, lanes)
             lo = lax.broadcasted_iota(jnp.int32, qp.shape, 1) < HEAD_DIM
             zero = jnp.zeros_like(qp)
-            qab = jnp.concatenate([jnp.where(lo, qp, zero), jnp.where(lo, zero, qp)], axis=0)
+            qs = qp * jnp.asarray(scale, qp.dtype)
+            qab = jnp.concatenate([jnp.where(lo, qs, zero), jnp.where(lo, zero, qs)], axis=0)
             gab = jnp.concatenate([jnp.where(lo, gp, zero), jnp.where(lo, zero, gp)], axis=0)
             ds, w = both_heads(qab, gab, kp, vp)
             dq_ab = jnp.dot(ds, kp, preferred_element_type=jnp.float32)
             dq = jnp.where(lo, dq_ab[:tq], dq_ab[tq:]) * scale
             dq_ref[pl.ds(t * tq, tq), lanes] = dq.astype(dq_ref.dtype)
-            dk = lax.dot_general(ds, qab, tn, preferred_element_type=jnp.float32) * scale
+            dk = lax.dot_general(ds, qab, tn, preferred_element_type=jnp.float32)
             dv = lax.dot_general(w, gab, tn, preferred_element_type=jnp.float32)
             scatter_grads(dk, dk_own, 0, t, lanes)
             scatter_grads(dv, dv_own, 1, t, lanes)

time: 89.9 us -> 88.6 us (0.986)
  Pallas kernels: 16.9 us -> 15.5 us
    pallas_call x1, Pallas kernels: 16.9 us -> 15.5 us  [attention_core(): pl.pallas_call(lambda *refs: attention_kernel(width, n_lat, *refs), out_s...]
  transfers between devices with their start and end apart: 12 -> 12, of which waited for: 4 -> 4; matrix products, arithmetic and copies ran while one was open for 13% -> 14% of each run, Pallas kernels for 0% -> 0%
where the time goes in v11:
time: 88.6 us; the launch traced here: 86.9 us
  starting transfers between devices  35.1 us (40%)
  local copies, waits for them, and re-layouts  16.2 us (18%)
  Pallas kernels  15.5 us (17%)
  waiting for transfers between devices  14.1 us (16%)
  other arithmetic  4.76 us (5%)
  between operations  1.21 us (1%)
    pallas_call x1, Pallas kernels, attention_core(): pl.pallas_call(lambda *refs: attention_kernel(width, n_lat, *refs), out_s...  15.5 us
    ppermute x1, starting transfers between devices, on_device(): lax.ppermute(jnp.where(at_north, top_mid, bottom_mid), both, pole_pairs)  8.2 us
    ppermute x1, waiting for transfers between devices, on_device(): pole_g_mid = lax.ppermute(pole_g_mid_send, both, pole_pairs)  6.68 us
    unnamed x30, local copies, waits for them, and re-layouts  5.25 us
    ppermute x1, starting transfers between devices, on_device(): lax.ppermute(jnp.where(at_north, top_send[:, edge:], bottom_send[:, edge:...  4.94 us
    ppermute x1, starting transfers between devices, on_device(): pole_g_corners = lax.ppermute(pole_g_corner_send, both, pole_pairs)  4.94 us
    ppermute x1, starting transfers between devices, on_device(): pole_g_mid = lax.ppermute(pole_g_mid_send, both, pole_pairs)  4.8 us
    ppermute x1, waiting for transfers between devices, on_device(): lax.ppermute(side_send(right_g, edge + corner), 'lon', right_pairs)  4.16 us
  transfers between devices with their start and end apart: 12, of which 4 were waited for; matrix products, arithmetic and copies ran while one was open for 14% of the time, Pallas kernels for 0%

profile of v11, /device:TPU:32, one launch (start us, length us, event | category | flops | bytes accessed | tf_op | source)
XLA Modules:
  0.0 86.9 jit_solution(3818267392204066528)
XLA Ops:
  0.6 1.2 %fusion.15 = (bf16[16,4,1024]{2,1,0:T(4,128)(2,1)S(1)}, bf16[16,4,1024]{2,1,0:T(4,128)(2,1)S(1)}) fusion(bf16[16,16,1024]{2,1,0:T(8,128)(2,1)} %param.21), kind=kLoop, calls=%fused_computation.87 | loop fusion | bytes 524288 | tf_op jit(solution)/shard_map/slice | solution.py:268
  2.1 1.7 %collective-permute-start = (bf16[2,64,1024]{2,1,0:T(8,128)(2,1)S(1)}, bf16[2,64,1024]{2,1,0:T(8,128)(2,1)S(1)}, u32[]{:S(2)}, u32[]{:S(2)}) collective-permute-start(bf16[2,64,1024]{2,1,0:T(8,128)(2,1)S(1)} %pad_maximum_fusion.2), channel_id=1, source_target_pairs={{0,1},{1,2},{2,3},{3,4},{4,5},{5,6},{6,7},{7,8},{8,9},{9,10},{10,1... | collective-permute-start | bytes 786440 | tf_op jit(solution)/shard_map/ppermute | solution.py:270
  3.8 1.4 %collective-permute-start.1 = (bf16[2,64,1024]{2,1,0:T(8,128)(2,1)S(1)}, bf16[2,64,1024]{2,1,0:T(8,128)(2,1)S(1)}, u32[]{:S(2)}, u32[]{:S(2)}) collective-permute-start(bf16[2,64,1024]{2,1,0:T(8,128)(2,1)S(1)} %pad_maximum_fusion.3), channel_id=1, source_target_pairs={{0,15},{1,0},{2,1},{3,2},{4,3},{5,4},{6,5},{7,6},{8,7},{9,8},{10,9... | collective-permute-start | bytes 786440 | tf_op jit(solution)/shard_map/ppermute | solution.py:271
  5.4 8.2 %collective-permute-start.4 = (bf16[2,64,1024]{2,1,0:T(8,128)(2,1)S(1)}, bf16[2,64,1024]{2,1,0:T(8,128)(2,1)S(1)}, u32[]{:S(2)}, u32[]{:S(2)}) collective-permute-start(bf16[2,64,1024]{2,1,0:T(8,128)(2,1)S(1)} %maximum_select_fusion), channel_id=1, source_target_pairs={{0,8},{1,9},{2,10},{3,11},{4,12},{5,13},{6,14},{7,15},{8,0},{9,1},... | collective-permute-start | bytes 786440 | tf_op jit(solution)/shard_map/ppermute | solution.py:274
  13.6 0.7 copy-done.8
  14.3 0.7 gather_fusion
  15.1 0.7 gather_fusion.4
  17.1 1.2 %gather_fusion.5 = s32[96]{0:T(128)S(1)} fusion(s32[24]{0:T(128)S(1)} %scatter_custom_fusion, s32[1024]{0:T(1024)S(1)} %pad_clamp_fusion.5), kind=kCustom, calls=%fused_computation.5.clone | custom fusion | bytes 1152 | tf_op jit(solution)/shard_map/jit(_take)/gather | solution.py:259
  18.4 1.2 %gather_fusion.1 = s32[96]{0:T(128)S(1)} fusion(s32[24]{0:T(128)S(1)} %get-tuple-element.64, s32[1024]{0:T(1024)S(1)} %pad_clamp_fusion.5), kind=kCustom, calls=%fused_computation.1.clone | custom fusion | bytes 1152 | tf_op jit(solution)/shard_map/jit(_take)/gather | solution.py:258
  20.7 4.9 %collective-permute-start.5 = (bf16[2,32,1024]{2,1,0:T(8,128)(2,1)S(1)}, bf16[2,32,1024]{2,1,0:T(8,128)(2,1)S(1)}, u32[]{:S(2)}, u32[]{:S(2)}) collective-permute-start(bf16[2,32,1024]{2,1,0:T(8,128)(2,1)S(1)} %maximum_select_fusion.1), channel_id=1, source_target_pairs={{0,8},{1,9},{2,10},{3,11},{4,12},{5,13},{6,14},{7,15},{8,0},{9,1},... | collective-permute-start | bytes 393224 | tf_op jit(solution)/shard_map/ppermute | solution.py:282
  25.7 1.3 %collective-permute-start.3 = (bf16[2,96,1024]{2,1,0:T(8,128)(2,1)S(1)}, bf16[2,96,1024]{2,1,0:T(8,128)(2,1)S(1)}, u32[]{:S(2)}, u32[]{:S(2)}) collective-permute-start(bf16[2,96,1024]{2,1,0:T(8,128)(2,1)S(1)} %pad_maximum_fusion.1), channel_id=1, source_target_pairs={{16,0},{17,1},{18,2},{19,3},{20,4},{21,5},{22,6},{23,7},{24,8},{25... | collective-permute-start | bytes 1179656 | tf_op jit(solution)/shard_map/ppermute | solution.py:281
  27.0 3.1 %collective-permute-start.2 = (bf16[2,96,1024]{2,1,0:T(8,128)(2,1)S(1)}, bf16[2,96,1024]{2,1,0:T(8,128)(2,1)S(1)}, u32[]{:S(2)}, u32[]{:S(2)}) collective-permute-start(bf16[2,96,1024]{2,1,0:T(8,128)(2,1)S(1)} %pad_maximum_fusion), channel_id=1, source_target_pairs={{0,16},{1,17},{2,18},{3,19},{4,20},{5,21},{6,22},{7,23},{8,24},{9,... | collective-permute-start | bytes 1179656 | tf_op jit(solution)/shard_map/ppermute | solution.py:280
  30.4 1.1 %gather_fusion.2 = bf16[64,2,1024]{2,1,0:T(2,128)(2,1)S(1)} fusion(bf16[2,64,1024]{2,0,1:T(2,128)(2,1)S(1)} %copy.15, s32[1024]{0:T(1024)S(1)} %pad_clamp_fusion.4), kind=kCustom, calls=%fused_computation.2.clone | custom fusion | bytes 524544 | tf_op jit(solution)/shard_map/jit(_take)/gather | solution.py:285
  31.4 0.8 fusion.2.refs_6_
  33.0 0.8 gather_fusion.3
  33.8 0.8 fusion.4.refs_7_
  34.6 0.7 copy-done.13
  35.5 15.5 %neighbourhood_attention_bwd.1 = (bf16[256,1024]{1,0:T(8,128)(2,1)}, f32[256,1024]{1,0:T(8,128)}, f32[256,1024]{1,0:T(8,128)}, bf16[2,96,1024]{2,1,0:T(8,128)(2,...) custom-call(bf16[256,1024]{1,0:T(8,128)(2,1)} %bitcast.43, ...), custom_call_target="tpu_custom_call" | custom-call | flops 2013265920 | bytes 8650752 | tf_op jit(solution)/shard_map/neighbourhood_attention_bwd/pallas_call | solution.py:195
  51.0 4.9 %collective-permute-start.6 = (bf16[2,32,1024]{2,1,0:T(8,128)(2,1)}, bf16[2,32,1024]{2,1,0:T(8,128)(2,1)S(1)}, u32[]{:S(2)}, u32[]{:S(2)}) collective-permute-start(bf16[2,32,1024]{2,1,0:T(8,128)(2,1)} %get-tuple-element.18), channel_id=1, source_target_pairs={{0,8},{1,9},{2,10},{3,11},{4,12},{5,13},{6,14},{7,15},{8,0},{9,1},... | collective-permute-start | bytes 393224 | tf_op jit(solution)/shard_map/ppermute | solution.py:296
  56.0 4.8 %collective-permute-start.8 = (bf16[2,64,1024]{2,1,0:T(8,128)(2,1)}, bf16[2,64,1024]{2,1,0:T(8,128)(2,1)S(1)}, u32[]{:S(2)}, u32[]{:S(2)}) collective-permute-start(bf16[2,64,1024]{2,1,0:T(8,128)(2,1)} %get-tuple-element.20), channel_id=1, source_target_pairs={{0,8},{1,9},{2,10},{3,11},{4,12},{5,13},{6,14},{7,15},{8,0},{9,1},... | collective-permute-start | bytes 786440 | tf_op jit(solution)/shard_map/ppermute | solution.py:317
  60.8 1.3 %collective-permute-start.7 = (bf16[2,96,1024]{2,1,0:T(8,128)(2,1)}, bf16[2,96,1024]{2,1,0:T(8,128)(2,1)S(1)}, u32[]{:S(2)}, u32[]{:S(2)}) collective-permute-start(bf16[2,96,1024]{2,1,0:T(8,128)(2,1)} %get-tuple-element.19), channel_id=1, source_target_pairs={{0,16},{1,17},{2,18},{3,19},{4,20},{5,21},{6,22},{7,23},{8,24},{9,... | collective-permute-start | bytes 1179656 | tf_op jit(solution)/shard_map/ppermute | solution.py:295
  62.1 1.3 %collective-permute-start.9 = (bf16[2,96,1024]{2,1,0:T(8,128)(2,1)}, bf16[2,96,1024]{2,1,0:T(8,128)(2,1)S(1)}, u32[]{:S(2)}, u32[]{:S(2)}) collective-permute-start(bf16[2,96,1024]{2,1,0:T(8,128)(2,1)} %get-tuple-element.21), channel_id=1, source_target_pairs={{16,0},{17,1},{18,2},{19,3},{20,4},{21,5},{22,6},{23,7},{24,8},{25... | collective-permute-start | bytes 1179656 | tf_op jit(solution)/shard_map/ppermute | solution.py:294
  63.6 0.8 gather_fusion.6
  64.5 6.7 %collective-permute-done.8 = bf16[2,64,1024]{2,1,0:T(8,128)(2,1)S(1)} collective-permute-done((bf16[2,64,1024]{2,1,0:T(8,128)(2,1)}, bf16[2,64,1024]{2,1,0:T(8,128)(2,1)S(1)}, u32[]{:S(2)}, u32[]{:S(2)}) %collective-permute-start.8) | collective-permute-done | bytes 262176 | tf_op jit(solution)/shard_map/ppermute | solution.py:317
  71.4 1.1 %gather_fusion.7 = bf16[64,2,1024]{2,1,0:T(2,128)(2,1)S(1)} fusion(bf16[2,64,1024]{2,0,1:T(2,128)(2,1)S(1)} %copy.21, s32[1024]{0:T(1024)S(1)} %pad_clamp_fusion), kind=kCustom, calls=%fused_computation.6.clone | custom fusion | bytes 524544 | tf_op jit(solution)/shard_map/jit(_take)/gather | solution.py:318
  73.0 1.0 %copy-done.5 = f32[2,64,1024]{2,1,0:T(8,128)S(1)} copy-done((f32[2,64,1024]{2,1,0:T(8,128)S(1)}, f32[2,64,1024]{2,1,0:T(8,128)}, u32[]{:S(2)}) %copy-start.5) | copy-done | bytes 524312
  74.1 0.9 %copy-done.4 = f32[2,64,1024]{2,1,0:T(8,128)S(1)} copy-done((f32[2,64,1024]{2,1,0:T(8,128)S(1)}, f32[2,64,1024]{2,1,0:T(8,128)}, u32[]{:S(2)}) %copy-start.4) | copy-done | bytes 524312
  75.1 2.1 %collective-permute-start.11 = (bf16[2,64,1024]{2,1,0:T(8,128)(2,1)S(1)}, bf16[2,64,1024]{2,1,0:T(8,128)(2,1)S(1)}, u32[]{:S(2)}, u32[]{:S(2)}) collective-permute-start(bf16[2,64,1024]{2,1,0:T(8,128)(2,1)S(1)} %add_convert_fusion.2), channel_id=1, source_target_pairs={{0,15},{1,0},{2,1},{3,2},{4,3},{5,4},{6,5},{7,6},{8,7},{9,8},{10,9... | collective-permute-start | bytes 786440 | tf_op jit(solution)/shard_map/ppermute | solution.py:315
  77.3 4.2 %collective-permute-done.10 = bf16[2,64,1024]{2,1,0:T(8,128)(2,1)S(1)} collective-permute-done((bf16[2,64,1024]{2,1,0:T(8,128)(2,1)S(1)}, bf16[2,64,1024]{2,1,0:T(8,128)(2,1)S(1)}, u32[]{:S(2)}, u32[]{:S(2)}) %collective-permute-start.10) | collective-permute-done | bytes 262176 | tf_op jit(solution)/shard_map/ppermute | solution.py:316
  81.6 2.6 %collective-permute-done.11 = bf16[2,64,1024]{2,1,0:T(8,128)(2,1)S(1)} collective-permute-done((bf16[2,64,1024]{2,1,0:T(8,128)(2,1)S(1)}, bf16[2,64,1024]{2,1,0:T(8,128)(2,1)S(1)}, u32[]{:S(2)}, u32[]{:S(2)}) %collective-permute-start.11) | collective-permute-done | bytes 262176 | tf_op jit(solution)/shard_map/ppermute | solution.py:315
  84.4 1.0 %add_convert_fusion = bf16[16,16,1024]{2,1,0:T(8,128)(2,1)} fusion(f32[4,16,1024]{2,1,0:T(8,128)S(1)} %bitcast.40, f32[16,16,1024]{2,1,0:T(8,128)S(1)} %bitcast.36, f32[4,16,1024]{2,1,0:T(8,128)S(1)} %bitcast.39, bf16[16,4,1024]{2,1,0:T(4,128)(2,1)S(1)} %convert_element_type.64, bf16[16,4,1024]{2,1,0:T(4,128)(2,1)S(1)} %convert_element_type.63), kind=kLoop, calls=%fused_computation.9 | loop fusion | flops 1835008 | bytes 2359296 | tf_op jit(solution)/shard_map/convert_element_type | solution.py:336
  85.8 1.0 %add_convert_fusion.1 = bf16[16,16,1024]{2,1,0:T(8,128)(2,1)} fusion(f32[4,16,1024]{2,1,0:T(8,128)S(1)} %bitcast.38, f32[16,16,1024]{2,1,0:T(8,128)S(1)} %bitcast.35, f32[4,16,1024]{2,1,0:T(8,128)S(1)} %bitcast.37, bf16[16,4,1024]{2,1,0:T(4,128)(2,1)S(1)} %convert_element_type.61, bf16[16,4,1024]{2,1,0:T(4,128)(2,1)S(1)} %convert_element_type.59), kind=kLoop, calls=%fused_computation.10 | loop fusion | flops 1835008 | bytes 2359296 | tf_op jit(solution)/shard_map/convert_element_type | solution.py:336
  (88 shorter events, 5.9 us)
Async XLA Ops:
  0.6 1.2 %copy-start.3 = (bf16[16,16,1024]{2,1,0:T(8,128)(2,1)S(1)}, bf16[16,16,1024]{2,1,0:T(8,128)(2,1)}, u32[]{:S(2)}) copy-start(bf16[16,16,1024]{2,1,0:T(8,128)(2,1)} %param.22) | copy-start | bytes 1572868
  2.1 17.8 %collective-permute-start = (bf16[2,64,1024]{2,1,0:T(8,128)(2,1)S(1)}, bf16[2,64,1024]{2,1,0:T(8,128)(2,1)S(1)}, u32[]{:S(2)}, u32[]{:S(2)}) collective-permute-start(bf16[2,64,1024]{2,1,0:T(8,128)(2,1)S(1)} %pad_maximum_fusion.2), channel_id=1, source_target_pairs={{0,1},{1,2},{2,3},{3,4},{4,5},{5,6},{6,7},{7,8},{8,9},{9,10},{10,1... | collective-permute-start | bytes 786440 | tf_op jit(solution)/shard_map/ppermute | solution.py:270
  3.7 1.5 %copy-start.2 = (bf16[16,16,1024]{2,1,0:T(8,128)(2,1)S(1)}, bf16[16,16,1024]{2,1,0:T(8,128)(2,1)}, u32[]{:S(2)}) copy-start(bf16[16,16,1024]{2,1,0:T(8,128)(2,1)} %param.21) | copy-start | bytes 1572868
  3.8 16.1 %collective-permute-start.1 = (bf16[2,64,1024]{2,1,0:T(8,128)(2,1)S(1)}, bf16[2,64,1024]{2,1,0:T(8,128)(2,1)S(1)}, u32[]{:S(2)}, u32[]{:S(2)}) collective-permute-start(bf16[2,64,1024]{2,1,0:T(8,128)(2,1)S(1)} %pad_maximum_fusion.3), channel_id=1, source_target_pairs={{0,15},{1,0},{2,1},{3,2},{4,3},{5,4},{6,5},{7,6},{8,7},{9,8},{10,9... | collective-permute-start | bytes 786440 | tf_op jit(solution)/shard_map/ppermute | solution.py:271
  5.4 24.7 %collective-permute-start.4 = (bf16[2,64,1024]{2,1,0:T(8,128)(2,1)S(1)}, bf16[2,64,1024]{2,1,0:T(8,128)(2,1)S(1)}, u32[]{:S(2)}, u32[]{:S(2)}) collective-permute-start(bf16[2,64,1024]{2,1,0:T(8,128)(2,1)S(1)} %maximum_select_fusion), channel_id=1, source_target_pairs={{0,8},{1,9},{2,10},{3,11},{4,12},{5,13},{6,14},{7,15},{8,0},{9,1},... | collective-permute-start | bytes 786440 | tf_op jit(solution)/shard_map/ppermute | solution.py:274
  13.6 0.7 copy-start.8
  15.8 0.7 copy-start.12
  18.3 1.3 %copy-start.9 = (s32[96]{0:T(128)S(1)}, s32[96]{0:T(128)}, u32[]{:S(2)}) copy-start(s32[96]{0:T(128)} %constant.133.clone) | copy-start | bytes 1156
  18.3 1.3 %copy-start.10 = (s32[96]{0:T(128)S(1)}, s32[96]{0:T(128)}, u32[]{:S(2)}) copy-start(s32[96]{0:T(128)} %constant.134.clone) | copy-start | bytes 1156
  18.4 1.3 %copy-start.11 = (s32[96]{0:T(128)S(1)}, s32[96]{0:T(128)}, u32[]{:S(2)}) copy-start(s32[96]{0:T(128)} %constant.135.clone) | copy-start | bytes 1156
  19.9 0.7 copy-start.6
  19.9 0.8 copy-start.7
  20.7 12.2 %collective-permute-start.5 = (bf16[2,32,1024]{2,1,0:T(8,128)(2,1)S(1)}, bf16[2,32,1024]{2,1,0:T(8,128)(2,1)S(1)}, u32[]{:S(2)}, u32[]{:S(2)}) collective-permute-start(bf16[2,32,1024]{2,1,0:T(8,128)(2,1)S(1)} %maximum_select_fusion.1), channel_id=1, source_target_pairs={{0,8},{1,9},{2,10},{3,11},{4,12},{5,13},{6,14},{7,15},{8,0},{9,1},... | collective-permute-start | bytes 393224 | tf_op jit(solution)/shard_map/ppermute | solution.py:282
  25.7 8.9 %collective-permute-start.3 = (bf16[2,96,1024]{2,1,0:T(8,128)(2,1)S(1)}, bf16[2,96,1024]{2,1,0:T(8,128)(2,1)S(1)}, u32[]{:S(2)}, u32[]{:S(2)}) collective-permute-start(bf16[2,96,1024]{2,1,0:T(8,128)(2,1)S(1)} %pad_maximum_fusion.1), channel_id=1, source_target_pairs={{16,0},{17,1},{18,2},{19,3},{20,4},{21,5},{22,6},{23,7},{24,8},{25... | collective-permute-start | bytes 1179656 | tf_op jit(solution)/shard_map/ppermute | solution.py:281
  27.0 7.6 %collective-permute-start.2 = (bf16[2,96,1024]{2,1,0:T(8,128)(2,1)S(1)}, bf16[2,96,1024]{2,1,0:T(8,128)(2,1)S(1)}, u32[]{:S(2)}, u32[]{:S(2)}) collective-permute-start(bf16[2,96,1024]{2,1,0:T(8,128)(2,1)S(1)} %pad_maximum_fusion), channel_id=1, source_target_pairs={{0,16},{1,17},{2,18},{3,19},{4,20},{5,21},{6,22},{7,23},{8,24},{9,... | collective-permute-start | bytes 1179656 | tf_op jit(solution)/shard_map/ppermute | solution.py:280
  34.6 0.7 copy-start.13
  34.6 0.9 %copy-start.14 = (bf16[2,96,1024]{2,1,0:T(8,128)(2,1)}, bf16[2,96,1024]{2,1,0:T(8,128)(2,1)S(1)}, u32[]{:S(2)}) copy-start(bf16[2,96,1024]{2,1,0:T(8,128)(2,1)S(1)} %collective-permute-done.2.refs_4_) | copy-start | bytes 1179652
  51.0 12.4 %collective-permute-start.6 = (bf16[2,32,1024]{2,1,0:T(8,128)(2,1)}, bf16[2,32,1024]{2,1,0:T(8,128)(2,1)S(1)}, u32[]{:S(2)}, u32[]{:S(2)}) collective-permute-start(bf16[2,32,1024]{2,1,0:T(8,128)(2,1)} %get-tuple-element.18), channel_id=1, source_target_pairs={{0,8},{1,9},{2,10},{3,11},{4,12},{5,13},{6,14},{7,15},{8,0},{9,1},... | collective-permute-start | bytes 393224 | tf_op jit(solution)/shard_map/ppermute | solution.py:296
  56.0 15.2 %collective-permute-start.8 = (bf16[2,64,1024]{2,1,0:T(8,128)(2,1)}, bf16[2,64,1024]{2,1,0:T(8,128)(2,1)S(1)}, u32[]{:S(2)}, u32[]{:S(2)}) collective-permute-start(bf16[2,64,1024]{2,1,0:T(8,128)(2,1)} %get-tuple-element.20), channel_id=1, source_target_pairs={{0,8},{1,9},{2,10},{3,11},{4,12},{5,13},{6,14},{7,15},{8,0},{9,1},... | collective-permute-start | bytes 786440 | tf_op jit(solution)/shard_map/ppermute | solution.py:317
  60.8 11.9 %collective-permute-start.7 = (bf16[2,96,1024]{2,1,0:T(8,128)(2,1)}, bf16[2,96,1024]{2,1,0:T(8,128)(2,1)S(1)}, u32[]{:S(2)}, u32[]{:S(2)}) collective-permute-start(bf16[2,96,1024]{2,1,0:T(8,128)(2,1)} %get-tuple-element.19), channel_id=1, source_target_pairs={{0,16},{1,17},{2,18},{3,19},{4,20},{5,21},{6,22},{7,23},{8,24},{9,... | collective-permute-start | bytes 1179656 | tf_op jit(solution)/shard_map/ppermute | solution.py:295
  62.1 10.6 %collective-permute-start.9 = (bf16[2,96,1024]{2,1,0:T(8,128)(2,1)}, bf16[2,96,1024]{2,1,0:T(8,128)(2,1)S(1)}, u32[]{:S(2)}, u32[]{:S(2)}) collective-permute-start(bf16[2,96,1024]{2,1,0:T(8,128)(2,1)} %get-tuple-element.21), channel_id=1, source_target_pairs={{16,0},{17,1},{18,2},{19,3},{20,4},{21,5},{22,6},{23,7},{24,8},{25... | collective-permute-start | bytes 1179656 | tf_op jit(solution)/shard_map/ppermute | solution.py:294
  73.0 1.0 %copy-start.5 = (f32[2,64,1024]{2,1,0:T(8,128)S(1)}, f32[2,64,1024]{2,1,0:T(8,128)}, u32[]{:S(2)}) copy-start(f32[2,64,1024]{2,1,0:T(8,128)} %get-tuple-element.22) | copy-start | bytes 1572868
  74.0 1.0 %copy-start.4 = (f32[2,64,1024]{2,1,0:T(8,128)S(1)}, f32[2,64,1024]{2,1,0:T(8,128)}, u32[]{:S(2)}) copy-start(f32[2,64,1024]{2,1,0:T(8,128)} %get-tuple-element.23) | copy-start | bytes 1572868
  74.1 7.4 %collective-permute-start.10 = (bf16[2,64,1024]{2,1,0:T(8,128)(2,1)S(1)}, bf16[2,64,1024]{2,1,0:T(8,128)(2,1)S(1)}, u32[]{:S(2)}, u32[]{:S(2)}) collective-permute-start(bf16[2,64,1024]{2,1,0:T(8,128)(2,1)S(1)} %add_convert_fusion.3), channel_id=1, source_target_pairs={{0,1},{1,2},{2,3},{3,4},{4,5},{5,6},{6,7},{7,8},{8,9},{9,10},{10,1... | collective-permute-start | bytes 786440 | tf_op jit(solution)/shard_map/ppermute | solution.py:316
  75.1 9.1 %collective-permute-start.11 = (bf16[2,64,1024]{2,1,0:T(8,128)(2,1)S(1)}, bf16[2,64,1024]{2,1,0:T(8,128)(2,1)S(1)}, u32[]{:S(2)}, u32[]{:S(2)}) collective-permute-start(bf16[2,64,1024]{2,1,0:T(8,128)(2,1)S(1)} %add_convert_fusion.2), channel_id=1, source_target_pairs={{0,15},{1,0},{2,1},{3,2},{4,3},{5,4},{6,5},{7,6},{8,7},{9,8},{10,9... | collective-permute-start | bytes 786440 | tf_op jit(solution)/shard_map/ppermute | solution.py:315
  77.3 7.1 %copy-start.1 = (f32[256,1024]{1,0:T(8,128)S(1)}, f32[256,1024]{1,0:T(8,128)}, u32[]{:S(2)}) copy-start(f32[256,1024]{1,0:T(8,128)} %get-tuple-element.24) | copy-start | bytes 3145732
  84.4 1.4 %copy-start = (f32[256,1024]{1,0:T(8,128)S(1)}, f32[256,1024]{1,0:T(8,128)}, u32[]{:S(2)}) copy-start(f32[256,1024]{1,0:T(8,128)} %get-tuple-element.17) | copy-start | bytes 3145732

commit v12 on v11

--- a/solution.py
+++ b/solution.py
@@ -17,8 +17,9 @@
 
 def attention_kernel(width, n_lat, *refs):
     (q_ref, g_ref, k_own, v_own, above_in, below_in, pole_mid_in, pole_corner_in, left_in, right_in) = refs[:10]
-    (dq_ref, dk_own, dv_own, top_out, bot_out, left_out, right_out, pole_mid_out, pole_corner_out) = refs[10:19]
-    bias_ref = refs[19]
+    (mid_pick, corner_pick) = refs[10:12]
+    (dq_ref, dk_own, dv_own, top_out, bot_out, left_out, right_out, pole_mid_out, pole_corner_out) = refs[12:21]
+    bias_ref = refs[21]
     lat = lax.axis_index("lat")
     north = lat == 0
     south = lat == n_lat - 1
@@ -29,10 +30,11 @@
 
         def __getitem__(self, index):
             c, cells, lanes = index
+            mid, corners = pole_now[0]
             if cells.start >= edge:
-                pole = self.pole_corner_ref[c, pl.ds(cells.start - edge, cells.size), lanes]
+                pole = corners[c][cells.start - edge : cells.start - edge + cells.size]
             else:
-                pole = pole_mid_in[c, cells, lanes]
+                pole = mid[c][cells.start : cells.start + cells.size]
             return jnp.where(self.pole, pole, self.neighbour[c, cells, lanes])
 
     top_in = Strip(above_in, north)
@@ -117,6 +119,10 @@
             pole_ref[index] = jnp.where(south, piece, pole_ref[index])
 
     lanes_now = [None]
+    pole_now = [None]
+
+    def fold(pick, ref, c, lanes):
+        return jnp.dot(pick[...], ref[c, :, lanes], preferred_element_type=jnp.float32).astype(jnp.bfloat16)
 
     def scatter_grads(d, own, c, t, lanes):
         rows = side - corner
@@ -145,6 +151,10 @@
 
     def body(p, carry):
         lanes = pl.ds(pl.multiple_of(p * LANES, LANES), LANES)
+        pole_now[0] = (
+            [fold(mid_pick, pole_mid_in, c, lanes) for c in range(2)],
+            [fold(corner_pick, pole_corner_in, c, lanes) for c in range(2)],
+        )
         for t in range(2):
             qp = q_ref[pl.ds(t * tq, tq), lanes]
             gp = g_ref[pl.ds(t * tq, tq), lanes]
@@ -168,7 +178,7 @@
     lax.fori_loop(0, pairs, body, 0)
 
 
-def attention_core(q2, g2, k2, v2, above, below, pole_mid, pole_corner, left_in, right_in, width, n_lat):
+def attention_core(q2, g2, k2, v2, above, below, pole_mid, pole_corner, left_in, right_in, picks, width, n_lat):
     cells, features = q2.shape
     r = RADIUS
     tq = TILE_ROWS * width
@@ -195,7 +205,7 @@
     return pl.pallas_call(
         lambda *refs: attention_kernel(width, n_lat, *refs),
         out_shape=outs,
-        in_specs=[vmem] * 10,
+        in_specs=[vmem] * 12,
         out_specs=tuple([vmem] * 9),
         scratch_shapes=[pltpu.VMEM((2 * tq, tk), jnp.float32)],
         cost_estimate=pl.CostEstimate(
@@ -204,7 +214,7 @@
             bytes_accessed=in_bytes + out_bytes,
         ),
         name="neighbourhood_attention_bwd",
-    )(q2, g2, k2, v2, above, below, pole_mid, pole_corner, left_in, right_in)
+    )(q2, g2, k2, v2, above, below, pole_mid, pole_corner, left_in, right_in, *picks)
 
 
 def on_device(queries, keys, values, grad_out, fold_cols):
@@ -282,13 +292,13 @@
     pole_corners = lax.ppermute(
         jnp.where(at_north, top_send[:, edge:], bottom_send[:, edge:]), both, pole_pairs
     )
-    pole_mid_rows = jnp.take(pole_mid, pole_src[:edge], axis=1)
-    pole_corner_rows = jnp.take(pole_corners, pole_src[edge:] - edge, axis=1)
+    mid_pick = (pole_src[:edge, None] == jnp.arange(edge)[None, :]).astype(bf16)
+    corner_pick = (pole_src[edge:, None] - edge == jnp.arange(2 * corner)[None, :]).astype(bf16)
 
     q2 = queries.reshape(cells, features)
     g2 = grad_out.reshape(cells, features)
     dq, dk_own, dv_own, top_g, bottom_g, left_g, right_g, pole_g_mid_send, pole_g_corner_send = attention_core(
-        q2, g2, kf, vf, from_above, from_below, pole_mid_rows, pole_corner_rows, from_left, from_right, width, n_lat
+        q2, g2, kf, vf, from_above, from_below, pole_mid, pole_corners, from_left, from_right, (mid_pick, corner_pick), width, n_lat
     )
 
     up_recv = lax.ppermute(top_g, both, up_pairs)

time: 88.6 us -> 93.3 us (1.053)
  the two profiles are of different devices: /device:TPU:32 before, /device:TPU:23 now
where the time goes in v12:
time: 93.3 us; the launch traced here: 92.8 us
  starting transfers between devices  36.9 us (40%)
  waiting for transfers between devices  19.8 us (21%)
  Pallas kernels  16.4 us (18%)
  local copies, waits for them, and re-layouts  13.9 us (15%)
  other arithmetic  4.53 us (5%)
  between operations  1.18 us (1%)
    pallas_call x1, Pallas kernels, attention_core(): pl.pallas_call(lambda *refs: attention_kernel(width, n_lat, *refs), out_s...  16.4 us
    ppermute x1, waiting for transfers between devices, on_device(): lax.ppermute(side_send(right_g, edge + corner), 'lon', right_pairs)  7.12 us
    ppermute x1, starting transfers between devices, on_device(): lax.ppermute(jnp.where(at_north, top_mid, bottom_mid), both, pole_pairs)  6.07 us
    ppermute x1, waiting for transfers between devices, on_device(): lax.ppermute(jnp.where(at_north, top_send[:, edge:], bottom_send[:, edge:...  5.86 us
    ppermute x1, starting transfers between devices, on_device(): lax.ppermute(pair(cols(keys, 0, r), cols(values, 0, r)), 'lon', left_pairs)  5.39 us
    unnamed x34, local copies, waits for them, and re-layouts  5.3 us
    ppermute x1, starting transfers between devices, on_device(): lax.ppermute(jnp.where(at_north, top_send[:, edge:], bottom_send[:, edge:...  5.12 us
    ppermute x1, starting transfers between devices, on_device(): pole_g_corners = lax.ppermute(pole_g_corner_send, both, pole_pairs)  4.89 us
  transfers between devices with their start and end apart: 12, of which 4 were waited for; matrix products, arithmetic and copies ran while one was open for 10% of the time, Pallas kernels for 0%

profile of v12, /device:TPU:23, one launch (start us, length us, event | category | flops | bytes accessed | tf_op | source)
XLA Modules:
  0.0 92.8 jit_solution(2913523852359372645)
XLA Ops:
  0.6 1.2 %fusion.17 = (bf16[16,4,1024]{2,1,0:T(4,128)(2,1)S(1)}, bf16[16,4,1024]{2,1,0:T(4,128)(2,1)S(1)}) fusion(bf16[16,16,1024]{2,1,0:T(8,128)(2,1)} %param.17), kind=kLoop, calls=%fused_computation.82 | loop fusion | bytes 524288 | tf_op jit(solution)/shard_map/slice | solution.py:278
  2.1 1.1 %collective-permute-start = (bf16[2,64,1024]{2,1,0:T(8,128)(2,1)S(1)}, bf16[2,64,1024]{2,1,0:T(8,128)(2,1)S(1)}, u32[]{:S(2)}, u32[]{:S(2)}) collective-permute-start(bf16[2,64,1024]{2,1,0:T(8,128)(2,1)S(1)} %pad_maximum_fusion.2), channel_id=1, source_target_pairs={{0,1},{1,2},{2,3},{3,4},{4,5},{5,6},{6,7},{7,8},{8,9},{9,10},{10,1... | collective-permute-start | bytes 786440 | tf_op jit(solution)/shard_map/ppermute | solution.py:280
  3.3 5.4 %collective-permute-start.1 = (bf16[2,64,1024]{2,1,0:T(8,128)(2,1)S(1)}, bf16[2,64,1024]{2,1,0:T(8,128)(2,1)S(1)}, u32[]{:S(2)}, u32[]{:S(2)}) collective-permute-start(bf16[2,64,1024]{2,1,0:T(8,128)(2,1)S(1)} %pad_maximum_fusion.3), channel_id=1, source_target_pairs={{0,15},{1,0},{2,1},{3,2},{4,3},{5,4},{6,5},{7,6},{8,7},{9,8},{10,9... | collective-permute-start | bytes 786440 | tf_op jit(solution)/shard_map/ppermute | solution.py:281
  8.8 6.1 %collective-permute-start.4 = (bf16[2,64,1024]{2,1,0:T(8,128)(2,1)S(1)}, bf16[2,64,1024]{2,1,0:T(8,128)(2,1)S(1)}, u32[]{:S(2)}, u32[]{:S(2)}) collective-permute-start(bf16[2,64,1024]{2,1,0:T(8,128)(2,1)S(1)} %maximum_select_fusion), channel_id=1, source_target_pairs={{0,8},{1,9},{2,10},{3,11},{4,12},{5,13},{6,14},{7,15},{8,0},{9,1},... | collective-permute-start | bytes 786440 | tf_op jit(solution)/shard_map/ppermute | solution.py:284
  14.9 0.7 copy-done.8
  15.6 0.7 gather_fusion.2
  16.3 0.7 gather_fusion.4
  17.7 0.6 scatter_custom_fusion
  18.4 1.2 %gather_fusion.5 = s32[96]{0:T(128)S(1)} fusion(s32[24]{0:T(128)S(1)} %scatter_custom_fusion, s32[1024]{0:T(1024)S(1)} %pad_clamp_fusion.3), kind=kCustom, calls=%fused_computation.3.clone | custom fusion | bytes 1152 | tf_op jit(solution)/shard_map/jit(_take)/gather | solution.py:269
  19.6 1.2 %gather_fusion.3 = s32[96]{0:T(128)S(1)} fusion(s32[24]{0:T(128)S(1)} %get-tuple-element.58, s32[1024]{0:T(1024)S(1)} %pad_clamp_fusion.3), kind=kCustom, calls=%fused_computation.1.clone | custom fusion | bytes 1152 | tf_op jit(solution)/shard_map/jit(_take)/gather | solution.py:268
  20.9 0.7 fusion.5.refs_10_
  21.7 0.7 fusion.6.refs_11_
  22.4 0.7 copy-done.6
  23.2 1.3 %collective-permute-start.3 = (bf16[2,96,1024]{2,1,0:T(8,128)(2,1)S(1)}, bf16[2,96,1024]{2,1,0:T(8,128)(2,1)S(1)}, u32[]{:S(2)}, u32[]{:S(2)}) collective-permute-start(bf16[2,96,1024]{2,1,0:T(8,128)(2,1)S(1)} %pad_maximum_fusion.1), channel_id=1, source_target_pairs={{16,0},{17,1},{18,2},{19,3},{20,4},{21,5},{22,6},{23,7},{24,8},{25... | collective-permute-start | bytes 1179656 | tf_op jit(solution)/shard_map/ppermute | solution.py:291
  24.5 1.3 %collective-permute-start.2 = (bf16[2,96,1024]{2,1,0:T(8,128)(2,1)S(1)}, bf16[2,96,1024]{2,1,0:T(8,128)(2,1)S(1)}, u32[]{:S(2)}, u32[]{:S(2)}) collective-permute-start(bf16[2,96,1024]{2,1,0:T(8,128)(2,1)S(1)} %pad_maximum_fusion), channel_id=1, source_target_pairs={{0,16},{1,17},{2,18},{3,19},{4,20},{5,21},{6,22},{7,23},{8,24},{9,... | collective-permute-start | bytes 1179656 | tf_op jit(solution)/shard_map/ppermute | solution.py:290
  25.9 5.1 %collective-permute-start.5 = (bf16[2,32,1024]{2,1,0:T(8,128)(2,1)S(1)}, bf16[2,32,1024]{2,1,0:T(8,128)(2,1)S(1)}, u32[]{:S(2)}, u32[]{:S(2)}) collective-permute-start(bf16[2,32,1024]{2,1,0:T(8,128)(2,1)S(1)} %maximum_select_fusion.1), channel_id=1, source_target_pairs={{0,8},{1,9},{2,10},{3,11},{4,12},{5,13},{6,14},{7,15},{8,0},{9,1},... | collective-permute-start | bytes 393224 | tf_op jit(solution)/shard_map/ppermute | solution.py:292
  31.1 5.9 %collective-permute-done.5.refs_7_ = bf16[2,32,1024]{2,1,0:T(8,128)(2,1)S(1)} collective-permute-done((bf16[2,32,1024]{2,1,0:T(8,128)(2,1)S(1)}, bf16[2,32,1024]{2,1,0:T(8,128)(2,1)S(1)}, u32[]{:S(2)}, u32[]{:S(2)}) %collective-permute-start.5) | collective-permute-done | bytes 131104 | tf_op jit(solution)/shard_map/ppermute | solution.py:292
  37.9 16.4 %neighbourhood_attention_bwd.1 = (bf16[256,1024]{1,0:T(8,128)(2,1)}, f32[256,1024]{1,0:T(8,128)}, f32[256,1024]{1,0:T(8,128)}, bf16[2,96,1024]{2,1,0:T(8,128)(2,...) custom-call(bf16[256,1024]{1,0:T(8,128)(2,1)} %bitcast.42, ...), custom_call_target="tpu_custom_call" | custom-call | flops 2013265920 | bytes 8650752 | tf_op jit(solution)/shard_map/neighbourhood_attention_bwd/pallas_call | solution.py:205
  54.3 4.9 %collective-permute-start.6 = (bf16[2,32,1024]{2,1,0:T(8,128)(2,1)}, bf16[2,32,1024]{2,1,0:T(8,128)(2,1)S(1)}, u32[]{:S(2)}, u32[]{:S(2)}) collective-permute-start(bf16[2,32,1024]{2,1,0:T(8,128)(2,1)} %get-tuple-element.16), channel_id=1, source_target_pairs={{0,8},{1,9},{2,10},{3,11},{4,12},{5,13},{6,14},{7,15},{8,0},{9,1},... | collective-permute-start | bytes 393224 | tf_op jit(solution)/shard_map/ppermute | solution.py:306
  59.2 4.3 %collective-permute-start.8 = (bf16[2,64,1024]{2,1,0:T(8,128)(2,1)}, bf16[2,64,1024]{2,1,0:T(8,128)(2,1)S(1)}, u32[]{:S(2)}, u32[]{:S(2)}) collective-permute-start(bf16[2,64,1024]{2,1,0:T(8,128)(2,1)} %get-tuple-element.18), channel_id=1, source_target_pairs={{0,8},{1,9},{2,10},{3,11},{4,12},{5,13},{6,14},{7,15},{8,0},{9,1},... | collective-permute-start | bytes 786440 | tf_op jit(solution)/shard_map/ppermute | solution.py:327
  63.5 1.3 %collective-permute-start.7 = (bf16[2,96,1024]{2,1,0:T(8,128)(2,1)}, bf16[2,96,1024]{2,1,0:T(8,128)(2,1)S(1)}, u32[]{:S(2)}, u32[]{:S(2)}) collective-permute-start(bf16[2,96,1024]{2,1,0:T(8,128)(2,1)} %get-tuple-element.17), channel_id=1, source_target_pairs={{0,16},{1,17},{2,18},{3,19},{4,20},{5,21},{6,22},{7,23},{8,24},{9,... | collective-permute-start | bytes 1179656 | tf_op jit(solution)/shard_map/ppermute | solution.py:305
  64.8 3.1 %collective-permute-start.9 = (bf16[2,96,1024]{2,1,0:T(8,128)(2,1)}, bf16[2,96,1024]{2,1,0:T(8,128)(2,1)S(1)}, u32[]{:S(2)}, u32[]{:S(2)}) collective-permute-start(bf16[2,96,1024]{2,1,0:T(8,128)(2,1)} %get-tuple-element.19), channel_id=1, source_target_pairs={{16,0},{17,1},{18,2},{19,3},{20,4},{21,5},{22,6},{23,7},{24,8},{25... | collective-permute-start | bytes 1179656 | tf_op jit(solution)/shard_map/ppermute | solution.py:304
  68.1 0.8 gather_fusion
  69.0 3.6 %collective-permute-done.8 = bf16[2,64,1024]{2,1,0:T(8,128)(2,1)S(1)} collective-permute-done((bf16[2,64,1024]{2,1,0:T(8,128)(2,1)}, bf16[2,64,1024]{2,1,0:T(8,128)(2,1)S(1)}, u32[]{:S(2)}, u32[]{:S(2)}) %collective-permute-start.8) | collective-permute-done | bytes 262176 | tf_op jit(solution)/shard_map/ppermute | solution.py:327
  72.8 1.1 %gather_fusion.1 = bf16[64,2,1024]{2,1,0:T(2,128)(2,1)S(1)} fusion(bf16[2,64,1024]{2,0,1:T(2,128)(2,1)S(1)} %copy.17, s32[1024]{0:T(1024)S(1)} %pad_clamp_fusion), kind=kCustom, calls=%fused_computation.5 | custom fusion | bytes 524544 | tf_op jit(solution)/shard_map/jit(_take)/gather | solution.py:328
  74.4 1.0 %copy-done.5 = f32[2,64,1024]{2,1,0:T(8,128)S(1)} copy-done((f32[2,64,1024]{2,1,0:T(8,128)S(1)}, f32[2,64,1024]{2,1,0:T(8,128)}, u32[]{:S(2)}) %copy-start.5) | copy-done | bytes 524312
  75.5 0.9 copy-done.4
  76.5 3.0 %collective-permute-start.11 = (bf16[2,64,1024]{2,1,0:T(8,128)(2,1)S(1)}, bf16[2,64,1024]{2,1,0:T(8,128)(2,1)S(1)}, u32[]{:S(2)}, u32[]{:S(2)}) collective-permute-start(bf16[2,64,1024]{2,1,0:T(8,128)(2,1)S(1)} %add_convert_fusion.2), channel_id=1, source_target_pairs={{0,15},{1,0},{2,1},{3,2},{4,3},{5,4},{6,5},{7,6},{8,7},{9,8},{10,9... | collective-permute-start | bytes 786440 | tf_op jit(solution)/shard_map/ppermute | solution.py:325
  79.7 7.1 %collective-permute-done.10 = bf16[2,64,1024]{2,1,0:T(8,128)(2,1)S(1)} collective-permute-done((bf16[2,64,1024]{2,1,0:T(8,128)(2,1)S(1)}, bf16[2,64,1024]{2,1,0:T(8,128)(2,1)S(1)}, u32[]{:S(2)}, u32[]{:S(2)}) %collective-permute-start.10) | collective-permute-done | bytes 262176 | tf_op jit(solution)/shard_map/ppermute | solution.py:326
  86.9 3.2 %collective-permute-done.11 = bf16[2,64,1024]{2,1,0:T(8,128)(2,1)S(1)} collective-permute-done((bf16[2,64,1024]{2,1,0:T(8,128)(2,1)S(1)}, bf16[2,64,1024]{2,1,0:T(8,128)(2,1)S(1)}, u32[]{:S(2)}, u32[]{:S(2)}) %collective-permute-start.11) | collective-permute-done | bytes 262176 | tf_op jit(solution)/shard_map/ppermute | solution.py:325
  90.3 1.0 %add_convert_fusion = bf16[16,16,1024]{2,1,0:T(8,128)(2,1)} fusion(f32[4,16,1024]{2,1,0:T(8,128)S(1)} %bitcast.38, f32[16,16,1024]{2,1,0:T(8,128)S(1)} %bitcast.34, f32[4,16,1024]{2,1,0:T(8,128)S(1)} %bitcast.37, bf16[16,4,1024]{2,1,0:T(4,128)(2,1)S(1)} %convert_element_type.72, bf16[16,4,1024]{2,1,0:T(4,128)(2,1)S(1)} %convert_element_type.71), kind=kLoop, calls=%fused_computation.7 | loop fusion | flops 1835008 | bytes 2359296 | tf_op jit(solution)/shard_map/convert_element_type | solution.py:346
  91.7 1.0 %add_convert_fusion.1 = bf16[16,16,1024]{2,1,0:T(8,128)(2,1)} fusion(f32[4,16,1024]{2,1,0:T(8,128)S(1)} %bitcast.36, f32[16,16,1024]{2,1,0:T(8,128)S(1)} %bitcast.33, f32[4,16,1024]{2,1,0:T(8,128)S(1)} %bitcast.35, bf16[16,4,1024]{2,1,0:T(4,128)(2,1)S(1)} %convert_element_type.69, bf16[16,4,1024]{2,1,0:T(4,128)(2,1)S(1)} %convert_element_type.67), kind=kLoop, calls=%fused_computation.8 | loop fusion | flops 1835008 | bytes 2359296 | tf_op jit(solution)/shard_map/convert_element_type | solution.py:346
  (85 shorter events, 4.4 us)
Async XLA Ops:
  0.6 1.2 %copy-start.3 = (bf16[16,16,1024]{2,1,0:T(8,128)(2,1)S(1)}, bf16[16,16,1024]{2,1,0:T(8,128)(2,1)}, u32[]{:S(2)}) copy-start(bf16[16,16,1024]{2,1,0:T(8,128)(2,1)} %param.18) | copy-start | bytes 1572868
  2.1 20.3 %collective-permute-start = (bf16[2,64,1024]{2,1,0:T(8,128)(2,1)S(1)}, bf16[2,64,1024]{2,1,0:T(8,128)(2,1)S(1)}, u32[]{:S(2)}, u32[]{:S(2)}) collective-permute-start(bf16[2,64,1024]{2,1,0:T(8,128)(2,1)S(1)} %pad_maximum_fusion.2), channel_id=1, source_target_pairs={{0,1},{1,2},{2,3},{3,4},{4,5},{5,6},{6,7},{7,8},{8,9},{9,10},{10,1... | collective-permute-start | bytes 786440 | tf_op jit(solution)/shard_map/ppermute | solution.py:280
  3.2 5.5 %copy-start.2 = (bf16[16,16,1024]{2,1,0:T(8,128)(2,1)S(1)}, bf16[16,16,1024]{2,1,0:T(8,128)(2,1)}, u32[]{:S(2)}) copy-start(bf16[16,16,1024]{2,1,0:T(8,128)(2,1)} %param.17) | copy-start | bytes 1572868
  3.3 19.1 %collective-permute-start.1 = (bf16[2,64,1024]{2,1,0:T(8,128)(2,1)S(1)}, bf16[2,64,1024]{2,1,0:T(8,128)(2,1)S(1)}, u32[]{:S(2)}, u32[]{:S(2)}) collective-permute-start(bf16[2,64,1024]{2,1,0:T(8,128)(2,1)S(1)} %pad_maximum_fusion.3), channel_id=1, source_target_pairs={{0,15},{1,0},{2,1},{3,2},{4,3},{5,4},{6,5},{7,6},{8,7},{9,8},{10,9... | collective-permute-start | bytes 786440 | tf_op jit(solution)/shard_map/ppermute | solution.py:281
  8.8 22.3 %collective-permute-start.4 = (bf16[2,64,1024]{2,1,0:T(8,128)(2,1)S(1)}, bf16[2,64,1024]{2,1,0:T(8,128)(2,1)S(1)}, u32[]{:S(2)}, u32[]{:S(2)}) collective-permute-start(bf16[2,64,1024]{2,1,0:T(8,128)(2,1)S(1)} %maximum_select_fusion), channel_id=1, source_target_pairs={{0,8},{1,9},{2,10},{3,11},{4,12},{5,13},{6,14},{7,15},{8,0},{9,1},... | collective-permute-start | bytes 786440 | tf_op jit(solution)/shard_map/ppermute | solution.py:284
  14.9 0.7 copy-start.8
  17.0 0.7 copy-start.12
  19.6 1.3 %copy-start.9 = (s32[96]{0:T(128)S(1)}, s32[96]{0:T(128)}, u32[]{:S(2)}) copy-start(s32[96]{0:T(128)} %constant.144.clone) | copy-start | bytes 1156
  19.6 1.3 %copy-start.10 = (s32[96]{0:T(128)S(1)}, s32[96]{0:T(128)}, u32[]{:S(2)}) copy-start(s32[96]{0:T(128)} %constant.145.clone) | copy-start | bytes 1156
  19.6 1.3 %copy-start.11 = (s32[96]{0:T(128)S(1)}, s32[96]{0:T(128)}, u32[]{:S(2)}) copy-start(s32[96]{0:T(128)} %constant.146.clone) | copy-start | bytes 1156
  22.3 0.7 copy-start.6
  22.4 0.8 copy-start.7
  23.2 13.8 %collective-permute-start.3 = (bf16[2,96,1024]{2,1,0:T(8,128)(2,1)S(1)}, bf16[2,96,1024]{2,1,0:T(8,128)(2,1)S(1)}, u32[]{:S(2)}, u32[]{:S(2)}) collective-permute-start(bf16[2,96,1024]{2,1,0:T(8,128)(2,1)S(1)} %pad_maximum_fusion.1), channel_id=1, source_target_pairs={{16,0},{17,1},{18,2},{19,3},{20,4},{21,5},{22,6},{23,7},{24,8},{25... | collective-permute-start | bytes 1179656 | tf_op jit(solution)/shard_map/ppermute | solution.py:291
  24.5 12.5 %collective-permute-start.2 = (bf16[2,96,1024]{2,1,0:T(8,128)(2,1)S(1)}, bf16[2,96,1024]{2,1,0:T(8,128)(2,1)S(1)}, u32[]{:S(2)}, u32[]{:S(2)}) collective-permute-start(bf16[2,96,1024]{2,1,0:T(8,128)(2,1)S(1)} %pad_maximum_fusion), channel_id=1, source_target_pairs={{0,16},{1,17},{2,18},{3,19},{4,20},{5,21},{6,22},{7,23},{8,24},{9,... | collective-permute-start | bytes 1179656 | tf_op jit(solution)/shard_map/ppermute | solution.py:290
  25.9 11.0 %collective-permute-start.5 = (bf16[2,32,1024]{2,1,0:T(8,128)(2,1)S(1)}, bf16[2,32,1024]{2,1,0:T(8,128)(2,1)S(1)}, u32[]{:S(2)}, u32[]{:S(2)}) collective-permute-start(bf16[2,32,1024]{2,1,0:T(8,128)(2,1)S(1)} %maximum_select_fusion.1), channel_id=1, source_target_pairs={{0,8},{1,9},{2,10},{3,11},{4,12},{5,13},{6,14},{7,15},{8,0},{9,1},... | collective-permute-start | bytes 393224 | tf_op jit(solution)/shard_map/ppermute | solution.py:292
  31.1 5.9 %copy-start.15 = (bf16[2,64,1024]{2,1,0:T(8,128)(2,1)}, bf16[2,64,1024]{2,1,0:T(8,128)(2,1)S(1)}, u32[]{:S(2)}) copy-start(bf16[2,64,1024]{2,1,0:T(8,128)(2,1)S(1)} %collective-permute-done.4.refs_6_) | copy-start | bytes 786436
  37.0 0.7 copy-start.16
  37.0 0.8 copy-start.13
  37.0 0.9 %copy-start.14 = (bf16[2,96,1024]{2,1,0:T(8,128)(2,1)}, bf16[2,96,1024]{2,1,0:T(8,128)(2,1)S(1)}, u32[]{:S(2)}) copy-start(bf16[2,96,1024]{2,1,0:T(8,128)(2,1)S(1)} %collective-permute-done.2.refs_4_) | copy-start | bytes 1179652
  54.3 13.6 %collective-permute-start.6 = (bf16[2,32,1024]{2,1,0:T(8,128)(2,1)}, bf16[2,32,1024]{2,1,0:T(8,128)(2,1)S(1)}, u32[]{:S(2)}, u32[]{:S(2)}) collective-permute-start(bf16[2,32,1024]{2,1,0:T(8,128)(2,1)} %get-tuple-element.16), channel_id=1, source_target_pairs={{0,8},{1,9},{2,10},{3,11},{4,12},{5,13},{6,14},{7,15},{8,0},{9,1},... | collective-permute-start | bytes 393224 | tf_op jit(solution)/shard_map/ppermute | solution.py:306
  59.2 13.3 %collective-permute-start.8 = (bf16[2,64,1024]{2,1,0:T(8,128)(2,1)}, bf16[2,64,1024]{2,1,0:T(8,128)(2,1)S(1)}, u32[]{:S(2)}, u32[]{:S(2)}) collective-permute-start(bf16[2,64,1024]{2,1,0:T(8,128)(2,1)} %get-tuple-element.18), channel_id=1, source_target_pairs={{0,8},{1,9},{2,10},{3,11},{4,12},{5,13},{6,14},{7,15},{8,0},{9,1},... | collective-permute-start | bytes 786440 | tf_op jit(solution)/shard_map/ppermute | solution.py:327
  63.5 10.6 %collective-permute-start.7 = (bf16[2,96,1024]{2,1,0:T(8,128)(2,1)}, bf16[2,96,1024]{2,1,0:T(8,128)(2,1)S(1)}, u32[]{:S(2)}, u32[]{:S(2)}) collective-permute-start(bf16[2,96,1024]{2,1,0:T(8,128)(2,1)} %get-tuple-element.17), channel_id=1, source_target_pairs={{0,16},{1,17},{2,18},{3,19},{4,20},{5,21},{6,22},{7,23},{8,24},{9,... | collective-permute-start | bytes 1179656 | tf_op jit(solution)/shard_map/ppermute | solution.py:305
  64.8 9.3 %collective-permute-start.9 = (bf16[2,96,1024]{2,1,0:T(8,128)(2,1)}, bf16[2,96,1024]{2,1,0:T(8,128)(2,1)S(1)}, u32[]{:S(2)}, u32[]{:S(2)}) collective-permute-start(bf16[2,96,1024]{2,1,0:T(8,128)(2,1)} %get-tuple-element.19), channel_id=1, source_target_pairs={{16,0},{17,1},{18,2},{19,3},{20,4},{21,5},{22,6},{23,7},{24,8},{25... | collective-permute-start | bytes 1179656 | tf_op jit(solution)/shard_map/ppermute | solution.py:304
  74.3 1.0 %copy-start.5 = (f32[2,64,1024]{2,1,0:T(8,128)S(1)}, f32[2,64,1024]{2,1,0:T(8,128)}, u32[]{:S(2)}) copy-start(f32[2,64,1024]{2,1,0:T(8,128)} %get-tuple-element.20) | copy-start | bytes 1572868
  75.4 1.0 %copy-start.4 = (f32[2,64,1024]{2,1,0:T(8,128)S(1)}, f32[2,64,1024]{2,1,0:T(8,128)}, u32[]{:S(2)}) copy-start(f32[2,64,1024]{2,1,0:T(8,128)} %get-tuple-element.21) | copy-start | bytes 1572868
  75.4 11.4 %collective-permute-start.10 = (bf16[2,64,1024]{2,1,0:T(8,128)(2,1)S(1)}, bf16[2,64,1024]{2,1,0:T(8,128)(2,1)S(1)}, u32[]{:S(2)}, u32[]{:S(2)}) collective-permute-start(bf16[2,64,1024]{2,1,0:T(8,128)(2,1)S(1)} %add_convert_fusion.3), channel_id=1, source_target_pairs={{0,1},{1,2},{2,3},{3,4},{4,5},{5,6},{6,7},{7,8},{8,9},{9,10},{10,1... | collective-permute-start | bytes 786440 | tf_op jit(solution)/shard_map/ppermute | solution.py:326
  76.5 13.6 %collective-permute-start.11 = (bf16[2,64,1024]{2,1,0:T(8,128)(2,1)S(1)}, bf16[2,64,1024]{2,1,0:T(8,128)(2,1)S(1)}, u32[]{:S(2)}, u32[]{:S(2)}) collective-permute-start(bf16[2,64,1024]{2,1,0:T(8,128)(2,1)S(1)} %add_convert_fusion.2), channel_id=1, source_target_pairs={{0,15},{1,0},{2,1},{3,2},{4,3},{5,4},{6,5},{7,6},{8,7},{9,8},{10,9... | collective-permute-start | bytes 786440 | tf_op jit(solution)/shard_map/ppermute | solution.py:325
  79.7 10.7 %copy-start.1 = (f32[256,1024]{1,0:T(8,128)S(1)}, f32[256,1024]{1,0:T(8,128)}, u32[]{:S(2)}) copy-start(f32[256,1024]{1,0:T(8,128)} %get-tuple-element.22) | copy-start | bytes 3145732
  90.3 1.4 %copy-start = (f32[256,1024]{1,0:T(8,128)S(1)}, f32[256,1024]{1,0:T(8,128)}, u32[]{:S(2)}) copy-start(f32[256,1024]{1,0:T(8,128)} %get-tuple-element.15) | copy-start | bytes 3145732

commit v13 on v11

--- a/solution.py
+++ b/solution.py
@@ -165,7 +165,7 @@
             scatter_grads(dv, dv_own, 1, t, lanes)
         return carry
 
-    lax.fori_loop(0, pairs, body, 0)
+    lax.fori_loop(0, pairs, body, 0, unroll=2)
 
 
 def attention_core(q2, g2, k2, v2, above, below, pole_mid, pole_corner, left_in, right_in, width, n_lat):

time: 88.6 us -> 87.9 us (level)
  no operation moved by 1% of the time
where the time goes in v13:
time: 87.9 us; the launch traced here: 86.1 us
  starting transfers between devices  35.1 us (40%)
  local copies, waits for them, and re-layouts  16.2 us (18%)
  Pallas kernels  14.8 us (17%)
  waiting for transfers between devices  14.1 us (16%)
  other arithmetic  4.76 us (5%)
  between operations  1.21 us (1%)
    pallas_call x1, Pallas kernels, attention_core(): pl.pallas_call(lambda *refs: attention_kernel(width, n_lat, *refs), out_s...  14.8 us
    ppermute x1, starting transfers between devices, on_device(): lax.ppermute(jnp.where(at_north, top_mid, bottom_mid), both, pole_pairs)  8.2 us
    ppermute x1, waiting for transfers between devices, on_device(): pole_g_mid = lax.ppermute(pole_g_mid_send, both, pole_pairs)  6.68 us
    unnamed x30, local copies, waits for them, and re-layouts  5.25 us
    ppermute x1, starting transfers between devices, on_device(): lax.ppermute(jnp.where(at_north, top_send[:, edge:], bottom_send[:, edge:...  4.94 us
    ppermute x1, starting transfers between devices, on_device(): pole_g_corners = lax.ppermute(pole_g_corner_send, both, pole_pairs)  4.94 us
    ppermute x1, starting transfers between devices, on_device(): pole_g_mid = lax.ppermute(pole_g_mid_send, both, pole_pairs)  4.8 us
    ppermute x1, waiting for transfers between devices, on_device(): lax.ppermute(side_send(right_g, edge + corner), 'lon', right_pairs)  4.16 us
  transfers between devices with their start and end apart: 12, of which 4 were waited for; matrix products, arithmetic and copies ran while one was open for 14% of the time, Pallas kernels for 0%

profile of v13, /device:TPU:32, one launch (start us, length us, event | category | flops | bytes accessed | tf_op | source)
XLA Modules:
  0.0 86.1 jit_solution(15802205621263317724)
XLA Ops:
  0.6 1.2 %fusion.15 = (bf16[16,4,1024]{2,1,0:T(4,128)(2,1)S(1)}, bf16[16,4,1024]{2,1,0:T(4,128)(2,1)S(1)}) fusion(bf16[16,16,1024]{2,1,0:T(8,128)(2,1)} %param.21), kind=kLoop, calls=%fused_computation.87 | loop fusion | bytes 524288 | tf_op jit(solution)/shard_map/slice | solution.py:268
  2.1 1.7 %collective-permute-start = (bf16[2,64,1024]{2,1,0:T(8,128)(2,1)S(1)}, bf16[2,64,1024]{2,1,0:T(8,128)(2,1)S(1)}, u32[]{:S(2)}, u32[]{:S(2)}) collective-permute-start(bf16[2,64,1024]{2,1,0:T(8,128)(2,1)S(1)} %pad_maximum_fusion.2), channel_id=1, source_target_pairs={{0,1},{1,2},{2,3},{3,4},{4,5},{5,6},{6,7},{7,8},{8,9},{9,10},{10,1... | collective-permute-start | bytes 786440 | tf_op jit(solution)/shard_map/ppermute | solution.py:270
  3.8 1.4 %collective-permute-start.1 = (bf16[2,64,1024]{2,1,0:T(8,128)(2,1)S(1)}, bf16[2,64,1024]{2,1,0:T(8,128)(2,1)S(1)}, u32[]{:S(2)}, u32[]{:S(2)}) collective-permute-start(bf16[2,64,1024]{2,1,0:T(8,128)(2,1)S(1)} %pad_maximum_fusion.3), channel_id=1, source_target_pairs={{0,15},{1,0},{2,1},{3,2},{4,3},{5,4},{6,5},{7,6},{8,7},{9,8},{10,9... | collective-permute-start | bytes 786440 | tf_op jit(solution)/shard_map/ppermute | solution.py:271
  5.4 8.2 %collective-permute-start.4 = (bf16[2,64,1024]{2,1,0:T(8,128)(2,1)S(1)}, bf16[2,64,1024]{2,1,0:T(8,128)(2,1)S(1)}, u32[]{:S(2)}, u32[]{:S(2)}) collective-permute-start(bf16[2,64,1024]{2,1,0:T(8,128)(2,1)S(1)} %maximum_select_fusion), channel_id=1, source_target_pairs={{0,8},{1,9},{2,10},{3,11},{4,12},{5,13},{6,14},{7,15},{8,0},{9,1},... | collective-permute-start | bytes 786440 | tf_op jit(solution)/shard_map/ppermute | solution.py:274
  13.6 0.7 copy-done.8
  14.3 0.7 gather_fusion
  15.1 0.7 gather_fusion.4
  17.1 1.2 %gather_fusion.5 = s32[96]{0:T(128)S(1)} fusion(s32[24]{0:T(128)S(1)} %scatter_custom_fusion, s32[1024]{0:T(1024)S(1)} %pad_clamp_fusion.5), kind=kCustom, calls=%fused_computation.5.clone | custom fusion | bytes 1152 | tf_op jit(solution)/shard_map/jit(_take)/gather | solution.py:259
  18.4 1.2 %gather_fusion.1 = s32[96]{0:T(128)S(1)} fusion(s32[24]{0:T(128)S(1)} %get-tuple-element.64, s32[1024]{0:T(1024)S(1)} %pad_clamp_fusion.5), kind=kCustom, calls=%fused_computation.1.clone | custom fusion | bytes 1152 | tf_op jit(solution)/shard_map/jit(_take)/gather | solution.py:258
  20.7 4.9 %collective-permute-start.5 = (bf16[2,32,1024]{2,1,0:T(8,128)(2,1)S(1)}, bf16[2,32,1024]{2,1,0:T(8,128)(2,1)S(1)}, u32[]{:S(2)}, u32[]{:S(2)}) collective-permute-start(bf16[2,32,1024]{2,1,0:T(8,128)(2,1)S(1)} %maximum_select_fusion.1), channel_id=1, source_target_pairs={{0,8},{1,9},{2,10},{3,11},{4,12},{5,13},{6,14},{7,15},{8,0},{9,1},... | collective-permute-start | bytes 393224 | tf_op jit(solution)/shard_map/ppermute | solution.py:282
  25.7 1.3 %collective-permute-start.3 = (bf16[2,96,1024]{2,1,0:T(8,128)(2,1)S(1)}, bf16[2,96,1024]{2,1,0:T(8,128)(2,1)S(1)}, u32[]{:S(2)}, u32[]{:S(2)}) collective-permute-start(bf16[2,96,1024]{2,1,0:T(8,128)(2,1)S(1)} %pad_maximum_fusion.1), channel_id=1, source_target_pairs={{16,0},{17,1},{18,2},{19,3},{20,4},{21,5},{22,6},{23,7},{24,8},{25... | collective-permute-start | bytes 1179656 | tf_op jit(solution)/shard_map/ppermute | solution.py:281
  27.0 3.1 %collective-permute-start.2 = (bf16[2,96,1024]{2,1,0:T(8,128)(2,1)S(1)}, bf16[2,96,1024]{2,1,0:T(8,128)(2,1)S(1)}, u32[]{:S(2)}, u32[]{:S(2)}) collective-permute-start(bf16[2,96,1024]{2,1,0:T(8,128)(2,1)S(1)} %pad_maximum_fusion), channel_id=1, source_target_pairs={{0,16},{1,17},{2,18},{3,19},{4,20},{5,21},{6,22},{7,23},{8,24},{9,... | collective-permute-start | bytes 1179656 | tf_op jit(solution)/shard_map/ppermute | solution.py:280
  30.4 1.1 %gather_fusion.2 = bf16[64,2,1024]{2,1,0:T(2,128)(2,1)S(1)} fusion(bf16[2,64,1024]{2,0,1:T(2,128)(2,1)S(1)} %copy.15, s32[1024]{0:T(1024)S(1)} %pad_clamp_fusion.4), kind=kCustom, calls=%fused_computation.2.clone | custom fusion | bytes 524544 | tf_op jit(solution)/shard_map/jit(_take)/gather | solution.py:285
  31.4 0.8 fusion.2.refs_6_
  33.0 0.8 gather_fusion.3
  33.8 0.8 fusion.4.refs_7_
  34.6 0.7 copy-done.13
  35.5 14.8 %neighbourhood_attention_bwd.1 = (bf16[256,1024]{1,0:T(8,128)(2,1)}, f32[256,1024]{1,0:T(8,128)}, f32[256,1024]{1,0:T(8,128)}, bf16[2,96,1024]{2,1,0:T(8,128)(2,...) custom-call(bf16[256,1024]{1,0:T(8,128)(2,1)} %bitcast.43, ...), custom_call_target="tpu_custom_call" | custom-call | flops 2013265920 | bytes 8650752 | tf_op jit(solution)/shard_map/neighbourhood_attention_bwd/pallas_call | solution.py:195
  50.3 4.9 %collective-permute-start.6 = (bf16[2,32,1024]{2,1,0:T(8,128)(2,1)}, bf16[2,32,1024]{2,1,0:T(8,128)(2,1)S(1)}, u32[]{:S(2)}, u32[]{:S(2)}) collective-permute-start(bf16[2,32,1024]{2,1,0:T(8,128)(2,1)} %get-tuple-element.18), channel_id=1, source_target_pairs={{0,8},{1,9},{2,10},{3,11},{4,12},{5,13},{6,14},{7,15},{8,0},{9,1},... | collective-permute-start | bytes 393224 | tf_op jit(solution)/shard_map/ppermute | solution.py:296
  55.2 4.8 %collective-permute-start.8 = (bf16[2,64,1024]{2,1,0:T(8,128)(2,1)}, bf16[2,64,1024]{2,1,0:T(8,128)(2,1)S(1)}, u32[]{:S(2)}, u32[]{:S(2)}) collective-permute-start(bf16[2,64,1024]{2,1,0:T(8,128)(2,1)} %get-tuple-element.20), channel_id=1, source_target_pairs={{0,8},{1,9},{2,10},{3,11},{4,12},{5,13},{6,14},{7,15},{8,0},{9,1},... | collective-permute-start | bytes 786440 | tf_op jit(solution)/shard_map/ppermute | solution.py:317
  60.1 1.3 %collective-permute-start.7 = (bf16[2,96,1024]{2,1,0:T(8,128)(2,1)}, bf16[2,96,1024]{2,1,0:T(8,128)(2,1)S(1)}, u32[]{:S(2)}, u32[]{:S(2)}) collective-permute-start(bf16[2,96,1024]{2,1,0:T(8,128)(2,1)} %get-tuple-element.19), channel_id=1, source_target_pairs={{0,16},{1,17},{2,18},{3,19},{4,20},{5,21},{6,22},{7,23},{8,24},{9,... | collective-permute-start | bytes 1179656 | tf_op jit(solution)/shard_map/ppermute | solution.py:295
  61.4 1.3 %collective-permute-start.9 = (bf16[2,96,1024]{2,1,0:T(8,128)(2,1)}, bf16[2,96,1024]{2,1,0:T(8,128)(2,1)S(1)}, u32[]{:S(2)}, u32[]{:S(2)}) collective-permute-start(bf16[2,96,1024]{2,1,0:T(8,128)(2,1)} %get-tuple-element.21), channel_id=1, source_target_pairs={{16,0},{17,1},{18,2},{19,3},{20,4},{21,5},{22,6},{23,7},{24,8},{25... | collective-permute-start | bytes 1179656 | tf_op jit(solution)/shard_map/ppermute | solution.py:294
  62.8 0.8 gather_fusion.6
  63.7 6.7 %collective-permute-done.8 = bf16[2,64,1024]{2,1,0:T(8,128)(2,1)S(1)} collective-permute-done((bf16[2,64,1024]{2,1,0:T(8,128)(2,1)}, bf16[2,64,1024]{2,1,0:T(8,128)(2,1)S(1)}, u32[]{:S(2)}, u32[]{:S(2)}) %collective-permute-start.8) | collective-permute-done | bytes 262176 | tf_op jit(solution)/shard_map/ppermute | solution.py:317
  70.7 1.1 %gather_fusion.7 = bf16[64,2,1024]{2,1,0:T(2,128)(2,1)S(1)} fusion(bf16[2,64,1024]{2,0,1:T(2,128)(2,1)S(1)} %copy.21, s32[1024]{0:T(1024)S(1)} %pad_clamp_fusion), kind=kCustom, calls=%fused_computation.6.clone | custom fusion | bytes 524544 | tf_op jit(solution)/shard_map/jit(_take)/gather | solution.py:318
  72.3 1.0 %copy-done.5 = f32[2,64,1024]{2,1,0:T(8,128)S(1)} copy-done((f32[2,64,1024]{2,1,0:T(8,128)S(1)}, f32[2,64,1024]{2,1,0:T(8,128)}, u32[]{:S(2)}) %copy-start.5) | copy-done | bytes 524312
  73.4 0.9 %copy-done.4 = f32[2,64,1024]{2,1,0:T(8,128)S(1)} copy-done((f32[2,64,1024]{2,1,0:T(8,128)S(1)}, f32[2,64,1024]{2,1,0:T(8,128)}, u32[]{:S(2)}) %copy-start.4) | copy-done | bytes 524312
  74.4 2.1 %collective-permute-start.11 = (bf16[2,64,1024]{2,1,0:T(8,128)(2,1)S(1)}, bf16[2,64,1024]{2,1,0:T(8,128)(2,1)S(1)}, u32[]{:S(2)}, u32[]{:S(2)}) collective-permute-start(bf16[2,64,1024]{2,1,0:T(8,128)(2,1)S(1)} %add_convert_fusion.2), channel_id=1, source_target_pairs={{0,15},{1,0},{2,1},{3,2},{4,3},{5,4},{6,5},{7,6},{8,7},{9,8},{10,9... | collective-permute-start | bytes 786440 | tf_op jit(solution)/shard_map/ppermute | solution.py:315
  76.6 4.2 %collective-permute-done.10 = bf16[2,64,1024]{2,1,0:T(8,128)(2,1)S(1)} collective-permute-done((bf16[2,64,1024]{2,1,0:T(8,128)(2,1)S(1)}, bf16[2,64,1024]{2,1,0:T(8,128)(2,1)S(1)}, u32[]{:S(2)}, u32[]{:S(2)}) %collective-permute-start.10) | collective-permute-done | bytes 262176 | tf_op jit(solution)/shard_map/ppermute | solution.py:316
  80.8 2.6 %collective-permute-done.11 = bf16[2,64,1024]{2,1,0:T(8,128)(2,1)S(1)} collective-permute-done((bf16[2,64,1024]{2,1,0:T(8,128)(2,1)S(1)}, bf16[2,64,1024]{2,1,0:T(8,128)(2,1)S(1)}, u32[]{:S(2)}, u32[]{:S(2)}) %collective-permute-start.11) | collective-permute-done | bytes 262176 | tf_op jit(solution)/shard_map/ppermute | solution.py:315
  83.7 1.0 %add_convert_fusion = bf16[16,16,1024]{2,1,0:T(8,128)(2,1)} fusion(f32[4,16,1024]{2,1,0:T(8,128)S(1)} %bitcast.40, f32[16,16,1024]{2,1,0:T(8,128)S(1)} %bitcast.36, f32[4,16,1024]{2,1,0:T(8,128)S(1)} %bitcast.39, bf16[16,4,1024]{2,1,0:T(4,128)(2,1)S(1)} %convert_element_type.64, bf16[16,4,1024]{2,1,0:T(4,128)(2,1)S(1)} %convert_element_type.63), kind=kLoop, calls=%fused_computation.9 | loop fusion | flops 1835008 | bytes 2359296 | tf_op jit(solution)/shard_map/convert_element_type | solution.py:336
  85.1 1.0 %add_convert_fusion.1 = bf16[16,16,1024]{2,1,0:T(8,128)(2,1)} fusion(f32[4,16,1024]{2,1,0:T(8,128)S(1)} %bitcast.38, f32[16,16,1024]{2,1,0:T(8,128)S(1)} %bitcast.35, f32[4,16,1024]{2,1,0:T(8,128)S(1)} %bitcast.37, bf16[16,4,1024]{2,1,0:T(4,128)(2,1)S(1)} %convert_element_type.61, bf16[16,4,1024]{2,1,0:T(4,128)(2,1)S(1)} %convert_element_type.59), kind=kLoop, calls=%fused_computation.10 | loop fusion | flops 1835008 | bytes 2359296 | tf_op jit(solution)/shard_map/convert_element_type | solution.py:336
  (88 shorter events, 5.9 us)
Async XLA Ops:
  0.6 1.2 %copy-start.3 = (bf16[16,16,1024]{2,1,0:T(8,128)(2,1)S(1)}, bf16[16,16,1024]{2,1,0:T(8,128)(2,1)}, u32[]{:S(2)}) copy-start(bf16[16,16,1024]{2,1,0:T(8,128)(2,1)} %param.22) | copy-start | bytes 1572868
  2.1 17.8 %collective-permute-start = (bf16[2,64,1024]{2,1,0:T(8,128)(2,1)S(1)}, bf16[2,64,1024]{2,1,0:T(8,128)(2,1)S(1)}, u32[]{:S(2)}, u32[]{:S(2)}) collective-permute-start(bf16[2,64,1024]{2,1,0:T(8,128)(2,1)S(1)} %pad_maximum_fusion.2), channel_id=1, source_target_pairs={{0,1},{1,2},{2,3},{3,4},{4,5},{5,6},{6,7},{7,8},{8,9},{9,10},{10,1... | collective-permute-start | bytes 786440 | tf_op jit(solution)/shard_map/ppermute | solution.py:270
  3.7 1.5 %copy-start.2 = (bf16[16,16,1024]{2,1,0:T(8,128)(2,1)S(1)}, bf16[16,16,1024]{2,1,0:T(8,128)(2,1)}, u32[]{:S(2)}) copy-start(bf16[16,16,1024]{2,1,0:T(8,128)(2,1)} %param.21) | copy-start | bytes 1572868
  3.8 16.1 %collective-permute-start.1 = (bf16[2,64,1024]{2,1,0:T(8,128)(2,1)S(1)}, bf16[2,64,1024]{2,1,0:T(8,128)(2,1)S(1)}, u32[]{:S(2)}, u32[]{:S(2)}) collective-permute-start(bf16[2,64,1024]{2,1,0:T(8,128)(2,1)S(1)} %pad_maximum_fusion.3), channel_id=1, source_target_pairs={{0,15},{1,0},{2,1},{3,2},{4,3},{5,4},{6,5},{7,6},{8,7},{9,8},{10,9... | collective-permute-start | bytes 786440 | tf_op jit(solution)/shard_map/ppermute | solution.py:271
  5.4 24.7 %collective-permute-start.4 = (bf16[2,64,1024]{2,1,0:T(8,128)(2,1)S(1)}, bf16[2,64,1024]{2,1,0:T(8,128)(2,1)S(1)}, u32[]{:S(2)}, u32[]{:S(2)}) collective-permute-start(bf16[2,64,1024]{2,1,0:T(8,128)(2,1)S(1)} %maximum_select_fusion), channel_id=1, source_target_pairs={{0,8},{1,9},{2,10},{3,11},{4,12},{5,13},{6,14},{7,15},{8,0},{9,1},... | collective-permute-start | bytes 786440 | tf_op jit(solution)/shard_map/ppermute | solution.py:274
  13.6 0.7 copy-start.8
  15.8 0.7 copy-start.12
  18.3 1.3 %copy-start.9 = (s32[96]{0:T(128)S(1)}, s32[96]{0:T(128)}, u32[]{:S(2)}) copy-start(s32[96]{0:T(128)} %constant.133.clone) | copy-start | bytes 1156
  18.3 1.3 %copy-start.10 = (s32[96]{0:T(128)S(1)}, s32[96]{0:T(128)}, u32[]{:S(2)}) copy-start(s32[96]{0:T(128)} %constant.134.clone) | copy-start | bytes 1156
  18.4 1.3 %copy-start.11 = (s32[96]{0:T(128)S(1)}, s32[96]{0:T(128)}, u32[]{:S(2)}) copy-start(s32[96]{0:T(128)} %constant.135.clone) | copy-start | bytes 1156
  19.9 0.7 copy-start.6
  19.9 0.8 copy-start.7
  20.7 12.2 %collective-permute-start.5 = (bf16[2,32,1024]{2,1,0:T(8,128)(2,1)S(1)}, bf16[2,32,1024]{2,1,0:T(8,128)(2,1)S(1)}, u32[]{:S(2)}, u32[]{:S(2)}) collective-permute-start(bf16[2,32,1024]{2,1,0:T(8,128)(2,1)S(1)} %maximum_select_fusion.1), channel_id=1, source_target_pairs={{0,8},{1,9},{2,10},{3,11},{4,12},{5,13},{6,14},{7,15},{8,0},{9,1},... | collective-permute-start | bytes 393224 | tf_op jit(solution)/shard_map/ppermute | solution.py:282
  25.7 8.9 %collective-permute-start.3 = (bf16[2,96,1024]{2,1,0:T(8,128)(2,1)S(1)}, bf16[2,96,1024]{2,1,0:T(8,128)(2,1)S(1)}, u32[]{:S(2)}, u32[]{:S(2)}) collective-permute-start(bf16[2,96,1024]{2,1,0:T(8,128)(2,1)S(1)} %pad_maximum_fusion.1), channel_id=1, source_target_pairs={{16,0},{17,1},{18,2},{19,3},{20,4},{21,5},{22,6},{23,7},{24,8},{25... | collective-permute-start | bytes 1179656 | tf_op jit(solution)/shard_map/ppermute | solution.py:281
  27.0 7.6 %collective-permute-start.2 = (bf16[2,96,1024]{2,1,0:T(8,128)(2,1)S(1)}, bf16[2,96,1024]{2,1,0:T(8,128)(2,1)S(1)}, u32[]{:S(2)}, u32[]{:S(2)}) collective-permute-start(bf16[2,96,1024]{2,1,0:T(8,128)(2,1)S(1)} %pad_maximum_fusion), channel_id=1, source_target_pairs={{0,16},{1,17},{2,18},{3,19},{4,20},{5,21},{6,22},{7,23},{8,24},{9,... | collective-permute-start | bytes 1179656 | tf_op jit(solution)/shard_map/ppermute | solution.py:280
  34.6 0.7 copy-start.13
  34.6 0.9 %copy-start.14 = (bf16[2,96,1024]{2,1,0:T(8,128)(2,1)}, bf16[2,96,1024]{2,1,0:T(8,128)(2,1)S(1)}, u32[]{:S(2)}) copy-start(bf16[2,96,1024]{2,1,0:T(8,128)(2,1)S(1)} %collective-permute-done.2.refs_4_) | copy-start | bytes 1179652
  50.3 12.4 %collective-permute-start.6 = (bf16[2,32,1024]{2,1,0:T(8,128)(2,1)}, bf16[2,32,1024]{2,1,0:T(8,128)(2,1)S(1)}, u32[]{:S(2)}, u32[]{:S(2)}) collective-permute-start(bf16[2,32,1024]{2,1,0:T(8,128)(2,1)} %get-tuple-element.18), channel_id=1, source_target_pairs={{0,8},{1,9},{2,10},{3,11},{4,12},{5,13},{6,14},{7,15},{8,0},{9,1},... | collective-permute-start | bytes 393224 | tf_op jit(solution)/shard_map/ppermute | solution.py:296
  55.2 15.2 %collective-permute-start.8 = (bf16[2,64,1024]{2,1,0:T(8,128)(2,1)}, bf16[2,64,1024]{2,1,0:T(8,128)(2,1)S(1)}, u32[]{:S(2)}, u32[]{:S(2)}) collective-permute-start(bf16[2,64,1024]{2,1,0:T(8,128)(2,1)} %get-tuple-element.20), channel_id=1, source_target_pairs={{0,8},{1,9},{2,10},{3,11},{4,12},{5,13},{6,14},{7,15},{8,0},{9,1},... | collective-permute-start | bytes 786440 | tf_op jit(solution)/shard_map/ppermute | solution.py:317
  60.1 11.9 %collective-permute-start.7 = (bf16[2,96,1024]{2,1,0:T(8,128)(2,1)}, bf16[2,96,1024]{2,1,0:T(8,128)(2,1)S(1)}, u32[]{:S(2)}, u32[]{:S(2)}) collective-permute-start(bf16[2,96,1024]{2,1,0:T(8,128)(2,1)} %get-tuple-element.19), channel_id=1, source_target_pairs={{0,16},{1,17},{2,18},{3,19},{4,20},{5,21},{6,22},{7,23},{8,24},{9,... | collective-permute-start | bytes 1179656 | tf_op jit(solution)/shard_map/ppermute | solution.py:295
  61.4 10.6 %collective-permute-start.9 = (bf16[2,96,1024]{2,1,0:T(8,128)(2,1)}, bf16[2,96,1024]{2,1,0:T(8,128)(2,1)S(1)}, u32[]{:S(2)}, u32[]{:S(2)}) collective-permute-start(bf16[2,96,1024]{2,1,0:T(8,128)(2,1)} %get-tuple-element.21), channel_id=1, source_target_pairs={{16,0},{17,1},{18,2},{19,3},{20,4},{21,5},{22,6},{23,7},{24,8},{25... | collective-permute-start | bytes 1179656 | tf_op jit(solution)/shard_map/ppermute | solution.py:294
  72.2 1.0 %copy-start.5 = (f32[2,64,1024]{2,1,0:T(8,128)S(1)}, f32[2,64,1024]{2,1,0:T(8,128)}, u32[]{:S(2)}) copy-start(f32[2,64,1024]{2,1,0:T(8,128)} %get-tuple-element.22) | copy-start | bytes 1572868
  73.3 1.0 %copy-start.4 = (f32[2,64,1024]{2,1,0:T(8,128)S(1)}, f32[2,64,1024]{2,1,0:T(8,128)}, u32[]{:S(2)}) copy-start(f32[2,64,1024]{2,1,0:T(8,128)} %get-tuple-element.23) | copy-start | bytes 1572868
  73.3 7.4 %collective-permute-start.10 = (bf16[2,64,1024]{2,1,0:T(8,128)(2,1)S(1)}, bf16[2,64,1024]{2,1,0:T(8,128)(2,1)S(1)}, u32[]{:S(2)}, u32[]{:S(2)}) collective-permute-start(bf16[2,64,1024]{2,1,0:T(8,128)(2,1)S(1)} %add_convert_fusion.3), channel_id=1, source_target_pairs={{0,1},{1,2},{2,3},{3,4},{4,5},{5,6},{6,7},{7,8},{8,9},{9,10},{10,1... | collective-permute-start | bytes 786440 | tf_op jit(solution)/shard_map/ppermute | solution.py:316
  74.4 9.1 %collective-permute-start.11 = (bf16[2,64,1024]{2,1,0:T(8,128)(2,1)S(1)}, bf16[2,64,1024]{2,1,0:T(8,128)(2,1)S(1)}, u32[]{:S(2)}, u32[]{:S(2)}) collective-permute-start(bf16[2,64,1024]{2,1,0:T(8,128)(2,1)S(1)} %add_convert_fusion.2), channel_id=1, source_target_pairs={{0,15},{1,0},{2,1},{3,2},{4,3},{5,4},{6,5},{7,6},{8,7},{9,8},{10,9... | collective-permute-start | bytes 786440 | tf_op jit(solution)/shard_map/ppermute | solution.py:315
  76.6 7.1 %copy-start.1 = (f32[256,1024]{1,0:T(8,128)S(1)}, f32[256,1024]{1,0:T(8,128)}, u32[]{:S(2)}) copy-start(f32[256,1024]{1,0:T(8,128)} %get-tuple-element.24) | copy-start | bytes 3145732
  83.7 1.4 %copy-start = (f32[256,1024]{1,0:T(8,128)S(1)}, f32[256,1024]{1,0:T(8,128)}, u32[]{:S(2)}) copy-start(f32[256,1024]{1,0:T(8,128)} %get-tuple-element.17) | copy-start | bytes 3145732

commit v14 on v13

--- a/solution.py
+++ b/solution.py
@@ -165,7 +165,7 @@
             scatter_grads(dv, dv_own, 1, t, lanes)
         return carry
 
-    lax.fori_loop(0, pairs, body, 0, unroll=2)
+    lax.fori_loop(0, pairs, body, 0, unroll=4)
 
 
 def attention_core(q2, g2, k2, v2, above, below, pole_mid, pole_corner, left_in, right_in, width, n_lat):

time: 87.9 us -> 87.5 us (level)
  no operation moved by 1% of the time
where the time goes in v14:
time: 87.5 us; the launch traced here: 85.7 us
  starting transfers between devices  35.1 us (40%)
  local copies, waits for them, and re-layouts  16.2 us (19%)
  Pallas kernels  14.4 us (16%)
  waiting for transfers between devices  14.1 us (16%)
  other arithmetic  4.76 us (5%)
  between operations  1.21 us (1%)
    pallas_call x1, Pallas kernels, attention_core(): pl.pallas_call(lambda *refs: attention_kernel(width, n_lat, *refs), out_s...  14.4 us
    ppermute x1, starting transfers between devices, on_device(): lax.ppermute(jnp.where(at_north, top_mid, bottom_mid), both, pole_pairs)  8.2 us
    ppermute x1, waiting for transfers between devices, on_device(): pole_g_mid = lax.ppermute(pole_g_mid_send, both, pole_pairs)  6.68 us
    unnamed x30, local copies, waits for them, and re-layouts  5.25 us
    ppermute x1, starting transfers between devices, on_device(): lax.ppermute(jnp.where(at_north, top_send[:, edge:], bottom_send[:, edge:...  4.94 us
    ppermute x1, starting transfers between devices, on_device(): pole_g_corners = lax.ppermute(pole_g_corner_send, both, pole_pairs)  4.94 us
    ppermute x1, starting transfers between devices, on_device(): pole_g_mid = lax.ppermute(pole_g_mid_send, both, pole_pairs)  4.8 us
    ppermute x1, waiting for transfers between devices, on_device(): lax.ppermute(side_send(right_g, edge + corner), 'lon', right_pairs)  4.16 us
  transfers between devices with their start and end apart: 12, of which 4 were waited for; matrix products, arithmetic and copies ran while one was open for 14% of the time, Pallas kernels for 0%

profile of v14, /device:TPU:32, one launch (start us, length us, event | category | flops | bytes accessed | tf_op | source)
XLA Modules:
  0.0 85.7 jit_solution(12592473344589299864)
XLA Ops:
  0.6 1.2 %fusion.15 = (bf16[16,4,1024]{2,1,0:T(4,128)(2,1)S(1)}, bf16[16,4,1024]{2,1,0:T(4,128)(2,1)S(1)}) fusion(bf16[16,16,1024]{2,1,0:T(8,128)(2,1)} %param.21), kind=kLoop, calls=%fused_computation.87 | loop fusion | bytes 524288 | tf_op jit(solution)/shard_map/slice | solution.py:268
  2.1 1.7 %collective-permute-start = (bf16[2,64,1024]{2,1,0:T(8,128)(2,1)S(1)}, bf16[2,64,1024]{2,1,0:T(8,128)(2,1)S(1)}, u32[]{:S(2)}, u32[]{:S(2)}) collective-permute-start(bf16[2,64,1024]{2,1,0:T(8,128)(2,1)S(1)} %pad_maximum_fusion.2), channel_id=1, source_target_pairs={{0,1},{1,2},{2,3},{3,4},{4,5},{5,6},{6,7},{7,8},{8,9},{9,10},{10,1... | collective-permute-start | bytes 786440 | tf_op jit(solution)/shard_map/ppermute | solution.py:270
  3.8 1.4 %collective-permute-start.1 = (bf16[2,64,1024]{2,1,0:T(8,128)(2,1)S(1)}, bf16[2,64,1024]{2,1,0:T(8,128)(2,1)S(1)}, u32[]{:S(2)}, u32[]{:S(2)}) collective-permute-start(bf16[2,64,1024]{2,1,0:T(8,128)(2,1)S(1)} %pad_maximum_fusion.3), channel_id=1, source_target_pairs={{0,15},{1,0},{2,1},{3,2},{4,3},{5,4},{6,5},{7,6},{8,7},{9,8},{10,9... | collective-permute-start | bytes 786440 | tf_op jit(solution)/shard_map/ppermute | solution.py:271
  5.4 8.2 %collective-permute-start.4 = (bf16[2,64,1024]{2,1,0:T(8,128)(2,1)S(1)}, bf16[2,64,1024]{2,1,0:T(8,128)(2,1)S(1)}, u32[]{:S(2)}, u32[]{:S(2)}) collective-permute-start(bf16[2,64,1024]{2,1,0:T(8,128)(2,1)S(1)} %maximum_select_fusion), channel_id=1, source_target_pairs={{0,8},{1,9},{2,10},{3,11},{4,12},{5,13},{6,14},{7,15},{8,0},{9,1},... | collective-permute-start | bytes 786440 | tf_op jit(solution)/shard_map/ppermute | solution.py:274
  13.6 0.7 copy-done.8
  14.3 0.7 gather_fusion
  15.1 0.7 gather_fusion.4
  17.1 1.2 %gather_fusion.5 = s32[96]{0:T(128)S(1)} fusion(s32[24]{0:T(128)S(1)} %scatter_custom_fusion, s32[1024]{0:T(1024)S(1)} %pad_clamp_fusion.5), kind=kCustom, calls=%fused_computation.5.clone | custom fusion | bytes 1152 | tf_op jit(solution)/shard_map/jit(_take)/gather | solution.py:259
  18.4 1.2 %gather_fusion.1 = s32[96]{0:T(128)S(1)} fusion(s32[24]{0:T(128)S(1)} %get-tuple-element.64, s32[1024]{0:T(1024)S(1)} %pad_clamp_fusion.5), kind=kCustom, calls=%fused_computation.1.clone | custom fusion | bytes 1152 | tf_op jit(solution)/shard_map/jit(_take)/gather | solution.py:258
  20.7 4.9 %collective-permute-start.5 = (bf16[2,32,1024]{2,1,0:T(8,128)(2,1)S(1)}, bf16[2,32,1024]{2,1,0:T(8,128)(2,1)S(1)}, u32[]{:S(2)}, u32[]{:S(2)}) collective-permute-start(bf16[2,32,1024]{2,1,0:T(8,128)(2,1)S(1)} %maximum_select_fusion.1), channel_id=1, source_target_pairs={{0,8},{1,9},{2,10},{3,11},{4,12},{5,13},{6,14},{7,15},{8,0},{9,1},... | collective-permute-start | bytes 393224 | tf_op jit(solution)/shard_map/ppermute | solution.py:282
  25.7 1.3 %collective-permute-start.3 = (bf16[2,96,1024]{2,1,0:T(8,128)(2,1)S(1)}, bf16[2,96,1024]{2,1,0:T(8,128)(2,1)S(1)}, u32[]{:S(2)}, u32[]{:S(2)}) collective-permute-start(bf16[2,96,1024]{2,1,0:T(8,128)(2,1)S(1)} %pad_maximum_fusion.1), channel_id=1, source_target_pairs={{16,0},{17,1},{18,2},{19,3},{20,4},{21,5},{22,6},{23,7},{24,8},{25... | collective-permute-start | bytes 1179656 | tf_op jit(solution)/shard_map/ppermute | solution.py:281
  27.0 3.1 %collective-permute-start.2 = (bf16[2,96,1024]{2,1,0:T(8,128)(2,1)S(1)}, bf16[2,96,1024]{2,1,0:T(8,128)(2,1)S(1)}, u32[]{:S(2)}, u32[]{:S(2)}) collective-permute-start(bf16[2,96,1024]{2,1,0:T(8,128)(2,1)S(1)} %pad_maximum_fusion), channel_id=1, source_target_pairs={{0,16},{1,17},{2,18},{3,19},{4,20},{5,21},{6,22},{7,23},{8,24},{9,... | collective-permute-start | bytes 1179656 | tf_op jit(solution)/shard_map/ppermute | solution.py:280
  30.4 1.1 %gather_fusion.2 = bf16[64,2,1024]{2,1,0:T(2,128)(2,1)S(1)} fusion(bf16[2,64,1024]{2,0,1:T(2,128)(2,1)S(1)} %copy.15, s32[1024]{0:T(1024)S(1)} %pad_clamp_fusion.4), kind=kCustom, calls=%fused_computation.2.clone | custom fusion | bytes 524544 | tf_op jit(solution)/shard_map/jit(_take)/gather | solution.py:285
  31.4 0.8 fusion.2.refs_6_
  33.0 0.8 gather_fusion.3
  33.8 0.8 fusion.4.refs_7_
  34.6 0.7 copy-done.13
  35.5 14.4 %neighbourhood_attention_bwd.1 = (bf16[256,1024]{1,0:T(8,128)(2,1)}, f32[256,1024]{1,0:T(8,128)}, f32[256,1024]{1,0:T(8,128)}, bf16[2,96,1024]{2,1,0:T(8,128)(2,...) custom-call(bf16[256,1024]{1,0:T(8,128)(2,1)} %bitcast.43, ...), custom_call_target="tpu_custom_call" | custom-call | flops 2013265920 | bytes 8650752 | tf_op jit(solution)/shard_map/neighbourhood_attention_bwd/pallas_call | solution.py:195
  49.9 4.9 %collective-permute-start.6 = (bf16[2,32,1024]{2,1,0:T(8,128)(2,1)}, bf16[2,32,1024]{2,1,0:T(8,128)(2,1)S(1)}, u32[]{:S(2)}, u32[]{:S(2)}) collective-permute-start(bf16[2,32,1024]{2,1,0:T(8,128)(2,1)} %get-tuple-element.18), channel_id=1, source_target_pairs={{0,8},{1,9},{2,10},{3,11},{4,12},{5,13},{6,14},{7,15},{8,0},{9,1},... | collective-permute-start | bytes 393224 | tf_op jit(solution)/shard_map/ppermute | solution.py:296
  54.8 4.8 %collective-permute-start.8 = (bf16[2,64,1024]{2,1,0:T(8,128)(2,1)}, bf16[2,64,1024]{2,1,0:T(8,128)(2,1)S(1)}, u32[]{:S(2)}, u32[]{:S(2)}) collective-permute-start(bf16[2,64,1024]{2,1,0:T(8,128)(2,1)} %get-tuple-element.20), channel_id=1, source_target_pairs={{0,8},{1,9},{2,10},{3,11},{4,12},{5,13},{6,14},{7,15},{8,0},{9,1},... | collective-permute-start | bytes 786440 | tf_op jit(solution)/shard_map/ppermute | solution.py:317
  59.7 1.3 %collective-permute-start.7 = (bf16[2,96,1024]{2,1,0:T(8,128)(2,1)}, bf16[2,96,1024]{2,1,0:T(8,128)(2,1)S(1)}, u32[]{:S(2)}, u32[]{:S(2)}) collective-permute-start(bf16[2,96,1024]{2,1,0:T(8,128)(2,1)} %get-tuple-element.19), channel_id=1, source_target_pairs={{0,16},{1,17},{2,18},{3,19},{4,20},{5,21},{6,22},{7,23},{8,24},{9,... | collective-permute-start | bytes 1179656 | tf_op jit(solution)/shard_map/ppermute | solution.py:295
  61.0 1.3 %collective-permute-start.9 = (bf16[2,96,1024]{2,1,0:T(8,128)(2,1)}, bf16[2,96,1024]{2,1,0:T(8,128)(2,1)S(1)}, u32[]{:S(2)}, u32[]{:S(2)}) collective-permute-start(bf16[2,96,1024]{2,1,0:T(8,128)(2,1)} %get-tuple-element.21), channel_id=1, source_target_pairs={{16,0},{17,1},{18,2},{19,3},{20,4},{21,5},{22,6},{23,7},{24,8},{25... | collective-permute-start | bytes 1179656 | tf_op jit(solution)/shard_map/ppermute | solution.py:294
  62.4 0.8 gather_fusion.6
  63.4 6.7 %collective-permute-done.8 = bf16[2,64,1024]{2,1,0:T(8,128)(2,1)S(1)} collective-permute-done((bf16[2,64,1024]{2,1,0:T(8,128)(2,1)}, bf16[2,64,1024]{2,1,0:T(8,128)(2,1)S(1)}, u32[]{:S(2)}, u32[]{:S(2)}) %collective-permute-start.8) | collective-permute-done | bytes 262176 | tf_op jit(solution)/shard_map/ppermute | solution.py:317
  70.3 1.1 %gather_fusion.7 = bf16[64,2,1024]{2,1,0:T(2,128)(2,1)S(1)} fusion(bf16[2,64,1024]{2,0,1:T(2,128)(2,1)S(1)} %copy.21, s32[1024]{0:T(1024)S(1)} %pad_clamp_fusion), kind=kCustom, calls=%fused_computation.6.clone | custom fusion | bytes 524544 | tf_op jit(solution)/shard_map/jit(_take)/gather | solution.py:318
  71.9 1.0 %copy-done.5 = f32[2,64,1024]{2,1,0:T(8,128)S(1)} copy-done((f32[2,64,1024]{2,1,0:T(8,128)S(1)}, f32[2,64,1024]{2,1,0:T(8,128)}, u32[]{:S(2)}) %copy-start.5) | copy-done | bytes 524312
  73.0 0.9 %copy-done.4 = f32[2,64,1024]{2,1,0:T(8,128)S(1)} copy-done((f32[2,64,1024]{2,1,0:T(8,128)S(1)}, f32[2,64,1024]{2,1,0:T(8,128)}, u32[]{:S(2)}) %copy-start.4) | copy-done | bytes 524312
  74.0 2.1 %collective-permute-start.11 = (bf16[2,64,1024]{2,1,0:T(8,128)(2,1)S(1)}, bf16[2,64,1024]{2,1,0:T(8,128)(2,1)S(1)}, u32[]{:S(2)}, u32[]{:S(2)}) collective-permute-start(bf16[2,64,1024]{2,1,0:T(8,128)(2,1)S(1)} %add_convert_fusion.2), channel_id=1, source_target_pairs={{0,15},{1,0},{2,1},{3,2},{4,3},{5,4},{6,5},{7,6},{8,7},{9,8},{10,9... | collective-permute-start | bytes 786440 | tf_op jit(solution)/shard_map/ppermute | solution.py:315
  76.2 4.2 %collective-permute-done.10 = bf16[2,64,1024]{2,1,0:T(8,128)(2,1)S(1)} collective-permute-done((bf16[2,64,1024]{2,1,0:T(8,128)(2,1)S(1)}, bf16[2,64,1024]{2,1,0:T(8,128)(2,1)S(1)}, u32[]{:S(2)}, u32[]{:S(2)}) %collective-permute-start.10) | collective-permute-done | bytes 262176 | tf_op jit(solution)/shard_map/ppermute | solution.py:316
  80.5 2.6 %collective-permute-done.11 = bf16[2,64,1024]{2,1,0:T(8,128)(2,1)S(1)} collective-permute-done((bf16[2,64,1024]{2,1,0:T(8,128)(2,1)S(1)}, bf16[2,64,1024]{2,1,0:T(8,128)(2,1)S(1)}, u32[]{:S(2)}, u32[]{:S(2)}) %collective-permute-start.11) | collective-permute-done | bytes 262176 | tf_op jit(solution)/shard_map/ppermute | solution.py:315
  83.3 1.0 %add_convert_fusion = bf16[16,16,1024]{2,1,0:T(8,128)(2,1)} fusion(f32[4,16,1024]{2,1,0:T(8,128)S(1)} %bitcast.40, f32[16,16,1024]{2,1,0:T(8,128)S(1)} %bitcast.36, f32[4,16,1024]{2,1,0:T(8,128)S(1)} %bitcast.39, bf16[16,4,1024]{2,1,0:T(4,128)(2,1)S(1)} %convert_element_type.64, bf16[16,4,1024]{2,1,0:T(4,128)(2,1)S(1)} %convert_element_type.63), kind=kLoop, calls=%fused_computation.9 | loop fusion | flops 1835008 | bytes 2359296 | tf_op jit(solution)/shard_map/convert_element_type | solution.py:336
  84.7 1.0 %add_convert_fusion.1 = bf16[16,16,1024]{2,1,0:T(8,128)(2,1)} fusion(f32[4,16,1024]{2,1,0:T(8,128)S(1)} %bitcast.38, f32[16,16,1024]{2,1,0:T(8,128)S(1)} %bitcast.35, f32[4,16,1024]{2,1,0:T(8,128)S(1)} %bitcast.37, bf16[16,4,1024]{2,1,0:T(4,128)(2,1)S(1)} %convert_element_type.61, bf16[16,4,1024]{2,1,0:T(4,128)(2,1)S(1)} %convert_element_type.59), kind=kLoop, calls=%fused_computation.10 | loop fusion | flops 1835008 | bytes 2359296 | tf_op jit(solution)/shard_map/convert_element_type | solution.py:336
  (88 shorter events, 5.9 us)
Async XLA Ops:
  0.6 1.2 %copy-start.3 = (bf16[16,16,1024]{2,1,0:T(8,128)(2,1)S(1)}, bf16[16,16,1024]{2,1,0:T(8,128)(2,1)}, u32[]{:S(2)}) copy-start(bf16[16,16,1024]{2,1,0:T(8,128)(2,1)} %param.22) | copy-start | bytes 1572868
  2.1 17.8 %collective-permute-start = (bf16[2,64,1024]{2,1,0:T(8,128)(2,1)S(1)}, bf16[2,64,1024]{2,1,0:T(8,128)(2,1)S(1)}, u32[]{:S(2)}, u32[]{:S(2)}) collective-permute-start(bf16[2,64,1024]{2,1,0:T(8,128)(2,1)S(1)} %pad_maximum_fusion.2), channel_id=1, source_target_pairs={{0,1},{1,2},{2,3},{3,4},{4,5},{5,6},{6,7},{7,8},{8,9},{9,10},{10,1... | collective-permute-start | bytes 786440 | tf_op jit(solution)/shard_map/ppermute | solution.py:270
  3.7 1.5 %copy-start.2 = (bf16[16,16,1024]{2,1,0:T(8,128)(2,1)S(1)}, bf16[16,16,1024]{2,1,0:T(8,128)(2,1)}, u32[]{:S(2)}) copy-start(bf16[16,16,1024]{2,1,0:T(8,128)(2,1)} %param.21) | copy-start | bytes 1572868
  3.8 16.1 %collective-permute-start.1 = (bf16[2,64,1024]{2,1,0:T(8,128)(2,1)S(1)}, bf16[2,64,1024]{2,1,0:T(8,128)(2,1)S(1)}, u32[]{:S(2)}, u32[]{:S(2)}) collective-permute-start(bf16[2,64,1024]{2,1,0:T(8,128)(2,1)S(1)} %pad_maximum_fusion.3), channel_id=1, source_target_pairs={{0,15},{1,0},{2,1},{3,2},{4,3},{5,4},{6,5},{7,6},{8,7},{9,8},{10,9... | collective-permute-start | bytes 786440 | tf_op jit(solution)/shard_map/ppermute | solution.py:271
  5.4 24.7 %collective-permute-start.4 = (bf16[2,64,1024]{2,1,0:T(8,128)(2,1)S(1)}, bf16[2,64,1024]{2,1,0:T(8,128)(2,1)S(1)}, u32[]{:S(2)}, u32[]{:S(2)}) collective-permute-start(bf16[2,64,1024]{2,1,0:T(8,128)(2,1)S(1)} %maximum_select_fusion), channel_id=1, source_target_pairs={{0,8},{1,9},{2,10},{3,11},{4,12},{5,13},{6,14},{7,15},{8,0},{9,1},... | collective-permute-start | bytes 786440 | tf_op jit(solution)/shard_map/ppermute | solution.py:274
  13.6 0.7 copy-start.8
  15.8 0.7 copy-start.12
  18.3 1.3 %copy-start.9 = (s32[96]{0:T(128)S(1)}, s32[96]{0:T(128)}, u32[]{:S(2)}) copy-start(s32[96]{0:T(128)} %constant.133.clone) | copy-start | bytes 1156
  18.3 1.3 %copy-start.10 = (s32[96]{0:T(128)S(1)}, s32[96]{0:T(128)}, u32[]{:S(2)}) copy-start(s32[96]{0:T(128)} %constant.134.clone) | copy-start | bytes 1156
  18.4 1.3 %copy-start.11 = (s32[96]{0:T(128)S(1)}, s32[96]{0:T(128)}, u32[]{:S(2)}) copy-start(s32[96]{0:T(128)} %constant.135.clone) | copy-start | bytes 1156
  19.9 0.7 copy-start.6
  19.9 0.8 copy-start.7
  20.7 12.2 %collective-permute-start.5 = (bf16[2,32,1024]{2,1,0:T(8,128)(2,1)S(1)}, bf16[2,32,1024]{2,1,0:T(8,128)(2,1)S(1)}, u32[]{:S(2)}, u32[]{:S(2)}) collective-permute-start(bf16[2,32,1024]{2,1,0:T(8,128)(2,1)S(1)} %maximum_select_fusion.1), channel_id=1, source_target_pairs={{0,8},{1,9},{2,10},{3,11},{4,12},{5,13},{6,14},{7,15},{8,0},{9,1},... | collective-permute-start | bytes 393224 | tf_op jit(solution)/shard_map/ppermute | solution.py:282
  25.7 8.9 %collective-permute-start.3 = (bf16[2,96,1024]{2,1,0:T(8,128)(2,1)S(1)}, bf16[2,96,1024]{2,1,0:T(8,128)(2,1)S(1)}, u32[]{:S(2)}, u32[]{:S(2)}) collective-permute-start(bf16[2,96,1024]{2,1,0:T(8,128)(2,1)S(1)} %pad_maximum_fusion.1), channel_id=1, source_target_pairs={{16,0},{17,1},{18,2},{19,3},{20,4},{21,5},{22,6},{23,7},{24,8},{25... | collective-permute-start | bytes 1179656 | tf_op jit(solution)/shard_map/ppermute | solution.py:281
  27.0 7.6 %collective-permute-start.2 = (bf16[2,96,1024]{2,1,0:T(8,128)(2,1)S(1)}, bf16[2,96,1024]{2,1,0:T(8,128)(2,1)S(1)}, u32[]{:S(2)}, u32[]{:S(2)}) collective-permute-start(bf16[2,96,1024]{2,1,0:T(8,128)(2,1)S(1)} %pad_maximum_fusion), channel_id=1, source_target_pairs={{0,16},{1,17},{2,18},{3,19},{4,20},{5,21},{6,22},{7,23},{8,24},{9,... | collective-permute-start | bytes 1179656 | tf_op jit(solution)/shard_map/ppermute | solution.py:280
  34.6 0.7 copy-start.13
  34.6 0.9 %copy-start.14 = (bf16[2,96,1024]{2,1,0:T(8,128)(2,1)}, bf16[2,96,1024]{2,1,0:T(8,128)(2,1)S(1)}, u32[]{:S(2)}) copy-start(bf16[2,96,1024]{2,1,0:T(8,128)(2,1)S(1)} %collective-permute-done.2.refs_4_) | copy-start | bytes 1179652
  49.9 12.4 %collective-permute-start.6 = (bf16[2,32,1024]{2,1,0:T(8,128)(2,1)}, bf16[2,32,1024]{2,1,0:T(8,128)(2,1)S(1)}, u32[]{:S(2)}, u32[]{:S(2)}) collective-permute-start(bf16[2,32,1024]{2,1,0:T(8,128)(2,1)} %get-tuple-element.18), channel_id=1, source_target_pairs={{0,8},{1,9},{2,10},{3,11},{4,12},{5,13},{6,14},{7,15},{8,0},{9,1},... | collective-permute-start | bytes 393224 | tf_op jit(solution)/shard_map/ppermute | solution.py:296
  54.8 15.2 %collective-permute-start.8 = (bf16[2,64,1024]{2,1,0:T(8,128)(2,1)}, bf16[2,64,1024]{2,1,0:T(8,128)(2,1)S(1)}, u32[]{:S(2)}, u32[]{:S(2)}) collective-permute-start(bf16[2,64,1024]{2,1,0:T(8,128)(2,1)} %get-tuple-element.20), channel_id=1, source_target_pairs={{0,8},{1,9},{2,10},{3,11},{4,12},{5,13},{6,14},{7,15},{8,0},{9,1},... | collective-permute-start | bytes 786440 | tf_op jit(solution)/shard_map/ppermute | solution.py:317
  59.7 11.9 %collective-permute-start.7 = (bf16[2,96,1024]{2,1,0:T(8,128)(2,1)}, bf16[2,96,1024]{2,1,0:T(8,128)(2,1)S(1)}, u32[]{:S(2)}, u32[]{:S(2)}) collective-permute-start(bf16[2,96,1024]{2,1,0:T(8,128)(2,1)} %get-tuple-element.19), channel_id=1, source_target_pairs={{0,16},{1,17},{2,18},{3,19},{4,20},{5,21},{6,22},{7,23},{8,24},{9,... | collective-permute-start | bytes 1179656 | tf_op jit(solution)/shard_map/ppermute | solution.py:295
  61.0 10.6 %collective-permute-start.9 = (bf16[2,96,1024]{2,1,0:T(8,128)(2,1)}, bf16[2,96,1024]{2,1,0:T(8,128)(2,1)S(1)}, u32[]{:S(2)}, u32[]{:S(2)}) collective-permute-start(bf16[2,96,1024]{2,1,0:T(8,128)(2,1)} %get-tuple-element.21), channel_id=1, source_target_pairs={{16,0},{17,1},{18,2},{19,3},{20,4},{21,5},{22,6},{23,7},{24,8},{25... | collective-permute-start | bytes 1179656 | tf_op jit(solution)/shard_map/ppermute | solution.py:294
  71.8 1.0 %copy-start.5 = (f32[2,64,1024]{2,1,0:T(8,128)S(1)}, f32[2,64,1024]{2,1,0:T(8,128)}, u32[]{:S(2)}) copy-start(f32[2,64,1024]{2,1,0:T(8,128)} %get-tuple-element.22) | copy-start | bytes 1572868
  72.9 1.0 %copy-start.4 = (f32[2,64,1024]{2,1,0:T(8,128)S(1)}, f32[2,64,1024]{2,1,0:T(8,128)}, u32[]{:S(2)}) copy-start(f32[2,64,1024]{2,1,0:T(8,128)} %get-tuple-element.23) | copy-start | bytes 1572868
  72.9 7.4 %collective-permute-start.10 = (bf16[2,64,1024]{2,1,0:T(8,128)(2,1)S(1)}, bf16[2,64,1024]{2,1,0:T(8,128)(2,1)S(1)}, u32[]{:S(2)}, u32[]{:S(2)}) collective-permute-start(bf16[2,64,1024]{2,1,0:T(8,128)(2,1)S(1)} %add_convert_fusion.3), channel_id=1, source_target_pairs={{0,1},{1,2},{2,3},{3,4},{4,5},{5,6},{6,7},{7,8},{8,9},{9,10},{10,1... | collective-permute-start | bytes 786440 | tf_op jit(solution)/shard_map/ppermute | solution.py:316
  74.0 9.1 %collective-permute-start.11 = (bf16[2,64,1024]{2,1,0:T(8,128)(2,1)S(1)}, bf16[2,64,1024]{2,1,0:T(8,128)(2,1)S(1)}, u32[]{:S(2)}, u32[]{:S(2)}) collective-permute-start(bf16[2,64,1024]{2,1,0:T(8,128)(2,1)S(1)} %add_convert_fusion.2), channel_id=1, source_target_pairs={{0,15},{1,0},{2,1},{3,2},{4,3},{5,4},{6,5},{7,6},{8,7},{9,8},{10,9... | collective-permute-start | bytes 786440 | tf_op jit(solution)/shard_map/ppermute | solution.py:315
  76.2 7.1 %copy-start.1 = (f32[256,1024]{1,0:T(8,128)S(1)}, f32[256,1024]{1,0:T(8,128)}, u32[]{:S(2)}) copy-start(f32[256,1024]{1,0:T(8,128)} %get-tuple-element.24) | copy-start | bytes 3145732
  83.3 1.4 %copy-start = (f32[256,1024]{1,0:T(8,128)S(1)}, f32[256,1024]{1,0:T(8,128)}, u32[]{:S(2)}) copy-start(f32[256,1024]{1,0:T(8,128)} %get-tuple-element.17) | copy-start | bytes 3145732

commit v15 on v14

--- a/solution.py
+++ b/solution.py
@@ -165,7 +165,7 @@
             scatter_grads(dv, dv_own, 1, t, lanes)
         return carry
 
-    lax.fori_loop(0, pairs, body, 0, unroll=4)
+    lax.fori_loop(0, pairs, body, 0, unroll=True)
 
 
 def attention_core(q2, g2, k2, v2, above, below, pole_mid, pole_corner, left_in, right_in, width, n_lat):

time: 87.5 us -> 87 us (level)
  no operation moved by 1% of the time
where the time goes in v15:
time: 87 us; the launch traced here: 85.3 us
  starting transfers between devices  35.3 us (41%)
  local copies, waits for them, and re-layouts  16.2 us (19%)
  Pallas kernels  14 us (16%)
  waiting for transfers between devices  13.9 us (16%)
  other arithmetic  4.76 us (5%)
  between operations  1.21 us (1%)
    pallas_call x1, Pallas kernels, attention_core(): pl.pallas_call(lambda *refs: attention_kernel(width, n_lat, *refs), out_s...  14 us
    ppermute x1, starting transfers between devices, on_device(): lax.ppermute(jnp.where(at_north, top_mid, bottom_mid), both, pole_pairs)  8.2 us
    ppermute x1, waiting for transfers between devices, on_device(): pole_g_mid = lax.ppermute(pole_g_mid_send, both, pole_pairs)  6.68 us
    unnamed x30, local copies, waits for them, and re-layouts  5.25 us
    ppermute x1, starting transfers between devices, on_device(): lax.ppermute(jnp.where(at_north, top_send[:, edge:], bottom_send[:, edge:...  4.94 us
    ppermute x1, starting transfers between devices, on_device(): pole_g_corners = lax.ppermute(pole_g_corner_send, both, pole_pairs)  4.94 us
    ppermute x1, starting transfers between devices, on_device(): pole_g_mid = lax.ppermute(pole_g_mid_send, both, pole_pairs)  4.8 us
    ppermute x1, waiting for transfers between devices, on_device(): lax.ppermute(side_send(right_g, edge + corner), 'lon', right_pairs)  4.16 us
  transfers between devices with their start and end apart: 12, of which 4 were waited for; matrix products, arithmetic and copies ran while one was open for 14% of the time, Pallas kernels for 0%

profile of v15, /device:TPU:32, one launch (start us, length us, event | category | flops | bytes accessed | tf_op | source)
XLA Modules:
  0.0 85.3 jit_solution(5069531180155111661)
XLA Ops:
  0.6 1.2 %fusion.15 = (bf16[16,4,1024]{2,1,0:T(4,128)(2,1)S(1)}, bf16[16,4,1024]{2,1,0:T(4,128)(2,1)S(1)}) fusion(bf16[16,16,1024]{2,1,0:T(8,128)(2,1)} %param.21), kind=kLoop, calls=%fused_computation.87 | loop fusion | bytes 524288 | tf_op jit(solution)/shard_map/slice | solution.py:268
  2.1 1.7 %collective-permute-start = (bf16[2,64,1024]{2,1,0:T(8,128)(2,1)S(1)}, bf16[2,64,1024]{2,1,0:T(8,128)(2,1)S(1)}, u32[]{:S(2)}, u32[]{:S(2)}) collective-permute-start(bf16[2,64,1024]{2,1,0:T(8,128)(2,1)S(1)} %pad_maximum_fusion.2), channel_id=1, source_target_pairs={{0,1},{1,2},{2,3},{3,4},{4,5},{5,6},{6,7},{7,8},{8,9},{9,10},{10,1... | collective-permute-start | bytes 786440 | tf_op jit(solution)/shard_map/ppermute | solution.py:270
  3.8 1.4 %collective-permute-start.1 = (bf16[2,64,1024]{2,1,0:T(8,128)(2,1)S(1)}, bf16[2,64,1024]{2,1,0:T(8,128)(2,1)S(1)}, u32[]{:S(2)}, u32[]{:S(2)}) collective-permute-start(bf16[2,64,1024]{2,1,0:T(8,128)(2,1)S(1)} %pad_maximum_fusion.3), channel_id=1, source_target_pairs={{0,15},{1,0},{2,1},{3,2},{4,3},{5,4},{6,5},{7,6},{8,7},{9,8},{10,9... | collective-permute-start | bytes 786440 | tf_op jit(solution)/shard_map/ppermute | solution.py:271
  5.4 8.2 %collective-permute-start.4 = (bf16[2,64,1024]{2,1,0:T(8,128)(2,1)S(1)}, bf16[2,64,1024]{2,1,0:T(8,128)(2,1)S(1)}, u32[]{:S(2)}, u32[]{:S(2)}) collective-permute-start(bf16[2,64,1024]{2,1,0:T(8,128)(2,1)S(1)} %maximum_select_fusion), channel_id=1, source_target_pairs={{0,8},{1,9},{2,10},{3,11},{4,12},{5,13},{6,14},{7,15},{8,0},{9,1},... | collective-permute-start | bytes 786440 | tf_op jit(solution)/shard_map/ppermute | solution.py:274
  13.6 0.7 copy-done.8
  14.3 0.7 gather_fusion
  15.1 0.7 gather_fusion.4
  17.1 1.2 %gather_fusion.5 = s32[96]{0:T(128)S(1)} fusion(s32[24]{0:T(128)S(1)} %scatter_custom_fusion, s32[1024]{0:T(1024)S(1)} %pad_clamp_fusion.5), kind=kCustom, calls=%fused_computation.5.clone | custom fusion | bytes 1152 | tf_op jit(solution)/shard_map/jit(_take)/gather | solution.py:259
  18.4 1.2 %gather_fusion.1 = s32[96]{0:T(128)S(1)} fusion(s32[24]{0:T(128)S(1)} %get-tuple-element.64, s32[1024]{0:T(1024)S(1)} %pad_clamp_fusion.5), kind=kCustom, calls=%fused_computation.1.clone | custom fusion | bytes 1152 | tf_op jit(solution)/shard_map/jit(_take)/gather | solution.py:258
  20.7 4.9 %collective-permute-start.5 = (bf16[2,32,1024]{2,1,0:T(8,128)(2,1)S(1)}, bf16[2,32,1024]{2,1,0:T(8,128)(2,1)S(1)}, u32[]{:S(2)}, u32[]{:S(2)}) collective-permute-start(bf16[2,32,1024]{2,1,0:T(8,128)(2,1)S(1)} %maximum_select_fusion.1), channel_id=1, source_target_pairs={{0,8},{1,9},{2,10},{3,11},{4,12},{5,13},{6,14},{7,15},{8,0},{9,1},... | collective-permute-start | bytes 393224 | tf_op jit(solution)/shard_map/ppermute | solution.py:282
  25.7 1.3 %collective-permute-start.3 = (bf16[2,96,1024]{2,1,0:T(8,128)(2,1)S(1)}, bf16[2,96,1024]{2,1,0:T(8,128)(2,1)S(1)}, u32[]{:S(2)}, u32[]{:S(2)}) collective-permute-start(bf16[2,96,1024]{2,1,0:T(8,128)(2,1)S(1)} %pad_maximum_fusion.1), channel_id=1, source_target_pairs={{16,0},{17,1},{18,2},{19,3},{20,4},{21,5},{22,6},{23,7},{24,8},{25... | collective-permute-start | bytes 1179656 | tf_op jit(solution)/shard_map/ppermute | solution.py:281
  27.0 3.2 %collective-permute-start.2 = (bf16[2,96,1024]{2,1,0:T(8,128)(2,1)S(1)}, bf16[2,96,1024]{2,1,0:T(8,128)(2,1)S(1)}, u32[]{:S(2)}, u32[]{:S(2)}) collective-permute-start(bf16[2,96,1024]{2,1,0:T(8,128)(2,1)S(1)} %pad_maximum_fusion), channel_id=1, source_target_pairs={{0,16},{1,17},{2,18},{3,19},{4,20},{5,21},{6,22},{7,23},{8,24},{9,... | collective-permute-start | bytes 1179656 | tf_op jit(solution)/shard_map/ppermute | solution.py:280
  30.5 1.1 %gather_fusion.2 = bf16[64,2,1024]{2,1,0:T(2,128)(2,1)S(1)} fusion(bf16[2,64,1024]{2,0,1:T(2,128)(2,1)S(1)} %copy.15, s32[1024]{0:T(1024)S(1)} %pad_clamp_fusion.4), kind=kCustom, calls=%fused_computation.2.clone | custom fusion | bytes 524544 | tf_op jit(solution)/shard_map/jit(_take)/gather | solution.py:285
  31.6 0.8 fusion.2.refs_6_
  33.0 0.8 gather_fusion.3
  33.8 0.8 fusion.4.refs_7_
  34.6 0.7 copy-done.13
  35.5 14.0 %neighbourhood_attention_bwd.1 = (bf16[256,1024]{1,0:T(8,128)(2,1)}, f32[256,1024]{1,0:T(8,128)}, f32[256,1024]{1,0:T(8,128)}, bf16[2,96,1024]{2,1,0:T(8,128)(2,...) custom-call(bf16[256,1024]{1,0:T(8,128)(2,1)} %bitcast.43, ...), custom_call_target="tpu_custom_call" | custom-call | flops 2013265920 | bytes 8650752 | tf_op jit(solution)/shard_map/neighbourhood_attention_bwd/pallas_call | solution.py:195
  49.4 4.9 %collective-permute-start.6 = (bf16[2,32,1024]{2,1,0:T(8,128)(2,1)}, bf16[2,32,1024]{2,1,0:T(8,128)(2,1)S(1)}, u32[]{:S(2)}, u32[]{:S(2)}) collective-permute-start(bf16[2,32,1024]{2,1,0:T(8,128)(2,1)} %get-tuple-element.18), channel_id=1, source_target_pairs={{0,8},{1,9},{2,10},{3,11},{4,12},{5,13},{6,14},{7,15},{8,0},{9,1},... | collective-permute-start | bytes 393224 | tf_op jit(solution)/shard_map/ppermute | solution.py:296
  54.4 4.8 %collective-permute-start.8 = (bf16[2,64,1024]{2,1,0:T(8,128)(2,1)}, bf16[2,64,1024]{2,1,0:T(8,128)(2,1)S(1)}, u32[]{:S(2)}, u32[]{:S(2)}) collective-permute-start(bf16[2,64,1024]{2,1,0:T(8,128)(2,1)} %get-tuple-element.20), channel_id=1, source_target_pairs={{0,8},{1,9},{2,10},{3,11},{4,12},{5,13},{6,14},{7,15},{8,0},{9,1},... | collective-permute-start | bytes 786440 | tf_op jit(solution)/shard_map/ppermute | solution.py:317
  59.2 1.3 %collective-permute-start.7 = (bf16[2,96,1024]{2,1,0:T(8,128)(2,1)}, bf16[2,96,1024]{2,1,0:T(8,128)(2,1)S(1)}, u32[]{:S(2)}, u32[]{:S(2)}) collective-permute-start(bf16[2,96,1024]{2,1,0:T(8,128)(2,1)} %get-tuple-element.19), channel_id=1, source_target_pairs={{0,16},{1,17},{2,18},{3,19},{4,20},{5,21},{6,22},{7,23},{8,24},{9,... | collective-permute-start | bytes 1179656 | tf_op jit(solution)/shard_map/ppermute | solution.py:295
  60.6 1.3 %collective-permute-start.9 = (bf16[2,96,1024]{2,1,0:T(8,128)(2,1)}, bf16[2,96,1024]{2,1,0:T(8,128)(2,1)S(1)}, u32[]{:S(2)}, u32[]{:S(2)}) collective-permute-start(bf16[2,96,1024]{2,1,0:T(8,128)(2,1)} %get-tuple-element.21), channel_id=1, source_target_pairs={{16,0},{17,1},{18,2},{19,3},{20,4},{21,5},{22,6},{23,7},{24,8},{25... | collective-permute-start | bytes 1179656 | tf_op jit(solution)/shard_map/ppermute | solution.py:294
  62.0 0.8 gather_fusion.6
  62.9 6.7 %collective-permute-done.8 = bf16[2,64,1024]{2,1,0:T(8,128)(2,1)S(1)} collective-permute-done((bf16[2,64,1024]{2,1,0:T(8,128)(2,1)}, bf16[2,64,1024]{2,1,0:T(8,128)(2,1)S(1)}, u32[]{:S(2)}, u32[]{:S(2)}) %collective-permute-start.8) | collective-permute-done | bytes 262176 | tf_op jit(solution)/shard_map/ppermute | solution.py:317
  69.9 1.1 %gather_fusion.7 = bf16[64,2,1024]{2,1,0:T(2,128)(2,1)S(1)} fusion(bf16[2,64,1024]{2,0,1:T(2,128)(2,1)S(1)} %copy.21, s32[1024]{0:T(1024)S(1)} %pad_clamp_fusion), kind=kCustom, calls=%fused_computation.6.clone | custom fusion | bytes 524544 | tf_op jit(solution)/shard_map/jit(_take)/gather | solution.py:318
  71.5 1.0 %copy-done.5 = f32[2,64,1024]{2,1,0:T(8,128)S(1)} copy-done((f32[2,64,1024]{2,1,0:T(8,128)S(1)}, f32[2,64,1024]{2,1,0:T(8,128)}, u32[]{:S(2)}) %copy-start.5) | copy-done | bytes 524312
  72.6 0.9 %copy-done.4 = f32[2,64,1024]{2,1,0:T(8,128)S(1)} copy-done((f32[2,64,1024]{2,1,0:T(8,128)S(1)}, f32[2,64,1024]{2,1,0:T(8,128)}, u32[]{:S(2)}) %copy-start.4) | copy-done | bytes 524312
  73.5 2.1 %collective-permute-start.11 = (bf16[2,64,1024]{2,1,0:T(8,128)(2,1)S(1)}, bf16[2,64,1024]{2,1,0:T(8,128)(2,1)S(1)}, u32[]{:S(2)}, u32[]{:S(2)}) collective-permute-start(bf16[2,64,1024]{2,1,0:T(8,128)(2,1)S(1)} %add_convert_fusion.2), channel_id=1, source_target_pairs={{0,15},{1,0},{2,1},{3,2},{4,3},{5,4},{6,5},{7,6},{8,7},{9,8},{10,9... | collective-permute-start | bytes 786440 | tf_op jit(solution)/shard_map/ppermute | solution.py:315
  75.8 4.2 %collective-permute-done.10 = bf16[2,64,1024]{2,1,0:T(8,128)(2,1)S(1)} collective-permute-done((bf16[2,64,1024]{2,1,0:T(8,128)(2,1)S(1)}, bf16[2,64,1024]{2,1,0:T(8,128)(2,1)S(1)}, u32[]{:S(2)}, u32[]{:S(2)}) %collective-permute-start.10) | collective-permute-done | bytes 262176 | tf_op jit(solution)/shard_map/ppermute | solution.py:316
  80.0 2.6 %collective-permute-done.11 = bf16[2,64,1024]{2,1,0:T(8,128)(2,1)S(1)} collective-permute-done((bf16[2,64,1024]{2,1,0:T(8,128)(2,1)S(1)}, bf16[2,64,1024]{2,1,0:T(8,128)(2,1)S(1)}, u32[]{:S(2)}, u32[]{:S(2)}) %collective-permute-start.11) | collective-permute-done | bytes 262176 | tf_op jit(solution)/shard_map/ppermute | solution.py:315
  82.9 1.0 %add_convert_fusion = bf16[16,16,1024]{2,1,0:T(8,128)(2,1)} fusion(f32[4,16,1024]{2,1,0:T(8,128)S(1)} %bitcast.40, f32[16,16,1024]{2,1,0:T(8,128)S(1)} %bitcast.36, f32[4,16,1024]{2,1,0:T(8,128)S(1)} %bitcast.39, bf16[16,4,1024]{2,1,0:T(4,128)(2,1)S(1)} %convert_element_type.64, bf16[16,4,1024]{2,1,0:T(4,128)(2,1)S(1)} %convert_element_type.63), kind=kLoop, calls=%fused_computation.9 | loop fusion | flops 1835008 | bytes 2359296 | tf_op jit(solution)/shard_map/convert_element_type | solution.py:336
  84.3 1.0 %add_convert_fusion.1 = bf16[16,16,1024]{2,1,0:T(8,128)(2,1)} fusion(f32[4,16,1024]{2,1,0:T(8,128)S(1)} %bitcast.38, f32[16,16,1024]{2,1,0:T(8,128)S(1)} %bitcast.35, f32[4,16,1024]{2,1,0:T(8,128)S(1)} %bitcast.37, bf16[16,4,1024]{2,1,0:T(4,128)(2,1)S(1)} %convert_element_type.61, bf16[16,4,1024]{2,1,0:T(4,128)(2,1)S(1)} %convert_element_type.59), kind=kLoop, calls=%fused_computation.10 | loop fusion | flops 1835008 | bytes 2359296 | tf_op jit(solution)/shard_map/convert_element_type | solution.py:336
  (88 shorter events, 5.7 us)
Async XLA Ops:
  0.6 1.2 %copy-start.3 = (bf16[16,16,1024]{2,1,0:T(8,128)(2,1)S(1)}, bf16[16,16,1024]{2,1,0:T(8,128)(2,1)}, u32[]{:S(2)}) copy-start(bf16[16,16,1024]{2,1,0:T(8,128)(2,1)} %param.22) | copy-start | bytes 1572868
  2.1 17.8 %collective-permute-start = (bf16[2,64,1024]{2,1,0:T(8,128)(2,1)S(1)}, bf16[2,64,1024]{2,1,0:T(8,128)(2,1)S(1)}, u32[]{:S(2)}, u32[]{:S(2)}) collective-permute-start(bf16[2,64,1024]{2,1,0:T(8,128)(2,1)S(1)} %pad_maximum_fusion.2), channel_id=1, source_target_pairs={{0,1},{1,2},{2,3},{3,4},{4,5},{5,6},{6,7},{7,8},{8,9},{9,10},{10,1... | collective-permute-start | bytes 786440 | tf_op jit(solution)/shard_map/ppermute | solution.py:270
  3.7 1.5 %copy-start.2 = (bf16[16,16,1024]{2,1,0:T(8,128)(2,1)S(1)}, bf16[16,16,1024]{2,1,0:T(8,128)(2,1)}, u32[]{:S(2)}) copy-start(bf16[16,16,1024]{2,1,0:T(8,128)(2,1)} %param.21) | copy-start | bytes 1572868
  3.8 16.1 %collective-permute-start.1 = (bf16[2,64,1024]{2,1,0:T(8,128)(2,1)S(1)}, bf16[2,64,1024]{2,1,0:T(8,128)(2,1)S(1)}, u32[]{:S(2)}, u32[]{:S(2)}) collective-permute-start(bf16[2,64,1024]{2,1,0:T(8,128)(2,1)S(1)} %pad_maximum_fusion.3), channel_id=1, source_target_pairs={{0,15},{1,0},{2,1},{3,2},{4,3},{5,4},{6,5},{7,6},{8,7},{9,8},{10,9... | collective-permute-start | bytes 786440 | tf_op jit(solution)/shard_map/ppermute | solution.py:271
  5.4 24.9 %collective-permute-start.4 = (bf16[2,64,1024]{2,1,0:T(8,128)(2,1)S(1)}, bf16[2,64,1024]{2,1,0:T(8,128)(2,1)S(1)}, u32[]{:S(2)}, u32[]{:S(2)}) collective-permute-start(bf16[2,64,1024]{2,1,0:T(8,128)(2,1)S(1)} %maximum_select_fusion), channel_id=1, source_target_pairs={{0,8},{1,9},{2,10},{3,11},{4,12},{5,13},{6,14},{7,15},{8,0},{9,1},... | collective-permute-start | bytes 786440 | tf_op jit(solution)/shard_map/ppermute | solution.py:274
  13.6 0.7 copy-start.8
  15.8 0.7 copy-start.12
  18.3 1.3 %copy-start.9 = (s32[96]{0:T(128)S(1)}, s32[96]{0:T(128)}, u32[]{:S(2)}) copy-start(s32[96]{0:T(128)} %constant.133.clone) | copy-start | bytes 1156
  18.3 1.3 %copy-start.10 = (s32[96]{0:T(128)S(1)}, s32[96]{0:T(128)}, u32[]{:S(2)}) copy-start(s32[96]{0:T(128)} %constant.134.clone) | copy-start | bytes 1156
  18.4 1.3 %copy-start.11 = (s32[96]{0:T(128)S(1)}, s32[96]{0:T(128)}, u32[]{:S(2)}) copy-start(s32[96]{0:T(128)} %constant.135.clone) | copy-start | bytes 1156
  19.9 0.7 copy-start.6
  19.9 0.8 copy-start.7
  20.7 12.2 %collective-permute-start.5 = (bf16[2,32,1024]{2,1,0:T(8,128)(2,1)S(1)}, bf16[2,32,1024]{2,1,0:T(8,128)(2,1)S(1)}, u32[]{:S(2)}, u32[]{:S(2)}) collective-permute-start(bf16[2,32,1024]{2,1,0:T(8,128)(2,1)S(1)} %maximum_select_fusion.1), channel_id=1, source_target_pairs={{0,8},{1,9},{2,10},{3,11},{4,12},{5,13},{6,14},{7,15},{8,0},{9,1},... | collective-permute-start | bytes 393224 | tf_op jit(solution)/shard_map/ppermute | solution.py:282
  25.7 8.9 %collective-permute-start.3 = (bf16[2,96,1024]{2,1,0:T(8,128)(2,1)S(1)}, bf16[2,96,1024]{2,1,0:T(8,128)(2,1)S(1)}, u32[]{:S(2)}, u32[]{:S(2)}) collective-permute-start(bf16[2,96,1024]{2,1,0:T(8,128)(2,1)S(1)} %pad_maximum_fusion.1), channel_id=1, source_target_pairs={{16,0},{17,1},{18,2},{19,3},{20,4},{21,5},{22,6},{23,7},{24,8},{25... | collective-permute-start | bytes 1179656 | tf_op jit(solution)/shard_map/ppermute | solution.py:281
  27.0 7.6 %collective-permute-start.2 = (bf16[2,96,1024]{2,1,0:T(8,128)(2,1)S(1)}, bf16[2,96,1024]{2,1,0:T(8,128)(2,1)S(1)}, u32[]{:S(2)}, u32[]{:S(2)}) collective-permute-start(bf16[2,96,1024]{2,1,0:T(8,128)(2,1)S(1)} %pad_maximum_fusion), channel_id=1, source_target_pairs={{0,16},{1,17},{2,18},{3,19},{4,20},{5,21},{6,22},{7,23},{8,24},{9,... | collective-permute-start | bytes 1179656 | tf_op jit(solution)/shard_map/ppermute | solution.py:280
  34.6 0.7 copy-start.13
  34.6 0.9 %copy-start.14 = (bf16[2,96,1024]{2,1,0:T(8,128)(2,1)}, bf16[2,96,1024]{2,1,0:T(8,128)(2,1)S(1)}, u32[]{:S(2)}) copy-start(bf16[2,96,1024]{2,1,0:T(8,128)(2,1)S(1)} %collective-permute-done.2.refs_4_) | copy-start | bytes 1179652
  49.4 12.4 %collective-permute-start.6 = (bf16[2,32,1024]{2,1,0:T(8,128)(2,1)}, bf16[2,32,1024]{2,1,0:T(8,128)(2,1)S(1)}, u32[]{:S(2)}, u32[]{:S(2)}) collective-permute-start(bf16[2,32,1024]{2,1,0:T(8,128)(2,1)} %get-tuple-element.18), channel_id=1, source_target_pairs={{0,8},{1,9},{2,10},{3,11},{4,12},{5,13},{6,14},{7,15},{8,0},{9,1},... | collective-permute-start | bytes 393224 | tf_op jit(solution)/shard_map/ppermute | solution.py:296
  54.4 15.2 %collective-permute-start.8 = (bf16[2,64,1024]{2,1,0:T(8,128)(2,1)}, bf16[2,64,1024]{2,1,0:T(8,128)(2,1)S(1)}, u32[]{:S(2)}, u32[]{:S(2)}) collective-permute-start(bf16[2,64,1024]{2,1,0:T(8,128)(2,1)} %get-tuple-element.20), channel_id=1, source_target_pairs={{0,8},{1,9},{2,10},{3,11},{4,12},{5,13},{6,14},{7,15},{8,0},{9,1},... | collective-permute-start | bytes 786440 | tf_op jit(solution)/shard_map/ppermute | solution.py:317
  59.2 11.9 %collective-permute-start.7 = (bf16[2,96,1024]{2,1,0:T(8,128)(2,1)}, bf16[2,96,1024]{2,1,0:T(8,128)(2,1)S(1)}, u32[]{:S(2)}, u32[]{:S(2)}) collective-permute-start(bf16[2,96,1024]{2,1,0:T(8,128)(2,1)} %get-tuple-element.19), channel_id=1, source_target_pairs={{0,16},{1,17},{2,18},{3,19},{4,20},{5,21},{6,22},{7,23},{8,24},{9,... | collective-permute-start | bytes 1179656 | tf_op jit(solution)/shard_map/ppermute | solution.py:295
  60.6 10.6 %collective-permute-start.9 = (bf16[2,96,1024]{2,1,0:T(8,128)(2,1)}, bf16[2,96,1024]{2,1,0:T(8,128)(2,1)S(1)}, u32[]{:S(2)}, u32[]{:S(2)}) collective-permute-start(bf16[2,96,1024]{2,1,0:T(8,128)(2,1)} %get-tuple-element.21), channel_id=1, source_target_pairs={{16,0},{17,1},{18,2},{19,3},{20,4},{21,5},{22,6},{23,7},{24,8},{25... | collective-permute-start | bytes 1179656 | tf_op jit(solution)/shard_map/ppermute | solution.py:294
  71.4 1.0 %copy-start.5 = (f32[2,64,1024]{2,1,0:T(8,128)S(1)}, f32[2,64,1024]{2,1,0:T(8,128)}, u32[]{:S(2)}) copy-start(f32[2,64,1024]{2,1,0:T(8,128)} %get-tuple-element.22) | copy-start | bytes 1572868
  72.4 1.0 %copy-start.4 = (f32[2,64,1024]{2,1,0:T(8,128)S(1)}, f32[2,64,1024]{2,1,0:T(8,128)}, u32[]{:S(2)}) copy-start(f32[2,64,1024]{2,1,0:T(8,128)} %get-tuple-element.23) | copy-start | bytes 1572868
  72.5 7.4 %collective-permute-start.10 = (bf16[2,64,1024]{2,1,0:T(8,128)(2,1)S(1)}, bf16[2,64,1024]{2,1,0:T(8,128)(2,1)S(1)}, u32[]{:S(2)}, u32[]{:S(2)}) collective-permute-start(bf16[2,64,1024]{2,1,0:T(8,128)(2,1)S(1)} %add_convert_fusion.3), channel_id=1, source_target_pairs={{0,1},{1,2},{2,3},{3,4},{4,5},{5,6},{6,7},{7,8},{8,9},{9,10},{10,1... | collective-permute-start | bytes 786440 | tf_op jit(solution)/shard_map/ppermute | solution.py:316
  73.5 9.1 %collective-permute-start.11 = (bf16[2,64,1024]{2,1,0:T(8,128)(2,1)S(1)}, bf16[2,64,1024]{2,1,0:T(8,128)(2,1)S(1)}, u32[]{:S(2)}, u32[]{:S(2)}) collective-permute-start(bf16[2,64,1024]{2,1,0:T(8,128)(2,1)S(1)} %add_convert_fusion.2), channel_id=1, source_target_pairs={{0,15},{1,0},{2,1},{3,2},{4,3},{5,4},{6,5},{7,6},{8,7},{9,8},{10,9... | collective-permute-start | bytes 786440 | tf_op jit(solution)/shard_map/ppermute | solution.py:315
  75.8 7.1 %copy-start.1 = (f32[256,1024]{1,0:T(8,128)S(1)}, f32[256,1024]{1,0:T(8,128)}, u32[]{:S(2)}) copy-start(f32[256,1024]{1,0:T(8,128)} %get-tuple-element.24) | copy-start | bytes 3145732
  82.9 1.4 %copy-start = (f32[256,1024]{1,0:T(8,128)S(1)}, f32[256,1024]{1,0:T(8,128)}, u32[]{:S(2)}) copy-start(f32[256,1024]{1,0:T(8,128)} %get-tuple-element.17) | copy-start | bytes 3145732

commit v16 on v15

--- a/solution.py
+++ b/solution.py
@@ -17,8 +17,8 @@
 
 def attention_kernel(width, n_lat, *refs):
     (q_ref, g_ref, k_own, v_own, above_in, below_in, pole_mid_in, pole_corner_in, left_in, right_in) = refs[:10]
-    (dq_ref, dk_own, dv_own, top_out, bot_out, left_out, right_out, pole_mid_out, pole_corner_out) = refs[10:19]
-    bias_ref = refs[19]
+    bias_ref = refs[10]
+    (dq_ref, dk_own, dv_own, top_out, bot_out, left_out, right_out, pole_mid_out, pole_corner_out) = refs[11:20]
     lat = lax.axis_index("lat")
     north = lat == 0
     south = lat == n_lat - 1
@@ -48,22 +48,6 @@
     edge = r * width
     corner = r * r
     pairs = q_ref.shape[1] // LANES
-
-    qi = lax.broadcasted_iota(jnp.int32, (2 * tq, tk), 0).astype(jnp.float32)
-    ki = lax.broadcasted_iota(jnp.int32, (2 * tq, tk), 1).astype(jnp.float32)
-    qi = jnp.where(qi >= tq, qi - tq, qi)
-    qr = jnp.floor((qi + 0.5) * (1.0 / width))
-    qc = qi - width * qr
-    in_main = ki < main
-    in_left = (ki >= main) & (ki < main + side)
-    kk = jnp.where(in_main, ki, jnp.where(in_left, ki - main, ki - main - side))
-    per_row = jnp.where(in_main, float(width), float(r))
-    kr = jnp.floor((kk + 0.5) / per_row)
-    kc = kk - per_row * kr + jnp.where(in_main, float(r), jnp.where(in_left, 0.0, float(width + r)))
-    dr = kr - qr
-    dc = kc - qc
-    ok = (dr >= 0) & (dr <= 2 * r) & (dc >= 0) & (dc <= 2 * r)
-    bias_ref[...] = jnp.where(ok, 0.0, -jnp.inf).astype(jnp.float32)
 
     nt = (((1,), (1,)), ((), ()))
     tn = (((0,), (0,)), ((), ()))
@@ -168,6 +152,25 @@
     lax.fori_loop(0, pairs, body, 0, unroll=True)
 
 
+def window_bias(width):
+    r = RADIUS
+    tq = TILE_ROWS * width
+    main = 2 * TILE_ROWS * width
+    side = 2 * TILE_ROWS * r
+    q = np.arange(2 * tq)[:, None] % tq
+    k = np.arange(main + 2 * side)[None, :]
+    in_main = k < main
+    in_left = (k >= main) & (k < main + side)
+    kk = np.where(in_main, k, np.where(in_left, k - main, k - main - side))
+    per_row = np.where(in_main, width, r)
+    kr = kk // per_row
+    kc = kk % per_row + np.where(in_main, r, np.where(in_left, 0, width + r))
+    dr = kr - q // width
+    dc = kc - q % width
+    ok = (dr >= 0) & (dr <= 2 * r) & (dc >= 0) & (dc <= 2 * r)
+    return jnp.asarray(np.where(ok, 0.0, -np.inf).astype(np.float32))
+
+
 def attention_core(q2, g2, k2, v2, above, below, pole_mid, pole_corner, left_in, right_in, width, n_lat):
     cells, features = q2.shape
     r = RADIUS
@@ -195,16 +198,15 @@
     return pl.pallas_call(
         lambda *refs: attention_kernel(width, n_lat, *refs),
         out_shape=outs,
-        in_specs=[vmem] * 10,
+        in_specs=[vmem] * 11,
         out_specs=tuple([vmem] * 9),
-        scratch_shapes=[pltpu.VMEM((2 * tq, tk), jnp.float32)],
         cost_estimate=pl.CostEstimate(
             flops=flops,
             transcendentals=2 * tq * tk * HEADS * tiles,
             bytes_accessed=in_bytes + out_bytes,
         ),
         name="neighbourhood_attention_bwd",
-    )(q2, g2, k2, v2, above, below, pole_mid, pole_corner, left_in, right_in)
+    )(q2, g2, k2, v2, above, below, pole_mid, pole_corner, left_in, right_in, window_bias(width))
 
 
 def on_device(queries, keys, values, grad_out, fold_cols):

time: 87 us -> 87.1 us (level)
  no operation moved by 1% of the time
where the time goes in v16:
time: 87.1 us; the launch traced here: 85.4 us
  starting transfers between devices  35.3 us (41%)
  local copies, waits for them, and re-layouts  16.2 us (19%)
  Pallas kernels  14.1 us (16%)
  waiting for transfers between devices  13.9 us (16%)
  other arithmetic  4.76 us (5%)
  between operations  1.21 us (1%)
    pallas_call x1, Pallas kernels, attention_core(): pl.pallas_call(lambda *refs: attention_kernel(width, n_lat, *refs), out_s...  14.1 us
    ppermute x1, starting transfers between devices, on_device(): lax.ppermute(jnp.where(at_north, top_mid, bottom_mid), both, pole_pairs)  8.2 us
    ppermute x1, waiting for transfers between devices, on_device(): pole_g_mid = lax.ppermute(pole_g_mid_send, both, pole_pairs)  6.68 us
    unnamed x30, local copies, waits for them, and re-layouts  5.25 us
    ppermute x1, starting transfers between devices, on_device(): lax.ppermute(jnp.where(at_north, top_send[:, edge:], bottom_send[:, edge:...  4.94 us
    ppermute x1, starting transfers between devices, on_device(): pole_g_corners = lax.ppermute(pole_g_corner_send, both, pole_pairs)  4.94 us
    ppermute x1, starting transfers between devices, on_device(): pole_g_mid = lax.ppermute(pole_g_mid_send, both, pole_pairs)  4.8 us
    ppermute x1, waiting for transfers between devices, on_device(): lax.ppermute(side_send(right_g, edge + corner), 'lon', right_pairs)  4.16 us
  transfers between devices with their start and end apart: 12, of which 4 were waited for; matrix products, arithmetic and copies ran while one was open for 14% of the time, Pallas kernels for 0%

profile of v16, /device:TPU:32, one launch (start us, length us, event | category | flops | bytes accessed | tf_op | source)
XLA Modules:
  0.0 85.4 jit_solution(1623520100829330375)
XLA Ops:
  0.6 1.2 %fusion.15 = (bf16[16,4,1024]{2,1,0:T(4,128)(2,1)S(1)}, bf16[16,4,1024]{2,1,0:T(4,128)(2,1)S(1)}) fusion(bf16[16,16,1024]{2,1,0:T(8,128)(2,1)} %param.22), kind=kLoop, calls=%fused_computation.87 | loop fusion | bytes 524288 | tf_op jit(solution)/shard_map/slice | solution.py:270
  2.1 1.7 %collective-permute-start = (bf16[2,64,1024]{2,1,0:T(8,128)(2,1)S(1)}, bf16[2,64,1024]{2,1,0:T(8,128)(2,1)S(1)}, u32[]{:S(2)}, u32[]{:S(2)}) collective-permute-start(bf16[2,64,1024]{2,1,0:T(8,128)(2,1)S(1)} %pad_maximum_fusion.2), channel_id=1, source_target_pairs={{0,1},{1,2},{2,3},{3,4},{4,5},{5,6},{6,7},{7,8},{8,9},{9,10},{10,1... | collective-permute-start | bytes 786440 | tf_op jit(solution)/shard_map/ppermute | solution.py:272
  3.8 1.4 %collective-permute-start.1 = (bf16[2,64,1024]{2,1,0:T(8,128)(2,1)S(1)}, bf16[2,64,1024]{2,1,0:T(8,128)(2,1)S(1)}, u32[]{:S(2)}, u32[]{:S(2)}) collective-permute-start(bf16[2,64,1024]{2,1,0:T(8,128)(2,1)S(1)} %pad_maximum_fusion.3), channel_id=1, source_target_pairs={{0,15},{1,0},{2,1},{3,2},{4,3},{5,4},{6,5},{7,6},{8,7},{9,8},{10,9... | collective-permute-start | bytes 786440 | tf_op jit(solution)/shard_map/ppermute | solution.py:273
  5.4 8.2 %collective-permute-start.4 = (bf16[2,64,1024]{2,1,0:T(8,128)(2,1)S(1)}, bf16[2,64,1024]{2,1,0:T(8,128)(2,1)S(1)}, u32[]{:S(2)}, u32[]{:S(2)}) collective-permute-start(bf16[2,64,1024]{2,1,0:T(8,128)(2,1)S(1)} %maximum_select_fusion), channel_id=1, source_target_pairs={{0,8},{1,9},{2,10},{3,11},{4,12},{5,13},{6,14},{7,15},{8,0},{9,1},... | collective-permute-start | bytes 786440 | tf_op jit(solution)/shard_map/ppermute | solution.py:276
  13.6 0.7 copy-done.8
  14.3 0.7 gather_fusion
  15.1 0.7 gather_fusion.4
  17.1 1.2 %gather_fusion.5 = s32[96]{0:T(128)S(1)} fusion(s32[24]{0:T(128)S(1)} %scatter_custom_fusion, s32[1024]{0:T(1024)S(1)} %pad_clamp_fusion.5), kind=kCustom, calls=%fused_computation.5.clone | custom fusion | bytes 1152 | tf_op jit(solution)/shard_map/jit(_take)/gather | solution.py:261
  18.4 1.2 %gather_fusion.1 = s32[96]{0:T(128)S(1)} fusion(s32[24]{0:T(128)S(1)} %get-tuple-element.64, s32[1024]{0:T(1024)S(1)} %pad_clamp_fusion.5), kind=kCustom, calls=%fused_computation.1.clone | custom fusion | bytes 1152 | tf_op jit(solution)/shard_map/jit(_take)/gather | solution.py:260
  20.7 4.9 %collective-permute-start.5 = (bf16[2,32,1024]{2,1,0:T(8,128)(2,1)S(1)}, bf16[2,32,1024]{2,1,0:T(8,128)(2,1)S(1)}, u32[]{:S(2)}, u32[]{:S(2)}) collective-permute-start(bf16[2,32,1024]{2,1,0:T(8,128)(2,1)S(1)} %maximum_select_fusion.1), channel_id=1, source_target_pairs={{0,8},{1,9},{2,10},{3,11},{4,12},{5,13},{6,14},{7,15},{8,0},{9,1},... | collective-permute-start | bytes 393224 | tf_op jit(solution)/shard_map/ppermute | solution.py:284
  25.7 1.3 %collective-permute-start.3 = (bf16[2,96,1024]{2,1,0:T(8,128)(2,1)S(1)}, bf16[2,96,1024]{2,1,0:T(8,128)(2,1)S(1)}, u32[]{:S(2)}, u32[]{:S(2)}) collective-permute-start(bf16[2,96,1024]{2,1,0:T(8,128)(2,1)S(1)} %pad_maximum_fusion.1), channel_id=1, source_target_pairs={{16,0},{17,1},{18,2},{19,3},{20,4},{21,5},{22,6},{23,7},{24,8},{25... | collective-permute-start | bytes 1179656 | tf_op jit(solution)/shard_map/ppermute | solution.py:283
  27.0 3.2 %collective-permute-start.2 = (bf16[2,96,1024]{2,1,0:T(8,128)(2,1)S(1)}, bf16[2,96,1024]{2,1,0:T(8,128)(2,1)S(1)}, u32[]{:S(2)}, u32[]{:S(2)}) collective-permute-start(bf16[2,96,1024]{2,1,0:T(8,128)(2,1)S(1)} %pad_maximum_fusion), channel_id=1, source_target_pairs={{0,16},{1,17},{2,18},{3,19},{4,20},{5,21},{6,22},{7,23},{8,24},{9,... | collective-permute-start | bytes 1179656 | tf_op jit(solution)/shard_map/ppermute | solution.py:282
  30.5 1.1 %gather_fusion.2 = bf16[64,2,1024]{2,1,0:T(2,128)(2,1)S(1)} fusion(bf16[2,64,1024]{2,0,1:T(2,128)(2,1)S(1)} %copy.16, s32[1024]{0:T(1024)S(1)} %pad_clamp_fusion.4), kind=kCustom, calls=%fused_computation.2.clone | custom fusion | bytes 524544 | tf_op jit(solution)/shard_map/jit(_take)/gather | solution.py:287
  31.6 0.8 fusion.2.refs_6_
  33.0 0.8 gather_fusion.3
  33.8 0.8 fusion.4.refs_7_
  34.6 0.7 copy-done.13
  35.5 14.1 %neighbourhood_attention_bwd.1 = (bf16[256,1024]{1,0:T(8,128)(2,1)}, f32[256,1024]{1,0:T(8,128)}, f32[256,1024]{1,0:T(8,128)}, bf16[2,96,1024]{2,1,0:T(8,128)(2,...) custom-call(bf16[256,1024]{1,0:T(8,128)(2,1)} %bitcast.43, ...), custom_call_target="tpu_custom_call" | custom-call | flops 2013265920 | bytes 8650752 | tf_op jit(solution)/shard_map/neighbourhood_attention_bwd/pallas_call | solution.py:198
  49.6 4.9 %collective-permute-start.6 = (bf16[2,32,1024]{2,1,0:T(8,128)(2,1)}, bf16[2,32,1024]{2,1,0:T(8,128)(2,1)S(1)}, u32[]{:S(2)}, u32[]{:S(2)}) collective-permute-start(bf16[2,32,1024]{2,1,0:T(8,128)(2,1)} %get-tuple-element.18), channel_id=1, source_target_pairs={{0,8},{1,9},{2,10},{3,11},{4,12},{5,13},{6,14},{7,15},{8,0},{9,1},... | collective-permute-start | bytes 393224 | tf_op jit(solution)/shard_map/ppermute | solution.py:298
  54.5 4.8 %collective-permute-start.8 = (bf16[2,64,1024]{2,1,0:T(8,128)(2,1)}, bf16[2,64,1024]{2,1,0:T(8,128)(2,1)S(1)}, u32[]{:S(2)}, u32[]{:S(2)}) collective-permute-start(bf16[2,64,1024]{2,1,0:T(8,128)(2,1)} %get-tuple-element.20), channel_id=1, source_target_pairs={{0,8},{1,9},{2,10},{3,11},{4,12},{5,13},{6,14},{7,15},{8,0},{9,1},... | collective-permute-start | bytes 786440 | tf_op jit(solution)/shard_map/ppermute | solution.py:319
  59.3 1.3 %collective-permute-start.7 = (bf16[2,96,1024]{2,1,0:T(8,128)(2,1)}, bf16[2,96,1024]{2,1,0:T(8,128)(2,1)S(1)}, u32[]{:S(2)}, u32[]{:S(2)}) collective-permute-start(bf16[2,96,1024]{2,1,0:T(8,128)(2,1)} %get-tuple-element.19), channel_id=1, source_target_pairs={{0,16},{1,17},{2,18},{3,19},{4,20},{5,21},{6,22},{7,23},{8,24},{9,... | collective-permute-start | bytes 1179656 | tf_op jit(solution)/shard_map/ppermute | solution.py:297
  60.7 1.3 %collective-permute-start.9 = (bf16[2,96,1024]{2,1,0:T(8,128)(2,1)}, bf16[2,96,1024]{2,1,0:T(8,128)(2,1)S(1)}, u32[]{:S(2)}, u32[]{:S(2)}) collective-permute-start(bf16[2,96,1024]{2,1,0:T(8,128)(2,1)} %get-tuple-element.21), channel_id=1, source_target_pairs={{16,0},{17,1},{18,2},{19,3},{20,4},{21,5},{22,6},{23,7},{24,8},{25... | collective-permute-start | bytes 1179656 | tf_op jit(solution)/shard_map/ppermute | solution.py:296
  62.1 0.8 gather_fusion.6
  63.0 6.7 %collective-permute-done.8 = bf16[2,64,1024]{2,1,0:T(8,128)(2,1)S(1)} collective-permute-done((bf16[2,64,1024]{2,1,0:T(8,128)(2,1)}, bf16[2,64,1024]{2,1,0:T(8,128)(2,1)S(1)}, u32[]{:S(2)}, u32[]{:S(2)}) %collective-permute-start.8) | collective-permute-done | bytes 262176 | tf_op jit(solution)/shard_map/ppermute | solution.py:319
  70.0 1.1 %gather_fusion.7 = bf16[64,2,1024]{2,1,0:T(2,128)(2,1)S(1)} fusion(bf16[2,64,1024]{2,0,1:T(2,128)(2,1)S(1)} %copy.22, s32[1024]{0:T(1024)S(1)} %pad_clamp_fusion), kind=kCustom, calls=%fused_computation.6.clone | custom fusion | bytes 524544 | tf_op jit(solution)/shard_map/jit(_take)/gather | solution.py:320
  71.6 1.0 %copy-done.5 = f32[2,64,1024]{2,1,0:T(8,128)S(1)} copy-done((f32[2,64,1024]{2,1,0:T(8,128)S(1)}, f32[2,64,1024]{2,1,0:T(8,128)}, u32[]{:S(2)}) %copy-start.5) | copy-done | bytes 524312
  72.7 0.9 %copy-done.4 = f32[2,64,1024]{2,1,0:T(8,128)S(1)} copy-done((f32[2,64,1024]{2,1,0:T(8,128)S(1)}, f32[2,64,1024]{2,1,0:T(8,128)}, u32[]{:S(2)}) %copy-start.4) | copy-done | bytes 524312
  73.7 2.1 %collective-permute-start.11 = (bf16[2,64,1024]{2,1,0:T(8,128)(2,1)S(1)}, bf16[2,64,1024]{2,1,0:T(8,128)(2,1)S(1)}, u32[]{:S(2)}, u32[]{:S(2)}) collective-permute-start(bf16[2,64,1024]{2,1,0:T(8,128)(2,1)S(1)} %add_convert_fusion.2), channel_id=1, source_target_pairs={{0,15},{1,0},{2,1},{3,2},{4,3},{5,4},{6,5},{7,6},{8,7},{9,8},{10,9... | collective-permute-start | bytes 786440 | tf_op jit(solution)/shard_map/ppermute | solution.py:317
  75.9 4.2 %collective-permute-done.10 = bf16[2,64,1024]{2,1,0:T(8,128)(2,1)S(1)} collective-permute-done((bf16[2,64,1024]{2,1,0:T(8,128)(2,1)S(1)}, bf16[2,64,1024]{2,1,0:T(8,128)(2,1)S(1)}, u32[]{:S(2)}, u32[]{:S(2)}) %collective-permute-start.10) | collective-permute-done | bytes 262176 | tf_op jit(solution)/shard_map/ppermute | solution.py:318
  80.1 2.6 %collective-permute-done.11 = bf16[2,64,1024]{2,1,0:T(8,128)(2,1)S(1)} collective-permute-done((bf16[2,64,1024]{2,1,0:T(8,128)(2,1)S(1)}, bf16[2,64,1024]{2,1,0:T(8,128)(2,1)S(1)}, u32[]{:S(2)}, u32[]{:S(2)}) %collective-permute-start.11) | collective-permute-done | bytes 262176 | tf_op jit(solution)/shard_map/ppermute | solution.py:317
  83.0 1.0 %add_convert_fusion = bf16[16,16,1024]{2,1,0:T(8,128)(2,1)} fusion(f32[4,16,1024]{2,1,0:T(8,128)S(1)} %bitcast.40, f32[16,16,1024]{2,1,0:T(8,128)S(1)} %bitcast.36, f32[4,16,1024]{2,1,0:T(8,128)S(1)} %bitcast.39, bf16[16,4,1024]{2,1,0:T(4,128)(2,1)S(1)} %convert_element_type.64, bf16[16,4,1024]{2,1,0:T(4,128)(2,1)S(1)} %convert_element_type.63), kind=kLoop, calls=%fused_computation.9 | loop fusion | flops 1835008 | bytes 2359296 | tf_op jit(solution)/shard_map/convert_element_type | solution.py:338
  84.4 1.0 %add_convert_fusion.1 = bf16[16,16,1024]{2,1,0:T(8,128)(2,1)} fusion(f32[4,16,1024]{2,1,0:T(8,128)S(1)} %bitcast.38, f32[16,16,1024]{2,1,0:T(8,128)S(1)} %bitcast.35, f32[4,16,1024]{2,1,0:T(8,128)S(1)} %bitcast.37, bf16[16,4,1024]{2,1,0:T(4,128)(2,1)S(1)} %convert_element_type.61, bf16[16,4,1024]{2,1,0:T(4,128)(2,1)S(1)} %convert_element_type.59), kind=kLoop, calls=%fused_computation.10 | loop fusion | flops 1835008 | bytes 2359296 | tf_op jit(solution)/shard_map/convert_element_type | solution.py:338
  (88 shorter events, 5.7 us)
Async XLA Ops:
  0.6 1.2 %copy-start.3 = (bf16[16,16,1024]{2,1,0:T(8,128)(2,1)S(1)}, bf16[16,16,1024]{2,1,0:T(8,128)(2,1)}, u32[]{:S(2)}) copy-start(bf16[16,16,1024]{2,1,0:T(8,128)(2,1)} %param.23) | copy-start | bytes 1572868
  2.1 17.8 %collective-permute-start = (bf16[2,64,1024]{2,1,0:T(8,128)(2,1)S(1)}, bf16[2,64,1024]{2,1,0:T(8,128)(2,1)S(1)}, u32[]{:S(2)}, u32[]{:S(2)}) collective-permute-start(bf16[2,64,1024]{2,1,0:T(8,128)(2,1)S(1)} %pad_maximum_fusion.2), channel_id=1, source_target_pairs={{0,1},{1,2},{2,3},{3,4},{4,5},{5,6},{6,7},{7,8},{8,9},{9,10},{10,1... | collective-permute-start | bytes 786440 | tf_op jit(solution)/shard_map/ppermute | solution.py:272
  3.7 1.5 %copy-start.2 = (bf16[16,16,1024]{2,1,0:T(8,128)(2,1)S(1)}, bf16[16,16,1024]{2,1,0:T(8,128)(2,1)}, u32[]{:S(2)}) copy-start(bf16[16,16,1024]{2,1,0:T(8,128)(2,1)} %param.22) | copy-start | bytes 1572868
  3.8 16.1 %collective-permute-start.1 = (bf16[2,64,1024]{2,1,0:T(8,128)(2,1)S(1)}, bf16[2,64,1024]{2,1,0:T(8,128)(2,1)S(1)}, u32[]{:S(2)}, u32[]{:S(2)}) collective-permute-start(bf16[2,64,1024]{2,1,0:T(8,128)(2,1)S(1)} %pad_maximum_fusion.3), channel_id=1, source_target_pairs={{0,15},{1,0},{2,1},{3,2},{4,3},{5,4},{6,5},{7,6},{8,7},{9,8},{10,9... | collective-permute-start | bytes 786440 | tf_op jit(solution)/shard_map/ppermute | solution.py:273
  5.4 24.9 %collective-permute-start.4 = (bf16[2,64,1024]{2,1,0:T(8,128)(2,1)S(1)}, bf16[2,64,1024]{2,1,0:T(8,128)(2,1)S(1)}, u32[]{:S(2)}, u32[]{:S(2)}) collective-permute-start(bf16[2,64,1024]{2,1,0:T(8,128)(2,1)S(1)} %maximum_select_fusion), channel_id=1, source_target_pairs={{0,8},{1,9},{2,10},{3,11},{4,12},{5,13},{6,14},{7,15},{8,0},{9,1},... | collective-permute-start | bytes 786440 | tf_op jit(solution)/shard_map/ppermute | solution.py:276
  13.6 0.7 copy-start.8
  15.8 0.7 copy-start.12
  18.3 1.3 %copy-start.9 = (s32[96]{0:T(128)S(1)}, s32[96]{0:T(128)}, u32[]{:S(2)}) copy-start(s32[96]{0:T(128)} %constant.135.clone) | copy-start | bytes 1156
  18.3 1.3 %copy-start.10 = (s32[96]{0:T(128)S(1)}, s32[96]{0:T(128)}, u32[]{:S(2)}) copy-start(s32[96]{0:T(128)} %constant.136.clone) | copy-start | bytes 1156
  18.4 1.3 %copy-start.11 = (s32[96]{0:T(128)S(1)}, s32[96]{0:T(128)}, u32[]{:S(2)}) copy-start(s32[96]{0:T(128)} %constant.137.clone) | copy-start | bytes 1156
  19.9 0.7 copy-start.6
  19.9 0.8 copy-start.7
  20.7 12.2 %collective-permute-start.5 = (bf16[2,32,1024]{2,1,0:T(8,128)(2,1)S(1)}, bf16[2,32,1024]{2,1,0:T(8,128)(2,1)S(1)}, u32[]{:S(2)}, u32[]{:S(2)}) collective-permute-start(bf16[2,32,1024]{2,1,0:T(8,128)(2,1)S(1)} %maximum_select_fusion.1), channel_id=1, source_target_pairs={{0,8},{1,9},{2,10},{3,11},{4,12},{5,13},{6,14},{7,15},{8,0},{9,1},... | collective-permute-start | bytes 393224 | tf_op jit(solution)/shard_map/ppermute | solution.py:284
  25.7 8.9 %collective-permute-start.3 = (bf16[2,96,1024]{2,1,0:T(8,128)(2,1)S(1)}, bf16[2,96,1024]{2,1,0:T(8,128)(2,1)S(1)}, u32[]{:S(2)}, u32[]{:S(2)}) collective-permute-start(bf16[2,96,1024]{2,1,0:T(8,128)(2,1)S(1)} %pad_maximum_fusion.1), channel_id=1, source_target_pairs={{16,0},{17,1},{18,2},{19,3},{20,4},{21,5},{22,6},{23,7},{24,8},{25... | collective-permute-start | bytes 1179656 | tf_op jit(solution)/shard_map/ppermute | solution.py:283
  27.0 7.6 %collective-permute-start.2 = (bf16[2,96,1024]{2,1,0:T(8,128)(2,1)S(1)}, bf16[2,96,1024]{2,1,0:T(8,128)(2,1)S(1)}, u32[]{:S(2)}, u32[]{:S(2)}) collective-permute-start(bf16[2,96,1024]{2,1,0:T(8,128)(2,1)S(1)} %pad_maximum_fusion), channel_id=1, source_target_pairs={{0,16},{1,17},{2,18},{3,19},{4,20},{5,21},{6,22},{7,23},{8,24},{9,... | collective-permute-start | bytes 1179656 | tf_op jit(solution)/shard_map/ppermute | solution.py:282
  34.6 0.7 copy-start.13
  34.6 0.9 %copy-start.14 = (bf16[2,96,1024]{2,1,0:T(8,128)(2,1)}, bf16[2,96,1024]{2,1,0:T(8,128)(2,1)S(1)}, u32[]{:S(2)}) copy-start(bf16[2,96,1024]{2,1,0:T(8,128)(2,1)S(1)} %collective-permute-done.2.refs_4_) | copy-start | bytes 1179652
  49.6 12.4 %collective-permute-start.6 = (bf16[2,32,1024]{2,1,0:T(8,128)(2,1)}, bf16[2,32,1024]{2,1,0:T(8,128)(2,1)S(1)}, u32[]{:S(2)}, u32[]{:S(2)}) collective-permute-start(bf16[2,32,1024]{2,1,0:T(8,128)(2,1)} %get-tuple-element.18), channel_id=1, source_target_pairs={{0,8},{1,9},{2,10},{3,11},{4,12},{5,13},{6,14},{7,15},{8,0},{9,1},... | collective-permute-start | bytes 393224 | tf_op jit(solution)/shard_map/ppermute | solution.py:298
  54.5 15.2 %collective-permute-start.8 = (bf16[2,64,1024]{2,1,0:T(8,128)(2,1)}, bf16[2,64,1024]{2,1,0:T(8,128)(2,1)S(1)}, u32[]{:S(2)}, u32[]{:S(2)}) collective-permute-start(bf16[2,64,1024]{2,1,0:T(8,128)(2,1)} %get-tuple-element.20), channel_id=1, source_target_pairs={{0,8},{1,9},{2,10},{3,11},{4,12},{5,13},{6,14},{7,15},{8,0},{9,1},... | collective-permute-start | bytes 786440 | tf_op jit(solution)/shard_map/ppermute | solution.py:319
  59.3 11.9 %collective-permute-start.7 = (bf16[2,96,1024]{2,1,0:T(8,128)(2,1)}, bf16[2,96,1024]{2,1,0:T(8,128)(2,1)S(1)}, u32[]{:S(2)}, u32[]{:S(2)}) collective-permute-start(bf16[2,96,1024]{2,1,0:T(8,128)(2,1)} %get-tuple-element.19), channel_id=1, source_target_pairs={{0,16},{1,17},{2,18},{3,19},{4,20},{5,21},{6,22},{7,23},{8,24},{9,... | collective-permute-start | bytes 1179656 | tf_op jit(solution)/shard_map/ppermute | solution.py:297
  60.7 10.6 %collective-permute-start.9 = (bf16[2,96,1024]{2,1,0:T(8,128)(2,1)}, bf16[2,96,1024]{2,1,0:T(8,128)(2,1)S(1)}, u32[]{:S(2)}, u32[]{:S(2)}) collective-permute-start(bf16[2,96,1024]{2,1,0:T(8,128)(2,1)} %get-tuple-element.21), channel_id=1, source_target_pairs={{16,0},{17,1},{18,2},{19,3},{20,4},{21,5},{22,6},{23,7},{24,8},{25... | collective-permute-start | bytes 1179656 | tf_op jit(solution)/shard_map/ppermute | solution.py:296
  71.5 1.0 %copy-start.5 = (f32[2,64,1024]{2,1,0:T(8,128)S(1)}, f32[2,64,1024]{2,1,0:T(8,128)}, u32[]{:S(2)}) copy-start(f32[2,64,1024]{2,1,0:T(8,128)} %get-tuple-element.22) | copy-start | bytes 1572868
  72.6 1.0 %copy-start.4 = (f32[2,64,1024]{2,1,0:T(8,128)S(1)}, f32[2,64,1024]{2,1,0:T(8,128)}, u32[]{:S(2)}) copy-start(f32[2,64,1024]{2,1,0:T(8,128)} %get-tuple-element.23) | copy-start | bytes 1572868
  72.6 7.4 %collective-permute-start.10 = (bf16[2,64,1024]{2,1,0:T(8,128)(2,1)S(1)}, bf16[2,64,1024]{2,1,0:T(8,128)(2,1)S(1)}, u32[]{:S(2)}, u32[]{:S(2)}) collective-permute-start(bf16[2,64,1024]{2,1,0:T(8,128)(2,1)S(1)} %add_convert_fusion.3), channel_id=1, source_target_pairs={{0,1},{1,2},{2,3},{3,4},{4,5},{5,6},{6,7},{7,8},{8,9},{9,10},{10,1... | collective-permute-start | bytes 786440 | tf_op jit(solution)/shard_map/ppermute | solution.py:318
  73.7 9.1 %collective-permute-start.11 = (bf16[2,64,1024]{2,1,0:T(8,128)(2,1)S(1)}, bf16[2,64,1024]{2,1,0:T(8,128)(2,1)S(1)}, u32[]{:S(2)}, u32[]{:S(2)}) collective-permute-start(bf16[2,64,1024]{2,1,0:T(8,128)(2,1)S(1)} %add_convert_fusion.2), channel_id=1, source_target_pairs={{0,15},{1,0},{2,1},{3,2},{4,3},{5,4},{6,5},{7,6},{8,7},{9,8},{10,9... | collective-permute-start | bytes 786440 | tf_op jit(solution)/shard_map/ppermute | solution.py:317
  75.9 7.1 %copy-start.1 = (f32[256,1024]{1,0:T(8,128)S(1)}, f32[256,1024]{1,0:T(8,128)}, u32[]{:S(2)}) copy-start(f32[256,1024]{1,0:T(8,128)} %get-tuple-element.24) | copy-start | bytes 3145732
  83.0 1.4 %copy-start = (f32[256,1024]{1,0:T(8,128)S(1)}, f32[256,1024]{1,0:T(8,128)}, u32[]{:S(2)}) copy-start(f32[256,1024]{1,0:T(8,128)} %get-tuple-element.17) | copy-start | bytes 3145732
